TPU v7x, 32 devices: a whole 2x2x4 slice. The times are simulated.
32 devices in a mesh: ep: 16 (over z, y, x), tp: 2 (over core).
Axes of the slice: x: 2, y: 2, z: 4, core: 2. Of those that a mesh axis runs over, the one named last changes fastest.
Arguments:
- tokens: bfloat16 [2048, 1536], P('ep', 'tp'), may hold values from -0.29882812 to 0.29882812
- queries: bfloat16 [2048, 1536], P('ep')
- kv_cache: bfloat16 [16, 2, 96, 16, 512], P('ep', 'tp')
- page_table: int32 [64, 48], P('ep'), may hold values from 0 to 95, as said below
- query_lens: int32 [16, 4], P('ep'), may hold values from 1 to 80, 128 in all within a row
- past_lens: int32 [16, 4], P('ep'), may hold values from 0 to 688
- out_weight: bfloat16 [1536, 1536], P(None, 'tp')
- norm_gain: float32 [1536], P('tp'), may hold values from 0.1 to 1.9
- route_ids: int32 [2048, 4], P('ep'), may hold values from 0 to 7, all different within a row; in each aligned block of 128 rows (0 to 127, 128 to 255, ...) at most 128 rows name the same one
- route_weights: float32 [2048, 4], P('ep'), may hold values from 0.1 to 1
- gate_w: bfloat16 [16, 1536, 768], P('ep', None, 'tp'), as said below
- up_w: bfloat16 [16, 1536, 768], P('ep', None, 'tp'), as said below
- down_w: bfloat16 [16, 768, 1536], P('ep', 'tp'), as said below
- final_gain: float32 [1536], P('tp'), may hold values from 0.1 to 1.9
Outputs:
- normed_out: bfloat16 [2048, 1536], P('ep', 'tp')
Inputs may be any that keep to these rules, and one draw needn't show every extreme that they name: `page_table`: for each group and each t below 2, the entries over the group's 4 requests and all j with j mod 2 = t are distinct. `query_lens`: the 4 requests of a group have 128 rows together; in every group one request has exactly 80. `route_ids`: each row names 4 different experts; in each aligned block of 128 rows no expert is named by more than 128 rows, a bound that some block reaches. `gate_w`: slot s and slot s + 8 hold the same weights, those of expert s. `up_w`: slot s and slot s + 8 hold the same weights, those of expert s. `down_w`: slot s and slot s + 8 hold the same weights, those of expert s.
All inputs are finite; a program needn't handle non-finite values.
Results may differ from a plain program's by a relative error of at most 0.025.
Values may be sent and summed in bfloat16 or wider, within the bound.
No kernel may reach another device: no remote copies, remote signals or barrier semaphores. Data moves between devices by JAX's collectives and lax.ppermute only.
A program may use at most 64 MiB of HBM per device.

v0:
```python
import jax
import jax.numpy as jnp
from jax import lax
from jax.sharding import PartitionSpec as P

QUERY_HEADS = 12
KEY_VALUE_HEADS = 2
HEAD_SIZE = 128
PAGE_POSITIONS = 16


EPSILON = 1e-06


def merged(shard, axis, join):
    gathered = jax.tree.map(
        lambda a, kind: lax.all_gather(a.astype(kind), axis),
        shard,
        (jnp.bfloat16, jnp.bfloat16, jnp.bfloat16),
    )

    def take(source):
        return jax.tree.map(
            lambda a, own: lax.dynamic_index_in_dim(a, source, 0, False).astype(own.dtype),
            gathered,
            shard,
        )

    return lax.fori_loop(
        1, lax.axis_size(axis), lambda source, state: join(state, take(source)), take(0)
    )


def merge_parts(first, second):
    joint_max = jnp.maximum(first[0], second[0])
    scale_first = jnp.exp(first[0] - joint_max)
    scale_second = jnp.exp(second[0] - joint_max)
    return (
        joint_max,
        first[1] * scale_first + second[1] * scale_second,
        first[2] * scale_first[..., None] + second[2] * scale_second[..., None],
    )


def shards(
    tokens,
    queries,
    kv_cache,
    page_table,
    query_lens,
    past_lens,
    out_weight,
    norm_gain,
    route_ids,
    route_weights,
    gate_w,
    up_w,
    down_w,
    final_gain,
):
    tp_index = lax.axis_index("tp")
    tp_count = lax.axis_size("tp")
    ep_count = lax.axis_size("ep")
    count_of_rows, feat_part = tokens.shape
    full_width = feat_part * tp_count
    local_groups = query_lens.shape[0]
    req_count = query_lens.shape[1]
    group_rows = count_of_rows // local_groups
    head_groups = QUERY_HEADS // KEY_VALUE_HEADS
    per_device = page_table.shape[1] // tp_count

    def one_group(local):
        query_count = lax.dynamic_index_in_dim(query_lens, local, 0, keepdims=False)
        past_count = lax.dynamic_index_in_dim(past_lens, local, 0, keepdims=False)
        row_ends = jnp.cumsum(query_count)
        row_starts = row_ends - query_count
        row_iota = jnp.arange(group_rows, dtype=jnp.int32)
        row_req = jnp.sum((row_iota[:, None] >= row_ends[None, :]).astype(jnp.int32), axis=1)
        req_onehot = (row_req[:, None] == jnp.arange(req_count, dtype=jnp.int32)[None, :]).astype(
            jnp.int32
        )
        row_pos = row_iota + jnp.sum(req_onehot * (past_count - row_starts)[None, :], axis=1)
        local_table = lax.dynamic_index_in_dim(
            page_table.reshape(req_count, per_device, tp_count), tp_index, axis=2, keepdims=False
        )
        group_pages = lax.dynamic_index_in_dim(kv_cache, local, 0, keepdims=False)[0]
        page_row_block = group_pages[local_table.reshape(-1)]
        key_count_total = page_row_block.shape[0] * PAGE_POSITIONS
        flattened_cache = page_row_block.reshape(key_count_total, 2 * KEY_VALUE_HEADS * HEAD_SIZE)
        gathered_keys = flattened_cache[:, : KEY_VALUE_HEADS * HEAD_SIZE].reshape(
            key_count_total, KEY_VALUE_HEADS, HEAD_SIZE
        )
        gathered_values = flattened_cache[:, KEY_VALUE_HEADS * HEAD_SIZE :].reshape(
            key_count_total, KEY_VALUE_HEADS, HEAD_SIZE
        )
        key_iota = jnp.arange(key_count_total, dtype=jnp.int32)
        key_req = key_iota // (per_device * PAGE_POSITIONS)
        within = key_iota % (per_device * PAGE_POSITIONS)
        key_pos = (
            within // PAGE_POSITIONS * tp_count + tp_index
        ) * PAGE_POSITIONS + within % PAGE_POSITIONS
        allowed = (row_req[:, None] == key_req[None, :]) & (key_pos[None, :] <= row_pos[:, None])
        query_head_rows = queries.reshape(group_rows, KEY_VALUE_HEADS, head_groups, HEAD_SIZE)
        scores = jnp.einsum(
            "rkgd,lkd->rkgl", query_head_rows, gathered_keys, preferred_element_type=jnp.float32
        ) * HEAD_SIZE ** (-0.5)
        score_mask = allowed[:, None, None, :]
        part_max = jnp.max(jnp.where(score_mask, scores, -1e30), axis=-1)
        soft = jnp.where(score_mask, jnp.exp(scores - part_max[..., None]), 0.0)
        part_sum = jnp.sum(soft, axis=-1)
        part_weighted = jnp.einsum(
            "rkgl,lkd->rkgd",
            soft.astype(jnp.bfloat16),
            gathered_values,
            preferred_element_type=jnp.float32,
        )
        return (part_max, part_sum, part_weighted)

    row_max, row_sum, weighted = lax.map(one_group, jnp.arange(local_groups, dtype=jnp.int32))
    row_max = row_max.reshape(count_of_rows, KEY_VALUE_HEADS, head_groups)
    row_sum = row_sum.reshape(count_of_rows, KEY_VALUE_HEADS, head_groups)
    weighted = weighted.reshape(count_of_rows, KEY_VALUE_HEADS, head_groups, HEAD_SIZE)
    row_max, row_sum, weighted = merged((row_max, row_sum, weighted), "tp", merge_parts)
    attended = (
        (weighted / row_sum[..., None])
        .reshape(count_of_rows, QUERY_HEADS * HEAD_SIZE)
        .astype(jnp.bfloat16)
    )
    resid = tokens.astype(jnp.float32) + jnp.dot(
        attended, out_weight, preferred_element_type=jnp.float32
    )
    mid_squares = lax.psum(jnp.sum(resid * resid, axis=1), "tp")
    normed = (resid * lax.rsqrt(mid_squares / full_width + EPSILON)[:, None] * norm_gain).astype(
        jnp.bfloat16
    )
    top_count = route_ids.shape[1]
    slots_local = gate_w.shape[0]
    slots_total = slots_local * ep_count
    experts = slots_total // 2
    capacity = count_of_rows * top_count // experts
    flat_ids = route_ids.reshape(-1)
    assign_count = flat_ids.shape[0]
    expert_onehot = (flat_ids[:, None] == jnp.arange(experts, dtype=jnp.int32)[None, :]).astype(
        jnp.int32
    )
    expert_rank = jnp.sum(
        (jnp.cumsum(expert_onehot, axis=0) - expert_onehot) * expert_onehot, axis=1
    )
    slot_ids = expert_rank % 2 * experts + flat_ids
    target = slot_ids * capacity + expert_rank // 2
    buffer_len = slots_total * capacity
    source = (
        jnp.full((buffer_len,), assign_count, jnp.int32)
        .at[target]
        .set(jnp.arange(assign_count, dtype=jnp.int32))
    )
    filled = source < assign_count
    source_row = jnp.minimum(source, assign_count - 1) // top_count
    full_rows = lax.all_gather(normed, "tp", axis=1, tiled=True)
    outgoing = jnp.where(filled[:, None], full_rows[source_row], jnp.zeros((), jnp.bfloat16))
    arrived = lax.all_to_all(
        outgoing.reshape(ep_count, slots_local * capacity, full_width),
        "ep",
        split_axis=0,
        concat_axis=0,
        tiled=True,
    )
    inputs = (
        arrived.reshape(ep_count, slots_local, capacity, full_width)
        .transpose(1, 0, 2, 3)
        .reshape(slots_local, ep_count * capacity, full_width)
    )
    gate_value = jnp.einsum("snd,sdf->snf", inputs, gate_w, preferred_element_type=jnp.float32)
    up_value = jnp.einsum("snd,sdf->snf", inputs, up_w, preferred_element_type=jnp.float32)
    hidden = (jnp.maximum(gate_value, 0.0) * up_value).astype(jnp.bfloat16)
    partial_value = jnp.einsum(
        "snf,sfd->snd", hidden, down_w, preferred_element_type=jnp.float32
    ).astype(jnp.bfloat16)
    summed = lax.psum_scatter(
        partial_value.astype(jnp.float32).astype(jnp.bfloat16),
        "tp",
        scatter_dimension=2,
        tiled=True,
    ).astype(jnp.float32)
    summed = (
        summed.reshape(slots_local, ep_count, capacity, feat_part)
        .transpose(1, 0, 2, 3)
        .reshape(ep_count, slots_local * capacity, feat_part)
    )
    returned = (
        lax.all_to_all(summed.astype(jnp.bfloat16), "ep", split_axis=0, concat_axis=0, tiled=True)
        .astype(summed.dtype)
        .reshape(buffer_len, feat_part)
    )
    gathered = returned[target].reshape(count_of_rows, top_count, feat_part)
    branch = jnp.sum(route_weights[:, :, None] * gathered, axis=1)
    mixed_rows = resid + branch
    out_squares = lax.psum(jnp.sum(mixed_rows * mixed_rows, axis=1), "tp")
    return (
        mixed_rows * lax.rsqrt(out_squares / full_width + EPSILON)[:, None] * final_gain
    ).astype(jnp.bfloat16)


def solution(mesh):
    placed = (
        P("ep", "tp"),
        P("ep", None),
        P("ep", "tp", None, None, None),
        P("ep", None),
        P("ep", None),
        P("ep", None),
        P(None, "tp"),
        P("tp"),
        P("ep", None),
        P("ep", None),
        P("ep", None, "tp"),
        P("ep", None, "tp"),
        P("ep", "tp", None),
        P("tp"),
    )
    return jax.shard_map(
        shards, mesh=mesh, in_specs=placed, out_specs=P("ep", "tp"), check_vma=False
    )
```

profile of v0, /device:TPU:0, one launch (start us, length us, event | category | flops | bytes accessed | tf_op | source)
XLA Modules:
  0.0 218.0 jit_solution(15813910761181112754)
XLA Ops:
  9.4 2.4 %scatter_custom_fusion = s32[1024]{0:T(1024)S(1)} fusion(s32[512]{0:T(512)S(1)} %bitcast.96, s32[512]{0:T(512)S(1)} %iota.39, s32[]{:T(128)} %constant.175.clone.1), kind=kCustom, calls=%fused_computation.94 | custom fusion | bytes 4100 | tf_op jit(solution)/shard_map/scatter | solution.py:155
  13.9 3.3 %gather_fusion = bf16[96,16,512]{2,1,0:T(8,128)(2,1)} fusion(bf16[96,16,512]{2,1,0:T(8,128)(2,1)} %bitcast.92, s32[1024]{0:T(1024)S(1)} %pad_clamp_fusion.1), kind=kCustom, calls=%fused_computation | custom fusion | bytes 3146112 | tf_op jit(solution)/shard_map/while/body/eval_jaxpr/gather | solution.py:87
  17.3 2.4 %fusion.58 = (bf16[1536,256]{1,0:T(8,128)(2,1)}, bf16[1536,256]{1,0:T(8,128)(2,1)S(1)}) fusion(bf16[1536,512]{1,0:T(8,128)(2,1)} %bitcast.86), kind=kLoop, calls=%fused_computation.111 | loop fusion | bytes 3145728 | tf_op jit(solution)/shard_map/while/body/eval_jaxpr/slice | solution.py:90
  27.7 1.9 fusion.3
  29.6 2.0 fusion.12
  31.6 2.4 %all-gather = bf16[256,2,6,128]{0,3,2,1:T(8,128)(2,1)S(1)} all-gather(bf16[128,2,6,128]{0,3,2,1:T(8,128)(2,1)S(1)} %fusion.12), channel_id=2, replica_groups=mesh['ep'=16,'tp'=2] {'tp'}, dimensions={0}, use_global_device_ids=true | all-gather | bytes 1179648 | tf_op jit(solution)/shard_map/all_gather | solution.py:17
  34.0 2.0 all-gather.1
  36.0 1.8 all-gather.2
  38.6 2.5 %psum.14 = f32[128]{0:T(128)S(1)} all-reduce(f32[128]{0:T(128)S(1)} %get-tuple-element.58), channel_id=1, replica_groups=mesh['ep'=16,'tp'=2] {'tp'}, use_global_device_ids=true, to_apply=%region_10.11 | all-reduce | flops 128 | bytes 1024 | tf_op jit(solution)/shard_map/psum | solution.py:132
  41.2 2.1 all_gather.18
  43.4 5.6 %gather_fusion.1 = bf16[1024,1536]{1,0:T(8,128)(2,1)} fusion(bf16[128,1536]{1,0:T(8,128)(2,1)S(1)} %all_gather.18, s32[1024]{0:T(1024)S(1)} %copy-done.4), kind=kCustom, calls=%fused_computation.1 | custom fusion | bytes 6295552 | tf_op jit(solution)/shard_map/gather | solution.py:160
  49.0 2.2 broadcast_select_fusion
  51.2 79.7 %all_to_all.10 = bf16[16,64,1536]{2,1,0:T(8,128)(2,1)S(1)} all-to-all(bf16[16,64,1536]{2,1,0:T(8,128)(2,1)S(1)} %broadcast_select_fusion), channel_id=1, replica_groups=mesh['ep'=16,'tp'=2] {'ep'}, dimensions={0} | all-to-all | bytes 6291456 | tf_op jit(solution)/shard_map/all_to_all | solution.py:161
  131.0 1.7 copy-done.1
  132.7 2.9 %fusion.17 = f32[1024,384]{1,0:T(8,128)} fusion(bf16[1024,1536]{1,0:T(8,128)(2,1)S(1)} %bitcast.88, bf16[1,1536,384]{2,1,0:T(8,128)(2,1)S(1)} %copy-done.14), kind=kOutput, calls=%fused_computation.24 | convolution fusion | flops 1207959552 | bytes 5898240 | tf_op jit(solution)/shard_map/snd,sdf->snf/dot_general | solution.py:173
  135.6 8.1 %fusion.8 = bf16[1,1024,1536]{2,1,0:T(8,128)(2,1)} fusion(bf16[1,384,1536]{2,1,0:T(8,128)(2,1)} %param.26, f32[1024,384]{1,0:T(8,128)} %fusion.17, bf16[1024,1536]{1,0:T(8,128)(2,1)} %bitcast.89, bf16[1,1536,384]{2,1,0:T(8,128)(2,1)} %param.25), kind=kOutput, calls=%fused_computation.14 | convolution fusion | flops 2418671616 | bytes 10223616 | tf_op jit(solution)/shard_map/snf,sfd->snd/dot_general | solution.py:176
  143.7 9.4 %reduce-scatter.2.cloned.1.call-done = bf16[1,1024,768]{2,1,0:T(8,128)(2,1)} async-done(((bf16[1,1024,1536]{2,1,0:T(8,128)(2,1)}), bf16[1,1024,768]{2,1,0:T(8,128)(2,1)}) %reduce-scatter.2.cloned.1.call-update) | async-done | bytes 1572880 | tf_op jit(solution)/shard_map/reduce_scatter | solution.py:179
  153.1 6.8 %all-to-all-start.1 = ((bf16[16,64,768]{2,1,0:T(8,128)(2,1)}), bf16[16,64,768]{2,1,0:T(8,128)(2,1)}, u32[]{:S(2)}, u32[]{:S(2)}) async-start(bf16[16,64,768]{2,1,0:T(8,128)(2,1)} %bitcast.91), calls=%async_computation.2 | async-start | bytes 3145728 | tf_op jit(solution)/shard_map/all_to_all | solution.py:191
  160.1 34.2 %all-to-all-done.1 = bf16[16,64,768]{2,1,0:T(8,128)(2,1)} async-done(((bf16[16,64,768]{2,1,0:T(8,128)(2,1)}), bf16[16,64,768]{2,1,0:T(8,128)(2,1)}, u32[]{:S(2)}, u32[]{:S(2)}) %all-to-all-start.1) | async-done | bytes 1572896 | tf_op jit(solution)/shard_map/all_to_all | solution.py:191
  194.2 3.3 %bitcast_convert_fusion = f32[1024,768]{1,0:T(8,128)} fusion(bf16[16,64,768]{2,1,0:T(8,128)(2,1)} %all-to-all-done.1), kind=kLoop, calls=%fused_computation.16 | loop fusion | flops 786432 | bytes 4718592 | tf_op jit(solution)/shard_map/reshape | solution.py:193
  197.5 5.1 %gather_fusion.2 = f32[512,768]{1,0:T(8,128)} fusion(f32[1024,768]{1,0:T(8,128)} %bitcast_convert_fusion, s32[1024]{0:T(1024)S(1)} %pad_clamp_fusion), kind=kCustom, calls=%fused_computation.2 | custom fusion | bytes 3147776 | tf_op jit(solution)/shard_map/gather | solution.py:195
  202.6 2.7 %reshape.428 = f32[128,4,768]{2,1,0:T(4,128)} reshape(f32[512,768]{1,0:T(8,128)} %gather_fusion.2) | data formatting | bytes 3145728 | tf_op jit(solution)/shard_map/reshape | solution.py:195
  205.3 2.4 %multiply_reduce_fusion = f32[128,768]{1,0:T(8,128)S(1)} fusion(f32[128,4,768]{2,1,0:T(4,128)} %reshape.428, f32[128,4]{1,0:T(8,128)S(1)} %copy.51), kind=kLoop, calls=%fused_computation.17 | loop fusion | flops 688128 | bytes 1968128 | tf_op jit(solution)/shard_map/reduce_sum | solution.py:196
  207.9 2.5 %psum.15 = f32[128]{0:T(128)S(1)} all-reduce(f32[128]{0:T(128)S(1)} %get-tuple-element.41), channel_id=1, replica_groups=mesh['ep'=16,'tp'=2] {'tp'}, use_global_device_ids=true, to_apply=%region_14.15 | all-reduce | flops 128 | bytes 1024 | tf_op jit(solution)/shard_map/psum | solution.py:198
  (74 shorter events, 15.0 us)
Async XLA Ops:
  6.5 31.5 %copy-start = (bf16[1536,768]{1,0:T(8,128)(2,1)S(1)}, bf16[1536,768]{1,0:T(8,128)(2,1)}, u32[]{:S(2)}) copy-start(bf16[1536,768]{1,0:T(8,128)(2,1)} %param.20) | copy-start | bytes 7077892
  6.5 146.6 %reduce-scatter.2.cloned.1.call-start = ((), (), s32[]{:S(2)}) async-start(), calls=%async_computation.3 | async-start | bytes 4718592 | tf_op jit(solution)/shard_map/reduce_scatter | solution.py:179
  9.4 3.1 %copy-start.5 = (s32[512,1]{0,1:T(1,128)}, s32[512,1]{0,1:T(1,128)S(1)}, u32[]{:S(2)}) copy-start(s32[512,1]{0,1:T(1,128)S(1)} %compare_select_fusion) | copy-start | bytes 6148
  17.3 3.5 %copy-start.13 = (s32[1,4]{1,0:T(1,128)S(1)}, s32[1,4]{1,0:T(1,128)}, u32[]{:S(2)}) copy-start(s32[1,4]{1,0:T(1,128)} %param.18) | copy-start | bytes 52
  17.3 3.7 %copy-start.12 = (s32[1,4]{1,0:T(1,128)S(1)}, s32[1,4]{1,0:T(1,128)}, u32[]{:S(2)}) copy-start(s32[1,4]{1,0:T(1,128)} %param.19) | copy-start | bytes 52
  21.1 0.7 copy-start.11
  27.7 1.9 copy-start.2
  29.6 8.4 %copy-start.3 = (bf16[128,768]{1,0:T(8,128)(2,1)S(1)}, bf16[128,768]{1,0:T(8,128)(2,1)}, u32[]{:S(2)}) copy-start(bf16[128,768]{1,0:T(8,128)(2,1)} %param.14) | copy-start | bytes 589828
  31.6 9.5 %copy-start.7 = (f32[768]{0:T(1024)S(1)}, f32[768]{0:T(1024)}, u32[]{:S(2)}) copy-start(f32[768]{0:T(1024)} %param.21) | copy-start | bytes 9220
  34.0 9.3 %copy-start.9 = (pred[1024]{0:T(1024)(128)(4,1)S(1)}, pred[1024]{0:T(1024)(128)(4,1)}, u32[]{:S(2)}) copy-start(pred[1024]{0:T(1024)(128)(4,1)} %broadcast_compare_fusion) | copy-start | bytes 3076
  34.0 9.4 %copy-start.4 = (s32[1024]{0:T(1024)S(1)}, s32[1024]{0:T(1024)}, u32[]{:S(2)}) copy-start(s32[1024]{0:T(1024)} %fusion.46) | copy-start | bytes 12292
  51.2 81.5 %copy-start.14 = (bf16[1,1536,384]{2,1,0:T(8,128)(2,1)S(1)}, bf16[1,1536,384]{2,1,0:T(8,128)(2,1)}, u32[]{:S(2)}) copy-start(bf16[1,1536,384]{2,1,0:T(8,128)(2,1)} %param.24) | copy-start | bytes 3538948
  131.0 1.7 copy-start.1
  143.7 16.2 %copy-start.10 = (f32[128,4]{0,1:T(4,128)S(1)}, f32[128,4]{0,1:T(4,128)}, u32[]{:S(2)}) copy-start(f32[128,4]{0,1:T(4,128)} %param.23) | copy-start | bytes 6148
  143.7 16.3 %copy-start.6 = (s32[512,1]{0,1:T(1,128)S(1)}, s32[512,1]{0,1:T(1,128)}, u32[]{:S(2)}) copy-start(s32[512,1]{0,1:T(1,128)} %copy-done.5) | copy-start | bytes 6148
  153.1 41.1 %all-to-all-start.1 = ((bf16[16,64,768]{2,1,0:T(8,128)(2,1)}), bf16[16,64,768]{2,1,0:T(8,128)(2,1)}, u32[]{:S(2)}, u32[]{:S(2)}) async-start(bf16[16,64,768]{2,1,0:T(8,128)(2,1)} %bitcast.91), calls=%async_computation.2 | async-start | bytes 3145728 | tf_op jit(solution)/shard_map/all_to_all | solution.py:191
  202.6 7.8 %copy-start.8 = (f32[768]{0:T(1024)S(1)}, f32[768]{0:T(1024)}, u32[]{:S(2)}) copy-start(f32[768]{0:T(1024)} %param.27) | copy-start | bytes 9220
Sparse Core Ops, SparseCore 0:
  143.8 9.2 reduce-scatter.1
where the time goes:
time: 221 us; the launch traced here: 218 us
  blocking collectives  93 us (42%)
  waiting for transfers between devices  43.6 us (20%)
  local copies, waits for them, and re-layouts  29.7 us (13%)
  other arithmetic  16.1 us (7%)
  matrix products  15.2 us (7%)
  between operations  13.6 us (6%)
  starting transfers between devices  6.82 us (3%)
    all_to_all x1, blocking collectives, shards(): lax.all_to_all(outgoing.reshape(ep_count, slots_local * capacity, full_wi...  79.7 us
    all_to_all x1, waiting for transfers between devices, shards(): lax.all_to_all(summed.astype(jnp.bfloat16), 'ep', split_axis=0, concat_ax...  34.2 us
    reduce_scatter x1, waiting for transfers between devices, shards(): lax.psum_scatter(partial_value.astype(jnp.float32).astype(jnp.bfloat16),...  9.37 us
    dot_general x1, matrix products, shards(): jnp.einsum('snf,sfd->snd', hidden, down_w, preferred_element_type=jnp.flo...  8.11 us
    all_to_all x1, starting transfers between devices, shards(): lax.all_to_all(summed.astype(jnp.bfloat16), 'ep', split_axis=0, concat_ax...  6.81 us
    all_gather x3, blocking collectives, merged(): lax.all_gather(a.astype(kind), axis)  6.2 us
    gather x1, local copies, waits for them, and re-layouts, shards(): full_rows[source_row]  5.61 us
    gather x1, local copies, waits for them, and re-layouts, shards(): gathered = returned[target].reshape(count_of_rows, top_count, feat_part)  5.07 us
  transfers between devices with their start and end apart: 2, of which 2 were waited for; matrix products, arithmetic and copies ran while one was open for 0% of the time, Pallas kernels for 0%

commit v1 on v0

--- a/solution.py
+++ b/solution.py
@@ -1,7 +1,7 @@
 import jax
 import jax.numpy as jnp
 from jax import lax
-from jax.sharding import PartitionSpec as P
+from jax.sharding import Mesh, NamedSharding, PartitionSpec as P
 
 QUERY_HEADS = 12
 KEY_VALUE_HEADS = 2
@@ -60,7 +60,6 @@
 ):
     tp_index = lax.axis_index("tp")
     tp_count = lax.axis_size("tp")
-    ep_count = lax.axis_size("ep")
     count_of_rows, feat_part = tokens.shape
     full_width = feat_part * tp_count
     local_groups = query_lens.shape[0]
@@ -134,66 +133,58 @@
         jnp.bfloat16
     )
     top_count = route_ids.shape[1]
-    slots_local = gate_w.shape[0]
-    slots_total = slots_local * ep_count
-    experts = slots_total // 2
-    capacity = count_of_rows * top_count // experts
+    half_count = lax.axis_size("el")
+    experts = half_count
+    capacity = count_of_rows * top_count * 2 // experts
+    buffer_len = experts * capacity
     flat_ids = route_ids.reshape(-1)
-    assign_count = flat_ids.shape[0]
     expert_onehot = (flat_ids[:, None] == jnp.arange(experts, dtype=jnp.int32)[None, :]).astype(
         jnp.int32
     )
     expert_rank = jnp.sum(
         (jnp.cumsum(expert_onehot, axis=0) - expert_onehot) * expert_onehot, axis=1
     )
-    slot_ids = expert_rank % 2 * experts + flat_ids
-    target = slot_ids * capacity + expert_rank // 2
-    buffer_len = slots_total * capacity
-    source = (
-        jnp.full((buffer_len,), assign_count, jnp.int32)
-        .at[target]
-        .set(jnp.arange(assign_count, dtype=jnp.int32))
-    )
-    filled = source < assign_count
-    source_row = jnp.minimum(source, assign_count - 1) // top_count
-    full_rows = lax.all_gather(normed, "tp", axis=1, tiled=True)
-    outgoing = jnp.where(filled[:, None], full_rows[source_row], jnp.zeros((), jnp.bfloat16))
+    target = (flat_ids * capacity + expert_rank).reshape(count_of_rows, top_count)
+    slot_iota = jnp.arange(buffer_len, dtype=jnp.int32)
+    hits = target[None, :, :] == slot_iota[:, None, None]
+    dispatch = jnp.any(hits, axis=2).astype(jnp.bfloat16)
+    outgoing = jnp.dot(dispatch, normed, preferred_element_type=jnp.float32).astype(jnp.bfloat16)
     arrived = lax.all_to_all(
-        outgoing.reshape(ep_count, slots_local * capacity, full_width),
-        "ep",
+        outgoing.reshape(experts, capacity, feat_part),
+        "el",
         split_axis=0,
         concat_axis=0,
         tiled=True,
     )
-    inputs = (
-        arrived.reshape(ep_count, slots_local, capacity, full_width)
-        .transpose(1, 0, 2, 3)
-        .reshape(slots_local, ep_count * capacity, full_width)
-    )
-    gate_value = jnp.einsum("snd,sdf->snf", inputs, gate_w, preferred_element_type=jnp.float32)
-    up_value = jnp.einsum("snd,sdf->snf", inputs, up_w, preferred_element_type=jnp.float32)
+    inputs = lax.all_gather(arrived, "tp", axis=2, tiled=True).reshape(buffer_len, full_width)
+    gate_value = jnp.dot(inputs, gate_w[0], preferred_element_type=jnp.float32)
+    up_value = jnp.dot(inputs, up_w[0], preferred_element_type=jnp.float32)
     hidden = (jnp.maximum(gate_value, 0.0) * up_value).astype(jnp.bfloat16)
-    partial_value = jnp.einsum(
-        "snf,sfd->snd", hidden, down_w, preferred_element_type=jnp.float32
-    ).astype(jnp.bfloat16)
-    summed = lax.psum_scatter(
-        partial_value.astype(jnp.float32).astype(jnp.bfloat16),
-        "tp",
-        scatter_dimension=2,
+    partial_value = jnp.dot(hidden, down_w[0], preferred_element_type=jnp.float32).astype(
+        jnp.bfloat16
+    )
+    summed = lax.psum_scatter(partial_value, "tp", scatter_dimension=1, tiled=True)
+    returned = lax.all_to_all(
+        summed.reshape(experts, capacity, feat_part),
+        "el",
+        split_axis=0,
+        concat_axis=0,
         tiled=True,
-    ).astype(jnp.float32)
-    summed = (
-        summed.reshape(slots_local, ep_count, capacity, feat_part)
-        .transpose(1, 0, 2, 3)
-        .reshape(ep_count, slots_local * capacity, feat_part)
-    )
-    returned = (
-        lax.all_to_all(summed.astype(jnp.bfloat16), "ep", split_axis=0, concat_axis=0, tiled=True)
-        .astype(summed.dtype)
-        .reshape(buffer_len, feat_part)
-    )
-    gathered = returned[target].reshape(count_of_rows, top_count, feat_part)
-    branch = jnp.sum(route_weights[:, :, None] * gathered, axis=1)
+    ).reshape(buffer_len, feat_part)
+    combine = jnp.sum(
+        jnp.where(
+            target[:, :, None] == slot_iota[None, None, :],
+            route_weights[:, :, None],
+            0.0,
+        ),
+        axis=1,
+    )
+    branch = jnp.dot(
+        combine,
+        returned.astype(jnp.float32),
+        precision=lax.Precision.HIGHEST,
+        preferred_element_type=jnp.float32,
+    )
     mixed_rows = resid + branch
     out_squares = lax.psum(jnp.sum(mixed_rows * mixed_rows, axis=1), "tp")
     return (
@@ -202,22 +193,31 @@
 
 
 def solution(mesh):
+    ep_count, tp_count = mesh.devices.shape
+    halves = Mesh(mesh.devices.reshape(2, ep_count // 2, tp_count), ("eh", "el", "tp"))
+    ep = ("eh", "el")
     placed = (
-        P("ep", "tp"),
-        P("ep", None),
-        P("ep", "tp", None, None, None),
-        P("ep", None),
-        P("ep", None),
-        P("ep", None),
+        P(ep, "tp"),
+        P(ep, None),
+        P(ep, "tp", None, None, None),
+        P(ep, None),
+        P(ep, None),
+        P(ep, None),
         P(None, "tp"),
         P("tp"),
-        P("ep", None),
-        P("ep", None),
-        P("ep", None, "tp"),
-        P("ep", None, "tp"),
-        P("ep", "tp", None),
+        P(ep, None),
+        P(ep, None),
+        P(ep, None, "tp"),
+        P(ep, None, "tp"),
+        P(ep, "tp", None),
         P("tp"),
     )
-    return jax.shard_map(
-        shards, mesh=mesh, in_specs=placed, out_specs=P("ep", "tp"), check_vma=False
-    )
+    inner = jax.shard_map(
+        shards, mesh=halves, in_specs=placed, out_specs=P(ep, "tp"), check_vma=False
+    )
+    result_sharding = NamedSharding(mesh, P("ep", "tp"))
+
+    def run(*args):
+        return lax.with_sharding_constraint(inner(*args), result_sharding)
+
+    return run

time: 221 us -> 143 us (0.65); the launches traced: 218 us -> 143 us
  blocking collectives: 93 us -> 38.1 us
  local copies, waits for them, and re-layouts: 29.7 us -> 13.2 us
  other arithmetic: 16.1 us -> 8.44 us
  matrix products: 15.2 us -> 21.1 us
    all_to_all x1, blocking collectives: 79.7 us -> 27 us  [shards(): lax.all_to_all(outgoing.reshape(experts, capacity, feat_part), 'el', spli...]
    all_to_all x1, waiting for transfers between devices: 34.2 us -> 20.5 us  [shards(): lax.all_to_all(summed.reshape(experts, capacity, feat_part), 'el', split_...]
    all_gather x0 -> x1, waiting for transfers between devices: none -> 10.8 us  [shards(): lax.all_gather(arrived, 'tp', axis=2, tiled=True)]
    gather x2 -> x0, local copies, waits for them, and re-layouts: 10.7 us -> none  [the longest x1 5.61 us: shards(): full_rows[source_row]]
    dot_general x2 -> x4, matrix products: 11 us -> 16.9 us  [the longest x1 8.15 us: shards(): jnp.dot(hidden, down_w[0], preferred_element_type=jnp.float32)]
    reshape x1 -> x0, other arithmetic: 3.31 us -> none  [shards(): returned = lax.all_to_all(summed.astype(jnp.bfloat16), 'ep', split_axis=0...]
    reduce_scatter x1, waiting for transfers between devices: 9.37 us -> 12.2 us  [shards(): lax.psum_scatter(partial_value, 'tp', scatter_dimension=1, tiled=True)]
    reshape x2 -> x0, local copies, waits for them, and re-layouts: 2.83 us -> none  [the longest x1 2.72 us: shards(): gathered = returned[target].reshape(count_of_rows, top_count, feat_part)]
  transfers between devices with their start and end apart: 2 -> 3, of which waited for: 2 -> 3; matrix products, arithmetic and copies ran while one was open for 0% -> 0% of each run, Pallas kernels for 0% -> 0%
where the time goes in v1:
time: 143 us
  waiting for transfers between devices  43.5 us (30%)
  blocking collectives  38.1 us (27%)
  matrix products  21.1 us (15%)
  between operations  13.6 us (10%)
  local copies, waits for them, and re-layouts  13.2 us (9%)
  other arithmetic  8.44 us (6%)
  starting transfers between devices  5.03 us (4%)
    all_to_all x1, blocking collectives, shards(): lax.all_to_all(outgoing.reshape(experts, capacity, feat_part), 'el', spli...  27 us
    all_to_all x1, waiting for transfers between devices, shards(): lax.all_to_all(summed.reshape(experts, capacity, feat_part), 'el', split_...  20.5 us
    reduce_scatter x1, waiting for transfers between devices, shards(): lax.psum_scatter(partial_value, 'tp', scatter_dimension=1, tiled=True)  12.2 us
    all_gather x1, waiting for transfers between devices, shards(): lax.all_gather(arrived, 'tp', axis=2, tiled=True)  10.8 us
    dot_general x1, matrix products, shards(): jnp.dot(hidden, down_w[0], preferred_element_type=jnp.float32)  8.15 us
    all_gather x3, blocking collectives, merged(): lax.all_gather(a.astype(kind), axis)  6.21 us
    dot_general x1, matrix products, shards(): gate_value = jnp.dot(inputs, gate_w[0], preferred_element_type=jnp.float32)  5.14 us
    all_to_all x1, starting transfers between devices, shards(): lax.all_to_all(summed.reshape(experts, capacity, feat_part), 'el', split_...  4.81 us
  transfers between devices with their start and end apart: 3, of which 3 were waited for; matrix products, arithmetic and copies ran while one was open for 0% of the time, Pallas kernels for 0%

profile of v1, /device:TPU:0, one launch (start us, length us, event | category | flops | bytes accessed | tf_op | source)
XLA Modules:
  0.0 142.9 jit_solution(4452719247950277870)
XLA Ops:
  9.9 3.3 %gather_fusion = bf16[96,16,512]{2,1,0:T(8,128)(2,1)} fusion(bf16[96,16,512]{2,1,0:T(8,128)(2,1)} %bitcast.87, s32[1024]{0:T(1024)S(1)} %pad_clamp_fusion), kind=kCustom, calls=%fused_computation | custom fusion | bytes 3146112 | tf_op jit(solution)/shard_map/while/body/eval_jaxpr/gather | solution.py:86
  13.2 2.4 %fusion.54 = (bf16[1536,256]{1,0:T(8,128)(2,1)}, bf16[1536,256]{1,0:T(8,128)(2,1)S(1)}) fusion(bf16[1536,512]{1,0:T(8,128)(2,1)} %bitcast.83), kind=kLoop, calls=%fused_computation.93 | loop fusion | bytes 3145728 | tf_op jit(solution)/shard_map/while/body/eval_jaxpr/slice | solution.py:89
  15.6 1.2 copy.63
  17.7 1.4 copy.64
  19.1 1.2 copy.65
  20.3 1.7 %compare_and_fusion = pred[128,1536]{0,1:T(8,128)(4,1)S(1)} fusion(s32[128]{0:T(128)} %iota_add_fusion, s32[128]{0:T(128)} %copy-done.9, s32[1536]{0:T(1024)S(1)} %get-tuple-element.61, s32[1536]{0:T(1024)S(1)} %get-tuple-element.60), kind=kLoop, calls=%fused_computation.27 | loop fusion | flops 589824 | bytes 209920 | tf_op jit(solution)/shard_map/while/body/eval_jaxpr/and | solution.py:101
  22.0 1.6 %fusion = (f32[128,2,6]{0,2,1:T(8,128)S(1)}, f32[2,1536,128,6]{2,1,3,0:T(8,128)S(1)}) fusion(pred[128,1536]{0,1:T(8,128)(4,1)S(1)} %compare_and_fusion, bf16[1536,2,128,1]{0,2,3,1:T(8,128)(2,1)S(1)} %bitcast.84, bf16[128,2,6,128]{0,3,2,1:T(8,128)(2,1)S(1)} %bitcast.85), kind=kOutput, calls=%fused_computation.3 | convolution fusion | flops 611056128 | bytes 10819584 | tf_op jit(solution)/shard_map/while/body/eval_jaxpr/rkgd,lkd->rkgl/dot_general | solution.py:103
  23.6 1.9 %fusion.3 = bf16[128,2,6]{0,2,1:T(8,128)(2,1)S(1)} fusion(f32[2,1536,128,6]{2,1,3,0:T(8,128)S(1)} %get-tuple-element.47, f32[128,2,6]{0,2,1:T(8,128)S(1)} %get-tuple-element.46, pred[128,1536]{0,1:T(8,128)(4,1)S(1)} %compare_and_fusion), kind=kLoop, calls=%fused_computation.6 | loop fusion | flops 9435648 | bytes 9643008 | tf_op jit(solution)/shard_map/while/body/eval_jaxpr/reduce_sum | solution.py:109
  25.5 2.0 %fusion.12 = bf16[128,2,6,128]{0,3,2,1:T(8,128)(2,1)S(1)} fusion(bf16[1536,2,128,1]{0,2,3,1:T(8,128)(2,1)S(1)} %bitcast.89, f32[2,1536,128,6]{2,1,3,0:T(8,128)S(1)} %get-tuple-element.47, f32[128,2,6]{0,2,1:T(8,128)S(1)} %get-tuple-element.46, pred[128,1536]{0,1:T(8,128)(4,1)S(1)} %compare_and_fusion), kind=kOutput, calls=%fused_computation.18 | convolution fusion | flops 613613568 | bytes 10819584 | tf_op jit(solution)/shard_map/while/body/eval_jaxpr/rkgl,lkd->rkgd/dot_general | solution.py:110
  27.5 2.6 %all-gather = bf16[256,2,6,128]{0,3,2,1:T(8,128)(2,1)S(1)} all-gather(bf16[128,2,6,128]{0,3,2,1:T(8,128)(2,1)S(1)} %fusion.12), channel_id=2, replica_groups=mesh['eh'=2,'el'=8,'tp'=2] {'tp'}, dimensions={0}, use_global_device_ids=true | all-gather | bytes 1179648 | tf_op jit(solution)/shard_map/all_gather | solution.py:17
  30.1 1.8 %all-gather.1 = bf16[256,2,6]{0,2,1:T(8,128)(2,1)S(1)} all-gather(bf16[128,2,6]{0,2,1:T(8,128)(2,1)S(1)} %convert_element_type.153), channel_id=3, replica_groups=mesh['eh'=2,'el'=8,'tp'=2] {'tp'}, dimensions={0}, use_global_device_ids=true | all-gather | bytes 9216 | tf_op jit(solution)/shard_map/all_gather | solution.py:17
  32.0 1.8 %all-gather.2 = bf16[256,2,6]{0,2,1:T(8,128)(2,1)S(1)} all-gather(bf16[128,2,6]{0,2,1:T(8,128)(2,1)S(1)} %fusion.3), channel_id=4, replica_groups=mesh['eh'=2,'el'=8,'tp'=2] {'tp'}, dimensions={0}, use_global_device_ids=true | all-gather | bytes 9216 | tf_op jit(solution)/shard_map/all_gather | solution.py:17
  33.8 1.1 reduce-window.11
  36.7 2.5 %psum.14 = f32[128]{0:T(128)S(1)} all-reduce(f32[128]{0:T(128)S(1)} %get-tuple-element.56), channel_id=1, replica_groups=mesh['eh'=2,'el'=8,'tp'=2] {'tp'}, use_global_device_ids=true, to_apply=%region_11.12 | all-reduce | flops 128 | bytes 1024 | tf_op jit(solution)/shard_map/psum | solution.py:131
  39.8 27.0 %all_to_all.10 = bf16[8,128,768]{2,1,0:T(8,128)(2,1)} all-to-all(bf16[8,128,768]{2,1,0:T(8,128)(2,1)S(1)} %bitcast.82), channel_id=1, replica_groups=mesh['eh'=2,'el'=8,'tp'=2] {'el'}, dimensions={0} | all-to-all | bytes 3145728 | tf_op jit(solution)/shard_map/all_to_all | solution.py:152
  67.0 10.8 %all-gather.5.cloned.1.call-done = bf16[8,128,1536]{2,1,0:T(8,128)(2,1)} async-done(((bf16[8,128,768]{2,1,0:T(8,128)(2,1)}), bf16[8,128,1536]{2,1,0:T(8,128)(2,1)}) %all-gather.5.cloned.1.call-update) | async-done | bytes 3145744 | tf_op jit(solution)/shard_map/all_gather | solution.py:159
  77.8 5.1 %fusion.17 = f32[1024,384]{1,0:T(8,128)} fusion(bf16[1024,1536]{1,0:T(8,128)(2,1)} %bitcast.93, bf16[1,1536,384]{2,1,0:T(8,128)(2,1)} %param.24), kind=kOutput, calls=%fused_computation.23 | convolution fusion | flops 1207959552 | bytes 5898240 | tf_op jit(solution)/shard_map/dot_general | solution.py:160
  82.9 8.2 %convolution_convert_fusion = bf16[1024,1536]{1,0:T(8,128)(2,1)} fusion(bf16[1,384,1536]{2,1,0:T(8,128)(2,1)} %param.26, f32[1024,384]{1,0:T(8,128)} %fusion.17, bf16[1024,1536]{1,0:T(8,128)(2,1)} %bitcast.94, bf16[1,1536,384]{2,1,0:T(8,128)(2,1)} %param.25), kind=kOutput, calls=%fused_computation.10 | convolution fusion | flops 2418671616 | bytes 10223616 | tf_op jit(solution)/shard_map/dot_general | solution.py:163
  91.1 12.2 %reduce-scatter.2.cloned.1.call-done = bf16[1024,768]{1,0:T(8,128)(2,1)} async-done(((bf16[1024,1536]{1,0:T(8,128)(2,1)}), bf16[1024,768]{1,0:T(8,128)(2,1)}) %reduce-scatter.2.cloned.1.call-update) | async-done | bytes 1572880 | tf_op jit(solution)/shard_map/reduce_scatter | solution.py:166
  103.3 4.8 %all-to-all-start.1 = ((bf16[8,128,768]{2,1,0:T(8,128)(2,1)}), bf16[8,128,768]{2,1,0:T(8,128)(2,1)}, u32[]{:S(2)}, u32[]{:S(2)}) async-start(bf16[8,128,768]{2,1,0:T(8,128)(2,1)} %bitcast.86), calls=%async_computation.2 | async-start | bytes 3145728 | tf_op jit(solution)/shard_map/all_to_all | solution.py:167
  108.4 20.5 %all-to-all-done.1 = bf16[8,128,768]{2,1,0:T(8,128)(2,1)} async-done(((bf16[8,128,768]{2,1,0:T(8,128)(2,1)}), bf16[8,128,768]{2,1,0:T(8,128)(2,1)}, u32[]{:S(2)}, u32[]{:S(2)}) %all-to-all-start.1) | async-done | bytes 1572896 | tf_op jit(solution)/shard_map/all_to_all | solution.py:167
  128.9 3.0 %multiply_reduce_fusion = (f32[128]{0:T(128)S(1)}, f32[128,768]{1,0:T(8,128)}) fusion(f32[128,768]{1,0:T(8,128)S(1)} %get-tuple-element.57, f32[128,1024]{1,0:T(8,128)S(1)} %select_reduce_fusion, bf16[1024,768]{1,0:T(8,128)(2,1)} %bitcast.25), kind=kOutput, calls=%fused_computation.29 | convolution fusion | flops 1208254336 | bytes 2884096 | tf_op jit(solution)/shard_map/dot_general | solution.py:182
  131.9 2.4 %psum.15 = f32[128]{0:T(128)S(1)} all-reduce(f32[128]{0:T(128)S(1)} %get-tuple-element.58), channel_id=1, replica_groups=mesh['eh'=2,'el'=8,'tp'=2] {'tp'}, use_global_device_ids=true, to_apply=%region_14.15 | all-reduce | flops 128 | bytes 1024 | tf_op jit(solution)/shard_map/psum | solution.py:189
  134.3 1.8 %multiply_convert_fusion.1 = bf16[128,768]{1,0:T(8,128)(2,1)} fusion(f32[128,768]{1,0:T(8,128)} %get-tuple-element.59, f32[768]{0:T(1024)S(1)} %copy-done.7, f32[128]{0:T(128)S(1)} %add_rsqrt_fusion), kind=kLoop, calls=%fused_computation.28 | loop fusion | flops 294912 | bytes 593408 | tf_op jit(solution)/shard_map/convert_element_type | solution.py:192
  (60 shorter events, 7.2 us)
Async XLA Ops:
  6.5 29.5 %copy-start = (bf16[1536,768]{1,0:T(8,128)(2,1)S(1)}, bf16[1536,768]{1,0:T(8,128)(2,1)}, u32[]{:S(2)}) copy-start(bf16[1536,768]{1,0:T(8,128)(2,1)} %param.20) | copy-start | bytes 7077892
  6.5 71.2 %all-gather.5.cloned.1.call-start = ((), (), s32[]{:S(2)}) async-start(), calls=%async_computation.3 | async-start | bytes 4718592 | tf_op jit(solution)/shard_map/all_gather | solution.py:159
  13.2 3.5 %copy-start.11 = (s32[1,4]{1,0:T(1,128)S(1)}, s32[1,4]{1,0:T(1,128)}, u32[]{:S(2)}) copy-start(s32[1,4]{1,0:T(1,128)} %param.18) | copy-start | bytes 52
  13.2 3.7 %copy-start.10 = (s32[1,4]{1,0:T(1,128)S(1)}, s32[1,4]{1,0:T(1,128)}, u32[]{:S(2)}) copy-start(s32[1,4]{1,0:T(1,128)} %param.19) | copy-start | bytes 52
  17.0 0.7 copy-start.9
  23.6 1.9 %copy-start.1 = (bf16[1536,256]{0,1:T(8,128)(2,1)S(1)}, bf16[1536,256]{0,1:T(8,128)(2,1)}, u32[]{:S(2)}) copy-start(bf16[1536,256]{0,1:T(8,128)(2,1)} %copy.63) | copy-start | bytes 2359300
  25.5 8.2 %copy-start.4 = (s32[4,128]{1,0:T(4,128)S(1)}, s32[4,128]{1,0:T(4,128)}, u32[]{:S(2)}) copy-start(s32[4,128]{1,0:T(4,128)} %eq.108) | copy-start | bytes 6148
  25.5 9.6 %copy-start.5 = (s32[512]{0:T(512)S(1)}, s32[512]{0:T(512)}, u32[]{:S(2)}) copy-start(s32[512]{0:T(512)} %eq.104) | copy-start | bytes 6148
  25.5 9.9 %copy-start.3 = (s32[128,4]{0,1:T(4,128)S(1)}, s32[128,4]{0,1:T(4,128)}, u32[]{:S(2)}) copy-start(s32[128,4]{0,1:T(4,128)} %param.22) | copy-start | bytes 6148
  27.5 8.5 %copy-start.2 = (bf16[128,768]{1,0:T(8,128)(2,1)S(1)}, bf16[128,768]{1,0:T(8,128)(2,1)}, u32[]{:S(2)}) copy-start(bf16[128,768]{1,0:T(8,128)(2,1)} %param.14) | copy-start | bytes 589828
  35.4 3.7 %copy-start.6 = (f32[768]{0:T(1024)S(1)}, f32[768]{0:T(1024)}, u32[]{:S(2)}) copy-start(f32[768]{0:T(1024)} %param.21) | copy-start | bytes 9220
  66.8 36.5 %reduce-scatter.2.cloned.1.call-start = ((), (), s32[]{:S(2)}) async-start(), calls=%async_computation.4 | async-start | bytes 4718592 | tf_op jit(solution)/shard_map/reduce_scatter | solution.py:166
  91.1 17.0 %copy-start.8 = (f32[128,4]{0,1:T(4,128)S(1)}, f32[128,4]{0,1:T(4,128)}, u32[]{:S(2)}) copy-start(f32[128,4]{0,1:T(4,128)} %param.23) | copy-start | bytes 6148
  103.3 25.6 %all-to-all-start.1 = ((bf16[8,128,768]{2,1,0:T(8,128)(2,1)}), bf16[8,128,768]{2,1,0:T(8,128)(2,1)}, u32[]{:S(2)}, u32[]{:S(2)}) async-start(bf16[8,128,768]{2,1,0:T(8,128)(2,1)} %bitcast.86), calls=%async_computation.2 | async-start | bytes 3145728 | tf_op jit(solution)/shard_map/all_to_all | solution.py:167
  108.1 26.2 %copy-start.7 = (f32[768]{0:T(1024)S(1)}, f32[768]{0:T(1024)}, u32[]{:S(2)}) copy-start(f32[768]{0:T(1024)} %param.27) | copy-start | bytes 9220
Sparse Core Ops, SparseCore 0:
  66.9 10.8 all-gather.4
  91.2 12.0 reduce-scatter.1

commit v2 on v1

--- a/solution.py
+++ b/solution.py
@@ -29,6 +29,27 @@
     return lax.fori_loop(
         1, lax.axis_size(axis), lambda source, state: join(state, take(source)), take(0)
     )
+
+
+def tp_gather(part, axis):
+    if lax.axis_size("tp") != 2:
+        return lax.all_gather(part, "tp", axis=axis, tiled=True)
+    other = lax.ppermute(part, "tp", perm=[(0, 1), (1, 0)])
+    first = lax.axis_index("tp") == 0
+    low = jnp.where(first, part, other)
+    high = jnp.where(first, other, part)
+    return jnp.concatenate([low, high], axis=axis)
+
+
+def tp_scatter_sum(full, axis):
+    if lax.axis_size("tp") != 2:
+        return lax.psum_scatter(full, "tp", scatter_dimension=axis, tiled=True)
+    low, high = jnp.split(full, 2, axis=axis)
+    first = lax.axis_index("tp") == 0
+    keep = jnp.where(first, low, high)
+    send = jnp.where(first, high, low)
+    other = lax.ppermute(send, "tp", perm=[(0, 1), (1, 0)])
+    return (keep.astype(jnp.float32) + other.astype(jnp.float32)).astype(full.dtype)
 
 
 def merge_parts(first, second):
@@ -156,14 +177,14 @@
         concat_axis=0,
         tiled=True,
     )
-    inputs = lax.all_gather(arrived, "tp", axis=2, tiled=True).reshape(buffer_len, full_width)
+    inputs = tp_gather(arrived, 2).reshape(buffer_len, full_width)
     gate_value = jnp.dot(inputs, gate_w[0], preferred_element_type=jnp.float32)
     up_value = jnp.dot(inputs, up_w[0], preferred_element_type=jnp.float32)
     hidden = (jnp.maximum(gate_value, 0.0) * up_value).astype(jnp.bfloat16)
     partial_value = jnp.dot(hidden, down_w[0], preferred_element_type=jnp.float32).astype(
         jnp.bfloat16
     )
-    summed = lax.psum_scatter(partial_value, "tp", scatter_dimension=1, tiled=True)
+    summed = tp_scatter_sum(partial_value, 1)
     returned = lax.all_to_all(
         summed.reshape(experts, capacity, feat_part),
         "el",

time: 143 us -> 120 us (0.84)
  waiting for transfers between devices: 43.5 us -> 27.5 us
  between operations: 13.6 us -> 0.26 us
  other arithmetic: 8.44 us -> 14.7 us
  matrix products: 21.1 us -> 18.8 us
  local copies, waits for them, and re-layouts: 13.2 us -> 14.9 us
    reduce_scatter x1 -> x0, waiting for transfers between devices: 12.2 us -> none  [shards(): lax.psum_scatter(partial_value, 'tp', scatter_dimension=1, tiled=True)]
    all_gather x1 -> x0, waiting for transfers between devices: 10.8 us -> none  [shards(): lax.all_gather(arrived, 'tp', axis=2, tiled=True)]
    ppermute x0 -> x2, waiting for transfers between devices: none -> 7.02 us  [the longest x1 3.75 us: tp_gather(): other = lax.ppermute(part, 'tp', perm=[(0, 1), (1, 0)])]
    select_n x0 -> x2, other arithmetic: none -> 4.28 us  [the longest x1 2.2 us: tp_scatter_sum(): send = jnp.where(first, high, low)]
    dot_general x1, matrix products: 5.14 us -> 2.93 us  [shards(): gate_value = jnp.dot(inputs, gate_w[0], preferred_element_type=jnp.float32)]
    convert_element_type x0 -> x1, other arithmetic: none -> 1.71 us  [tp_scatter_sum(): (keep.astype(jnp.float32) + other.astype(jnp.float32)).astype(full.dtype)]
    unnamed x27 -> x33, local copies, waits for them, and re-layouts: 2.99 us -> 4.65 us
where the time goes in v2:
time: 120 us; the launch traced here: 119 us
  blocking collectives  38.1 us (32%)
  waiting for transfers between devices  27.5 us (23%)
  matrix products  18.8 us (16%)
  local copies, waits for them, and re-layouts  14.9 us (12%)
  other arithmetic  14.7 us (12%)
  starting transfers between devices  4.62 us (4%)
    all_to_all x1, blocking collectives, shards(): lax.all_to_all(outgoing.reshape(experts, capacity, feat_part), 'el', spli...  27 us
    all_to_all x1, waiting for transfers between devices, shards(): lax.all_to_all(summed.reshape(experts, capacity, feat_part), 'el', split_...  20.5 us
    dot_general x1, matrix products, shards(): jnp.dot(hidden, down_w[0], preferred_element_type=jnp.float32)  8.15 us
    all_gather x3, blocking collectives, merged(): lax.all_gather(a.astype(kind), axis)  6.21 us
    unnamed x33, local copies, waits for them, and re-layouts  4.65 us
    all_to_all x1, starting transfers between devices, shards(): lax.all_to_all(summed.reshape(experts, capacity, feat_part), 'el', split_...  4.42 us
    slice x2, local copies, waits for them, and re-layouts, one_group(): flattened_cache[:, :KEY_VALUE_HEADS * HEAD_SIZE]  3.79 us
    ppermute x1, waiting for transfers between devices, tp_gather(): other = lax.ppermute(part, 'tp', perm=[(0, 1), (1, 0)])  3.75 us
  transfers between devices with their start and end apart: 3, of which 3 were waited for; matrix products, arithmetic and copies ran while one was open for 0% of the time, Pallas kernels for 0%

profile of v2, /device:TPU:0, one launch (start us, length us, event | category | flops | bytes accessed | tf_op | source)
XLA Modules:
  0.0 118.9 jit_solution(9472752186871814273)
XLA Ops:
  3.3 3.3 %gather_fusion = bf16[96,16,512]{2,1,0:T(8,128)(2,1)} fusion(bf16[96,16,512]{2,1,0:T(8,128)(2,1)} %bitcast.89, s32[1024]{0:T(1024)S(1)} %pad_clamp_fusion), kind=kCustom, calls=%fused_computation | custom fusion | bytes 3146112 | tf_op jit(solution)/shard_map/while/body/eval_jaxpr/gather | solution.py:107
  6.7 2.4 %fusion.54 = (bf16[1536,256]{1,0:T(8,128)(2,1)}, bf16[1536,256]{1,0:T(8,128)(2,1)S(1)}) fusion(bf16[1536,512]{1,0:T(8,128)(2,1)} %bitcast.84), kind=kLoop, calls=%fused_computation.98 | loop fusion | bytes 3145728 | tf_op jit(solution)/shard_map/while/body/eval_jaxpr/slice | solution.py:110
  13.8 1.7 %compare_and_fusion = pred[128,1536]{0,1:T(8,128)(4,1)S(1)} fusion(s32[128]{0:T(128)} %iota_add_fusion, s32[128]{0:T(128)} %copy-done.11, s32[1536]{0:T(1024)S(1)} %get-tuple-element.63, s32[1536]{0:T(1024)S(1)} %get-tuple-element.62), kind=kLoop, calls=%fused_computation.32 | loop fusion | flops 589824 | bytes 209920 | tf_op jit(solution)/shard_map/while/body/eval_jaxpr/and | solution.py:122
  15.4 1.6 %fusion = (f32[128,2,6]{0,2,1:T(8,128)S(1)}, f32[2,1536,128,6]{2,1,3,0:T(8,128)S(1)}) fusion(pred[128,1536]{0,1:T(8,128)(4,1)S(1)} %compare_and_fusion, bf16[1536,2,128,1]{0,2,3,1:T(8,128)(2,1)S(1)} %bitcast.85, bf16[128,2,6,128]{0,3,2,1:T(8,128)(2,1)S(1)} %bitcast.88), kind=kOutput, calls=%fused_computation.3 | convolution fusion | flops 611056128 | bytes 10819584 | tf_op jit(solution)/shard_map/while/body/eval_jaxpr/rkgd,lkd->rkgl/dot_general | solution.py:124
  17.1 1.9 %fusion.3 = bf16[128,2,6]{0,2,1:T(8,128)(2,1)S(1)} fusion(f32[2,1536,128,6]{2,1,3,0:T(8,128)S(1)} %get-tuple-element.57, f32[128,2,6]{0,2,1:T(8,128)S(1)} %get-tuple-element.56, pred[128,1536]{0,1:T(8,128)(4,1)S(1)} %compare_and_fusion), kind=kLoop, calls=%fused_computation.6 | loop fusion | flops 9435648 | bytes 9643008 | tf_op jit(solution)/shard_map/while/body/eval_jaxpr/reduce_sum | solution.py:130
  19.0 2.0 %fusion.12 = bf16[128,2,6,128]{0,3,2,1:T(8,128)(2,1)S(1)} fusion(bf16[1536,2,128,1]{0,2,3,1:T(8,128)(2,1)S(1)} %bitcast.91, f32[2,1536,128,6]{2,1,3,0:T(8,128)S(1)} %get-tuple-element.57, f32[128,2,6]{0,2,1:T(8,128)S(1)} %get-tuple-element.56, pred[128,1536]{0,1:T(8,128)(4,1)S(1)} %compare_and_fusion), kind=kOutput, calls=%fused_computation.23 | convolution fusion | flops 613613568 | bytes 10819584 | tf_op jit(solution)/shard_map/while/body/eval_jaxpr/rkgl,lkd->rkgd/dot_general | solution.py:131
  21.0 2.6 %all-gather = bf16[256,2,6,128]{0,3,2,1:T(8,128)(2,1)S(1)} all-gather(bf16[128,2,6,128]{0,3,2,1:T(8,128)(2,1)S(1)} %fusion.12), channel_id=2, replica_groups=mesh['eh'=2,'el'=8,'tp'=2] {'tp'}, dimensions={0}, use_global_device_ids=true | all-gather | bytes 1179648 | tf_op jit(solution)/shard_map/all_gather | solution.py:17
  23.6 1.8 %all-gather.1 = bf16[256,2,6]{0,2,1:T(8,128)(2,1)S(1)} all-gather(bf16[128,2,6]{0,2,1:T(8,128)(2,1)S(1)} %convert_element_type.162), channel_id=3, replica_groups=mesh['eh'=2,'el'=8,'tp'=2] {'tp'}, dimensions={0}, use_global_device_ids=true | all-gather | bytes 9216 | tf_op jit(solution)/shard_map/all_gather | solution.py:17
  25.4 1.8 %all-gather.2 = bf16[256,2,6]{0,2,1:T(8,128)(2,1)S(1)} all-gather(bf16[128,2,6]{0,2,1:T(8,128)(2,1)S(1)} %fusion.3), channel_id=4, replica_groups=mesh['eh'=2,'el'=8,'tp'=2] {'tp'}, dimensions={0}, use_global_device_ids=true | all-gather | bytes 9216 | tf_op jit(solution)/shard_map/all_gather | solution.py:17
  30.1 2.5 %psum.14 = f32[128]{0:T(128)S(1)} all-reduce(f32[128]{0:T(128)S(1)} %get-tuple-element.58), channel_id=1, replica_groups=mesh['eh'=2,'el'=8,'tp'=2] {'tp'}, use_global_device_ids=true, to_apply=%region_11.12 | all-reduce | flops 128 | bytes 1024 | tf_op jit(solution)/shard_map/psum | solution.py:152
  33.3 27.0 %all_to_all.10 = bf16[8,128,768]{2,1,0:T(8,128)(2,1)} all-to-all(bf16[8,128,768]{2,1,0:T(8,128)(2,1)S(1)} %bitcast.82), channel_id=1, replica_groups=mesh['eh'=2,'el'=8,'tp'=2] {'el'}, dimensions={0} | all-to-all | bytes 3145728 | tf_op jit(solution)/shard_map/all_to_all | solution.py:173
  60.2 3.7 %collective-permute-done = bf16[8,128,768]{2,1,0:T(8,128)(2,1)} collective-permute-done((bf16[8,128,768]{2,1,0:T(8,128)(2,1)}, bf16[8,128,768]{2,1,0:T(8,128)(2,1)}, u32[]{:S(2)}, u32[]{:S(2)}) %collective-permute-start) | collective-permute-done | bytes 1572896 | tf_op jit(solution)/shard_map/ppermute | solution.py:37
  64.0 2.1 %broadcast_select_fusion.1 = (bf16[8,128,768]{2,1,0:T(8,128)(2,1)S(1)}, bf16[8,128,768]{2,1,0:T(8,128)(2,1)S(1)}) fusion(bf16[8,128,768]{2,1,0:T(8,128)(2,1)} %all_to_all.10, bf16[8,128,768]{2,1,0:T(8,128)(2,1)} %collective-permute-done, pred[]{:T(512)S(6)} %eq.119), kind=kLoop, calls=%fused_computation.20 | loop fusion | flops 1572864 | bytes 6291457 | tf_op jit(solution)/shard_map/jit(_where)/select_n | solution.py:39
  66.4 1.7 %copy-done.2 = bf16[8,128,1536]{2,1,0:T(8,128)(2,1)} copy-done((bf16[8,128,1536]{2,1,0:T(8,128)(2,1)}, bf16[8,128,1536]{2,1,0:T(8,128)(2,1)S(1)}, u32[]{:S(2)}) %copy-start.2) | copy-done | bytes 3145752
  68.0 2.9 %fusion.17 = f32[1024,384]{1,0:T(8,128)} fusion(bf16[1024,1536]{1,0:T(8,128)(2,1)S(1)} %bitcast.86, bf16[1,1536,384]{2,1,0:T(8,128)(2,1)S(1)} %copy-done.14), kind=kOutput, calls=%fused_computation.28 | convolution fusion | flops 1207959552 | bytes 5898240 | tf_op jit(solution)/shard_map/dot_general | solution.py:181
  71.0 8.2 %convolution_convert_fusion = bf16[1024,1536]{1,0:T(8,128)(2,1)} fusion(bf16[1,384,1536]{2,1,0:T(8,128)(2,1)} %param.26, f32[1024,384]{1,0:T(8,128)} %fusion.17, bf16[1024,1536]{1,0:T(8,128)(2,1)} %bitcast.87, bf16[1,1536,384]{2,1,0:T(8,128)(2,1)} %param.25), kind=kOutput, calls=%fused_computation.10 | convolution fusion | flops 2418671616 | bytes 10223616 | tf_op jit(solution)/shard_map/dot_general | solution.py:184
  79.1 2.2 %broadcast_select_fusion.2 = bf16[1024,768]{1,0:T(8,128)(2,1)S(1)} fusion(pred[]{:T(512)S(6)} %eq.119, bf16[1024,1536]{1,0:T(8,128)(2,1)} %convolution_convert_fusion), kind=kLoop, calls=%fused_computation.21 | loop fusion | flops 786432 | bytes 4718593 | tf_op jit(solution)/shard_map/jit(_where)/select_n | solution.py:50
  81.5 3.3 %collective-permute-done.1 = bf16[1024,768]{1,0:T(8,128)(2,1)S(1)} collective-permute-done((bf16[1024,768]{1,0:T(8,128)(2,1)S(1)}, bf16[1024,768]{1,0:T(8,128)(2,1)S(1)}, u32[]{:S(2)}, u32[]{:S(2)}) %collective-permute-start.1) | collective-permute-done | bytes 1572896 | tf_op jit(solution)/shard_map/ppermute | solution.py:51
  84.8 1.7 %add_convert_fusion = bf16[1024,768]{1,0:T(8,128)(2,1)} fusion(bf16[1024,768]{1,0:T(8,128)(2,1)S(1)} %collective-permute-done.1, pred[]{:T(512)S(6)} %eq.119, bf16[1024,1536]{1,0:T(8,128)(2,1)S(1)} %copy-done.1), kind=kLoop, calls=%fused_computation.12 | loop fusion | flops 3932160 | bytes 6291457 | tf_op jit(solution)/shard_map/convert_element_type | solution.py:52
  86.5 4.4 %all-to-all-start.1 = ((bf16[8,128,768]{2,1,0:T(8,128)(2,1)}), bf16[8,128,768]{2,1,0:T(8,128)(2,1)}, u32[]{:S(2)}, u32[]{:S(2)}) async-start(bf16[8,128,768]{2,1,0:T(8,128)(2,1)} %bitcast.83), calls=%async_computation.1 | async-start | bytes 3145728 | tf_op jit(solution)/shard_map/all_to_all | solution.py:188
  91.2 20.5 %all-to-all-done.1 = bf16[8,128,768]{2,1,0:T(8,128)(2,1)} async-done(((bf16[8,128,768]{2,1,0:T(8,128)(2,1)}), bf16[8,128,768]{2,1,0:T(8,128)(2,1)}, u32[]{:S(2)}, u32[]{:S(2)}) %all-to-all-start.1) | async-done | bytes 1572896 | tf_op jit(solution)/shard_map/all_to_all | solution.py:188
  111.7 3.0 %multiply_reduce_fusion = (f32[128]{0:T(128)S(1)}, f32[128,768]{1,0:T(8,128)}) fusion(f32[128,768]{1,0:T(8,128)S(1)} %get-tuple-element.59, f32[128,1024]{1,0:T(8,128)S(1)} %select_reduce_fusion, bf16[1024,768]{1,0:T(8,128)(2,1)} %bitcast.25), kind=kOutput, calls=%fused_computation.34 | convolution fusion | flops 1208254336 | bytes 2884096 | tf_op jit(solution)/shard_map/dot_general | solution.py:203
  114.7 2.4 %psum.15 = f32[128]{0:T(128)S(1)} all-reduce(f32[128]{0:T(128)S(1)} %get-tuple-element.60), channel_id=1, replica_groups=mesh['eh'=2,'el'=8,'tp'=2] {'tp'}, use_global_device_ids=true, to_apply=%region_13.14 | all-reduce | flops 128 | bytes 1024 | tf_op jit(solution)/shard_map/psum | solution.py:210
  117.1 1.8 %multiply_convert_fusion.1 = bf16[128,768]{1,0:T(8,128)(2,1)} fusion(f32[128,768]{1,0:T(8,128)} %get-tuple-element.61, f32[768]{0:T(1024)S(1)} %copy-done.9, f32[128]{0:T(128)S(1)} %add_rsqrt_fusion), kind=kLoop, calls=%fused_computation.33 | loop fusion | flops 294912 | bytes 593408 | tf_op jit(solution)/shard_map/convert_element_type | solution.py:213
  (68 shorter events, 12.3 us)
Async XLA Ops:
  0.0 29.5 %copy-start = (bf16[1536,768]{1,0:T(8,128)(2,1)S(1)}, bf16[1536,768]{1,0:T(8,128)(2,1)}, u32[]{:S(2)}) copy-start(bf16[1536,768]{1,0:T(8,128)(2,1)} %param.20) | copy-start | bytes 7077892
  6.6 3.5 %copy-start.13 = (s32[1,4]{1,0:T(1,128)S(1)}, s32[1,4]{1,0:T(1,128)}, u32[]{:S(2)}) copy-start(s32[1,4]{1,0:T(1,128)} %param.18) | copy-start | bytes 52
  6.7 3.7 %copy-start.12 = (s32[1,4]{1,0:T(1,128)S(1)}, s32[1,4]{1,0:T(1,128)}, u32[]{:S(2)}) copy-start(s32[1,4]{1,0:T(1,128)} %param.19) | copy-start | bytes 52
  10.5 0.7 copy-start.11
  17.0 1.9 %copy-start.3 = (bf16[1536,256]{0,1:T(8,128)(2,1)S(1)}, bf16[1536,256]{0,1:T(8,128)(2,1)}, u32[]{:S(2)}) copy-start(bf16[1536,256]{0,1:T(8,128)(2,1)} %copy.63) | copy-start | bytes 2359300
  19.0 8.2 %copy-start.6 = (s32[4,128]{1,0:T(4,128)S(1)}, s32[4,128]{1,0:T(4,128)}, u32[]{:S(2)}) copy-start(s32[4,128]{1,0:T(4,128)} %eq.112) | copy-start | bytes 6148
  19.0 9.6 %copy-start.7 = (s32[512]{0:T(512)S(1)}, s32[512]{0:T(512)}, u32[]{:S(2)}) copy-start(s32[512]{0:T(512)} %eq.108) | copy-start | bytes 6148
  19.0 9.9 %copy-start.5 = (s32[128,4]{0,1:T(4,128)S(1)}, s32[128,4]{0,1:T(4,128)}, u32[]{:S(2)}) copy-start(s32[128,4]{0,1:T(4,128)} %param.22) | copy-start | bytes 6148
  21.0 8.5 %copy-start.4 = (bf16[128,768]{1,0:T(8,128)(2,1)S(1)}, bf16[128,768]{1,0:T(8,128)(2,1)}, u32[]{:S(2)}) copy-start(bf16[128,768]{1,0:T(8,128)(2,1)} %param.14) | copy-start | bytes 589828
  29.3 3.3 %copy-start.8 = (f32[768]{0:T(1024)S(1)}, f32[768]{0:T(1024)}, u32[]{:S(2)}) copy-start(f32[768]{0:T(1024)} %param.21) | copy-start | bytes 9220
  60.2 3.8 %collective-permute-start = (bf16[8,128,768]{2,1,0:T(8,128)(2,1)}, bf16[8,128,768]{2,1,0:T(8,128)(2,1)}, u32[]{:S(2)}, u32[]{:S(2)}) collective-permute-start(bf16[8,128,768]{2,1,0:T(8,128)(2,1)} %all_to_all.10), channel_id=1, source_target_pairs={{0,1},{1,0},{2,3},{3,2},{4,5},{5,4},{6,7},{7,6},{8,9},{9,8},{10,11... | collective-permute-start | bytes 4718600 | tf_op jit(solution)/shard_map/ppermute | solution.py:37
  66.1 1.9 %copy-start.14 = (bf16[1,1536,384]{2,1,0:T(8,128)(2,1)S(1)}, bf16[1,1536,384]{2,1,0:T(8,128)(2,1)}, u32[]{:S(2)}) copy-start(bf16[1,1536,384]{2,1,0:T(8,128)(2,1)} %param.24) | copy-start | bytes 3538948
  66.4 1.7 %copy-start.2 = (bf16[8,128,1536]{2,1,0:T(8,128)(2,1)}, bf16[8,128,1536]{2,1,0:T(8,128)(2,1)S(1)}, u32[]{:S(2)}) copy-start(bf16[8,128,1536]{2,1,0:T(8,128)(2,1)S(1)} %pad_maximum_fusion) | copy-start | bytes 9437188
  79.1 5.7 %copy-start.1 = (bf16[1024,1536]{1,0:T(8,128)(2,1)S(1)}, bf16[1024,1536]{1,0:T(8,128)(2,1)}, u32[]{:S(2)}) copy-start(bf16[1024,1536]{1,0:T(8,128)(2,1)} %convolution_convert_fusion) | copy-start | bytes 9437188
  81.3 3.5 %collective-permute-start.1 = (bf16[1024,768]{1,0:T(8,128)(2,1)S(1)}, bf16[1024,768]{1,0:T(8,128)(2,1)S(1)}, u32[]{:S(2)}, u32[]{:S(2)}) collective-permute-start(bf16[1024,768]{1,0:T(8,128)(2,1)S(1)} %broadcast_select_fusion.2), channel_id=1, source_target_pairs={{0,1},{1,0},{2,3},{3,2},{4,5},{5,4},{6,7},{7,6},{8,9},{9,8},{10,11... | collective-permute-start | bytes 4718600 | tf_op jit(solution)/shard_map/ppermute | solution.py:51
  86.5 4.4 %copy-start.10 = (f32[128,4]{0,1:T(4,128)S(1)}, f32[128,4]{0,1:T(4,128)}, u32[]{:S(2)}) copy-start(f32[128,4]{0,1:T(4,128)} %param.23) | copy-start | bytes 6148
  86.5 25.2 %all-to-all-start.1 = ((bf16[8,128,768]{2,1,0:T(8,128)(2,1)}), bf16[8,128,768]{2,1,0:T(8,128)(2,1)}, u32[]{:S(2)}, u32[]{:S(2)}) async-start(bf16[8,128,768]{2,1,0:T(8,128)(2,1)} %bitcast.83), calls=%async_computation.1 | async-start | bytes 3145728 | tf_op jit(solution)/shard_map/all_to_all | solution.py:188
  90.9 26.2 %copy-start.9 = (f32[768]{0:T(1024)S(1)}, f32[768]{0:T(1024)}, u32[]{:S(2)}) copy-start(f32[768]{0:T(1024)} %param.27) | copy-start | bytes 9220

commit v3 on v2

--- a/solution.py
+++ b/solution.py
@@ -29,6 +29,23 @@
     return lax.fori_loop(
         1, lax.axis_size(axis), lambda source, state: join(state, take(source)), take(0)
     )
+
+
+def relative(expert, me, count):
+    if count & (count - 1) == 0:
+        return jnp.bitwise_xor(expert, me)
+    return (expert - me) % count
+
+
+def exchange(chunks, count):
+    pieces = [chunks[0]]
+    for step in range(1, count):
+        if count & (count - 1) == 0:
+            pairs = [(i, i ^ step) for i in range(count)]
+        else:
+            pairs = [(i, (i + step) % count) for i in range(count)]
+        pieces.append(lax.ppermute(chunks[step], "el", perm=pairs))
+    return jnp.stack(pieces)
 
 
 def tp_gather(part, axis):
@@ -165,18 +182,15 @@
     expert_rank = jnp.sum(
         (jnp.cumsum(expert_onehot, axis=0) - expert_onehot) * expert_onehot, axis=1
     )
-    target = (flat_ids * capacity + expert_rank).reshape(count_of_rows, top_count)
+    my_half = lax.axis_index("el")
+    target = (relative(flat_ids, my_half, half_count) * capacity + expert_rank).reshape(
+        count_of_rows, top_count
+    )
     slot_iota = jnp.arange(buffer_len, dtype=jnp.int32)
     hits = target[None, :, :] == slot_iota[:, None, None]
     dispatch = jnp.any(hits, axis=2).astype(jnp.bfloat16)
     outgoing = jnp.dot(dispatch, normed, preferred_element_type=jnp.float32).astype(jnp.bfloat16)
-    arrived = lax.all_to_all(
-        outgoing.reshape(experts, capacity, feat_part),
-        "el",
-        split_axis=0,
-        concat_axis=0,
-        tiled=True,
-    )
+    arrived = exchange(outgoing.reshape(experts, capacity, feat_part), half_count)
     inputs = tp_gather(arrived, 2).reshape(buffer_len, full_width)
     gate_value = jnp.dot(inputs, gate_w[0], preferred_element_type=jnp.float32)
     up_value = jnp.dot(inputs, up_w[0], preferred_element_type=jnp.float32)
@@ -185,13 +199,9 @@
         jnp.bfloat16
     )
     summed = tp_scatter_sum(partial_value, 1)
-    returned = lax.all_to_all(
-        summed.reshape(experts, capacity, feat_part),
-        "el",
-        split_axis=0,
-        concat_axis=0,
-        tiled=True,
-    ).reshape(buffer_len, feat_part)
+    returned = exchange(summed.reshape(experts, capacity, feat_part), half_count).reshape(
+        buffer_len, feat_part
+    )
     combine = jnp.sum(
         jnp.where(
             target[:, :, None] == slot_iota[None, None, :],

time: 120 us -> 119 us (level)
  blocking collectives: 38.1 us -> 11.3 us
  starting transfers between devices: 4.62 us -> 21.8 us
  local copies, waits for them, and re-layouts: 14.9 us -> 23.8 us
    all_to_all x1 -> x0, blocking collectives: 27 us -> none  [shards(): lax.all_to_all(outgoing.reshape(experts, capacity, feat_part), 'el', spli...]
    ppermute x0 -> x14, starting transfers between devices: none -> 21.6 us  [exchange(): pieces.append(lax.ppermute(chunks[step], 'el', perm=pairs))]
    ppermute x0 -> x14, waiting for transfers between devices: none -> 21.3 us  [exchange(): pieces.append(lax.ppermute(chunks[step], 'el', perm=pairs))]
    all_to_all x1 -> x0, waiting for transfers between devices: 20.5 us -> none  [shards(): lax.all_to_all(summed.reshape(experts, capacity, feat_part), 'el', split_...]
    concatenate x0 -> x1, local copies, waits for them, and re-layouts: none -> 4.64 us  [tp_gather(): return jnp.concatenate([low, high], axis=axis)]
    all_to_all x1 -> x0, starting transfers between devices: 4.42 us -> none  [shards(): lax.all_to_all(summed.reshape(experts, capacity, feat_part), 'el', split_...]
    unnamed x33 -> x43, local copies, waits for them, and re-layouts: 4.65 us -> 7.92 us
    dot_general x1, matrix products: 2.93 us -> 5.14 us  [shards(): gate_value = jnp.dot(inputs, gate_w[0], preferred_element_type=jnp.float32)]
  transfers between devices with their start and end apart: 3 -> 16, of which waited for: 3 -> 10; matrix products, arithmetic and copies ran while one was open for 0% -> 4% of each run, Pallas kernels for 0% -> 0%
where the time goes in v3:
time: 119 us
  waiting for transfers between devices  28 us (24%)
  local copies, waits for them, and re-layouts  23.8 us (20%)
  starting transfers between devices  21.8 us (18%)
  matrix products  19.1 us (16%)
  other arithmetic  14.3 us (12%)
  blocking collectives  11.3 us (9%)
    ppermute x14, starting transfers between devices, exchange(): pieces.append(lax.ppermute(chunks[step], 'el', perm=pairs))  21.6 us
    ppermute x14, waiting for transfers between devices, exchange(): pieces.append(lax.ppermute(chunks[step], 'el', perm=pairs))  21.3 us
    dot_general x1, matrix products, shards(): jnp.dot(hidden, down_w[0], preferred_element_type=jnp.float32)  8.15 us
    unnamed x43, local copies, waits for them, and re-layouts  7.92 us
    all_gather x3, blocking collectives, merged(): lax.all_gather(a.astype(kind), axis)  6.21 us
    dot_general x1, matrix products, shards(): gate_value = jnp.dot(inputs, gate_w[0], preferred_element_type=jnp.float32)  5.14 us
    concatenate x1, local copies, waits for them, and re-layouts, tp_gather(): return jnp.concatenate([low, high], axis=axis)  4.64 us
    slice x2, local copies, waits for them, and re-layouts, one_group(): flattened_cache[:, :KEY_VALUE_HEADS * HEAD_SIZE]  3.77 us
  transfers between devices with their start and end apart: 16, of which 10 were waited for; matrix products, arithmetic and copies ran while one was open for 4% of the time, Pallas kernels for 0%

profile of v3, /device:TPU:0, one launch (start us, length us, event | category | flops | bytes accessed | tf_op | source)
XLA Modules:
  0.0 118.7 jit_solution(18254024092520673013)
XLA Ops:
  3.3 3.3 %gather_fusion = bf16[96,16,512]{2,1,0:T(8,128)(2,1)} fusion(bf16[96,16,512]{2,1,0:T(8,128)(2,1)} %bitcast.122, s32[1024]{0:T(1024)S(1)} %pad_clamp_fusion), kind=kCustom, calls=%fused_computation | custom fusion | bytes 3146112 | tf_op jit(solution)/shard_map/while/body/eval_jaxpr/gather | solution.py:124
  6.6 2.4 %fusion.58 = (bf16[1536,256]{1,0:T(8,128)(2,1)}, bf16[1536,256]{1,0:T(8,128)(2,1)S(1)}) fusion(bf16[1536,512]{1,0:T(8,128)(2,1)} %bitcast.116), kind=kLoop, calls=%fused_computation.118 | loop fusion | bytes 3145728 | tf_op jit(solution)/shard_map/while/body/eval_jaxpr/slice | solution.py:127
  21.0 2.6 %all-gather = bf16[256,2,6,128]{0,3,2,1:T(8,128)(2,1)S(1)} all-gather(bf16[128,2,6,128]{0,3,2,1:T(8,128)(2,1)S(1)} %fusion.12), channel_id=2, replica_groups=mesh['eh'=2,'el'=8,'tp'=2] {'tp'}, dimensions={0}, use_global_device_ids=true | all-gather | bytes 1179648 | tf_op jit(solution)/shard_map/all_gather | solution.py:17
  30.1 2.6 %psum.14 = f32[128]{0:T(128)S(1)} all-reduce(f32[128]{0:T(128)S(1)} %get-tuple-element.82), channel_id=1, replica_groups=mesh['eh'=2,'el'=8,'tp'=2] {'tp'}, use_global_device_ids=true, to_apply=%region_11.12 | all-reduce | flops 128 | bytes 1024 | tf_op jit(solution)/shard_map/psum | solution.py:169
  33.7 2.9 %collective-permute-start = (bf16[128,768]{0,1:T(8,128)(2,1)S(1)}, bf16[128,768]{0,1:T(8,128)(2,1)S(1)}, u32[]{:S(2)}, u32[]{:S(2)}) collective-permute-start(bf16[128,768]{0,1:T(8,128)(2,1)S(1)} %get-tuple-element.72), channel_id=1, source_target_pairs={{0,2},{2,0},{4,6},{6,4},{8,10},{10,8},{12,14},{14,12},{1,3},{3,1},... | collective-permute-start | bytes 589832 | tf_op jit(solution)/shard_map/ppermute | solution.py:47
  38.1 2.0 %collective-permute-start.3 = (bf16[128,768]{0,1:T(8,128)(2,1)S(1)}, bf16[128,768]{0,1:T(8,128)(2,1)S(1)}, u32[]{:S(2)}, u32[]{:S(2)}) collective-permute-start(bf16[128,768]{0,1:T(8,128)(2,1)S(1)} %get-tuple-element.61), channel_id=1, source_target_pairs={{0,8},{2,10},{4,12},{6,14},{8,0},{10,2},{12,4},{14,6},{1,9},{3,11}... | collective-permute-start | bytes 589832 | tf_op jit(solution)/shard_map/ppermute | solution.py:47
  42.3 3.1 %collective-permute-start.5 = (bf16[128,768]{0,1:T(8,128)(2,1)S(1)}, bf16[128,768]{0,1:T(8,128)(2,1)S(1)}, u32[]{:S(2)}, u32[]{:S(2)}) collective-permute-start(bf16[128,768]{0,1:T(8,128)(2,1)S(1)} %get-tuple-element.59), channel_id=1, source_target_pairs={{0,12},{2,14},{4,8},{6,10},{8,4},{10,6},{12,0},{14,2},{1,13},{3,15... | collective-permute-start | bytes 589832 | tf_op jit(solution)/shard_map/ppermute | solution.py:47
  48.1 2.4 %collective-permute-done.2 = bf16[128,768]{0,1:T(8,128)(2,1)S(1)} collective-permute-done((bf16[128,768]{0,1:T(8,128)(2,1)S(1)}, bf16[128,768]{0,1:T(8,128)(2,1)S(1)}, u32[]{:S(2)}, u32[]{:S(2)}) %collective-permute-start.2) | collective-permute-done | bytes 196640 | tf_op jit(solution)/shard_map/ppermute | solution.py:47
  52.6 3.2 %collective-permute-done.5 = bf16[128,768]{0,1:T(8,128)(2,1)S(1)} collective-permute-done((bf16[128,768]{0,1:T(8,128)(2,1)S(1)}, bf16[128,768]{0,1:T(8,128)(2,1)S(1)}, u32[]{:S(2)}, u32[]{:S(2)}) %collective-permute-start.5) | collective-permute-done | bytes 196640 | tf_op jit(solution)/shard_map/ppermute | solution.py:47
  56.5 2.8 %collective-permute-done.6 = bf16[128,768]{0,1:T(8,128)(2,1)S(1)} collective-permute-done((bf16[128,768]{0,1:T(8,128)(2,1)S(1)}, bf16[128,768]{0,1:T(8,128)(2,1)S(1)}, u32[]{:S(2)}, u32[]{:S(2)}) %collective-permute-start.6) | collective-permute-done | bytes 196640 | tf_op jit(solution)/shard_map/ppermute | solution.py:47
  60.0 3.7 %collective-permute-done.7 = bf16[8,128,768]{1,2,0:T(8,128)(2,1)} collective-permute-done((bf16[8,128,768]{1,2,0:T(8,128)(2,1)}, bf16[8,128,768]{1,2,0:T(8,128)(2,1)}, u32[]{:S(2)}, u32[]{:S(2)}) %collective-permute-start.7) | collective-permute-done | bytes 1572896 | tf_op jit(solution)/shard_map/ppermute | solution.py:54
  63.7 2.1 %broadcast_select_fusion.1 = (bf16[8,128,768]{1,2,0:T(8,128)(2,1)S(1)}, bf16[8,128,768]{1,2,0:T(8,128)(2,1)S(1)}) fusion(bf16[8,128,768]{1,2,0:T(8,128)(2,1)} %bitcast_dynamic-update-slice_fusion.7, bf16[8,128,768]{1,2,0:T(8,128)(2,1)} %collective-permute-done.7, pred[]{:T(512)S(6)} %eq.119), kind=kLoop, calls=%fused_computation.20 | loop fusion | flops 1572864 | bytes 6291457 | tf_op jit(solution)/shard_map/jit(_where)/select_n | solution.py:56
  67.8 4.6 %copy.72 = bf16[8,128,1536]{2,1,0:T(8,128)(2,1)} copy(bf16[8,128,1536]{1,2,0:T(8,128)(2,1)} %pad_maximum_fusion) | data formatting | bytes 6291456 | tf_op jit(solution)/shard_map/concatenate | solution.py:58
  72.4 5.1 %fusion.17 = f32[1024,384]{1,0:T(8,128)} fusion(bf16[1024,1536]{1,0:T(8,128)(2,1)} %bitcast.118, bf16[1,1536,384]{2,1,0:T(8,128)(2,1)} %param.24), kind=kOutput, calls=%fused_computation.28 | convolution fusion | flops 1207959552 | bytes 5898240 | tf_op jit(solution)/shard_map/dot_general | solution.py:195
  77.5 8.2 %convolution_convert_fusion = bf16[1024,1536]{1,0:T(8,128)(2,1)} fusion(bf16[1,384,1536]{2,1,0:T(8,128)(2,1)} %param.26, f32[1024,384]{1,0:T(8,128)} %fusion.17, bf16[1024,1536]{1,0:T(8,128)(2,1)} %bitcast.119, bf16[1,1536,384]{2,1,0:T(8,128)(2,1)} %param.25), kind=kOutput, calls=%fused_computation.10 | convolution fusion | flops 2418671616 | bytes 10223616 | tf_op jit(solution)/shard_map/dot_general | solution.py:198
  85.7 2.2 %broadcast_select_fusion.2 = bf16[1024,768]{1,0:T(8,128)(2,1)S(1)} fusion(pred[]{:T(512)S(6)} %eq.119, bf16[1024,1536]{1,0:T(8,128)(2,1)} %convolution_convert_fusion), kind=kLoop, calls=%fused_computation.21 | loop fusion | flops 786432 | bytes 4718593 | tf_op jit(solution)/shard_map/jit(_where)/select_n | solution.py:67
  88.4 3.0 %collective-permute-done.8 = bf16[1024,768]{1,0:T(8,128)(2,1)S(1)} collective-permute-done((bf16[1024,768]{1,0:T(8,128)(2,1)S(1)}, bf16[1024,768]{1,0:T(8,128)(2,1)S(1)}, u32[]{:S(2)}, u32[]{:S(2)}) %collective-permute-start.8) | collective-permute-done | bytes 1572896 | tf_op jit(solution)/shard_map/ppermute | solution.py:68
  93.3 2.3 %collective-permute-start.11 = (bf16[128,768]{1,0:T(8,128)(2,1)S(1)}, bf16[128,768]{1,0:T(8,128)(2,1)S(1)}, u32[]{:S(2)}, u32[]{:S(2)}) collective-permute-start(bf16[128,768]{1,0:T(8,128)(2,1)S(1)} %get-tuple-element.47), channel_id=1, source_target_pairs={{0,6},{2,4},{4,2},{6,0},{8,14},{10,12},{12,10},{14,8},{1,7},{3,5},... | collective-permute-start | bytes 589832 | tf_op jit(solution)/shard_map/ppermute | solution.py:47
  97.7 2.2 %collective-permute-done.9 = bf16[128,768]{1,0:T(8,128)(2,1)S(1)} collective-permute-done((bf16[128,768]{1,0:T(8,128)(2,1)S(1)}, bf16[128,768]{1,0:T(8,128)(2,1)S(1)}, u32[]{:S(2)}, u32[]{:S(2)}) %collective-permute-start.9) | collective-permute-done | bytes 196640 | tf_op jit(solution)/shard_map/ppermute | solution.py:47
  101.4 2.3 %collective-permute-start.15 = (bf16[128,768]{1,0:T(8,128)(2,1)S(1)}, bf16[128,768]{1,0:T(8,128)(2,1)S(1)}, u32[]{:S(2)}, u32[]{:S(2)}) collective-permute-start(bf16[128,768]{1,0:T(8,128)(2,1)S(1)} %get-tuple-element.43), channel_id=1, source_target_pairs={{0,14},{2,12},{4,10},{6,8},{8,6},{10,4},{12,2},{14,0},{1,15},{3,13... | collective-permute-start | bytes 589832 | tf_op jit(solution)/shard_map/ppermute | solution.py:47
  103.7 3.4 %collective-permute-done.11 = bf16[128,768]{1,0:T(8,128)(2,1)S(1)} collective-permute-done((bf16[128,768]{1,0:T(8,128)(2,1)S(1)}, bf16[128,768]{1,0:T(8,128)(2,1)S(1)}, u32[]{:S(2)}, u32[]{:S(2)}) %collective-permute-start.11) | collective-permute-done | bytes 196640 | tf_op jit(solution)/shard_map/ppermute | solution.py:47
  107.7 4.2 %collective-permute-done.14 = bf16[128,768]{1,0:T(8,128)(2,1)S(1)} collective-permute-done((bf16[128,768]{1,0:T(8,128)(2,1)S(1)}, bf16[128,768]{1,0:T(8,128)(2,1)S(1)}, u32[]{:S(2)}, u32[]{:S(2)}) %collective-permute-start.14) | collective-permute-done | bytes 196640 | tf_op jit(solution)/shard_map/ppermute | solution.py:47
  111.9 2.5 %collective-permute-done.15 = bf16[128,768]{1,0:T(8,128)(2,1)S(1)} collective-permute-done((bf16[128,768]{1,0:T(8,128)(2,1)S(1)}, bf16[128,768]{1,0:T(8,128)(2,1)S(1)}, u32[]{:S(2)}, u32[]{:S(2)}) %collective-permute-start.15) | collective-permute-done | bytes 196640 | tf_op jit(solution)/shard_map/ppermute | solution.py:47
  115.4 2.5 %psum.15 = f32[128]{0:T(128)S(1)} all-reduce(f32[128]{0:T(128)S(1)} %get-tuple-element.84), channel_id=1, replica_groups=mesh['eh'=2,'el'=8,'tp'=2] {'tp'}, use_global_device_ids=true, to_apply=%region_13.14 | all-reduce | flops 128 | bytes 1024 | tf_op jit(solution)/shard_map/psum | solution.py:220
  (108 shorter events, 42.6 us)
Async XLA Ops:
  0.0 29.5 %copy-start = (bf16[1536,768]{1,0:T(8,128)(2,1)S(1)}, bf16[1536,768]{1,0:T(8,128)(2,1)}, u32[]{:S(2)}) copy-start(bf16[1536,768]{1,0:T(8,128)(2,1)} %param.20) | copy-start | bytes 7077892
  18.9 8.2 %copy-start.4 = (s32[4,128]{1,0:T(4,128)S(1)}, s32[4,128]{1,0:T(4,128)}, u32[]{:S(2)}) copy-start(s32[4,128]{1,0:T(4,128)} %eq.112) | copy-start | bytes 6148
  19.0 9.7 %copy-start.6 = (s32[512]{0:T(512)S(1)}, s32[512]{0:T(512)}, u32[]{:S(2)}) copy-start(s32[512]{0:T(512)} %eq.108) | copy-start | bytes 6148
  19.0 9.9 %copy-start.5 = (s32[128,4]{0,1:T(4,128)S(1)}, s32[128,4]{0,1:T(4,128)}, u32[]{:S(2)}) copy-start(s32[128,4]{0,1:T(4,128)} %param.22) | copy-start | bytes 6148
  21.0 8.5 %copy-start.3 = (bf16[128,768]{1,0:T(8,128)(2,1)S(1)}, bf16[128,768]{1,0:T(8,128)(2,1)}, u32[]{:S(2)}) copy-start(bf16[128,768]{1,0:T(8,128)(2,1)} %param.14) | copy-start | bytes 589828
  29.5 3.3 %copy-start.7 = (f32[768]{0:T(1024)S(1)}, f32[768]{0:T(1024)}, u32[]{:S(2)}) copy-start(f32[768]{0:T(1024)} %param.21) | copy-start | bytes 9220
  33.7 8.6 %collective-permute-start = (bf16[128,768]{0,1:T(8,128)(2,1)S(1)}, bf16[128,768]{0,1:T(8,128)(2,1)S(1)}, u32[]{:S(2)}, u32[]{:S(2)}) collective-permute-start(bf16[128,768]{0,1:T(8,128)(2,1)S(1)} %get-tuple-element.72), channel_id=1, source_target_pairs={{0,2},{2,0},{4,6},{6,4},{8,10},{10,8},{12,14},{14,12},{1,3},{3,1},... | collective-permute-start | bytes 589832 | tf_op jit(solution)/shard_map/ppermute | solution.py:47
  36.6 9.5 %collective-permute-start.1 = (bf16[128,768]{0,1:T(8,128)(2,1)S(1)}, bf16[128,768]{0,1:T(8,128)(2,1)S(1)}, u32[]{:S(2)}, u32[]{:S(2)}) collective-permute-start(bf16[128,768]{0,1:T(8,128)(2,1)S(1)} %get-tuple-element.63), channel_id=1, source_target_pairs={{0,4},{2,6},{4,0},{6,2},{8,12},{10,14},{12,8},{14,10},{1,5},{3,7},... | collective-permute-start | bytes 589832 | tf_op jit(solution)/shard_map/ppermute | solution.py:47
  38.1 12.4 %collective-permute-start.2 = (bf16[128,768]{0,1:T(8,128)(2,1)S(1)}, bf16[128,768]{0,1:T(8,128)(2,1)S(1)}, u32[]{:S(2)}, u32[]{:S(2)}) collective-permute-start(bf16[128,768]{0,1:T(8,128)(2,1)S(1)} %get-tuple-element.62), channel_id=1, source_target_pairs={{0,6},{2,4},{4,2},{6,0},{8,14},{10,12},{12,10},{14,8},{1,7},{3,5},... | collective-permute-start | bytes 589832 | tf_op jit(solution)/shard_map/ppermute | solution.py:47
  38.1 13.1 %collective-permute-start.3 = (bf16[128,768]{0,1:T(8,128)(2,1)S(1)}, bf16[128,768]{0,1:T(8,128)(2,1)S(1)}, u32[]{:S(2)}, u32[]{:S(2)}) collective-permute-start(bf16[128,768]{0,1:T(8,128)(2,1)S(1)} %get-tuple-element.61), channel_id=1, source_target_pairs={{0,8},{2,10},{4,12},{6,14},{8,0},{10,2},{12,4},{14,6},{1,9},{3,11}... | collective-permute-start | bytes 589832 | tf_op jit(solution)/shard_map/ppermute | solution.py:47
  40.2 11.7 %collective-permute-start.4 = (bf16[128,768]{0,1:T(8,128)(2,1)S(1)}, bf16[128,768]{0,1:T(8,128)(2,1)S(1)}, u32[]{:S(2)}, u32[]{:S(2)}) collective-permute-start(bf16[128,768]{0,1:T(8,128)(2,1)S(1)} %get-tuple-element.60), channel_id=1, source_target_pairs={{0,10},{2,8},{4,14},{6,12},{8,2},{10,0},{12,6},{14,4},{1,11},{3,9}... | collective-permute-start | bytes 589832 | tf_op jit(solution)/shard_map/ppermute | solution.py:47
  42.3 13.5 %collective-permute-start.5 = (bf16[128,768]{0,1:T(8,128)(2,1)S(1)}, bf16[128,768]{0,1:T(8,128)(2,1)S(1)}, u32[]{:S(2)}, u32[]{:S(2)}) collective-permute-start(bf16[128,768]{0,1:T(8,128)(2,1)S(1)} %get-tuple-element.59), channel_id=1, source_target_pairs={{0,12},{2,14},{4,8},{6,10},{8,4},{10,6},{12,0},{14,2},{1,13},{3,15... | collective-permute-start | bytes 589832 | tf_op jit(solution)/shard_map/ppermute | solution.py:47
  46.1 13.2 %collective-permute-start.6 = (bf16[128,768]{0,1:T(8,128)(2,1)S(1)}, bf16[128,768]{0,1:T(8,128)(2,1)S(1)}, u32[]{:S(2)}, u32[]{:S(2)}) collective-permute-start(bf16[128,768]{0,1:T(8,128)(2,1)S(1)} %get-tuple-element.58), channel_id=1, source_target_pairs={{0,14},{2,12},{4,10},{6,8},{8,6},{10,4},{12,2},{14,0},{1,15},{3,13... | collective-permute-start | bytes 589832 | tf_op jit(solution)/shard_map/ppermute | solution.py:47
  60.0 3.8 %collective-permute-start.7 = (bf16[8,128,768]{1,2,0:T(8,128)(2,1)}, bf16[8,128,768]{1,2,0:T(8,128)(2,1)}, u32[]{:S(2)}, u32[]{:S(2)}) collective-permute-start(bf16[8,128,768]{1,2,0:T(8,128)(2,1)} %bitcast_dynamic-update-slice_fusion.7), channel_id=1, source_target_pairs={{0,1},{1,0},{2,3},{3,2},{4,5},{5,4},{6,7},{7,6},{8,9},{9,8},{10,11... | collective-permute-start | bytes 4718600 | tf_op jit(solution)/shard_map/ppermute | solution.py:54
  85.7 5.7 %copy-start.1 = (bf16[1024,1536]{1,0:T(8,128)(2,1)S(1)}, bf16[1024,1536]{1,0:T(8,128)(2,1)}, u32[]{:S(2)}) copy-start(bf16[1024,1536]{1,0:T(8,128)(2,1)} %convolution_convert_fusion) | copy-start | bytes 9437188
  87.9 3.5 %collective-permute-start.8 = (bf16[1024,768]{1,0:T(8,128)(2,1)S(1)}, bf16[1024,768]{1,0:T(8,128)(2,1)S(1)}, u32[]{:S(2)}, u32[]{:S(2)}) collective-permute-start(bf16[1024,768]{1,0:T(8,128)(2,1)S(1)} %broadcast_select_fusion.2), channel_id=1, source_target_pairs={{0,1},{1,0},{2,3},{3,2},{4,5},{5,4},{6,7},{7,6},{8,9},{9,8},{10,11... | collective-permute-start | bytes 4718600 | tf_op jit(solution)/shard_map/ppermute | solution.py:68
  92.1 7.8 %collective-permute-start.9 = (bf16[128,768]{1,0:T(8,128)(2,1)S(1)}, bf16[128,768]{1,0:T(8,128)(2,1)S(1)}, u32[]{:S(2)}, u32[]{:S(2)}) collective-permute-start(bf16[128,768]{1,0:T(8,128)(2,1)S(1)} %get-tuple-element.57), channel_id=1, source_target_pairs={{0,2},{2,0},{4,6},{6,4},{8,10},{10,8},{12,14},{14,12},{1,3},{3,1},... | collective-permute-start | bytes 589832 | tf_op jit(solution)/shard_map/ppermute | solution.py:47
  92.7 8.7 %collective-permute-start.10 = (bf16[128,768]{1,0:T(8,128)(2,1)S(1)}, bf16[128,768]{1,0:T(8,128)(2,1)S(1)}, u32[]{:S(2)}, u32[]{:S(2)}) collective-permute-start(bf16[128,768]{1,0:T(8,128)(2,1)S(1)} %get-tuple-element.56), channel_id=1, source_target_pairs={{0,4},{2,6},{4,0},{6,2},{8,12},{10,14},{12,8},{14,10},{1,5},{3,7},... | collective-permute-start | bytes 589832 | tf_op jit(solution)/shard_map/ppermute | solution.py:47
  93.3 13.9 %collective-permute-start.11 = (bf16[128,768]{1,0:T(8,128)(2,1)S(1)}, bf16[128,768]{1,0:T(8,128)(2,1)S(1)}, u32[]{:S(2)}, u32[]{:S(2)}) collective-permute-start(bf16[128,768]{1,0:T(8,128)(2,1)S(1)} %get-tuple-element.47), channel_id=1, source_target_pairs={{0,6},{2,4},{4,2},{6,0},{8,14},{10,12},{12,10},{14,8},{1,7},{3,5},... | collective-permute-start | bytes 589832 | tf_op jit(solution)/shard_map/ppermute | solution.py:47
  95.6 11.6 %collective-permute-start.12 = (bf16[128,768]{1,0:T(8,128)(2,1)S(1)}, bf16[128,768]{1,0:T(8,128)(2,1)S(1)}, u32[]{:S(2)}, u32[]{:S(2)}) collective-permute-start(bf16[128,768]{1,0:T(8,128)(2,1)S(1)} %get-tuple-element.46), channel_id=1, source_target_pairs={{0,8},{2,10},{4,12},{6,14},{8,0},{10,2},{12,4},{14,6},{1,9},{3,11}... | collective-permute-start | bytes 589832 | tf_op jit(solution)/shard_map/ppermute | solution.py:47
  97.2 10.5 %collective-permute-start.13 = (bf16[128,768]{1,0:T(8,128)(2,1)S(1)}, bf16[128,768]{1,0:T(8,128)(2,1)S(1)}, u32[]{:S(2)}, u32[]{:S(2)}) collective-permute-start(bf16[128,768]{1,0:T(8,128)(2,1)S(1)} %get-tuple-element.45), channel_id=1, source_target_pairs={{0,10},{2,8},{4,14},{6,12},{8,2},{10,0},{12,6},{14,4},{1,11},{3,9}... | collective-permute-start | bytes 589832 | tf_op jit(solution)/shard_map/ppermute | solution.py:47
  99.9 12.0 %collective-permute-start.14 = (bf16[128,768]{1,0:T(8,128)(2,1)S(1)}, bf16[128,768]{1,0:T(8,128)(2,1)S(1)}, u32[]{:S(2)}, u32[]{:S(2)}) collective-permute-start(bf16[128,768]{1,0:T(8,128)(2,1)S(1)} %get-tuple-element.44), channel_id=1, source_target_pairs={{0,12},{2,14},{4,8},{6,10},{8,4},{10,6},{12,0},{14,2},{1,13},{3,15... | collective-permute-start | bytes 589832 | tf_op jit(solution)/shard_map/ppermute | solution.py:47
  101.4 13.0 %collective-permute-start.15 = (bf16[128,768]{1,0:T(8,128)(2,1)S(1)}, bf16[128,768]{1,0:T(8,128)(2,1)S(1)}, u32[]{:S(2)}, u32[]{:S(2)}) collective-permute-start(bf16[128,768]{1,0:T(8,128)(2,1)S(1)} %get-tuple-element.43), channel_id=1, source_target_pairs={{0,14},{2,12},{4,10},{6,8},{8,6},{10,4},{12,2},{14,0},{1,15},{3,13... | collective-permute-start | bytes 589832 | tf_op jit(solution)/shard_map/ppermute | solution.py:47
  111.9 6.0 %copy-start.8 = (f32[768]{0:T(1024)S(1)}, f32[768]{0:T(1024)}, u32[]{:S(2)}) copy-start(f32[768]{0:T(1024)} %param.27) | copy-start | bytes 9220
  (5 other events, 7.5 us)

commit v4 on v3

--- a/solution.py
+++ b/solution.py
@@ -46,6 +46,41 @@
             pairs = [(i, (i + step) % count) for i in range(count)]
         pieces.append(lax.ppermute(chunks[step], "el", perm=pairs))
     return jnp.stack(pieces)
+
+
+def expert_block(rows, gate_w, up_w, down_w):
+    feat_part = rows.shape[1]
+    if lax.axis_size("tp") != 2:
+        inputs = lax.all_gather(rows, "tp", axis=1, tiled=True)
+        gate_value = jnp.dot(inputs, gate_w, preferred_element_type=jnp.float32)
+        up_value = jnp.dot(inputs, up_w, preferred_element_type=jnp.float32)
+        hidden = (jnp.maximum(gate_value, 0.0) * up_value).astype(jnp.bfloat16)
+        partial_value = jnp.dot(hidden, down_w, preferred_element_type=jnp.float32)
+        return lax.psum_scatter(
+            partial_value.astype(jnp.bfloat16), "tp", scatter_dimension=1, tiled=True
+        )
+    swap = [(0, 1), (1, 0)]
+    mine = lax.axis_index("tp")
+    other = 1 - mine
+    rows_other = lax.ppermute(rows, "tp", perm=swap)
+    gate_parts = gate_w.reshape(2, feat_part, gate_w.shape[1])
+    up_parts = up_w.reshape(2, feat_part, up_w.shape[1])
+
+    def half_product(parts, x, which):
+        weight = lax.dynamic_index_in_dim(parts, which, 0, keepdims=False)
+        return jnp.dot(x, weight, preferred_element_type=jnp.float32)
+
+    gate_value = half_product(gate_parts, rows, mine) + half_product(gate_parts, rows_other, other)
+    up_value = half_product(up_parts, rows, mine) + half_product(up_parts, rows_other, other)
+    hidden = (jnp.maximum(gate_value, 0.0) * up_value).astype(jnp.bfloat16)
+
+    def down_product(which):
+        weight = lax.dynamic_slice_in_dim(down_w, which * feat_part, feat_part, axis=1)
+        return jnp.dot(hidden, weight, preferred_element_type=jnp.float32).astype(jnp.bfloat16)
+
+    sent = lax.ppermute(down_product(other), "tp", perm=swap)
+    kept = down_product(mine)
+    return (kept.astype(jnp.float32) + sent.astype(jnp.float32)).astype(jnp.bfloat16)
 
 
 def tp_gather(part, axis):
@@ -191,14 +226,7 @@
     dispatch = jnp.any(hits, axis=2).astype(jnp.bfloat16)
     outgoing = jnp.dot(dispatch, normed, preferred_element_type=jnp.float32).astype(jnp.bfloat16)
     arrived = exchange(outgoing.reshape(experts, capacity, feat_part), half_count)
-    inputs = tp_gather(arrived, 2).reshape(buffer_len, full_width)
-    gate_value = jnp.dot(inputs, gate_w[0], preferred_element_type=jnp.float32)
-    up_value = jnp.dot(inputs, up_w[0], preferred_element_type=jnp.float32)
-    hidden = (jnp.maximum(gate_value, 0.0) * up_value).astype(jnp.bfloat16)
-    partial_value = jnp.dot(hidden, down_w[0], preferred_element_type=jnp.float32).astype(
-        jnp.bfloat16
-    )
-    summed = tp_scatter_sum(partial_value, 1)
+    summed = expert_block(arrived.reshape(buffer_len, feat_part), gate_w[0], up_w[0], down_w[0])
     returned = exchange(summed.reshape(experts, capacity, feat_part), half_count).reshape(
         buffer_len, feat_part
     )

time: 119 us -> 107 us (0.90)
  other arithmetic: 14.3 us -> 7.46 us
  local copies, waits for them, and re-layouts: 23.8 us -> 19 us
  waiting for transfers between devices: 28 us -> 25.7 us
  matrix products: 19.1 us -> 20.3 us
    concatenate x1 -> x0, local copies, waits for them, and re-layouts: 4.64 us -> none  [tp_gather(): return jnp.concatenate([low, high], axis=axis)]
    select_n x2 -> x0, other arithmetic: 4.28 us -> none  [the longest x1 2.2 us: tp_scatter_sum(): send = jnp.where(first, high, low)]
    ppermute x2, waiting for transfers between devices: 6.72 us -> 4.45 us  [the longest x1 3.32 us: expert_block(): sent = lax.ppermute(down_product(other), 'tp', perm=swap)]
    concatenate x1 -> x0, other arithmetic: 1.93 us -> none  [tp_gather(): return jnp.concatenate([low, high], axis=axis)]
    dot_general x2 -> x6, matrix products: 13.3 us -> 14.6 us  [the longest x4 9.93 us: half_product(): return jnp.dot(x, weight, preferred_element_type=jnp.float32)]
    unnamed x43 -> x47, local copies, waits for them, and re-layouts: 7.92 us -> 7.9 us
  transfers between devices with their start and end apart: 16 -> 16, of which waited for: 10 -> 10; matrix products, arithmetic and copies ran while one was open for 4% -> 7% of each run, Pallas kernels for 0% -> 0%
where the time goes in v4:
time: 107 us; the launch traced here: 106 us
  waiting for transfers between devices  25.7 us (24%)
  starting transfers between devices  21.8 us (20%)
  matrix products  20.3 us (19%)
  local copies, waits for them, and re-layouts  19 us (18%)
  blocking collectives  11.3 us (11%)
  other arithmetic  7.46 us (7%)
    ppermute x14, starting transfers between devices, exchange(): pieces.append(lax.ppermute(chunks[step], 'el', perm=pairs))  21.7 us
    ppermute x14, waiting for transfers between devices, exchange(): pieces.append(lax.ppermute(chunks[step], 'el', perm=pairs))  21.3 us
    dot_general x4, matrix products, half_product(): return jnp.dot(x, weight, preferred_element_type=jnp.float32)  9.93 us
    unnamed x47, local copies, waits for them, and re-layouts  7.9 us
    all_gather x3, blocking collectives, merged(): lax.all_gather(a.astype(kind), axis)  6.21 us
    dot_general x2, matrix products, down_product(): jnp.dot(hidden, weight, preferred_element_type=jnp.float32)  4.71 us
    slice x2, local copies, waits for them, and re-layouts, one_group(): flattened_cache[:, :KEY_VALUE_HEADS * HEAD_SIZE]  3.77 us
    gather x1, local copies, waits for them, and re-layouts, one_group(): page_row_block = group_pages[local_table.reshape(-1)]  3.32 us
  transfers between devices with their start and end apart: 16, of which 10 were waited for; matrix products, arithmetic and copies ran while one was open for 7% of the time, Pallas kernels for 0%

profile of v4, /device:TPU:0, one launch (start us, length us, event | category | flops | bytes accessed | tf_op | source)
XLA Modules:
  0.0 106.0 jit_solution(17121074748247785869)
XLA Ops:
  3.3 3.3 %gather_fusion = bf16[96,16,512]{2,1,0:T(8,128)(2,1)} fusion(bf16[96,16,512]{2,1,0:T(8,128)(2,1)} %bitcast.133, s32[1024]{0:T(1024)S(1)} %pad_clamp_fusion), kind=kCustom, calls=%fused_computation | custom fusion | bytes 3146112 | tf_op jit(solution)/shard_map/while/body/eval_jaxpr/gather | solution.py:159
  6.6 2.4 %fusion.71 = (bf16[1536,256]{1,0:T(8,128)(2,1)}, bf16[1536,256]{1,0:T(8,128)(2,1)S(1)}) fusion(bf16[1536,512]{1,0:T(8,128)(2,1)} %bitcast.129), kind=kLoop, calls=%fused_computation.130 | loop fusion | bytes 3145728 | tf_op jit(solution)/shard_map/while/body/eval_jaxpr/slice | solution.py:162
  21.0 2.6 %all-gather = bf16[256,2,6,128]{0,3,2,1:T(8,128)(2,1)S(1)} all-gather(bf16[128,2,6,128]{0,3,2,1:T(8,128)(2,1)S(1)} %fusion.12), channel_id=2, replica_groups=mesh['eh'=2,'el'=8,'tp'=2] {'tp'}, dimensions={0}, use_global_device_ids=true | all-gather | bytes 1179648 | tf_op jit(solution)/shard_map/all_gather | solution.py:17
  30.1 2.6 %psum.14 = f32[128]{0:T(128)S(1)} all-reduce(f32[128]{0:T(128)S(1)} %get-tuple-element.80), channel_id=1, replica_groups=mesh['eh'=2,'el'=8,'tp'=2] {'tp'}, use_global_device_ids=true, to_apply=%region_11.12 | all-reduce | flops 128 | bytes 1024 | tf_op jit(solution)/shard_map/psum | solution.py:204
  33.5 2.9 %collective-permute-start = (bf16[128,768]{1,0:T(8,128)(2,1)S(1)}, bf16[128,768]{1,0:T(8,128)(2,1)S(1)}, u32[]{:S(2)}, u32[]{:S(2)}) collective-permute-start(bf16[128,768]{1,0:T(8,128)(2,1)S(1)} %get-tuple-element.62), channel_id=1, source_target_pairs={{0,2},{2,0},{4,6},{6,4},{8,10},{10,8},{12,14},{14,12},{1,3},{3,1},... | collective-permute-start | bytes 589832 | tf_op jit(solution)/shard_map/ppermute | solution.py:47
  37.9 2.0 %collective-permute-start.3 = (bf16[128,768]{1,0:T(8,128)(2,1)S(1)}, bf16[128,768]{1,0:T(8,128)(2,1)S(1)}, u32[]{:S(2)}, u32[]{:S(2)}) collective-permute-start(bf16[128,768]{1,0:T(8,128)(2,1)S(1)} %get-tuple-element.59), channel_id=1, source_target_pairs={{0,8},{2,10},{4,12},{6,14},{8,0},{10,2},{12,4},{14,6},{1,9},{3,11}... | collective-permute-start | bytes 589832 | tf_op jit(solution)/shard_map/ppermute | solution.py:47
  42.1 3.1 %collective-permute-start.5 = (bf16[128,768]{1,0:T(8,128)(2,1)S(1)}, bf16[128,768]{1,0:T(8,128)(2,1)S(1)}, u32[]{:S(2)}, u32[]{:S(2)}) collective-permute-start(bf16[128,768]{1,0:T(8,128)(2,1)S(1)} %get-tuple-element.57), channel_id=1, source_target_pairs={{0,12},{2,14},{4,8},{6,10},{8,4},{10,6},{12,0},{14,2},{1,13},{3,15... | collective-permute-start | bytes 589832 | tf_op jit(solution)/shard_map/ppermute | solution.py:47
  47.9 2.4 %collective-permute-done.2 = bf16[128,768]{1,0:T(8,128)(2,1)S(1)} collective-permute-done((bf16[128,768]{1,0:T(8,128)(2,1)S(1)}, bf16[128,768]{1,0:T(8,128)(2,1)S(1)}, u32[]{:S(2)}, u32[]{:S(2)}) %collective-permute-start.2) | collective-permute-done | bytes 196640 | tf_op jit(solution)/shard_map/ppermute | solution.py:47
  52.4 3.2 %collective-permute-done.5 = bf16[128,768]{1,0:T(8,128)(2,1)S(1)} collective-permute-done((bf16[128,768]{1,0:T(8,128)(2,1)S(1)}, bf16[128,768]{1,0:T(8,128)(2,1)S(1)}, u32[]{:S(2)}, u32[]{:S(2)}) %collective-permute-start.5) | collective-permute-done | bytes 196640 | tf_op jit(solution)/shard_map/ppermute | solution.py:47
  56.3 2.8 %collective-permute-done.6 = bf16[128,768]{1,0:T(8,128)(2,1)S(1)} collective-permute-done((bf16[128,768]{1,0:T(8,128)(2,1)S(1)}, bf16[128,768]{1,0:T(8,128)(2,1)S(1)}, u32[]{:S(2)}, u32[]{:S(2)}) %collective-permute-start.6) | collective-permute-done | bytes 196640 | tf_op jit(solution)/shard_map/ppermute | solution.py:47
  59.8 2.6 %fusion.22 = f32[1024,384]{1,0:T(8,128)S(1)} fusion(bf16[1024,768]{1,0:T(8,128)(2,1)} %bitcast.27, bf16[2,768,384]{2,1,0:T(8,128)(2,1)} %bitcast.141, s32[]{:T(128)S(6)} %select_n.100), kind=kOutput, calls=%fused_computation.32 | convolution fusion | flops 603979776 | bytes 3735556 | tf_op jit(solution)/shard_map/dot_general | solution.py:71
  63.5 2.4 %fusion.20 = f32[1024,384]{1,0:T(8,128)S(1)} fusion(bf16[1024,768]{1,0:T(8,128)(2,1)} %collective-permute-done.7, bf16[2,768,384]{2,1,0:T(8,128)(2,1)S(1)} %bitcast.142, s32[]{:T(128)S(6)} %select_n.109), kind=kOutput, calls=%fused_computation.30 | convolution fusion | flops 603979776 | bytes 3735556 | tf_op jit(solution)/shard_map/dot_general | solution.py:71
  65.9 2.4 %fusion.17 = f32[1024,384]{1,0:T(8,128)S(1)} fusion(bf16[1024,768]{1,0:T(8,128)(2,1)} %collective-permute-done.7, bf16[2,768,384]{2,1,0:T(8,128)(2,1)S(1)} %bitcast.136, s32[]{:T(128)S(6)} %select_n.109), kind=kOutput, calls=%fused_computation.27 | convolution fusion | flops 603979776 | bytes 3735556 | tf_op jit(solution)/shard_map/dot_general | solution.py:71
  68.3 2.6 %multiply_convert_fusion = bf16[1024,384]{1,0:T(8,128)(2,1)S(1)} fusion(f32[1024,384]{1,0:T(8,128)S(1)} %fusion.17, f32[1024,384]{1,0:T(8,128)S(1)} %fusion.22, f32[1024,384]{1,0:T(8,128)S(1)} %fusion.20, bf16[1024,768]{1,0:T(8,128)(2,1)} %bitcast.27, bf16[2,768,384]{2,1,0:T(8,128)(2,1)S(1)} %bitcast.137, s32[]{:T(128)S(6)} %select_n.100), kind=kOutput, calls=%fused_computation.18 | convolution fusion | flops 605945856 | bytes 7667716 | tf_op jit(solution)/shard_map/dot_general | solution.py:71
  70.9 2.1 %convolution_convert_fusion.1 = bf16[1024,768]{1,0:T(8,128)(2,1)} fusion(bf16[1024,384]{1,0:T(8,128)(2,1)S(1)} %multiply_convert_fusion, bf16[1,384,1536]{2,1,0:T(8,128)(2,1)S(1)} %copy-done.2, s32[]{:T(128)S(6)} %select_n.111), kind=kOutput, calls=%fused_computation.16 | convolution fusion | flops 604766208 | bytes 2949124 | tf_op jit(solution)/shard_map/dot_general | solution.py:79
  73.5 3.3 %collective-permute-done.8 = bf16[1024,768]{1,0:T(8,128)(2,1)} collective-permute-done((bf16[1024,768]{1,0:T(8,128)(2,1)}, bf16[1024,768]{1,0:T(8,128)(2,1)}, u32[]{:S(2)}, u32[]{:S(2)}) %collective-permute-start.8) | collective-permute-done | bytes 1572896 | tf_op jit(solution)/shard_map/ppermute | solution.py:81
  76.8 2.6 %add_convert_fusion = bf16[1024,768]{1,0:T(8,128)(2,1)S(1)} fusion(bf16[1024,768]{1,0:T(8,128)(2,1)} %collective-permute-done.8, bf16[1024,384]{1,0:T(8,128)(2,1)S(1)} %multiply_convert_fusion, bf16[1,384,1536]{2,1,0:T(8,128)(2,1)} %param.26, s32[]{:T(128)S(6)} %select_n.110), kind=kOutput, calls=%fused_computation.10 | convolution fusion | flops 607911936 | bytes 4521988 | tf_op jit(solution)/shard_map/dot_general | solution.py:79
  80.7 2.3 %collective-permute-start.11 = (bf16[128,768]{1,0:T(8,128)(2,1)S(1)}, bf16[128,768]{1,0:T(8,128)(2,1)S(1)}, u32[]{:S(2)}, u32[]{:S(2)}) collective-permute-start(bf16[128,768]{1,0:T(8,128)(2,1)S(1)} %get-tuple-element.45), channel_id=1, source_target_pairs={{0,6},{2,4},{4,2},{6,0},{8,14},{10,12},{12,10},{14,8},{1,7},{3,5},... | collective-permute-start | bytes 589832 | tf_op jit(solution)/shard_map/ppermute | solution.py:47
  85.1 2.2 %collective-permute-done.9 = bf16[128,768]{1,0:T(8,128)(2,1)S(1)} collective-permute-done((bf16[128,768]{1,0:T(8,128)(2,1)S(1)}, bf16[128,768]{1,0:T(8,128)(2,1)S(1)}, u32[]{:S(2)}, u32[]{:S(2)}) %collective-permute-start.9) | collective-permute-done | bytes 196640 | tf_op jit(solution)/shard_map/ppermute | solution.py:47
  88.8 2.3 %collective-permute-start.15 = (bf16[128,768]{1,0:T(8,128)(2,1)S(1)}, bf16[128,768]{1,0:T(8,128)(2,1)S(1)}, u32[]{:S(2)}, u32[]{:S(2)}) collective-permute-start(bf16[128,768]{1,0:T(8,128)(2,1)S(1)} %get-tuple-element.41), channel_id=1, source_target_pairs={{0,14},{2,12},{4,10},{6,8},{8,6},{10,4},{12,2},{14,0},{1,15},{3,13... | collective-permute-start | bytes 589832 | tf_op jit(solution)/shard_map/ppermute | solution.py:47
  91.2 3.4 %collective-permute-done.11 = bf16[128,768]{1,0:T(8,128)(2,1)S(1)} collective-permute-done((bf16[128,768]{1,0:T(8,128)(2,1)S(1)}, bf16[128,768]{1,0:T(8,128)(2,1)S(1)}, u32[]{:S(2)}, u32[]{:S(2)}) %collective-permute-start.11) | collective-permute-done | bytes 196640 | tf_op jit(solution)/shard_map/ppermute | solution.py:47
  95.1 4.2 %collective-permute-done.14 = bf16[128,768]{1,0:T(8,128)(2,1)S(1)} collective-permute-done((bf16[128,768]{1,0:T(8,128)(2,1)S(1)}, bf16[128,768]{1,0:T(8,128)(2,1)S(1)}, u32[]{:S(2)}, u32[]{:S(2)}) %collective-permute-start.14) | collective-permute-done | bytes 196640 | tf_op jit(solution)/shard_map/ppermute | solution.py:47
  99.3 2.5 %collective-permute-done.15 = bf16[128,768]{1,0:T(8,128)(2,1)S(1)} collective-permute-done((bf16[128,768]{1,0:T(8,128)(2,1)S(1)}, bf16[128,768]{1,0:T(8,128)(2,1)S(1)}, u32[]{:S(2)}, u32[]{:S(2)}) %collective-permute-start.15) | collective-permute-done | bytes 196640 | tf_op jit(solution)/shard_map/ppermute | solution.py:47
  102.8 2.5 %psum.15 = f32[128]{0:T(128)S(1)} all-reduce(f32[128]{0:T(128)S(1)} %get-tuple-element.82), channel_id=1, replica_groups=mesh['eh'=2,'el'=8,'tp'=2] {'tp'}, use_global_device_ids=true, to_apply=%region_13.14 | all-reduce | flops 128 | bytes 1024 | tf_op jit(solution)/shard_map/psum | solution.py:248
  (111 shorter events, 41.0 us)
Async XLA Ops:
  0.0 29.5 %copy-start = (bf16[1536,768]{1,0:T(8,128)(2,1)S(1)}, bf16[1536,768]{1,0:T(8,128)(2,1)}, u32[]{:S(2)}) copy-start(bf16[1536,768]{1,0:T(8,128)(2,1)} %param.20) | copy-start | bytes 7077892
  18.9 8.2 %copy-start.5 = (s32[4,128]{1,0:T(4,128)S(1)}, s32[4,128]{1,0:T(4,128)}, u32[]{:S(2)}) copy-start(s32[4,128]{1,0:T(4,128)} %eq.108) | copy-start | bytes 6148
  19.0 9.7 %copy-start.7 = (s32[512]{0:T(512)S(1)}, s32[512]{0:T(512)}, u32[]{:S(2)}) copy-start(s32[512]{0:T(512)} %eq.104) | copy-start | bytes 6148
  19.0 9.9 %copy-start.6 = (s32[128,4]{0,1:T(4,128)S(1)}, s32[128,4]{0,1:T(4,128)}, u32[]{:S(2)}) copy-start(s32[128,4]{0,1:T(4,128)} %param.22) | copy-start | bytes 6148
  21.0 8.5 %copy-start.4 = (bf16[128,768]{1,0:T(8,128)(2,1)S(1)}, bf16[128,768]{1,0:T(8,128)(2,1)}, u32[]{:S(2)}) copy-start(bf16[128,768]{1,0:T(8,128)(2,1)} %param.14) | copy-start | bytes 589828
  33.5 8.6 %collective-permute-start = (bf16[128,768]{1,0:T(8,128)(2,1)S(1)}, bf16[128,768]{1,0:T(8,128)(2,1)S(1)}, u32[]{:S(2)}, u32[]{:S(2)}) collective-permute-start(bf16[128,768]{1,0:T(8,128)(2,1)S(1)} %get-tuple-element.62), channel_id=1, source_target_pairs={{0,2},{2,0},{4,6},{6,4},{8,10},{10,8},{12,14},{14,12},{1,3},{3,1},... | collective-permute-start | bytes 589832 | tf_op jit(solution)/shard_map/ppermute | solution.py:47
  36.4 9.5 %collective-permute-start.1 = (bf16[128,768]{1,0:T(8,128)(2,1)S(1)}, bf16[128,768]{1,0:T(8,128)(2,1)S(1)}, u32[]{:S(2)}, u32[]{:S(2)}) collective-permute-start(bf16[128,768]{1,0:T(8,128)(2,1)S(1)} %get-tuple-element.61), channel_id=1, source_target_pairs={{0,4},{2,6},{4,0},{6,2},{8,12},{10,14},{12,8},{14,10},{1,5},{3,7},... | collective-permute-start | bytes 589832 | tf_op jit(solution)/shard_map/ppermute | solution.py:47
  37.9 12.4 %collective-permute-start.2 = (bf16[128,768]{1,0:T(8,128)(2,1)S(1)}, bf16[128,768]{1,0:T(8,128)(2,1)S(1)}, u32[]{:S(2)}, u32[]{:S(2)}) collective-permute-start(bf16[128,768]{1,0:T(8,128)(2,1)S(1)} %get-tuple-element.60), channel_id=1, source_target_pairs={{0,6},{2,4},{4,2},{6,0},{8,14},{10,12},{12,10},{14,8},{1,7},{3,5},... | collective-permute-start | bytes 589832 | tf_op jit(solution)/shard_map/ppermute | solution.py:47
  37.9 13.1 %collective-permute-start.3 = (bf16[128,768]{1,0:T(8,128)(2,1)S(1)}, bf16[128,768]{1,0:T(8,128)(2,1)S(1)}, u32[]{:S(2)}, u32[]{:S(2)}) collective-permute-start(bf16[128,768]{1,0:T(8,128)(2,1)S(1)} %get-tuple-element.59), channel_id=1, source_target_pairs={{0,8},{2,10},{4,12},{6,14},{8,0},{10,2},{12,4},{14,6},{1,9},{3,11}... | collective-permute-start | bytes 589832 | tf_op jit(solution)/shard_map/ppermute | solution.py:47
  40.0 11.7 %collective-permute-start.4 = (bf16[128,768]{1,0:T(8,128)(2,1)S(1)}, bf16[128,768]{1,0:T(8,128)(2,1)S(1)}, u32[]{:S(2)}, u32[]{:S(2)}) collective-permute-start(bf16[128,768]{1,0:T(8,128)(2,1)S(1)} %get-tuple-element.58), channel_id=1, source_target_pairs={{0,10},{2,8},{4,14},{6,12},{8,2},{10,0},{12,6},{14,4},{1,11},{3,9}... | collective-permute-start | bytes 589832 | tf_op jit(solution)/shard_map/ppermute | solution.py:47
  42.1 13.5 %collective-permute-start.5 = (bf16[128,768]{1,0:T(8,128)(2,1)S(1)}, bf16[128,768]{1,0:T(8,128)(2,1)S(1)}, u32[]{:S(2)}, u32[]{:S(2)}) collective-permute-start(bf16[128,768]{1,0:T(8,128)(2,1)S(1)} %get-tuple-element.57), channel_id=1, source_target_pairs={{0,12},{2,14},{4,8},{6,10},{8,4},{10,6},{12,0},{14,2},{1,13},{3,15... | collective-permute-start | bytes 589832 | tf_op jit(solution)/shard_map/ppermute | solution.py:47
  45.9 13.2 %collective-permute-start.6 = (bf16[128,768]{1,0:T(8,128)(2,1)S(1)}, bf16[128,768]{1,0:T(8,128)(2,1)S(1)}, u32[]{:S(2)}, u32[]{:S(2)}) collective-permute-start(bf16[128,768]{1,0:T(8,128)(2,1)S(1)} %get-tuple-element.56), channel_id=1, source_target_pairs={{0,14},{2,12},{4,10},{6,8},{8,6},{10,4},{12,2},{14,0},{1,15},{3,13... | collective-permute-start | bytes 589832 | tf_op jit(solution)/shard_map/ppermute | solution.py:47
  59.8 3.8 %collective-permute-start.7 = (bf16[1024,768]{1,0:T(8,128)(2,1)}, bf16[1024,768]{1,0:T(8,128)(2,1)}, u32[]{:S(2)}, u32[]{:S(2)}) collective-permute-start(bf16[1024,768]{1,0:T(8,128)(2,1)} %bitcast.27), channel_id=1, source_target_pairs={{0,1},{1,0},{2,3},{3,2},{4,5},{5,4},{6,7},{7,6},{8,9},{9,8},{10,11... | collective-permute-start | bytes 4718600 | tf_op jit(solution)/shard_map/ppermute | solution.py:65
  59.8 3.8 %copy-start.14 = (bf16[1,1536,384]{2,1,0:T(8,128)(2,1)S(1)}, bf16[1,1536,384]{2,1,0:T(8,128)(2,1)}, u32[]{:S(2)}) copy-start(bf16[1,1536,384]{2,1,0:T(8,128)(2,1)} %param.24) | copy-start | bytes 3538948
  62.4 3.5 %copy-start.3 = (bf16[1,1536,384]{2,1,0:T(8,128)(2,1)S(1)}, bf16[1,1536,384]{2,1,0:T(8,128)(2,1)}, u32[]{:S(2)}) copy-start(bf16[1,1536,384]{2,1,0:T(8,128)(2,1)} %param.25) | copy-start | bytes 3538948
  73.1 3.8 %collective-permute-start.8 = (bf16[1024,768]{1,0:T(8,128)(2,1)}, bf16[1024,768]{1,0:T(8,128)(2,1)}, u32[]{:S(2)}, u32[]{:S(2)}) collective-permute-start(bf16[1024,768]{1,0:T(8,128)(2,1)} %convolution_convert_fusion.1), channel_id=1, source_target_pairs={{0,1},{1,0},{2,3},{3,2},{4,5},{5,4},{6,7},{7,6},{8,9},{9,8},{10,11... | collective-permute-start | bytes 4718600 | tf_op jit(solution)/shard_map/ppermute | solution.py:81
  79.5 7.8 %collective-permute-start.9 = (bf16[128,768]{1,0:T(8,128)(2,1)S(1)}, bf16[128,768]{1,0:T(8,128)(2,1)S(1)}, u32[]{:S(2)}, u32[]{:S(2)}) collective-permute-start(bf16[128,768]{1,0:T(8,128)(2,1)S(1)} %get-tuple-element.47), channel_id=1, source_target_pairs={{0,2},{2,0},{4,6},{6,4},{8,10},{10,8},{12,14},{14,12},{1,3},{3,1},... | collective-permute-start | bytes 589832 | tf_op jit(solution)/shard_map/ppermute | solution.py:47
  80.1 8.7 %collective-permute-start.10 = (bf16[128,768]{1,0:T(8,128)(2,1)S(1)}, bf16[128,768]{1,0:T(8,128)(2,1)S(1)}, u32[]{:S(2)}, u32[]{:S(2)}) collective-permute-start(bf16[128,768]{1,0:T(8,128)(2,1)S(1)} %get-tuple-element.46), channel_id=1, source_target_pairs={{0,4},{2,6},{4,0},{6,2},{8,12},{10,14},{12,8},{14,10},{1,5},{3,7},... | collective-permute-start | bytes 589832 | tf_op jit(solution)/shard_map/ppermute | solution.py:47
  80.7 13.9 %collective-permute-start.11 = (bf16[128,768]{1,0:T(8,128)(2,1)S(1)}, bf16[128,768]{1,0:T(8,128)(2,1)S(1)}, u32[]{:S(2)}, u32[]{:S(2)}) collective-permute-start(bf16[128,768]{1,0:T(8,128)(2,1)S(1)} %get-tuple-element.45), channel_id=1, source_target_pairs={{0,6},{2,4},{4,2},{6,0},{8,14},{10,12},{12,10},{14,8},{1,7},{3,5},... | collective-permute-start | bytes 589832 | tf_op jit(solution)/shard_map/ppermute | solution.py:47
  83.0 11.6 %collective-permute-start.12 = (bf16[128,768]{1,0:T(8,128)(2,1)S(1)}, bf16[128,768]{1,0:T(8,128)(2,1)S(1)}, u32[]{:S(2)}, u32[]{:S(2)}) collective-permute-start(bf16[128,768]{1,0:T(8,128)(2,1)S(1)} %get-tuple-element.44), channel_id=1, source_target_pairs={{0,8},{2,10},{4,12},{6,14},{8,0},{10,2},{12,4},{14,6},{1,9},{3,11}... | collective-permute-start | bytes 589832 | tf_op jit(solution)/shard_map/ppermute | solution.py:47
  84.6 10.5 %collective-permute-start.13 = (bf16[128,768]{1,0:T(8,128)(2,1)S(1)}, bf16[128,768]{1,0:T(8,128)(2,1)S(1)}, u32[]{:S(2)}, u32[]{:S(2)}) collective-permute-start(bf16[128,768]{1,0:T(8,128)(2,1)S(1)} %get-tuple-element.43), channel_id=1, source_target_pairs={{0,10},{2,8},{4,14},{6,12},{8,2},{10,0},{12,6},{14,4},{1,11},{3,9}... | collective-permute-start | bytes 589832 | tf_op jit(solution)/shard_map/ppermute | solution.py:47
  87.3 12.0 %collective-permute-start.14 = (bf16[128,768]{1,0:T(8,128)(2,1)S(1)}, bf16[128,768]{1,0:T(8,128)(2,1)S(1)}, u32[]{:S(2)}, u32[]{:S(2)}) collective-permute-start(bf16[128,768]{1,0:T(8,128)(2,1)S(1)} %get-tuple-element.42), channel_id=1, source_target_pairs={{0,12},{2,14},{4,8},{6,10},{8,4},{10,6},{12,0},{14,2},{1,13},{3,15... | collective-permute-start | bytes 589832 | tf_op jit(solution)/shard_map/ppermute | solution.py:47
  88.8 13.0 %collective-permute-start.15 = (bf16[128,768]{1,0:T(8,128)(2,1)S(1)}, bf16[128,768]{1,0:T(8,128)(2,1)S(1)}, u32[]{:S(2)}, u32[]{:S(2)}) collective-permute-start(bf16[128,768]{1,0:T(8,128)(2,1)S(1)} %get-tuple-element.41), channel_id=1, source_target_pairs={{0,14},{2,12},{4,10},{6,8},{8,6},{10,4},{12,2},{14,0},{1,15},{3,13... | collective-permute-start | bytes 589832 | tf_op jit(solution)/shard_map/ppermute | solution.py:47
  99.3 5.9 %copy-start.9 = (f32[768]{0:T(1024)S(1)}, f32[768]{0:T(1024)}, u32[]{:S(2)}) copy-start(f32[768]{0:T(1024)} %param.27) | copy-start | bytes 9220
  (7 other events, 13.2 us)

commit v5 on v4

--- a/solution.py
+++ b/solution.py
@@ -1,6 +1,8 @@
 import jax
 import jax.numpy as jnp
 from jax import lax
+from jax.experimental import pallas as pl
+from jax.experimental.pallas import tpu as pltpu
 from jax.sharding import Mesh, NamedSharding, PartitionSpec as P
 
 QUERY_HEADS = 12
@@ -13,6 +15,11 @@
 
 
 def merged(shard, axis, join):
+    if lax.axis_size(axis) == 2:
+        rounded = jax.tree.map(lambda a: a.astype(jnp.bfloat16), shard)
+        other = jax.tree.map(lambda a: lax.ppermute(a, axis, perm=[(0, 1), (1, 0)]), rounded)
+        widen = lambda tree: jax.tree.map(lambda a, own: a.astype(own.dtype), tree, shard)
+        return join(widen(rounded), widen(other))
     gathered = jax.tree.map(
         lambda a, kind: lax.all_gather(a.astype(kind), axis),
         shard,
@@ -79,8 +86,14 @@
         return jnp.dot(hidden, weight, preferred_element_type=jnp.float32).astype(jnp.bfloat16)
 
     sent = lax.ppermute(down_product(other), "tp", perm=swap)
-    kept = down_product(mine)
+    kept = lax.optimization_barrier(down_product(mine))
     return (kept.astype(jnp.float32) + sent.astype(jnp.float32)).astype(jnp.bfloat16)
+
+
+def tp_sum(value):
+    if lax.axis_size("tp") != 2:
+        return lax.psum(value, "tp")
+    return value + lax.ppermute(value, "tp", perm=[(0, 1), (1, 0)])
 
 
 def tp_gather(part, axis):
@@ -112,6 +125,94 @@
         joint_max,
         first[1] * scale_first + second[1] * scale_second,
         first[2] * scale_first[..., None] + second[2] * scale_second[..., None],
+    )
+
+
+ATTN_BLOCK = 32
+
+
+def attention_kernel(bounds_ref, q_ref, kv_ref, rreq_ref, rpos_ref, kpos_ref, w_ref, m_ref, l_ref):
+    head_groups = QUERY_HEADS // KEY_VALUE_HEADS
+    keys = kpos_ref.shape[1]
+    scale = HEAD_SIZE ** (-0.5)
+    w_ref[...] = jnp.zeros(w_ref.shape, jnp.float32)
+    m_ref[...] = jnp.zeros(m_ref.shape, jnp.float32)
+    l_ref[...] = jnp.zeros(l_ref.shape, jnp.float32)
+    for block in range(q_ref.shape[0] // ATTN_BLOCK):
+        rows = pl.ds(block * ATTN_BLOCK, ATTN_BLOCK)
+        row_req = rreq_ref[rows, :]
+        allowed = kpos_ref[...] <= rpos_ref[rows, :]
+        allowed_heads = jnp.concatenate([allowed] * head_groups, axis=0)
+
+        def body(request, carry, rows=rows, row_req=row_req, allowed_heads=allowed_heads):
+            picked = row_req == request
+            first_key = pl.multiple_of(request * keys, 128)
+            for kv_head in range(KEY_VALUE_HEADS):
+                stacked = jnp.concatenate(
+                    [
+                        q_ref[rows, pl.ds((kv_head * head_groups + g) * HEAD_SIZE, HEAD_SIZE)]
+                        for g in range(head_groups)
+                    ],
+                    axis=0,
+                )
+                key_block = kv_ref[pl.ds(first_key, keys), pl.ds(kv_head * HEAD_SIZE, HEAD_SIZE)]
+                value_block = kv_ref[
+                    pl.ds(first_key, keys),
+                    pl.ds((KEY_VALUE_HEADS + kv_head) * HEAD_SIZE, HEAD_SIZE),
+                ]
+                scores = lax.dot_general(
+                    stacked,
+                    key_block,
+                    (((1,), (1,)), ((), ())),
+                    preferred_element_type=jnp.float32,
+                ) * scale
+                scores = jnp.where(allowed_heads, scores, -1e30)
+                top = jnp.max(scores, axis=1, keepdims=True)
+                soft = jnp.where(allowed_heads, jnp.exp(scores - top), 0.0)
+                total = jnp.sum(soft, axis=1, keepdims=True)
+                weighted = jnp.dot(
+                    soft.astype(jnp.bfloat16), value_block, preferred_element_type=jnp.float32
+                )
+                for g in range(head_groups):
+                    head = kv_head * head_groups + g
+                    part = slice(g * ATTN_BLOCK, (g + 1) * ATTN_BLOCK)
+                    cols = pl.ds(head * HEAD_SIZE, HEAD_SIZE)
+                    w_ref[rows, cols] = jnp.where(picked, weighted[part], w_ref[rows, cols])
+                    one = pl.ds(head, 1)
+                    m_ref[rows, one] = jnp.where(picked, top[part], m_ref[rows, one])
+                    l_ref[rows, one] = jnp.where(picked, total[part], l_ref[rows, one])
+            return carry
+
+        lax.fori_loop(bounds_ref[2 * block], bounds_ref[2 * block + 1] + 1, body, 0)
+
+
+def paged_attention(queries, cache_rows, row_req, row_pos, key_pos):
+    rows = queries.shape[0]
+    blocks = rows // ATTN_BLOCK
+    bounds = jnp.stack(
+        [row_req[0::ATTN_BLOCK], row_req[ATTN_BLOCK - 1 :: ATTN_BLOCK]], axis=1
+    ).reshape(2 * blocks)
+    vmem = pl.BlockSpec(memory_space=pltpu.VMEM)
+    weighted, top, total = pl.pallas_call(
+        attention_kernel,
+        out_shape=(
+            jax.ShapeDtypeStruct((rows, QUERY_HEADS * HEAD_SIZE), jnp.float32),
+            jax.ShapeDtypeStruct((rows, QUERY_HEADS), jnp.float32),
+            jax.ShapeDtypeStruct((rows, QUERY_HEADS), jnp.float32),
+        ),
+        in_specs=[pl.BlockSpec(memory_space=pltpu.SMEM)] + [vmem] * 5,
+        out_specs=(vmem, vmem, vmem),
+        cost_estimate=pl.CostEstimate(
+            flops=4 * rows * QUERY_HEADS * HEAD_SIZE * key_pos.shape[1] * 2,
+            transcendentals=rows * QUERY_HEADS * key_pos.shape[1] * 2,
+            bytes_accessed=queries.size * 2 + cache_rows.size * 2 + rows * QUERY_HEADS * HEAD_SIZE * 4,
+        ),
+    )(bounds, queries, cache_rows, row_req[:, None], row_pos[:, None], key_pos)
+    head_groups = QUERY_HEADS // KEY_VALUE_HEADS
+    return (
+        top.reshape(rows, KEY_VALUE_HEADS, head_groups),
+        total.reshape(rows, KEY_VALUE_HEADS, head_groups),
+        weighted.reshape(rows, KEY_VALUE_HEADS, head_groups, HEAD_SIZE),
     )
 
 
@@ -171,6 +272,11 @@
         key_pos = (
             within // PAGE_POSITIONS * tp_count + tp_index
         ) * PAGE_POSITIONS + within % PAGE_POSITIONS
+        keys_per_req = per_device * PAGE_POSITIONS
+        if keys_per_req % 128 == 0 and group_rows % ATTN_BLOCK == 0:
+            return paged_attention(
+                queries, flattened_cache, row_req, row_pos, key_pos[None, :keys_per_req]
+            )
         allowed = (row_req[:, None] == key_req[None, :]) & (key_pos[None, :] <= row_pos[:, None])
         query_head_rows = queries.reshape(group_rows, KEY_VALUE_HEADS, head_groups, HEAD_SIZE)
         scores = jnp.einsum(
@@ -201,7 +307,7 @@
     resid = tokens.astype(jnp.float32) + jnp.dot(
         attended, out_weight, preferred_element_type=jnp.float32
     )
-    mid_squares = lax.psum(jnp.sum(resid * resid, axis=1), "tp")
+    mid_squares = tp_sum(jnp.sum(resid * resid, axis=1))
     normed = (resid * lax.rsqrt(mid_squares / full_width + EPSILON)[:, None] * norm_gain).astype(
         jnp.bfloat16
     )
@@ -214,9 +320,12 @@
     expert_onehot = (flat_ids[:, None] == jnp.arange(experts, dtype=jnp.int32)[None, :]).astype(
         jnp.int32
     )
-    expert_rank = jnp.sum(
-        (jnp.cumsum(expert_onehot, axis=0) - expert_onehot) * expert_onehot, axis=1
-    )
+    assign_iota = jnp.arange(flat_ids.shape[0], dtype=jnp.int32)
+    earlier = (assign_iota[None, :] < assign_iota[:, None]).astype(jnp.bfloat16)
+    before = jnp.dot(
+        earlier, expert_onehot.astype(jnp.bfloat16), preferred_element_type=jnp.float32
+    ).astype(jnp.int32)
+    expert_rank = jnp.sum(before * expert_onehot, axis=1)
     my_half = lax.axis_index("el")
     target = (relative(flat_ids, my_half, half_count) * capacity + expert_rank).reshape(
         count_of_rows, top_count
@@ -226,7 +335,17 @@
     dispatch = jnp.any(hits, axis=2).astype(jnp.bfloat16)
     outgoing = jnp.dot(dispatch, normed, preferred_element_type=jnp.float32).astype(jnp.bfloat16)
     arrived = exchange(outgoing.reshape(experts, capacity, feat_part), half_count)
-    summed = expert_block(arrived.reshape(buffer_len, feat_part), gate_w[0], up_w[0], down_w[0])
+    flat_rows = lax.optimization_barrier(arrived.reshape(buffer_len, feat_part))
+    group_rows = buffer_len // 2
+    summed = jnp.concatenate(
+        [
+            expert_block(
+                flat_rows[start : start + group_rows], gate_w[0], up_w[0], down_w[0]
+            )
+            for start in (0, group_rows)
+        ],
+        axis=0,
+    )
     returned = exchange(summed.reshape(experts, capacity, feat_part), half_count).reshape(
         buffer_len, feat_part
     )
@@ -245,7 +364,7 @@
         preferred_element_type=jnp.float32,
     )
     mixed_rows = resid + branch
-    out_squares = lax.psum(jnp.sum(mixed_rows * mixed_rows, axis=1), "tp")
+    out_squares = tp_sum(jnp.sum(mixed_rows * mixed_rows, axis=1))
     return (
         mixed_rows * lax.rsqrt(out_squares / full_width + EPSILON)[:, None] * final_gain
     ).astype(jnp.bfloat16)

time: 107 us -> 102 us (0.953)
  Pallas kernels: 0 us -> 17.1 us
  blocking collectives: 11.3 us -> 0 us
  matrix products: 20.3 us -> 10.3 us
  local copies, waits for them, and re-layouts: 19 us -> 10.2 us
  waiting for transfers between devices: 25.7 us -> 31 us
  starting transfers between devices: 21.8 us -> 23.8 us
    pallas_call x0 -> x1, Pallas kernels: none -> 17.1 us  [paged_attention(): pl.pallas_call(attention_kernel, out_shape=(jax.ShapeDtypeStruct((rows, Q...]
    ppermute x14, waiting for transfers between devices: 21.3 us -> 29 us  [exchange(): pieces.append(lax.ppermute(chunks[step], 'el', perm=pairs))]
    all_gather x3 -> x0, blocking collectives: 6.21 us -> none  [merged(): lax.all_gather(a.astype(kind), axis)]
    dot_general x4 -> x8, matrix products: 9.93 us -> 4.67 us  [half_product(): return jnp.dot(x, weight, preferred_element_type=jnp.float32)]
    psum x2 -> x0, blocking collectives: 5.12 us -> none  [the longest x1 2.65 us: shards(): mid_squares = lax.psum(jnp.sum(resid * resid, axis=1), 'tp')]
    slice x3, local copies, waits for them, and re-layouts: 4.92 us -> 0.29 us  [the longest x1 0.1 us: shards(): flat_rows[start:start + group_rows]]
    unnamed x47 -> x32, local copies, waits for them, and re-layouts: 7.9 us -> 3.45 us
    ppermute x1 -> x2, waiting for transfers between devices: 3.32 us -> 0.01 us  [expert_block(): sent = lax.ppermute(down_product(other), 'tp', perm=swap)]
  transfers between devices with their start and end apart: 16 -> 23, of which waited for: 10 -> 13; matrix products, arithmetic and copies ran while one was open for 7% -> 11% of each run, Pallas kernels for 0% -> 0%
where the time goes in v5:
time: 102 us; the launch traced here: 101 us
  waiting for transfers between devices  31 us (30%)
  starting transfers between devices  23.8 us (23%)
  Pallas kernels  17.1 us (17%)
  matrix products  10.3 us (10%)
  local copies, waits for them, and re-layouts  10.2 us (10%)
  other arithmetic  8.46 us (8%)
    ppermute x14, waiting for transfers between devices, exchange(): pieces.append(lax.ppermute(chunks[step], 'el', perm=pairs))  29 us
    ppermute x14, starting transfers between devices, exchange(): pieces.append(lax.ppermute(chunks[step], 'el', perm=pairs))  21.3 us
    pallas_call x1, Pallas kernels, paged_attention(): pl.pallas_call(attention_kernel, out_shape=(jax.ShapeDtypeStruct((rows, Q...  17.1 us
    dot_general x8, matrix products, half_product(): return jnp.dot(x, weight, preferred_element_type=jnp.float32)  4.67 us
    unnamed x32, local copies, waits for them, and re-layouts  3.45 us
    gather x1, local copies, waits for them, and re-layouts, one_group(): page_row_block = group_pages[local_table.reshape(-1)]  3.34 us
    convert_element_type x3, other arithmetic, merged(): rounded = jax.tree.map(lambda a: a.astype(jnp.bfloat16), shard)  2.89 us
    dot_general x4, matrix products, down_product(): jnp.dot(hidden, weight, preferred_element_type=jnp.float32)  2.3 us
  transfers between devices with their start and end apart: 23, of which 13 were waited for; matrix products, arithmetic and copies ran while one was open for 11% of the time, Pallas kernels for 0%

profile of v5, /device:TPU:0, one launch (start us, length us, event | category | flops | bytes accessed | tf_op | source)
XLA Modules:
  0.0 101.3 jit_solution(18128251508202009199)
XLA Ops:
  5.8 3.3 %gather_fusion = bf16[96,16,512]{2,1,0:T(8,128)(2,1)} fusion(bf16[96,16,512]{2,1,0:T(8,128)(2,1)} %bitcast.126, s32[1024]{0:T(1024)S(1)} %pad_clamp_fusion), kind=kCustom, calls=%fused_computation | custom fusion | bytes 3146112 | tf_op jit(solution)/shard_map/while/body/eval_jaxpr/gather | solution.py:260
  9.1 17.1 %eval_jaxpr.2 = (f32[128,1536]{1,0:T(8,128)}, f32[128,12]{1,0:T(8,128)}, f32[128,12]{1,0:T(8,128)}) custom-call(s32[8]{0:T(128)} %reshape.151.bounds_ref, bf16[128,1536]{1,0:T(8,128)(2,1)} %q_ref, bf16[1536,512]{1,0:T(8,128)(2,1)} %bitcast.127, s32[128,1]{1,0:T(8,128)} %copy.49.rreq_ref, s32[128,1]{1,0:T(8,128)} %iota_add_fusion.rpos_ref, ...), custom_call_target="tpu_custom_call" | custom-call | flops 603979776 | bytes 2752512 | tf_op jit(solution)/shard_map/while/body/eval_jaxpr/pallas_call | solution.py:196
  28.7 1.2 %convert_element_type.110 = bf16[128,1536]{1,0:T(8,128)(2,1)S(1)} convert(f32[128,1536]{1,0:T(8,128)} %get-tuple-element.25) | non-fusion elementwise | flops 196608 | bytes 1179648 | tf_op jit(solution)/shard_map/convert_element_type | solution.py:19
  32.2 1.2 %divide_convert_fusion = bf16[128,2,6,128]{0,3,2,1:T(8,128)(2,1)S(1)} fusion(bf16[128,2,6,128]{0,3,2,1:T(8,128)(2,1)} %collective-permute-done.1, bf16[128,2,6,128]{0,3,2,1:T(8,128)(2,1)S(1)} %bitcast.125, f32[128,2,6]{0,2,1:T(8,128)S(1)} %get-tuple-element.57, f32[128,2,6]{0,2,1:T(8,128)S(1)} %get-tuple-element.58, f32[128,2,6]{0,2,1:T(8,128)S(1)} %get-tuple-element.56), kind=kLoop, calls=%fused_computation.28 | loop fusion | flops 1376256 | bytes 1198080 | tf_op jit(solution)/shard_map/convert_element_type | solution.py:305
  33.4 1.5 %multiply_reduce_fusion.1 = (f32[128]{0:T(128)S(1)}, f32[128,768]{1,0:T(8,128)S(1)}) fusion(bf16[128,1536]{0,1:T(8,128)(2,1)S(1)} %bitcast.128, bf16[1536,768]{1,0:T(8,128)(2,1)S(1)} %copy-done, bf16[128,768]{1,0:T(8,128)(2,1)} %param.14), kind=kOutput, calls=%fused_computation.60 | convolution fusion | flops 302382976 | bytes 3342848 | tf_op jit(solution)/shard_map/dot_general | solution.py:307
  36.9 2.8 %collective-permute-start.4 = (bf16[128,768]{1,0:T(8,128)(2,1)S(1)}, bf16[128,768]{1,0:T(8,128)(2,1)S(1)}, u32[]{:S(2)}, u32[]{:S(2)}) collective-permute-start(bf16[128,768]{1,0:T(8,128)(2,1)S(1)} %get-tuple-element.48), channel_id=1, source_target_pairs={{0,2},{2,0},{4,6},{6,4},{8,10},{10,8},{12,14},{14,12},{1,3},{3,1},... | collective-permute-start | bytes 589832 | tf_op jit(solution)/shard_map/ppermute | solution.py:54
  39.8 1.5 %collective-permute-start.5 = (bf16[128,768]{1,0:T(8,128)(2,1)S(1)}, bf16[128,768]{1,0:T(8,128)(2,1)S(1)}, u32[]{:S(2)}, u32[]{:S(2)}) collective-permute-start(bf16[128,768]{1,0:T(8,128)(2,1)S(1)} %get-tuple-element.47), channel_id=1, source_target_pairs={{0,4},{2,6},{4,0},{6,2},{8,12},{10,14},{12,8},{14,10},{1,5},{3,7},... | collective-permute-start | bytes 589832 | tf_op jit(solution)/shard_map/ppermute | solution.py:54
  41.3 2.0 %collective-permute-start.7 = (bf16[128,768]{1,0:T(8,128)(2,1)S(1)}, bf16[128,768]{1,0:T(8,128)(2,1)S(1)}, u32[]{:S(2)}, u32[]{:S(2)}) collective-permute-start(bf16[128,768]{1,0:T(8,128)(2,1)S(1)} %get-tuple-element.45), channel_id=1, source_target_pairs={{0,8},{2,10},{4,12},{6,14},{8,0},{10,2},{12,4},{14,6},{1,9},{3,11}... | collective-permute-start | bytes 589832 | tf_op jit(solution)/shard_map/ppermute | solution.py:54
  43.3 1.4 %collective-permute-start.8 = (bf16[128,768]{1,0:T(8,128)(2,1)S(1)}, bf16[128,768]{1,0:T(8,128)(2,1)S(1)}, u32[]{:S(2)}, u32[]{:S(2)}) collective-permute-start(bf16[128,768]{1,0:T(8,128)(2,1)S(1)} %get-tuple-element.44), channel_id=1, source_target_pairs={{0,10},{2,8},{4,14},{6,12},{8,2},{10,0},{12,6},{14,4},{1,11},{3,9}... | collective-permute-start | bytes 589832 | tf_op jit(solution)/shard_map/ppermute | solution.py:54
  45.4 3.1 %collective-permute-start.9 = (bf16[128,768]{1,0:T(8,128)(2,1)S(1)}, bf16[128,768]{1,0:T(8,128)(2,1)S(1)}, u32[]{:S(2)}, u32[]{:S(2)}) collective-permute-start(bf16[128,768]{1,0:T(8,128)(2,1)S(1)} %get-tuple-element.42), channel_id=1, source_target_pairs={{0,12},{2,14},{4,8},{6,10},{8,4},{10,6},{12,0},{14,2},{1,13},{3,15... | collective-permute-start | bytes 589832 | tf_op jit(solution)/shard_map/ppermute | solution.py:54
  49.0 1.3 %collective-permute-start.10 = (bf16[128,768]{1,0:T(8,128)(2,1)S(1)}, bf16[128,768]{1,0:T(8,128)(2,1)S(1)}, u32[]{:S(2)}, u32[]{:S(2)}) collective-permute-start(bf16[128,768]{1,0:T(8,128)(2,1)S(1)} %get-tuple-element.40), channel_id=1, source_target_pairs={{0,14},{2,12},{4,10},{6,8},{8,6},{10,4},{12,2},{14,0},{1,15},{3,13... | collective-permute-start | bytes 589832 | tf_op jit(solution)/shard_map/ppermute | solution.py:54
  50.3 3.4 %collective-permute-done.6 = bf16[128,768]{1,0:T(8,128)(2,1)S(1)} collective-permute-done((bf16[128,768]{1,0:T(8,128)(2,1)S(1)}, bf16[128,768]{1,0:T(8,128)(2,1)S(1)}, u32[]{:S(2)}, u32[]{:S(2)}) %collective-permute-start.6) | collective-permute-done | bytes 196640 | tf_op jit(solution)/shard_map/ppermute | solution.py:54
  53.7 1.0 %collective-permute-done.8 = bf16[128,768]{1,0:T(8,128)(2,1)S(1)} collective-permute-done((bf16[128,768]{1,0:T(8,128)(2,1)S(1)}, bf16[128,768]{1,0:T(8,128)(2,1)S(1)}, u32[]{:S(2)}, u32[]{:S(2)}) %collective-permute-start.8) | collective-permute-done | bytes 196640 | tf_op jit(solution)/shard_map/ppermute | solution.py:54
  54.7 4.2 %collective-permute-done.9 = bf16[128,768]{1,0:T(8,128)(2,1)S(1)} collective-permute-done((bf16[128,768]{1,0:T(8,128)(2,1)S(1)}, bf16[128,768]{1,0:T(8,128)(2,1)S(1)}, u32[]{:S(2)}, u32[]{:S(2)}) %collective-permute-start.9) | collective-permute-done | bytes 196640 | tf_op jit(solution)/shard_map/ppermute | solution.py:54
  59.0 3.5 %collective-permute-done.10 = bf16[128,768]{1,0:T(8,128)(2,1)S(1)} collective-permute-done((bf16[128,768]{1,0:T(8,128)(2,1)S(1)}, bf16[128,768]{1,0:T(8,128)(2,1)S(1)}, u32[]{:S(2)}, u32[]{:S(2)}) %collective-permute-start.10) | collective-permute-done | bytes 196640 | tf_op jit(solution)/shard_map/ppermute | solution.py:54
  62.7 1.1 %copy-done.1 = bf16[1,1536,384]{2,1,0:T(8,128)(2,1)S(1)} copy-done((bf16[1,1536,384]{2,1,0:T(8,128)(2,1)S(1)}, bf16[1,1536,384]{2,1,0:T(8,128)(2,1)}, u32[]{:S(2)}) %copy-start.1) | copy-done | bytes 1179672
  73.1 1.6 %collective-permute-start.18 = (bf16[128,768]{1,0:T(8,128)(2,1)S(1)}, bf16[128,768]{1,0:T(8,128)(2,1)S(1)}, u32[]{:S(2)}, u32[]{:S(2)}) collective-permute-start(bf16[128,768]{1,0:T(8,128)(2,1)S(1)} %get-tuple-element.52), channel_id=1, source_target_pairs={{0,8},{2,10},{4,12},{6,14},{8,0},{10,2},{12,4},{14,6},{1,9},{3,11}... | collective-permute-start | bytes 589832 | tf_op jit(solution)/shard_map/ppermute | solution.py:54
  76.1 2.4 %collective-permute-start.15 = (bf16[128,768]{1,0:T(8,128)(2,1)S(1)}, bf16[128,768]{1,0:T(8,128)(2,1)S(1)}, u32[]{:S(2)}, u32[]{:S(2)}) collective-permute-start(bf16[128,768]{1,0:T(8,128)(2,1)S(1)} %get-tuple-element.53), channel_id=1, source_target_pairs={{0,6},{2,4},{4,2},{6,0},{8,14},{10,12},{12,10},{14,8},{1,7},{3,5},... | collective-permute-start | bytes 589832 | tf_op jit(solution)/shard_map/ppermute | solution.py:54
  79.5 7.5 %collective-permute-done.13 = bf16[128,768]{1,0:T(8,128)(2,1)S(1)} collective-permute-done((bf16[128,768]{1,0:T(8,128)(2,1)S(1)}, bf16[128,768]{1,0:T(8,128)(2,1)S(1)}, u32[]{:S(2)}, u32[]{:S(2)}) %collective-permute-start.13) | collective-permute-done | bytes 196640 | tf_op jit(solution)/shard_map/ppermute | solution.py:54
  87.9 2.2 %collective-permute-start.21 = (bf16[128,768]{1,0:T(8,128)(2,1)S(1)}, bf16[128,768]{1,0:T(8,128)(2,1)S(1)}, u32[]{:S(2)}, u32[]{:S(2)}) collective-permute-start(bf16[128,768]{1,0:T(8,128)(2,1)S(1)} %get-tuple-element.49), channel_id=1, source_target_pairs={{0,14},{2,12},{4,10},{6,8},{8,6},{10,4},{12,2},{14,0},{1,15},{3,13... | collective-permute-start | bytes 589832 | tf_op jit(solution)/shard_map/ppermute | solution.py:54
  90.1 2.0 %collective-permute-done.15 = bf16[128,768]{1,0:T(8,128)(2,1)S(1)} collective-permute-done((bf16[128,768]{1,0:T(8,128)(2,1)S(1)}, bf16[128,768]{1,0:T(8,128)(2,1)S(1)}, u32[]{:S(2)}, u32[]{:S(2)}) %collective-permute-start.15) | collective-permute-done | bytes 196640 | tf_op jit(solution)/shard_map/ppermute | solution.py:54
  92.2 4.3 %collective-permute-done.20 = bf16[128,768]{1,0:T(8,128)(2,1)S(1)} collective-permute-done((bf16[128,768]{1,0:T(8,128)(2,1)S(1)}, bf16[128,768]{1,0:T(8,128)(2,1)S(1)}, u32[]{:S(2)}, u32[]{:S(2)}) %collective-permute-start.20) | collective-permute-done | bytes 196640 | tf_op jit(solution)/shard_map/ppermute | solution.py:54
  96.5 1.9 %collective-permute-done.21 = bf16[128,768]{1,0:T(8,128)(2,1)S(1)} collective-permute-done((bf16[128,768]{1,0:T(8,128)(2,1)S(1)}, bf16[128,768]{1,0:T(8,128)(2,1)S(1)}, u32[]{:S(2)}, u32[]{:S(2)}) %collective-permute-start.21) | collective-permute-done | bytes 196640 | tf_op jit(solution)/shard_map/ppermute | solution.py:54
  99.4 1.1 %collective-permute-done.22 = f32[128]{0:T(128)S(1)} collective-permute-done((f32[128]{0:T(128)S(1)}, f32[128]{0:T(128)S(1)}, u32[]{:S(2)}, u32[]{:S(2)}) %collective-permute-start.22) | collective-permute-done | bytes 544 | tf_op jit(solution)/shard_map/ppermute | solution.py:96
  (120 shorter events, 28.2 us)
Async XLA Ops:
  0.0 33.4 %copy-start = (bf16[1536,768]{1,0:T(8,128)(2,1)S(1)}, bf16[1536,768]{1,0:T(8,128)(2,1)}, u32[]{:S(2)}) copy-start(bf16[1536,768]{1,0:T(8,128)(2,1)} %param.20) | copy-start | bytes 7077892
  27.2 4.9 %collective-permute-start = (bf16[128,2,6]{0,2,1:T(8,128)(2,1)S(1)}, bf16[128,2,6]{0,2,1:T(8,128)(2,1)S(1)}, u32[]{:S(2)}, u32[]{:S(2)}) collective-permute-start(bf16[128,2,6]{0,2,1:T(8,128)(2,1)S(1)} %convert_element_type.114), channel_id=1, source_target_pairs={{0,1},{1,0},{2,3},{3,2},{4,5},{5,4},{6,7},{7,6},{8,9},{9,8},{10,11... | collective-permute-start | bytes 9224 | tf_op jit(solution)/shard_map/ppermute | solution.py:20
  28.6 3.4 %collective-permute-start.2 = (bf16[128,2,6]{0,2,1:T(8,128)(2,1)S(1)}, bf16[128,2,6]{0,2,1:T(8,128)(2,1)S(1)}, u32[]{:S(2)}, u32[]{:S(2)}) collective-permute-start(bf16[128,2,6]{0,2,1:T(8,128)(2,1)S(1)} %convert_element_type.119), channel_id=1, source_target_pairs={{0,1},{1,0},{2,3},{3,2},{4,5},{5,4},{6,7},{7,6},{8,9},{9,8},{10,11... | collective-permute-start | bytes 9224 | tf_op jit(solution)/shard_map/ppermute | solution.py:20
  30.1 2.0 %collective-permute-start.1 = (bf16[128,2,6,128]{0,3,2,1:T(8,128)(2,1)S(1)}, bf16[128,2,6,128]{0,3,2,1:T(8,128)(2,1)}, u32[]{:S(2)}, u32[]{:S(2)}) collective-permute-start(bf16[128,2,6,128]{0,3,2,1:T(8,128)(2,1)S(1)} %bitcast.124), channel_id=1, source_target_pairs={{0,1},{1,0},{2,3},{3,2},{4,5},{5,4},{6,7},{7,6},{8,9},{9,8},{10,11... | collective-permute-start | bytes 1179656 | tf_op jit(solution)/shard_map/ppermute | solution.py:20
  34.9 1.3 %collective-permute-start.3 = (f32[128]{0:T(128)S(1)}, f32[128]{0:T(128)S(1)}, u32[]{:S(2)}, u32[]{:S(2)}) collective-permute-start(f32[128]{0:T(128)S(1)} %get-tuple-element.59), channel_id=1, source_target_pairs={{0,1},{1,0},{2,3},{3,2},{4,5},{5,4},{6,7},{7,6},{8,9},{9,8},{10,11... | collective-permute-start | bytes 1544 | tf_op jit(solution)/shard_map/ppermute | solution.py:96
  36.9 8.5 %collective-permute-start.4 = (bf16[128,768]{1,0:T(8,128)(2,1)S(1)}, bf16[128,768]{1,0:T(8,128)(2,1)S(1)}, u32[]{:S(2)}, u32[]{:S(2)}) collective-permute-start(bf16[128,768]{1,0:T(8,128)(2,1)S(1)} %get-tuple-element.48), channel_id=1, source_target_pairs={{0,2},{2,0},{4,6},{6,4},{8,10},{10,8},{12,14},{14,12},{1,3},{3,1},... | collective-permute-start | bytes 589832 | tf_op jit(solution)/shard_map/ppermute | solution.py:54
  39.8 9.2 %collective-permute-start.5 = (bf16[128,768]{1,0:T(8,128)(2,1)S(1)}, bf16[128,768]{1,0:T(8,128)(2,1)S(1)}, u32[]{:S(2)}, u32[]{:S(2)}) collective-permute-start(bf16[128,768]{1,0:T(8,128)(2,1)S(1)} %get-tuple-element.47), channel_id=1, source_target_pairs={{0,4},{2,6},{4,0},{6,2},{8,12},{10,14},{12,8},{14,10},{1,5},{3,7},... | collective-permute-start | bytes 589832 | tf_op jit(solution)/shard_map/ppermute | solution.py:54
  41.3 12.4 %collective-permute-start.6 = (bf16[128,768]{1,0:T(8,128)(2,1)S(1)}, bf16[128,768]{1,0:T(8,128)(2,1)S(1)}, u32[]{:S(2)}, u32[]{:S(2)}) collective-permute-start(bf16[128,768]{1,0:T(8,128)(2,1)S(1)} %get-tuple-element.46), channel_id=1, source_target_pairs={{0,6},{2,4},{4,2},{6,0},{8,14},{10,12},{12,10},{14,8},{1,7},{3,5},... | collective-permute-start | bytes 589832 | tf_op jit(solution)/shard_map/ppermute | solution.py:54
  41.3 12.4 %collective-permute-start.7 = (bf16[128,768]{1,0:T(8,128)(2,1)S(1)}, bf16[128,768]{1,0:T(8,128)(2,1)S(1)}, u32[]{:S(2)}, u32[]{:S(2)}) collective-permute-start(bf16[128,768]{1,0:T(8,128)(2,1)S(1)} %get-tuple-element.45), channel_id=1, source_target_pairs={{0,8},{2,10},{4,12},{6,14},{8,0},{10,2},{12,4},{14,6},{1,9},{3,11}... | collective-permute-start | bytes 589832 | tf_op jit(solution)/shard_map/ppermute | solution.py:54
  43.3 11.4 %collective-permute-start.8 = (bf16[128,768]{1,0:T(8,128)(2,1)S(1)}, bf16[128,768]{1,0:T(8,128)(2,1)S(1)}, u32[]{:S(2)}, u32[]{:S(2)}) collective-permute-start(bf16[128,768]{1,0:T(8,128)(2,1)S(1)} %get-tuple-element.44), channel_id=1, source_target_pairs={{0,10},{2,8},{4,14},{6,12},{8,2},{10,0},{12,6},{14,4},{1,11},{3,9}... | collective-permute-start | bytes 589832 | tf_op jit(solution)/shard_map/ppermute | solution.py:54
  45.4 13.5 %collective-permute-start.9 = (bf16[128,768]{1,0:T(8,128)(2,1)S(1)}, bf16[128,768]{1,0:T(8,128)(2,1)S(1)}, u32[]{:S(2)}, u32[]{:S(2)}) collective-permute-start(bf16[128,768]{1,0:T(8,128)(2,1)S(1)} %get-tuple-element.42), channel_id=1, source_target_pairs={{0,12},{2,14},{4,8},{6,10},{8,4},{10,6},{12,0},{14,2},{1,13},{3,15... | collective-permute-start | bytes 589832 | tf_op jit(solution)/shard_map/ppermute | solution.py:54
  49.0 13.5 %collective-permute-start.10 = (bf16[128,768]{1,0:T(8,128)(2,1)S(1)}, bf16[128,768]{1,0:T(8,128)(2,1)S(1)}, u32[]{:S(2)}, u32[]{:S(2)}) collective-permute-start(bf16[128,768]{1,0:T(8,128)(2,1)S(1)} %get-tuple-element.40), channel_id=1, source_target_pairs={{0,14},{2,12},{4,10},{6,8},{8,6},{10,4},{12,2},{14,0},{1,15},{3,13... | collective-permute-start | bytes 589832 | tf_op jit(solution)/shard_map/ppermute | solution.py:54
  62.6 4.2 %collective-permute-start.16 = (bf16[512,768]{1,0:T(8,128)(2,1)S(1)}, bf16[512,768]{1,0:T(8,128)(2,1)S(1)}, u32[]{:S(2)}, u32[]{:S(2)}) collective-permute-start(bf16[512,768]{1,0:T(8,128)(2,1)S(1)} %get-tuple-element.28), channel_id=1, source_target_pairs={{0,1},{1,0},{2,3},{3,2},{4,5},{5,4},{6,7},{7,6},{8,9},{9,8},{10,11... | collective-permute-start | bytes 2359304 | tf_op jit(solution)/shard_map/ppermute | solution.py:72
  64.3 5.6 %collective-permute-start.11 = (bf16[512,768]{1,0:T(8,128)(2,1)S(1)}, bf16[512,768]{1,0:T(8,128)(2,1)S(1)}, u32[]{:S(2)}, u32[]{:S(2)}) collective-permute-start(bf16[512,768]{1,0:T(8,128)(2,1)S(1)} %get-tuple-element.29), channel_id=1, source_target_pairs={{0,1},{1,0},{2,3},{3,2},{4,5},{5,4},{6,7},{7,6},{8,9},{9,8},{10,11... | collective-permute-start | bytes 2359304 | tf_op jit(solution)/shard_map/ppermute | solution.py:72
  69.2 3.6 %collective-permute-start.17 = (bf16[512,768]{1,0:T(8,128)(2,1)S(1)}, bf16[512,768]{1,0:T(8,128)(2,1)S(1)}, u32[]{:S(2)}, u32[]{:S(2)}) collective-permute-start(bf16[512,768]{1,0:T(8,128)(2,1)S(1)} %convolution_convert_fusion.1), channel_id=1, source_target_pairs={{0,1},{1,0},{2,3},{3,2},{4,5},{5,4},{6,7},{7,6},{8,9},{9,8},{10,11... | collective-permute-start | bytes 2359304 | tf_op jit(solution)/shard_map/ppermute | solution.py:88
  71.7 3.1 %collective-permute-start.12 = (bf16[512,768]{1,0:T(8,128)(2,1)S(1)}, bf16[512,768]{1,0:T(8,128)(2,1)S(1)}, u32[]{:S(2)}, u32[]{:S(2)}) collective-permute-start(bf16[512,768]{1,0:T(8,128)(2,1)S(1)} %convolution_convert_fusion.3), channel_id=1, source_target_pairs={{0,1},{1,0},{2,3},{3,2},{4,5},{5,4},{6,7},{7,6},{8,9},{9,8},{10,11... | collective-permute-start | bytes 2359304 | tf_op jit(solution)/shard_map/ppermute | solution.py:88
  73.1 19.0 %collective-permute-start.18 = (bf16[128,768]{1,0:T(8,128)(2,1)S(1)}, bf16[128,768]{1,0:T(8,128)(2,1)S(1)}, u32[]{:S(2)}, u32[]{:S(2)}) collective-permute-start(bf16[128,768]{1,0:T(8,128)(2,1)S(1)} %get-tuple-element.52), channel_id=1, source_target_pairs={{0,8},{2,10},{4,12},{6,14},{8,0},{10,2},{12,4},{14,6},{1,9},{3,11}... | collective-permute-start | bytes 589832 | tf_op jit(solution)/shard_map/ppermute | solution.py:54
  75.0 12.1 %collective-permute-start.13 = (bf16[128,768]{1,0:T(8,128)(2,1)S(1)}, bf16[128,768]{1,0:T(8,128)(2,1)S(1)}, u32[]{:S(2)}, u32[]{:S(2)}) collective-permute-start(bf16[128,768]{1,0:T(8,128)(2,1)S(1)} %get-tuple-element.55), channel_id=1, source_target_pairs={{0,2},{2,0},{4,6},{6,4},{8,10},{10,8},{12,14},{14,12},{1,3},{3,1},... | collective-permute-start | bytes 589832 | tf_op jit(solution)/shard_map/ppermute | solution.py:54
  75.6 12.3 %collective-permute-start.14 = (bf16[128,768]{1,0:T(8,128)(2,1)S(1)}, bf16[128,768]{1,0:T(8,128)(2,1)S(1)}, u32[]{:S(2)}, u32[]{:S(2)}) collective-permute-start(bf16[128,768]{1,0:T(8,128)(2,1)S(1)} %get-tuple-element.54), channel_id=1, source_target_pairs={{0,4},{2,6},{4,0},{6,2},{8,12},{10,14},{12,8},{14,10},{1,5},{3,7},... | collective-permute-start | bytes 589832 | tf_op jit(solution)/shard_map/ppermute | solution.py:54
  76.1 16.0 %collective-permute-start.15 = (bf16[128,768]{1,0:T(8,128)(2,1)S(1)}, bf16[128,768]{1,0:T(8,128)(2,1)S(1)}, u32[]{:S(2)}, u32[]{:S(2)}) collective-permute-start(bf16[128,768]{1,0:T(8,128)(2,1)S(1)} %get-tuple-element.53), channel_id=1, source_target_pairs={{0,6},{2,4},{4,2},{6,0},{8,14},{10,12},{12,10},{14,8},{1,7},{3,5},... | collective-permute-start | bytes 589832 | tf_op jit(solution)/shard_map/ppermute | solution.py:54
  78.5 13.6 %collective-permute-start.19 = (bf16[128,768]{1,0:T(8,128)(2,1)S(1)}, bf16[128,768]{1,0:T(8,128)(2,1)S(1)}, u32[]{:S(2)}, u32[]{:S(2)}) collective-permute-start(bf16[128,768]{1,0:T(8,128)(2,1)S(1)} %get-tuple-element.51), channel_id=1, source_target_pairs={{0,10},{2,8},{4,14},{6,12},{8,2},{10,0},{12,6},{14,4},{1,11},{3,9}... | collective-permute-start | bytes 589832 | tf_op jit(solution)/shard_map/ppermute | solution.py:54
  87.0 9.5 %collective-permute-start.20 = (bf16[128,768]{1,0:T(8,128)(2,1)S(1)}, bf16[128,768]{1,0:T(8,128)(2,1)S(1)}, u32[]{:S(2)}, u32[]{:S(2)}) collective-permute-start(bf16[128,768]{1,0:T(8,128)(2,1)S(1)} %get-tuple-element.50), channel_id=1, source_target_pairs={{0,12},{2,14},{4,8},{6,10},{8,4},{10,6},{12,0},{14,2},{1,13},{3,15... | collective-permute-start | bytes 589832 | tf_op jit(solution)/shard_map/ppermute | solution.py:54
  87.9 10.5 %collective-permute-start.21 = (bf16[128,768]{1,0:T(8,128)(2,1)S(1)}, bf16[128,768]{1,0:T(8,128)(2,1)S(1)}, u32[]{:S(2)}, u32[]{:S(2)}) collective-permute-start(bf16[128,768]{1,0:T(8,128)(2,1)S(1)} %get-tuple-element.49), channel_id=1, source_target_pairs={{0,14},{2,12},{4,10},{6,8},{8,6},{10,4},{12,2},{14,0},{1,15},{3,13... | collective-permute-start | bytes 589832 | tf_op jit(solution)/shard_map/ppermute | solution.py:54
  99.3 1.2 %collective-permute-start.22 = (f32[128]{0:T(128)S(1)}, f32[128]{0:T(128)S(1)}, u32[]{:S(2)}, u32[]{:S(2)}) collective-permute-start(f32[128]{0:T(128)S(1)} %get-tuple-element.61), channel_id=1, source_target_pairs={{0,1},{1,0},{2,3},{3,2},{4,5},{5,4},{6,7},{7,6},{8,9},{9,8},{10,11... | collective-permute-start | bytes 1544 | tf_op jit(solution)/shard_map/ppermute | solution.py:96
  (7 other events, 20.3 us)

commit v6 on v5

--- a/solution.py
+++ b/solution.py
@@ -132,55 +132,40 @@
 
 
 def attention_kernel(bounds_ref, q_ref, kv_ref, rreq_ref, rpos_ref, kpos_ref, w_ref, m_ref, l_ref):
-    head_groups = QUERY_HEADS // KEY_VALUE_HEADS
     keys = kpos_ref.shape[1]
     scale = HEAD_SIZE ** (-0.5)
     w_ref[...] = jnp.zeros(w_ref.shape, jnp.float32)
     m_ref[...] = jnp.zeros(m_ref.shape, jnp.float32)
     l_ref[...] = jnp.zeros(l_ref.shape, jnp.float32)
-    for block in range(q_ref.shape[0] // ATTN_BLOCK):
-        rows = pl.ds(block * ATTN_BLOCK, ATTN_BLOCK)
-        row_req = rreq_ref[rows, :]
-        allowed = kpos_ref[...] <= rpos_ref[rows, :]
-        allowed_heads = jnp.concatenate([allowed] * head_groups, axis=0)
-
-        def body(request, carry, rows=rows, row_req=row_req, allowed_heads=allowed_heads):
+    for block in range(q_ref.shape[1]):
+        row_req = rreq_ref[block]
+        allowed = kpos_ref[...] <= rpos_ref[block]
+
+        def body(request, carry, block=block, row_req=row_req, allowed=allowed):
             picked = row_req == request
             first_key = pl.multiple_of(request * keys, 128)
             for kv_head in range(KEY_VALUE_HEADS):
-                stacked = jnp.concatenate(
-                    [
-                        q_ref[rows, pl.ds((kv_head * head_groups + g) * HEAD_SIZE, HEAD_SIZE)]
-                        for g in range(head_groups)
-                    ],
-                    axis=0,
-                )
                 key_block = kv_ref[pl.ds(first_key, keys), pl.ds(kv_head * HEAD_SIZE, HEAD_SIZE)]
                 value_block = kv_ref[
                     pl.ds(first_key, keys),
                     pl.ds((KEY_VALUE_HEADS + kv_head) * HEAD_SIZE, HEAD_SIZE),
                 ]
                 scores = lax.dot_general(
-                    stacked,
+                    q_ref[kv_head, block],
                     key_block,
                     (((1,), (1,)), ((), ())),
                     preferred_element_type=jnp.float32,
                 ) * scale
-                scores = jnp.where(allowed_heads, scores, -1e30)
+                scores = jnp.where(allowed, scores, -1e30)
                 top = jnp.max(scores, axis=1, keepdims=True)
-                soft = jnp.where(allowed_heads, jnp.exp(scores - top), 0.0)
+                soft = jnp.where(allowed, jnp.exp(scores - top), 0.0)
                 total = jnp.sum(soft, axis=1, keepdims=True)
                 weighted = jnp.dot(
                     soft.astype(jnp.bfloat16), value_block, preferred_element_type=jnp.float32
                 )
-                for g in range(head_groups):
-                    head = kv_head * head_groups + g
-                    part = slice(g * ATTN_BLOCK, (g + 1) * ATTN_BLOCK)
-                    cols = pl.ds(head * HEAD_SIZE, HEAD_SIZE)
-                    w_ref[rows, cols] = jnp.where(picked, weighted[part], w_ref[rows, cols])
-                    one = pl.ds(head, 1)
-                    m_ref[rows, one] = jnp.where(picked, top[part], m_ref[rows, one])
-                    l_ref[rows, one] = jnp.where(picked, total[part], l_ref[rows, one])
+                w_ref[kv_head, block] = jnp.where(picked, weighted, w_ref[kv_head, block])
+                m_ref[kv_head, block] = jnp.where(picked, top, m_ref[kv_head, block])
+                l_ref[kv_head, block] = jnp.where(picked, total, l_ref[kv_head, block])
             return carry
 
         lax.fori_loop(bounds_ref[2 * block], bounds_ref[2 * block + 1] + 1, body, 0)
@@ -189,16 +174,29 @@
 def paged_attention(queries, cache_rows, row_req, row_pos, key_pos):
     rows = queries.shape[0]
     blocks = rows // ATTN_BLOCK
+    head_groups = QUERY_HEADS // KEY_VALUE_HEADS
+    stack = head_groups * ATTN_BLOCK
     bounds = jnp.stack(
         [row_req[0::ATTN_BLOCK], row_req[ATTN_BLOCK - 1 :: ATTN_BLOCK]], axis=1
     ).reshape(2 * blocks)
+    stacked_q = (
+        queries.reshape(blocks, ATTN_BLOCK, KEY_VALUE_HEADS, head_groups, HEAD_SIZE)
+        .transpose(2, 0, 3, 1, 4)
+        .reshape(KEY_VALUE_HEADS, blocks, stack, HEAD_SIZE)
+    )
+
+    def per_row(values):
+        return jnp.broadcast_to(
+            values.reshape(blocks, 1, ATTN_BLOCK), (blocks, head_groups, ATTN_BLOCK)
+        ).reshape(blocks, stack, 1)
+
     vmem = pl.BlockSpec(memory_space=pltpu.VMEM)
     weighted, top, total = pl.pallas_call(
         attention_kernel,
         out_shape=(
-            jax.ShapeDtypeStruct((rows, QUERY_HEADS * HEAD_SIZE), jnp.float32),
-            jax.ShapeDtypeStruct((rows, QUERY_HEADS), jnp.float32),
-            jax.ShapeDtypeStruct((rows, QUERY_HEADS), jnp.float32),
+            jax.ShapeDtypeStruct((KEY_VALUE_HEADS, blocks, stack, HEAD_SIZE), jnp.float32),
+            jax.ShapeDtypeStruct((KEY_VALUE_HEADS, blocks, stack, 1), jnp.float32),
+            jax.ShapeDtypeStruct((KEY_VALUE_HEADS, blocks, stack, 1), jnp.float32),
         ),
         in_specs=[pl.BlockSpec(memory_space=pltpu.SMEM)] + [vmem] * 5,
         out_specs=(vmem, vmem, vmem),
@@ -207,13 +205,16 @@
             transcendentals=rows * QUERY_HEADS * key_pos.shape[1] * 2,
             bytes_accessed=queries.size * 2 + cache_rows.size * 2 + rows * QUERY_HEADS * HEAD_SIZE * 4,
         ),
-    )(bounds, queries, cache_rows, row_req[:, None], row_pos[:, None], key_pos)
-    head_groups = QUERY_HEADS // KEY_VALUE_HEADS
-    return (
-        top.reshape(rows, KEY_VALUE_HEADS, head_groups),
-        total.reshape(rows, KEY_VALUE_HEADS, head_groups),
-        weighted.reshape(rows, KEY_VALUE_HEADS, head_groups, HEAD_SIZE),
-    )
+    )(bounds, stacked_q, cache_rows, per_row(row_req), per_row(row_pos), key_pos)
+
+    def unstack(values):
+        return (
+            values.reshape(KEY_VALUE_HEADS, blocks, head_groups, ATTN_BLOCK, -1)
+            .transpose(1, 3, 0, 2, 4)
+            .reshape(rows, KEY_VALUE_HEADS, head_groups, -1)
+        )
+
+    return (unstack(top)[..., 0], unstack(total)[..., 0], unstack(weighted))
 
 
 def shards(

time: 102 us -> 102 us (level)
  Pallas kernels: 17.1 us -> 8.93 us
  local copies, waits for them, and re-layouts: 10.2 us -> 16.1 us
  other arithmetic: 8.46 us -> 10.4 us
    pallas_call x1, Pallas kernels: 17.1 us -> 8.93 us  [paged_attention(): pl.pallas_call(attention_kernel, out_shape=(jax.ShapeDtypeStruct((KEY_VAL...]
    reshape x0 -> x3, local copies, waits for them, and re-layouts: none -> 3.77 us  [the longest x2 2.32 us: per_row(): return jnp.broadcast_to(values.reshape(blocks, 1, ATTN_BLOCK), (blocks, h...]
    convert_element_type x0 -> x1, local copies, waits for them, and re-layouts: none -> 1.92 us  [shards(): attended = (weighted / row_sum[..., None]).reshape(count_of_rows, QUERY_H...]
    convert_element_type x1, other arithmetic: 1.18 us -> 2.52 us  [shards(): attended = (weighted / row_sum[..., None]).reshape(count_of_rows, QUERY_H...]
    convert_element_type x3, other arithmetic: 2.89 us -> 4.16 us  [merged(): rounded = jax.tree.map(lambda a: a.astype(jnp.bfloat16), shard)]
  transfers between devices with their start and end apart: 23 -> 23, of which waited for: 13 -> 12; matrix products, arithmetic and copies ran while one was open for 11% -> 12% of each run, Pallas kernels for 0% -> 0%
where the time goes in v6:
time: 102 us; the launch traced here: 101 us
  waiting for transfers between devices  31.3 us (31%)
  starting transfers between devices  23.5 us (23%)
  local copies, waits for them, and re-layouts  16.1 us (16%)
  other arithmetic  10.4 us (10%)
  matrix products  10.4 us (10%)
  Pallas kernels  8.93 us (9%)
    ppermute x14, waiting for transfers between devices, exchange(): pieces.append(lax.ppermute(chunks[step], 'el', perm=pairs))  29.3 us
    ppermute x14, starting transfers between devices, exchange(): pieces.append(lax.ppermute(chunks[step], 'el', perm=pairs))  21.3 us
    pallas_call x1, Pallas kernels, paged_attention(): pl.pallas_call(attention_kernel, out_shape=(jax.ShapeDtypeStruct((KEY_VAL...  8.93 us
    dot_general x8, matrix products, half_product(): return jnp.dot(x, weight, preferred_element_type=jnp.float32)  4.68 us
    convert_element_type x3, other arithmetic, merged(): rounded = jax.tree.map(lambda a: a.astype(jnp.bfloat16), shard)  4.16 us
    unnamed x32, local copies, waits for them, and re-layouts  3.45 us
    gather x1, local copies, waits for them, and re-layouts, one_group(): page_row_block = group_pages[local_table.reshape(-1)]  3.32 us
    convert_element_type x1, other arithmetic, shards(): attended = (weighted / row_sum[..., None]).reshape(count_of_rows, QUERY_H...  2.52 us
  transfers between devices with their start and end apart: 23, of which 12 were waited for; matrix products, arithmetic and copies ran while one was open for 12% of the time, Pallas kernels for 0%

profile of v6, /device:TPU:0, one launch (start us, length us, event | category | flops | bytes accessed | tf_op | source)
XLA Modules:
  0.0 101.2 jit_solution(18424703419291660131)
XLA Ops:
  6.8 1.4 %reshape.180 = bf16[4,32,2,6,128]{4,3,2,1,0:T(8,128)(2,1)S(1)} reshape(bf16[128,1536]{1,0:T(8,128)(2,1)} %param.15) | data formatting | bytes 786432 | tf_op jit(solution)/shard_map/while/body/eval_jaxpr/reshape | solution.py:183
  9.1 3.3 %gather_fusion = bf16[96,16,512]{2,1,0:T(8,128)(2,1)} fusion(bf16[96,16,512]{2,1,0:T(8,128)(2,1)} %bitcast.135, s32[1024]{0:T(1024)S(1)} %pad_clamp_fusion), kind=kCustom, calls=%fused_computation | custom fusion | bytes 3146112 | tf_op jit(solution)/shard_map/while/body/eval_jaxpr/gather | solution.py:261
  12.5 8.9 %eval_jaxpr.2 = (f32[2,4,192,128]{3,2,1,0:T(8,128)}, f32[2,4,192,1]{3,2,1,0:T(8,128)}, f32[2,4,192,1]{3,2,1,0:T(8,128)}) custom-call(s32[8]{0:T(128)} %reshape.179.bounds_ref, bf16[2,4,192,128]{3,2,1,0:T(8,128)(2,1)} %bitcast.132, bf16[1536,512]{1,0:T(8,128)(2,1)} %bitcast.121, s32[4,192,1]{2,1,0:T(8,128)} %reshape.198.rreq_ref, ...), custom_call_target="tpu_custom_call" | custom-call | flops 603979776 | bytes 2752512 | tf_op jit(solution)/shard_map/while/body/eval_jaxpr/pallas_call | solution.py:194
  21.4 1.5 %convert_reduce_fusion.1 = bf16[2,4,192]{2,1,0:T(4,128)(2,1)S(1)} fusion(f32[2,4,192,1]{3,2,1,0:T(8,128)} %get-tuple-element.27), kind=kLoop, calls=%fused_computation.62 | loop fusion | flops 1536 | bytes 9216 | tf_op jit(solution)/shard_map/convert_element_type | solution.py:19
  23.6 1.5 %convert_reduce_fusion = bf16[2,4,192]{2,1,0:T(4,128)(2,1)S(1)} fusion(f32[2,4,192,1]{3,2,1,0:T(8,128)} %get-tuple-element.28), kind=kLoop, calls=%fused_computation.61 | loop fusion | flops 1536 | bytes 9216 | tf_op jit(solution)/shard_map/convert_element_type | solution.py:19
  25.4 1.2 %convert_element_type.128 = bf16[2,4,192,128]{3,2,1,0:T(8,128)(2,1)S(1)} convert(f32[2,4,192,128]{3,2,1,0:T(8,128)} %get-tuple-element.26) | non-fusion elementwise | flops 196608 | bytes 1179648 | tf_op jit(solution)/shard_map/convert_element_type | solution.py:19
  28.6 2.5 %divide_convert_fusion = bf16[128,2,6,128]{3,0,2,1:T(8,128)(2,1)} fusion(bf16[128,2,6,128]{3,0,2,1:T(8,128)(2,1)} %collective-permute-done.1, f32[128,2,6]{0,2,1:T(8,128)S(1)} %copy.65, f32[128,2,6]{0,2,1:T(8,128)S(1)} %copy.63, f32[128,2,6]{0,2,1:T(8,128)S(1)} %copy.62, bf16[2,4,6,32,128]{4,3,1,2,0:T(8,128)(2,1)S(1)} %copy.60), kind=kLoop, calls=%fused_computation.28 | loop fusion | flops 1376256 | bytes 1198080 | tf_op jit(solution)/shard_map/convert_element_type | solution.py:306
  31.1 1.9 %copy.66 = bf16[128,2,6,128]{0,3,2,1:T(8,128)(2,1)} copy(bf16[128,2,6,128]{3,0,2,1:T(8,128)(2,1)} %divide_convert_fusion) | data formatting | bytes 786432 | tf_op jit(solution)/shard_map/convert_element_type | solution.py:306
  33.0 1.7 %multiply_reduce_fusion.1 = (f32[128]{0:T(128)S(1)}, f32[128,768]{1,0:T(8,128)S(1)}) fusion(bf16[128,1536]{0,1:T(8,128)(2,1)} %bitcast.136, bf16[1536,768]{1,0:T(8,128)(2,1)S(1)} %copy-done, bf16[128,768]{1,0:T(8,128)(2,1)} %param.14), kind=kOutput, calls=%fused_computation.60 | convolution fusion | flops 302382976 | bytes 3342848 | tf_op jit(solution)/shard_map/dot_general | solution.py:308
  36.6 2.8 %collective-permute-start.4 = (bf16[128,768]{1,0:T(8,128)(2,1)S(1)}, bf16[128,768]{1,0:T(8,128)(2,1)S(1)}, u32[]{:S(2)}, u32[]{:S(2)}) collective-permute-start(bf16[128,768]{1,0:T(8,128)(2,1)S(1)} %get-tuple-element.49), channel_id=1, source_target_pairs={{0,2},{2,0},{4,6},{6,4},{8,10},{10,8},{12,14},{14,12},{1,3},{3,1},... | collective-permute-start | bytes 589832 | tf_op jit(solution)/shard_map/ppermute | solution.py:54
  39.4 1.5 %collective-permute-start.5 = (bf16[128,768]{1,0:T(8,128)(2,1)S(1)}, bf16[128,768]{1,0:T(8,128)(2,1)S(1)}, u32[]{:S(2)}, u32[]{:S(2)}) collective-permute-start(bf16[128,768]{1,0:T(8,128)(2,1)S(1)} %get-tuple-element.48), channel_id=1, source_target_pairs={{0,4},{2,6},{4,0},{6,2},{8,12},{10,14},{12,8},{14,10},{1,5},{3,7},... | collective-permute-start | bytes 589832 | tf_op jit(solution)/shard_map/ppermute | solution.py:54
  40.9 2.0 %collective-permute-start.7 = (bf16[128,768]{1,0:T(8,128)(2,1)S(1)}, bf16[128,768]{1,0:T(8,128)(2,1)S(1)}, u32[]{:S(2)}, u32[]{:S(2)}) collective-permute-start(bf16[128,768]{1,0:T(8,128)(2,1)S(1)} %get-tuple-element.46), channel_id=1, source_target_pairs={{0,8},{2,10},{4,12},{6,14},{8,0},{10,2},{12,4},{14,6},{1,9},{3,11}... | collective-permute-start | bytes 589832 | tf_op jit(solution)/shard_map/ppermute | solution.py:54
  43.0 1.4 %collective-permute-start.8 = (bf16[128,768]{1,0:T(8,128)(2,1)S(1)}, bf16[128,768]{1,0:T(8,128)(2,1)S(1)}, u32[]{:S(2)}, u32[]{:S(2)}) collective-permute-start(bf16[128,768]{1,0:T(8,128)(2,1)S(1)} %get-tuple-element.45), channel_id=1, source_target_pairs={{0,10},{2,8},{4,14},{6,12},{8,2},{10,0},{12,6},{14,4},{1,11},{3,9}... | collective-permute-start | bytes 589832 | tf_op jit(solution)/shard_map/ppermute | solution.py:54
  45.1 3.1 %collective-permute-start.9 = (bf16[128,768]{1,0:T(8,128)(2,1)S(1)}, bf16[128,768]{1,0:T(8,128)(2,1)S(1)}, u32[]{:S(2)}, u32[]{:S(2)}) collective-permute-start(bf16[128,768]{1,0:T(8,128)(2,1)S(1)} %get-tuple-element.44), channel_id=1, source_target_pairs={{0,12},{2,14},{4,8},{6,10},{8,4},{10,6},{12,0},{14,2},{1,13},{3,15... | collective-permute-start | bytes 589832 | tf_op jit(solution)/shard_map/ppermute | solution.py:54
  48.8 1.3 %collective-permute-start.10 = (bf16[128,768]{1,0:T(8,128)(2,1)S(1)}, bf16[128,768]{1,0:T(8,128)(2,1)S(1)}, u32[]{:S(2)}, u32[]{:S(2)}) collective-permute-start(bf16[128,768]{1,0:T(8,128)(2,1)S(1)} %get-tuple-element.42), channel_id=1, source_target_pairs={{0,14},{2,12},{4,10},{6,8},{8,6},{10,4},{12,2},{14,0},{1,15},{3,13... | collective-permute-start | bytes 589832 | tf_op jit(solution)/shard_map/ppermute | solution.py:54
  50.1 3.4 %collective-permute-done.6 = bf16[128,768]{1,0:T(8,128)(2,1)S(1)} collective-permute-done((bf16[128,768]{1,0:T(8,128)(2,1)S(1)}, bf16[128,768]{1,0:T(8,128)(2,1)S(1)}, u32[]{:S(2)}, u32[]{:S(2)}) %collective-permute-start.6) | collective-permute-done | bytes 196640 | tf_op jit(solution)/shard_map/ppermute | solution.py:54
  54.4 4.2 %collective-permute-done.9 = bf16[128,768]{1,0:T(8,128)(2,1)S(1)} collective-permute-done((bf16[128,768]{1,0:T(8,128)(2,1)S(1)}, bf16[128,768]{1,0:T(8,128)(2,1)S(1)}, u32[]{:S(2)}, u32[]{:S(2)}) %collective-permute-start.9) | collective-permute-done | bytes 196640 | tf_op jit(solution)/shard_map/ppermute | solution.py:54
  58.7 3.5 %collective-permute-done.10 = bf16[128,768]{1,0:T(8,128)(2,1)S(1)} collective-permute-done((bf16[128,768]{1,0:T(8,128)(2,1)S(1)}, bf16[128,768]{1,0:T(8,128)(2,1)S(1)}, u32[]{:S(2)}, u32[]{:S(2)}) %collective-permute-start.10) | collective-permute-done | bytes 196640 | tf_op jit(solution)/shard_map/ppermute | solution.py:54
  72.9 1.6 %collective-permute-start.18 = (bf16[128,768]{1,0:T(8,128)(2,1)S(1)}, bf16[128,768]{1,0:T(8,128)(2,1)S(1)}, u32[]{:S(2)}, u32[]{:S(2)}) collective-permute-start(bf16[128,768]{1,0:T(8,128)(2,1)S(1)} %get-tuple-element.53), channel_id=1, source_target_pairs={{0,8},{2,10},{4,12},{6,14},{8,0},{10,2},{12,4},{14,6},{1,9},{3,11}... | collective-permute-start | bytes 589832 | tf_op jit(solution)/shard_map/ppermute | solution.py:54
  75.9 2.4 %collective-permute-start.15 = (bf16[128,768]{1,0:T(8,128)(2,1)S(1)}, bf16[128,768]{1,0:T(8,128)(2,1)S(1)}, u32[]{:S(2)}, u32[]{:S(2)}) collective-permute-start(bf16[128,768]{1,0:T(8,128)(2,1)S(1)} %get-tuple-element.54), channel_id=1, source_target_pairs={{0,6},{2,4},{4,2},{6,0},{8,14},{10,12},{12,10},{14,8},{1,7},{3,5},... | collective-permute-start | bytes 589832 | tf_op jit(solution)/shard_map/ppermute | solution.py:54
  79.3 7.5 %collective-permute-done.13 = bf16[128,768]{1,0:T(8,128)(2,1)S(1)} collective-permute-done((bf16[128,768]{1,0:T(8,128)(2,1)S(1)}, bf16[128,768]{1,0:T(8,128)(2,1)S(1)}, u32[]{:S(2)}, u32[]{:S(2)}) %collective-permute-start.13) | collective-permute-done | bytes 196640 | tf_op jit(solution)/shard_map/ppermute | solution.py:54
  87.7 2.1 %collective-permute-start.21 = (bf16[128,768]{1,0:T(8,128)(2,1)S(1)}, bf16[128,768]{1,0:T(8,128)(2,1)S(1)}, u32[]{:S(2)}, u32[]{:S(2)}) collective-permute-start(bf16[128,768]{1,0:T(8,128)(2,1)S(1)} %get-tuple-element.50), channel_id=1, source_target_pairs={{0,14},{2,12},{4,10},{6,8},{8,6},{10,4},{12,2},{14,0},{1,15},{3,13... | collective-permute-start | bytes 589832 | tf_op jit(solution)/shard_map/ppermute | solution.py:54
  89.8 6.1 %collective-permute-done.15 = bf16[128,768]{1,0:T(8,128)(2,1)S(1)} collective-permute-done((bf16[128,768]{1,0:T(8,128)(2,1)S(1)}, bf16[128,768]{1,0:T(8,128)(2,1)S(1)}, u32[]{:S(2)}, u32[]{:S(2)}) %collective-permute-start.15) | collective-permute-done | bytes 196640 | tf_op jit(solution)/shard_map/ppermute | solution.py:54
  96.4 1.9 %collective-permute-done.21 = bf16[128,768]{1,0:T(8,128)(2,1)S(1)} collective-permute-done((bf16[128,768]{1,0:T(8,128)(2,1)S(1)}, bf16[128,768]{1,0:T(8,128)(2,1)S(1)}, u32[]{:S(2)}, u32[]{:S(2)}) %collective-permute-start.21) | collective-permute-done | bytes 196640 | tf_op jit(solution)/shard_map/ppermute | solution.py:54
  (132 shorter events, 31.9 us)
Async XLA Ops:
  0.0 33.0 %copy-start = (bf16[1536,768]{1,0:T(8,128)(2,1)S(1)}, bf16[1536,768]{1,0:T(8,128)(2,1)}, u32[]{:S(2)}) copy-start(bf16[1536,768]{1,0:T(8,128)(2,1)} %param.20) | copy-start | bytes 7077892
  23.1 5.4 %collective-permute-start = (bf16[128,2,6]{0,1,2:T(2,128)(2,1)S(1)}, bf16[128,2,6]{0,1,2:T(2,128)(2,1)S(1)}, u32[]{:S(2)}, u32[]{:S(2)}) collective-permute-start(bf16[128,2,6]{0,1,2:T(2,128)(2,1)S(1)} %convert_element_type.136), channel_id=1, source_target_pairs={{0,1},{1,0},{2,3},{3,2},{4,5},{5,4},{6,7},{7,6},{8,9},{9,8},{10,11... | collective-permute-start | bytes 9224 | tf_op jit(solution)/shard_map/ppermute | solution.py:20
  25.3 3.2 %collective-permute-start.2 = (bf16[128,2,6]{0,1,2:T(2,128)(2,1)S(1)}, bf16[128,2,6]{0,1,2:T(2,128)(2,1)S(1)}, u32[]{:S(2)}, u32[]{:S(2)}) collective-permute-start(bf16[128,2,6]{0,1,2:T(2,128)(2,1)S(1)} %convert_element_type.143), channel_id=1, source_target_pairs={{0,1},{1,0},{2,3},{3,2},{4,5},{5,4},{6,7},{7,6},{8,9},{9,8},{10,11... | collective-permute-start | bytes 9224 | tf_op jit(solution)/shard_map/ppermute | solution.py:20
  26.6 2.0 %collective-permute-start.1 = (bf16[128,2,6,128]{3,0,2,1:T(8,128)(2,1)S(1)}, bf16[128,2,6,128]{3,0,2,1:T(8,128)(2,1)}, u32[]{:S(2)}, u32[]{:S(2)}) collective-permute-start(bf16[128,2,6,128]{3,0,2,1:T(8,128)(2,1)S(1)} %bitcast.133), channel_id=1, source_target_pairs={{0,1},{1,0},{2,3},{3,2},{4,5},{5,4},{6,7},{7,6},{8,9},{9,8},{10,11... | collective-permute-start | bytes 1179656 | tf_op jit(solution)/shard_map/ppermute | solution.py:20
  34.7 1.2 %collective-permute-start.3 = (f32[128]{0:T(128)S(1)}, f32[128]{0:T(128)S(1)}, u32[]{:S(2)}, u32[]{:S(2)}) collective-permute-start(f32[128]{0:T(128)S(1)} %get-tuple-element.60), channel_id=1, source_target_pairs={{0,1},{1,0},{2,3},{3,2},{4,5},{5,4},{6,7},{7,6},{8,9},{9,8},{10,11... | collective-permute-start | bytes 1544 | tf_op jit(solution)/shard_map/ppermute | solution.py:96
  36.6 8.4 %collective-permute-start.4 = (bf16[128,768]{1,0:T(8,128)(2,1)S(1)}, bf16[128,768]{1,0:T(8,128)(2,1)S(1)}, u32[]{:S(2)}, u32[]{:S(2)}) collective-permute-start(bf16[128,768]{1,0:T(8,128)(2,1)S(1)} %get-tuple-element.49), channel_id=1, source_target_pairs={{0,2},{2,0},{4,6},{6,4},{8,10},{10,8},{12,14},{14,12},{1,3},{3,1},... | collective-permute-start | bytes 589832 | tf_op jit(solution)/shard_map/ppermute | solution.py:54
  39.4 9.4 %collective-permute-start.5 = (bf16[128,768]{1,0:T(8,128)(2,1)S(1)}, bf16[128,768]{1,0:T(8,128)(2,1)S(1)}, u32[]{:S(2)}, u32[]{:S(2)}) collective-permute-start(bf16[128,768]{1,0:T(8,128)(2,1)S(1)} %get-tuple-element.48), channel_id=1, source_target_pairs={{0,4},{2,6},{4,0},{6,2},{8,12},{10,14},{12,8},{14,10},{1,5},{3,7},... | collective-permute-start | bytes 589832 | tf_op jit(solution)/shard_map/ppermute | solution.py:54
  40.9 12.6 %collective-permute-start.6 = (bf16[128,768]{1,0:T(8,128)(2,1)S(1)}, bf16[128,768]{1,0:T(8,128)(2,1)S(1)}, u32[]{:S(2)}, u32[]{:S(2)}) collective-permute-start(bf16[128,768]{1,0:T(8,128)(2,1)S(1)} %get-tuple-element.47), channel_id=1, source_target_pairs={{0,6},{2,4},{4,2},{6,0},{8,14},{10,12},{12,10},{14,8},{1,7},{3,5},... | collective-permute-start | bytes 589832 | tf_op jit(solution)/shard_map/ppermute | solution.py:54
  40.9 12.6 %collective-permute-start.7 = (bf16[128,768]{1,0:T(8,128)(2,1)S(1)}, bf16[128,768]{1,0:T(8,128)(2,1)S(1)}, u32[]{:S(2)}, u32[]{:S(2)}) collective-permute-start(bf16[128,768]{1,0:T(8,128)(2,1)S(1)} %get-tuple-element.46), channel_id=1, source_target_pairs={{0,8},{2,10},{4,12},{6,14},{8,0},{10,2},{12,4},{14,6},{1,9},{3,11}... | collective-permute-start | bytes 589832 | tf_op jit(solution)/shard_map/ppermute | solution.py:54
  43.0 11.5 %collective-permute-start.8 = (bf16[128,768]{1,0:T(8,128)(2,1)S(1)}, bf16[128,768]{1,0:T(8,128)(2,1)S(1)}, u32[]{:S(2)}, u32[]{:S(2)}) collective-permute-start(bf16[128,768]{1,0:T(8,128)(2,1)S(1)} %get-tuple-element.45), channel_id=1, source_target_pairs={{0,10},{2,8},{4,14},{6,12},{8,2},{10,0},{12,6},{14,4},{1,11},{3,9}... | collective-permute-start | bytes 589832 | tf_op jit(solution)/shard_map/ppermute | solution.py:54
  45.1 13.6 %collective-permute-start.9 = (bf16[128,768]{1,0:T(8,128)(2,1)S(1)}, bf16[128,768]{1,0:T(8,128)(2,1)S(1)}, u32[]{:S(2)}, u32[]{:S(2)}) collective-permute-start(bf16[128,768]{1,0:T(8,128)(2,1)S(1)} %get-tuple-element.44), channel_id=1, source_target_pairs={{0,12},{2,14},{4,8},{6,10},{8,4},{10,6},{12,0},{14,2},{1,13},{3,15... | collective-permute-start | bytes 589832 | tf_op jit(solution)/shard_map/ppermute | solution.py:54
  48.8 13.4 %collective-permute-start.10 = (bf16[128,768]{1,0:T(8,128)(2,1)S(1)}, bf16[128,768]{1,0:T(8,128)(2,1)S(1)}, u32[]{:S(2)}, u32[]{:S(2)}) collective-permute-start(bf16[128,768]{1,0:T(8,128)(2,1)S(1)} %get-tuple-element.42), channel_id=1, source_target_pairs={{0,14},{2,12},{4,10},{6,8},{8,6},{10,4},{12,2},{14,0},{1,15},{3,13... | collective-permute-start | bytes 589832 | tf_op jit(solution)/shard_map/ppermute | solution.py:54
  62.4 4.2 %collective-permute-start.16 = (bf16[512,768]{1,0:T(8,128)(2,1)S(1)}, bf16[512,768]{1,0:T(8,128)(2,1)S(1)}, u32[]{:S(2)}, u32[]{:S(2)}) collective-permute-start(bf16[512,768]{1,0:T(8,128)(2,1)S(1)} %get-tuple-element.29), channel_id=1, source_target_pairs={{0,1},{1,0},{2,3},{3,2},{4,5},{5,4},{6,7},{7,6},{8,9},{9,8},{10,11... | collective-permute-start | bytes 2359304 | tf_op jit(solution)/shard_map/ppermute | solution.py:72
  64.1 5.6 %collective-permute-start.11 = (bf16[512,768]{1,0:T(8,128)(2,1)S(1)}, bf16[512,768]{1,0:T(8,128)(2,1)S(1)}, u32[]{:S(2)}, u32[]{:S(2)}) collective-permute-start(bf16[512,768]{1,0:T(8,128)(2,1)S(1)} %get-tuple-element.40), channel_id=1, source_target_pairs={{0,1},{1,0},{2,3},{3,2},{4,5},{5,4},{6,7},{7,6},{8,9},{9,8},{10,11... | collective-permute-start | bytes 2359304 | tf_op jit(solution)/shard_map/ppermute | solution.py:72
  69.0 3.6 %collective-permute-start.17 = (bf16[512,768]{1,0:T(8,128)(2,1)S(1)}, bf16[512,768]{1,0:T(8,128)(2,1)S(1)}, u32[]{:S(2)}, u32[]{:S(2)}) collective-permute-start(bf16[512,768]{1,0:T(8,128)(2,1)S(1)} %convolution_convert_fusion.1), channel_id=1, source_target_pairs={{0,1},{1,0},{2,3},{3,2},{4,5},{5,4},{6,7},{7,6},{8,9},{9,8},{10,11... | collective-permute-start | bytes 2359304 | tf_op jit(solution)/shard_map/ppermute | solution.py:88
  71.4 3.1 %collective-permute-start.12 = (bf16[512,768]{1,0:T(8,128)(2,1)S(1)}, bf16[512,768]{1,0:T(8,128)(2,1)S(1)}, u32[]{:S(2)}, u32[]{:S(2)}) collective-permute-start(bf16[512,768]{1,0:T(8,128)(2,1)S(1)} %convolution_convert_fusion.3), channel_id=1, source_target_pairs={{0,1},{1,0},{2,3},{3,2},{4,5},{5,4},{6,7},{7,6},{8,9},{9,8},{10,11... | collective-permute-start | bytes 2359304 | tf_op jit(solution)/shard_map/ppermute | solution.py:88
  72.9 23.1 %collective-permute-start.18 = (bf16[128,768]{1,0:T(8,128)(2,1)S(1)}, bf16[128,768]{1,0:T(8,128)(2,1)S(1)}, u32[]{:S(2)}, u32[]{:S(2)}) collective-permute-start(bf16[128,768]{1,0:T(8,128)(2,1)S(1)} %get-tuple-element.53), channel_id=1, source_target_pairs={{0,8},{2,10},{4,12},{6,14},{8,0},{10,2},{12,4},{14,6},{1,9},{3,11}... | collective-permute-start | bytes 589832 | tf_op jit(solution)/shard_map/ppermute | solution.py:54
  74.7 12.1 %collective-permute-start.13 = (bf16[128,768]{1,0:T(8,128)(2,1)S(1)}, bf16[128,768]{1,0:T(8,128)(2,1)S(1)}, u32[]{:S(2)}, u32[]{:S(2)}) collective-permute-start(bf16[128,768]{1,0:T(8,128)(2,1)S(1)} %get-tuple-element.56), channel_id=1, source_target_pairs={{0,2},{2,0},{4,6},{6,4},{8,10},{10,8},{12,14},{14,12},{1,3},{3,1},... | collective-permute-start | bytes 589832 | tf_op jit(solution)/shard_map/ppermute | solution.py:54
  75.4 12.3 %collective-permute-start.14 = (bf16[128,768]{1,0:T(8,128)(2,1)S(1)}, bf16[128,768]{1,0:T(8,128)(2,1)S(1)}, u32[]{:S(2)}, u32[]{:S(2)}) collective-permute-start(bf16[128,768]{1,0:T(8,128)(2,1)S(1)} %get-tuple-element.55), channel_id=1, source_target_pairs={{0,4},{2,6},{4,0},{6,2},{8,12},{10,14},{12,8},{14,10},{1,5},{3,7},... | collective-permute-start | bytes 589832 | tf_op jit(solution)/shard_map/ppermute | solution.py:54
  75.9 20.1 %collective-permute-start.15 = (bf16[128,768]{1,0:T(8,128)(2,1)S(1)}, bf16[128,768]{1,0:T(8,128)(2,1)S(1)}, u32[]{:S(2)}, u32[]{:S(2)}) collective-permute-start(bf16[128,768]{1,0:T(8,128)(2,1)S(1)} %get-tuple-element.54), channel_id=1, source_target_pairs={{0,6},{2,4},{4,2},{6,0},{8,14},{10,12},{12,10},{14,8},{1,7},{3,5},... | collective-permute-start | bytes 589832 | tf_op jit(solution)/shard_map/ppermute | solution.py:54
  78.3 17.7 %collective-permute-start.19 = (bf16[128,768]{1,0:T(8,128)(2,1)S(1)}, bf16[128,768]{1,0:T(8,128)(2,1)S(1)}, u32[]{:S(2)}, u32[]{:S(2)}) collective-permute-start(bf16[128,768]{1,0:T(8,128)(2,1)S(1)} %get-tuple-element.52), channel_id=1, source_target_pairs={{0,10},{2,8},{4,14},{6,12},{8,2},{10,0},{12,6},{14,4},{1,11},{3,9}... | collective-permute-start | bytes 589832 | tf_op jit(solution)/shard_map/ppermute | solution.py:54
  86.8 9.6 %collective-permute-start.20 = (bf16[128,768]{1,0:T(8,128)(2,1)S(1)}, bf16[128,768]{1,0:T(8,128)(2,1)S(1)}, u32[]{:S(2)}, u32[]{:S(2)}) collective-permute-start(bf16[128,768]{1,0:T(8,128)(2,1)S(1)} %get-tuple-element.51), channel_id=1, source_target_pairs={{0,12},{2,14},{4,8},{6,10},{8,4},{10,6},{12,0},{14,2},{1,13},{3,15... | collective-permute-start | bytes 589832 | tf_op jit(solution)/shard_map/ppermute | solution.py:54
  87.7 10.6 %collective-permute-start.21 = (bf16[128,768]{1,0:T(8,128)(2,1)S(1)}, bf16[128,768]{1,0:T(8,128)(2,1)S(1)}, u32[]{:S(2)}, u32[]{:S(2)}) collective-permute-start(bf16[128,768]{1,0:T(8,128)(2,1)S(1)} %get-tuple-element.50), channel_id=1, source_target_pairs={{0,14},{2,12},{4,10},{6,8},{8,6},{10,4},{12,2},{14,0},{1,15},{3,13... | collective-permute-start | bytes 589832 | tf_op jit(solution)/shard_map/ppermute | solution.py:54
  99.2 1.2 %collective-permute-start.22 = (f32[128]{0:T(128)S(1)}, f32[128]{0:T(128)S(1)}, u32[]{:S(2)}, u32[]{:S(2)}) collective-permute-start(f32[128]{0:T(128)S(1)} %get-tuple-element.62), channel_id=1, source_target_pairs={{0,1},{1,0},{2,3},{3,2},{4,5},{5,4},{6,7},{7,6},{8,9},{9,8},{10,11... | collective-permute-start | bytes 1544 | tf_op jit(solution)/shard_map/ppermute | solution.py:96
  (7 other events, 19.2 us)

commit v7 on v4

--- a/solution.py
+++ b/solution.py
@@ -13,6 +13,11 @@
 
 
 def merged(shard, axis, join):
+    if lax.axis_size(axis) == 2:
+        rounded = jax.tree.map(lambda a: a.astype(jnp.bfloat16), shard)
+        other = jax.tree.map(lambda a: lax.ppermute(a, axis, perm=[(0, 1), (1, 0)]), rounded)
+        widen = lambda tree: jax.tree.map(lambda a, own: a.astype(own.dtype), tree, shard)
+        return join(widen(rounded), widen(other))
     gathered = jax.tree.map(
         lambda a, kind: lax.all_gather(a.astype(kind), axis),
         shard,
@@ -79,8 +84,14 @@
         return jnp.dot(hidden, weight, preferred_element_type=jnp.float32).astype(jnp.bfloat16)
 
     sent = lax.ppermute(down_product(other), "tp", perm=swap)
-    kept = down_product(mine)
+    kept = lax.optimization_barrier(down_product(mine))
     return (kept.astype(jnp.float32) + sent.astype(jnp.float32)).astype(jnp.bfloat16)
+
+
+def tp_sum(value):
+    if lax.axis_size("tp") != 2:
+        return lax.psum(value, "tp")
+    return value + lax.ppermute(value, "tp", perm=[(0, 1), (1, 0)])
 
 
 def tp_gather(part, axis):
@@ -172,20 +183,31 @@
             within // PAGE_POSITIONS * tp_count + tp_index
         ) * PAGE_POSITIONS + within % PAGE_POSITIONS
         allowed = (row_req[:, None] == key_req[None, :]) & (key_pos[None, :] <= row_pos[:, None])
-        query_head_rows = queries.reshape(group_rows, KEY_VALUE_HEADS, head_groups, HEAD_SIZE)
-        scores = jnp.einsum(
-            "rkgd,lkd->rkgl", query_head_rows, gathered_keys, preferred_element_type=jnp.float32
-        ) * HEAD_SIZE ** (-0.5)
-        score_mask = allowed[:, None, None, :]
-        part_max = jnp.max(jnp.where(score_mask, scores, -1e30), axis=-1)
-        soft = jnp.where(score_mask, jnp.exp(scores - part_max[..., None]), 0.0)
-        part_sum = jnp.sum(soft, axis=-1)
-        part_weighted = jnp.einsum(
-            "rkgl,lkd->rkgd",
-            soft.astype(jnp.bfloat16),
-            gathered_values,
-            preferred_element_type=jnp.float32,
-        )
+        score_mask = allowed[:, None, :]
+        outs = []
+        for kv_head in range(KEY_VALUE_HEADS):
+            head_rows = queries[:, kv_head * head_groups * HEAD_SIZE : (kv_head + 1) * head_groups * HEAD_SIZE]
+            head_rows = head_rows.reshape(group_rows, head_groups, HEAD_SIZE)
+            head_keys = flattened_cache[:, kv_head * HEAD_SIZE : (kv_head + 1) * HEAD_SIZE]
+            head_values = flattened_cache[
+                :, (KEY_VALUE_HEADS + kv_head) * HEAD_SIZE : (KEY_VALUE_HEADS + kv_head + 1) * HEAD_SIZE
+            ]
+            scores = jnp.einsum(
+                "rgd,ld->rgl", head_rows, head_keys, preferred_element_type=jnp.float32
+            ) * HEAD_SIZE ** (-0.5)
+            top = jnp.max(jnp.where(score_mask, scores, -1e30), axis=-1)
+            soft = jnp.where(score_mask, jnp.exp(scores - top[..., None]), 0.0)
+            total = jnp.sum(soft, axis=-1)
+            weighted_part = jnp.einsum(
+                "rgl,ld->rgd",
+                soft.astype(jnp.bfloat16),
+                head_values,
+                preferred_element_type=jnp.float32,
+            )
+            outs.append((top, total, weighted_part))
+        part_max = jnp.stack([o[0] for o in outs], axis=1)
+        part_sum = jnp.stack([o[1] for o in outs], axis=1)
+        part_weighted = jnp.stack([o[2] for o in outs], axis=1)
         return (part_max, part_sum, part_weighted)
 
     row_max, row_sum, weighted = lax.map(one_group, jnp.arange(local_groups, dtype=jnp.int32))
@@ -201,7 +223,7 @@
     resid = tokens.astype(jnp.float32) + jnp.dot(
         attended, out_weight, preferred_element_type=jnp.float32
     )
-    mid_squares = lax.psum(jnp.sum(resid * resid, axis=1), "tp")
+    mid_squares = tp_sum(jnp.sum(resid * resid, axis=1))
     normed = (resid * lax.rsqrt(mid_squares / full_width + EPSILON)[:, None] * norm_gain).astype(
         jnp.bfloat16
     )
@@ -214,9 +236,12 @@
     expert_onehot = (flat_ids[:, None] == jnp.arange(experts, dtype=jnp.int32)[None, :]).astype(
         jnp.int32
     )
-    expert_rank = jnp.sum(
-        (jnp.cumsum(expert_onehot, axis=0) - expert_onehot) * expert_onehot, axis=1
-    )
+    assign_iota = jnp.arange(flat_ids.shape[0], dtype=jnp.int32)
+    earlier = (assign_iota[None, :] < assign_iota[:, None]).astype(jnp.bfloat16)
+    before = jnp.dot(
+        earlier, expert_onehot.astype(jnp.bfloat16), preferred_element_type=jnp.float32
+    ).astype(jnp.int32)
+    expert_rank = jnp.sum(before * expert_onehot, axis=1)
     my_half = lax.axis_index("el")
     target = (relative(flat_ids, my_half, half_count) * capacity + expert_rank).reshape(
         count_of_rows, top_count
@@ -226,7 +251,17 @@
     dispatch = jnp.any(hits, axis=2).astype(jnp.bfloat16)
     outgoing = jnp.dot(dispatch, normed, preferred_element_type=jnp.float32).astype(jnp.bfloat16)
     arrived = exchange(outgoing.reshape(experts, capacity, feat_part), half_count)
-    summed = expert_block(arrived.reshape(buffer_len, feat_part), gate_w[0], up_w[0], down_w[0])
+    flat_rows = lax.optimization_barrier(arrived.reshape(buffer_len, feat_part))
+    group_rows = buffer_len // 2
+    summed = jnp.concatenate(
+        [
+            expert_block(
+                flat_rows[start : start + group_rows], gate_w[0], up_w[0], down_w[0]
+            )
+            for start in (0, group_rows)
+        ],
+        axis=0,
+    )
     returned = exchange(summed.reshape(experts, capacity, feat_part), half_count).reshape(
         buffer_len, feat_part
     )
@@ -245,7 +280,7 @@
         preferred_element_type=jnp.float32,
     )
     mixed_rows = resid + branch
-    out_squares = lax.psum(jnp.sum(mixed_rows * mixed_rows, axis=1), "tp")
+    out_squares = tp_sum(jnp.sum(mixed_rows * mixed_rows, axis=1))
     return (
         mixed_rows * lax.rsqrt(out_squares / full_width + EPSILON)[:, None] * final_gain
     ).astype(jnp.bfloat16)

time: 107 us -> 88.9 us (0.83)
  blocking collectives: 11.3 us -> 0 us
  local copies, waits for them, and re-layouts: 19 us -> 9.06 us
  waiting for transfers between devices: 25.7 us -> 31.2 us
  matrix products: 20.3 us -> 16.5 us
  starting transfers between devices: 21.8 us -> 23.7 us
    ppermute x14, waiting for transfers between devices: 21.3 us -> 29 us  [exchange(): pieces.append(lax.ppermute(chunks[step], 'el', perm=pairs))]
    all_gather x3 -> x0, blocking collectives: 6.21 us -> none  [merged(): lax.all_gather(a.astype(kind), axis)]
    dot_general x4 -> x8, matrix products: 9.93 us -> 4.67 us  [half_product(): return jnp.dot(x, weight, preferred_element_type=jnp.float32)]
    psum x2 -> x0, blocking collectives: 5.12 us -> none  [the longest x1 2.65 us: shards(): mid_squares = lax.psum(jnp.sum(resid * resid, axis=1), 'tp')]
    unnamed x47 -> x36, local copies, waits for them, and re-layouts: 7.9 us -> 3.93 us
    slice x3 -> x2, local copies, waits for them, and re-layouts: 4.92 us -> 1.15 us  [the longest x1 1.05 us: one_group(): queries[:, kv_head * head_groups * HEAD_SIZE:(kv_head + 1) * head_groups...]
    ppermute x1 -> x2, waiting for transfers between devices: 3.32 us -> 0.01 us  [expert_block(): sent = lax.ppermute(down_product(other), 'tp', perm=swap)]
    dot_general x2 -> x5, matrix products: 3.58 us -> 6.31 us  [the longest x2 3.85 us: one_group(): jnp.einsum('rgd,ld->rgl', head_rows, head_keys, preferred_element_type=jn...]
  transfers between devices with their start and end apart: 16 -> 23, of which waited for: 10 -> 13; matrix products, arithmetic and copies ran while one was open for 7% -> 14% of each run, Pallas kernels for 0% -> 0%
where the time goes in v7:
time: 88.9 us; the launch traced here: 88.5 us
  waiting for transfers between devices  31.2 us (35%)
  starting transfers between devices  23.7 us (27%)
  matrix products  16.5 us (19%)
  local copies, waits for them, and re-layouts  9.06 us (10%)
  other arithmetic  7.52 us (8%)
    ppermute x14, waiting for transfers between devices, exchange(): pieces.append(lax.ppermute(chunks[step], 'el', perm=pairs))  29 us
    ppermute x14, starting transfers between devices, exchange(): pieces.append(lax.ppermute(chunks[step], 'el', perm=pairs))  21.4 us
    dot_general x8, matrix products, half_product(): return jnp.dot(x, weight, preferred_element_type=jnp.float32)  4.67 us
    unnamed x36, local copies, waits for them, and re-layouts  3.93 us
    dot_general x2, matrix products, one_group(): jnp.einsum('rgd,ld->rgl', head_rows, head_keys, preferred_element_type=jn...  3.85 us
    gather x1, local copies, waits for them, and re-layouts, one_group(): page_row_block = group_pages[local_table.reshape(-1)]  3.32 us
    dot_general x4, matrix products, down_product(): jnp.dot(hidden, weight, preferred_element_type=jnp.float32)  2.51 us
    dot_general x2, matrix products, one_group(): jnp.einsum('rgl,ld->rgd', soft.astype(jnp.bfloat16), head_values, preferr...  2.19 us
  transfers between devices with their start and end apart: 23, of which 13 were waited for; matrix products, arithmetic and copies ran while one was open for 14% of the time, Pallas kernels for 0%

profile of v7, /device:TPU:0, one launch (start us, length us, event | category | flops | bytes accessed | tf_op | source)
XLA Modules:
  0.0 88.5 jit_solution(5288920605972785651)
XLA Ops:
  4.2 3.3 %gather_fusion = bf16[96,16,512]{2,1,0:T(8,128)(2,1)} fusion(bf16[96,16,512]{2,1,0:T(8,128)(2,1)} %bitcast.189, s32[1024]{0:T(1024)S(1)} %pad_clamp_fusion), kind=kCustom, calls=%fused_computation | custom fusion | bytes 3146112 | tf_op jit(solution)/shard_map/while/body/eval_jaxpr/gather | solution.py:170
  8.5 1.9 %fusion.3 = (f32[128,6]{0,1:T(8,128)S(1)}, f32[1536,128,6]{1,0,2:T(8,128)S(1)}) fusion(pred[128,1536]{0,1:T(8,128)(4,1)S(1)} %compare_and_fusion, bf16[128,6,128]{0,2,1:T(8,128)(2,1)S(1)} %bitcast.191, bf16[1536,512]{1,0:T(8,128)(2,1)} %bitcast.184), kind=kOutput, calls=%fused_computation.8 | convolution fusion | flops 305528064 | bytes 5508096 | tf_op jit(solution)/shard_map/while/body/eval_jaxpr/rgd,ld->rgl/dot_general | solution.py:195
  10.5 1.9 %fusion.6 = (bf16[128,6]{0,1:T(8,128)(2,1)S(1)}, f32[128,6]{0,1:T(8,128)S(1)}, f32[1536,128,6]{1,0,2:T(8,128)S(1)}) fusion(f32[1536,128,6]{1,0,2:T(8,128)S(1)} %get-tuple-element.59, f32[128,6]{0,1:T(8,128)S(1)} %get-tuple-element.58, pred[128,1536]{0,1:T(8,128)(4,1)S(1)} %compare_and_fusion, bf16[128,6,128]{0,2,1:T(8,128)(2,1)S(1)} %bitcast.192, ...), kind=kOutput, calls=%fused_computation.11 | convolution fusion | flops 310245888 | bytes 10232320 | tf_op jit(solution)/shard_map/while/body/eval_jaxpr/rgd,ld->rgl/dot_general | solution.py:195
  14.0 1.1 %fusion.29 = bf16[128,1,6,128]{0,3,2,1:T(8,128)(2,1)S(1)} fusion(f32[1536,128,6]{1,0,2:T(8,128)S(1)} %get-tuple-element.60, f32[128,6]{0,1:T(8,128)S(1)} %get-tuple-element.24, pred[128,1536]{0,1:T(8,128)(4,1)S(1)} %compare_and_fusion, bf16[1536,512]{1,0:T(8,128)(2,1)S(1)} %bitcast.186), kind=kOutput, calls=%fused_computation.44 | convolution fusion | flops 306806784 | bytes 5509120 | tf_op jit(solution)/shard_map/while/body/eval_jaxpr/rgl,ld->rgd/dot_general | solution.py:201
  15.1 1.1 %fusion.32 = bf16[128,1,6,128]{0,3,2,1:T(8,128)(2,1)S(1)} fusion(f32[1536,128,6]{1,0,2:T(8,128)S(1)} %get-tuple-element.59, f32[128,6]{0,1:T(8,128)S(1)} %get-tuple-element.58, pred[128,1536]{0,1:T(8,128)(4,1)S(1)} %compare_and_fusion, bf16[1536,512]{1,0:T(8,128)(2,1)S(1)} %bitcast.187), kind=kOutput, calls=%fused_computation.45 | convolution fusion | flops 306806784 | bytes 5509120 | tf_op jit(solution)/shard_map/while/body/eval_jaxpr/rgl,ld->rgd/dot_general | solution.py:201
  19.2 1.2 %divide_convert_fusion = bf16[128,2,6,128]{0,3,2,1:T(8,128)(2,1)S(1)} fusion(bf16[128,2,6,128]{0,3,2,1:T(8,128)(2,1)} %collective-permute-done.1, f32[128,2,6]{0,2,1:T(8,128)S(1)} %get-tuple-element.56, f32[128,2,6]{0,2,1:T(8,128)S(1)} %get-tuple-element.57, f32[128,2,6]{0,2,1:T(8,128)S(1)} %get-tuple-element.55, bf16[128,1,6,128]{0,3,2,1:T(8,128)(2,1)S(1)} %fusion.29, ...), kind=kLoop, calls=%fused_computation.50 | loop fusion | flops 1572864 | bytes 1198080 | tf_op jit(solution)/shard_map/convert_element_type | solution.py:221
  20.4 1.5 %multiply_reduce_fusion.1 = (f32[128]{0:T(128)S(1)}, f32[128,768]{1,0:T(8,128)S(1)}) fusion(bf16[128,1536]{0,1:T(8,128)(2,1)S(1)} %bitcast.190, bf16[1536,768]{1,0:T(8,128)(2,1)S(1)} %copy-done, bf16[128,768]{1,0:T(8,128)(2,1)} %param.14), kind=kOutput, calls=%fused_computation.90 | convolution fusion | flops 302382976 | bytes 3342848 | tf_op jit(solution)/shard_map/dot_general | solution.py:223
  23.9 2.9 %collective-permute-start.4 = (bf16[128,768]{1,0:T(8,128)(2,1)S(1)}, bf16[128,768]{1,0:T(8,128)(2,1)S(1)}, u32[]{:S(2)}, u32[]{:S(2)}) collective-permute-start(bf16[128,768]{1,0:T(8,128)(2,1)S(1)} %get-tuple-element.45), channel_id=1, source_target_pairs={{0,2},{2,0},{4,6},{6,4},{8,10},{10,8},{12,14},{14,12},{1,3},{3,1},... | collective-permute-start | bytes 589832 | tf_op jit(solution)/shard_map/ppermute | solution.py:52
  26.8 1.5 %collective-permute-start.5 = (bf16[128,768]{1,0:T(8,128)(2,1)S(1)}, bf16[128,768]{1,0:T(8,128)(2,1)S(1)}, u32[]{:S(2)}, u32[]{:S(2)}) collective-permute-start(bf16[128,768]{1,0:T(8,128)(2,1)S(1)} %get-tuple-element.44), channel_id=1, source_target_pairs={{0,4},{2,6},{4,0},{6,2},{8,12},{10,14},{12,8},{14,10},{1,5},{3,7},... | collective-permute-start | bytes 589832 | tf_op jit(solution)/shard_map/ppermute | solution.py:52
  28.3 2.0 %collective-permute-start.7 = (bf16[128,768]{1,0:T(8,128)(2,1)S(1)}, bf16[128,768]{1,0:T(8,128)(2,1)S(1)}, u32[]{:S(2)}, u32[]{:S(2)}) collective-permute-start(bf16[128,768]{1,0:T(8,128)(2,1)S(1)} %get-tuple-element.40), channel_id=1, source_target_pairs={{0,8},{2,10},{4,12},{6,14},{8,0},{10,2},{12,4},{14,6},{1,9},{3,11}... | collective-permute-start | bytes 589832 | tf_op jit(solution)/shard_map/ppermute | solution.py:52
  30.4 1.4 %collective-permute-start.8 = (bf16[128,768]{1,0:T(8,128)(2,1)S(1)}, bf16[128,768]{1,0:T(8,128)(2,1)S(1)}, u32[]{:S(2)}, u32[]{:S(2)}) collective-permute-start(bf16[128,768]{1,0:T(8,128)(2,1)S(1)} %get-tuple-element.29), channel_id=1, source_target_pairs={{0,10},{2,8},{4,14},{6,12},{8,2},{10,0},{12,6},{14,4},{1,11},{3,9}... | collective-permute-start | bytes 589832 | tf_op jit(solution)/shard_map/ppermute | solution.py:52
  32.5 3.1 %collective-permute-start.9 = (bf16[128,768]{1,0:T(8,128)(2,1)S(1)}, bf16[128,768]{1,0:T(8,128)(2,1)S(1)}, u32[]{:S(2)}, u32[]{:S(2)}) collective-permute-start(bf16[128,768]{1,0:T(8,128)(2,1)S(1)} %get-tuple-element.28), channel_id=1, source_target_pairs={{0,12},{2,14},{4,8},{6,10},{8,4},{10,6},{12,0},{14,2},{1,13},{3,15... | collective-permute-start | bytes 589832 | tf_op jit(solution)/shard_map/ppermute | solution.py:52
  36.0 1.3 %collective-permute-start.10 = (bf16[128,768]{1,0:T(8,128)(2,1)S(1)}, bf16[128,768]{1,0:T(8,128)(2,1)S(1)}, u32[]{:S(2)}, u32[]{:S(2)}) collective-permute-start(bf16[128,768]{1,0:T(8,128)(2,1)S(1)} %get-tuple-element.27), channel_id=1, source_target_pairs={{0,14},{2,12},{4,10},{6,8},{8,6},{10,4},{12,2},{14,0},{1,15},{3,13... | collective-permute-start | bytes 589832 | tf_op jit(solution)/shard_map/ppermute | solution.py:52
  37.3 3.5 %collective-permute-done.6 = bf16[128,768]{1,0:T(8,128)(2,1)S(1)} collective-permute-done((bf16[128,768]{1,0:T(8,128)(2,1)S(1)}, bf16[128,768]{1,0:T(8,128)(2,1)S(1)}, u32[]{:S(2)}, u32[]{:S(2)}) %collective-permute-start.6) | collective-permute-done | bytes 196640 | tf_op jit(solution)/shard_map/ppermute | solution.py:52
  41.8 4.2 %collective-permute-done.9 = bf16[128,768]{1,0:T(8,128)(2,1)S(1)} collective-permute-done((bf16[128,768]{1,0:T(8,128)(2,1)S(1)}, bf16[128,768]{1,0:T(8,128)(2,1)S(1)}, u32[]{:S(2)}, u32[]{:S(2)}) %collective-permute-start.9) | collective-permute-done | bytes 196640 | tf_op jit(solution)/shard_map/ppermute | solution.py:52
  46.0 3.4 %collective-permute-done.10 = bf16[128,768]{1,0:T(8,128)(2,1)S(1)} collective-permute-done((bf16[128,768]{1,0:T(8,128)(2,1)S(1)}, bf16[128,768]{1,0:T(8,128)(2,1)S(1)}, u32[]{:S(2)}, u32[]{:S(2)}) %collective-permute-start.10) | collective-permute-done | bytes 196640 | tf_op jit(solution)/shard_map/ppermute | solution.py:52
  60.3 1.6 %collective-permute-start.18 = (bf16[128,768]{1,0:T(8,128)(2,1)S(1)}, bf16[128,768]{1,0:T(8,128)(2,1)S(1)}, u32[]{:S(2)}, u32[]{:S(2)}) collective-permute-start(bf16[128,768]{1,0:T(8,128)(2,1)S(1)} %get-tuple-element.49), channel_id=1, source_target_pairs={{0,8},{2,10},{4,12},{6,14},{8,0},{10,2},{12,4},{14,6},{1,9},{3,11}... | collective-permute-start | bytes 589832 | tf_op jit(solution)/shard_map/ppermute | solution.py:52
  63.3 2.4 %collective-permute-start.15 = (bf16[128,768]{1,0:T(8,128)(2,1)S(1)}, bf16[128,768]{1,0:T(8,128)(2,1)S(1)}, u32[]{:S(2)}, u32[]{:S(2)}) collective-permute-start(bf16[128,768]{1,0:T(8,128)(2,1)S(1)} %get-tuple-element.50), channel_id=1, source_target_pairs={{0,6},{2,4},{4,2},{6,0},{8,14},{10,12},{12,10},{14,8},{1,7},{3,5},... | collective-permute-start | bytes 589832 | tf_op jit(solution)/shard_map/ppermute | solution.py:52
  66.7 7.5 %collective-permute-done.13 = bf16[128,768]{1,0:T(8,128)(2,1)S(1)} collective-permute-done((bf16[128,768]{1,0:T(8,128)(2,1)S(1)}, bf16[128,768]{1,0:T(8,128)(2,1)S(1)}, u32[]{:S(2)}, u32[]{:S(2)}) %collective-permute-start.13) | collective-permute-done | bytes 196640 | tf_op jit(solution)/shard_map/ppermute | solution.py:52
  75.2 2.1 %collective-permute-start.21 = (bf16[128,768]{1,0:T(8,128)(2,1)S(1)}, bf16[128,768]{1,0:T(8,128)(2,1)S(1)}, u32[]{:S(2)}, u32[]{:S(2)}) collective-permute-start(bf16[128,768]{1,0:T(8,128)(2,1)S(1)} %get-tuple-element.46), channel_id=1, source_target_pairs={{0,14},{2,12},{4,10},{6,8},{8,6},{10,4},{12,2},{14,0},{1,15},{3,13... | collective-permute-start | bytes 589832 | tf_op jit(solution)/shard_map/ppermute | solution.py:52
  77.3 2.0 %collective-permute-done.15 = bf16[128,768]{1,0:T(8,128)(2,1)S(1)} collective-permute-done((bf16[128,768]{1,0:T(8,128)(2,1)S(1)}, bf16[128,768]{1,0:T(8,128)(2,1)S(1)}, u32[]{:S(2)}, u32[]{:S(2)}) %collective-permute-start.15) | collective-permute-done | bytes 196640 | tf_op jit(solution)/shard_map/ppermute | solution.py:52
  79.4 4.3 %collective-permute-done.20 = bf16[128,768]{1,0:T(8,128)(2,1)S(1)} collective-permute-done((bf16[128,768]{1,0:T(8,128)(2,1)S(1)}, bf16[128,768]{1,0:T(8,128)(2,1)S(1)}, u32[]{:S(2)}, u32[]{:S(2)}) %collective-permute-start.20) | collective-permute-done | bytes 196640 | tf_op jit(solution)/shard_map/ppermute | solution.py:52
  83.8 1.9 %collective-permute-done.21 = bf16[128,768]{1,0:T(8,128)(2,1)S(1)} collective-permute-done((bf16[128,768]{1,0:T(8,128)(2,1)S(1)}, bf16[128,768]{1,0:T(8,128)(2,1)S(1)}, u32[]{:S(2)}, u32[]{:S(2)}) %collective-permute-start.21) | collective-permute-done | bytes 196640 | tf_op jit(solution)/shard_map/ppermute | solution.py:52
  86.6 1.1 %collective-permute-done.22 = f32[128]{0:T(128)S(1)} collective-permute-done((f32[128]{0:T(128)S(1)}, f32[128]{0:T(128)S(1)}, u32[]{:S(2)}, u32[]{:S(2)}) %collective-permute-start.22) | collective-permute-done | bytes 544 | tf_op jit(solution)/shard_map/ppermute | solution.py:94
  (117 shorter events, 29.6 us)
Async XLA Ops:
  0.0 20.4 %copy-start = (bf16[1536,768]{1,0:T(8,128)(2,1)S(1)}, bf16[1536,768]{1,0:T(8,128)(2,1)}, u32[]{:S(2)}) copy-start(bf16[1536,768]{1,0:T(8,128)(2,1)} %param.20) | copy-start | bytes 7077892
  13.4 5.5 %collective-permute-start.2 = (bf16[128,2,6]{0,2,1:T(8,128)(2,1)S(1)}, bf16[128,2,6]{0,2,1:T(8,128)(2,1)S(1)}, u32[]{:S(2)}, u32[]{:S(2)}) collective-permute-start(bf16[128,2,6]{0,2,1:T(8,128)(2,1)S(1)} %pad_maximum_fusion.2), channel_id=1, source_target_pairs={{0,1},{1,0},{2,3},{3,2},{4,5},{5,4},{6,7},{7,6},{8,9},{9,8},{10,11... | collective-permute-start | bytes 9224 | tf_op jit(solution)/shard_map/ppermute | solution.py:18
  13.9 5.0 %collective-permute-start = (bf16[128,2,6]{0,2,1:T(8,128)(2,1)S(1)}, bf16[128,2,6]{0,2,1:T(8,128)(2,1)S(1)}, u32[]{:S(2)}, u32[]{:S(2)}) collective-permute-start(bf16[128,2,6]{0,2,1:T(8,128)(2,1)S(1)} %pad_maximum_fusion.1), channel_id=1, source_target_pairs={{0,1},{1,0},{2,3},{3,2},{4,5},{5,4},{6,7},{7,6},{8,9},{9,8},{10,11... | collective-permute-start | bytes 9224 | tf_op jit(solution)/shard_map/ppermute | solution.py:18
  17.0 2.1 %collective-permute-start.1 = (bf16[128,2,6,128]{0,3,2,1:T(8,128)(2,1)}, bf16[128,2,6,128]{0,3,2,1:T(8,128)(2,1)}, u32[]{:S(2)}, u32[]{:S(2)}) collective-permute-start(bf16[128,2,6,128]{0,3,2,1:T(8,128)(2,1)} %pad_maximum_fusion), channel_id=1, source_target_pairs={{0,1},{1,0},{2,3},{3,2},{4,5},{5,4},{6,7},{7,6},{8,9},{9,8},{10,11... | collective-permute-start | bytes 1179656 | tf_op jit(solution)/shard_map/ppermute | solution.py:18
  21.9 1.3 %collective-permute-start.3 = (f32[128]{0:T(128)S(1)}, f32[128]{0:T(128)S(1)}, u32[]{:S(2)}, u32[]{:S(2)}) collective-permute-start(f32[128]{0:T(128)S(1)} %get-tuple-element.61), channel_id=1, source_target_pairs={{0,1},{1,0},{2,3},{3,2},{4,5},{5,4},{6,7},{7,6},{8,9},{9,8},{10,11... | collective-permute-start | bytes 1544 | tf_op jit(solution)/shard_map/ppermute | solution.py:94
  23.9 8.5 %collective-permute-start.4 = (bf16[128,768]{1,0:T(8,128)(2,1)S(1)}, bf16[128,768]{1,0:T(8,128)(2,1)S(1)}, u32[]{:S(2)}, u32[]{:S(2)}) collective-permute-start(bf16[128,768]{1,0:T(8,128)(2,1)S(1)} %get-tuple-element.45), channel_id=1, source_target_pairs={{0,2},{2,0},{4,6},{6,4},{8,10},{10,8},{12,14},{14,12},{1,3},{3,1},... | collective-permute-start | bytes 589832 | tf_op jit(solution)/shard_map/ppermute | solution.py:52
  26.8 9.2 %collective-permute-start.5 = (bf16[128,768]{1,0:T(8,128)(2,1)S(1)}, bf16[128,768]{1,0:T(8,128)(2,1)S(1)}, u32[]{:S(2)}, u32[]{:S(2)}) collective-permute-start(bf16[128,768]{1,0:T(8,128)(2,1)S(1)} %get-tuple-element.44), channel_id=1, source_target_pairs={{0,4},{2,6},{4,0},{6,2},{8,12},{10,14},{12,8},{14,10},{1,5},{3,7},... | collective-permute-start | bytes 589832 | tf_op jit(solution)/shard_map/ppermute | solution.py:52
  28.3 12.5 %collective-permute-start.6 = (bf16[128,768]{1,0:T(8,128)(2,1)S(1)}, bf16[128,768]{1,0:T(8,128)(2,1)S(1)}, u32[]{:S(2)}, u32[]{:S(2)}) collective-permute-start(bf16[128,768]{1,0:T(8,128)(2,1)S(1)} %get-tuple-element.42), channel_id=1, source_target_pairs={{0,6},{2,4},{4,2},{6,0},{8,14},{10,12},{12,10},{14,8},{1,7},{3,5},... | collective-permute-start | bytes 589832 | tf_op jit(solution)/shard_map/ppermute | solution.py:52
  28.3 12.5 %collective-permute-start.7 = (bf16[128,768]{1,0:T(8,128)(2,1)S(1)}, bf16[128,768]{1,0:T(8,128)(2,1)S(1)}, u32[]{:S(2)}, u32[]{:S(2)}) collective-permute-start(bf16[128,768]{1,0:T(8,128)(2,1)S(1)} %get-tuple-element.40), channel_id=1, source_target_pairs={{0,8},{2,10},{4,12},{6,14},{8,0},{10,2},{12,4},{14,6},{1,9},{3,11}... | collective-permute-start | bytes 589832 | tf_op jit(solution)/shard_map/ppermute | solution.py:52
  30.4 11.4 %collective-permute-start.8 = (bf16[128,768]{1,0:T(8,128)(2,1)S(1)}, bf16[128,768]{1,0:T(8,128)(2,1)S(1)}, u32[]{:S(2)}, u32[]{:S(2)}) collective-permute-start(bf16[128,768]{1,0:T(8,128)(2,1)S(1)} %get-tuple-element.29), channel_id=1, source_target_pairs={{0,10},{2,8},{4,14},{6,12},{8,2},{10,0},{12,6},{14,4},{1,11},{3,9}... | collective-permute-start | bytes 589832 | tf_op jit(solution)/shard_map/ppermute | solution.py:52
  32.5 13.6 %collective-permute-start.9 = (bf16[128,768]{1,0:T(8,128)(2,1)S(1)}, bf16[128,768]{1,0:T(8,128)(2,1)S(1)}, u32[]{:S(2)}, u32[]{:S(2)}) collective-permute-start(bf16[128,768]{1,0:T(8,128)(2,1)S(1)} %get-tuple-element.28), channel_id=1, source_target_pairs={{0,12},{2,14},{4,8},{6,10},{8,4},{10,6},{12,0},{14,2},{1,13},{3,15... | collective-permute-start | bytes 589832 | tf_op jit(solution)/shard_map/ppermute | solution.py:52
  36.0 13.5 %collective-permute-start.10 = (bf16[128,768]{1,0:T(8,128)(2,1)S(1)}, bf16[128,768]{1,0:T(8,128)(2,1)S(1)}, u32[]{:S(2)}, u32[]{:S(2)}) collective-permute-start(bf16[128,768]{1,0:T(8,128)(2,1)S(1)} %get-tuple-element.27), channel_id=1, source_target_pairs={{0,14},{2,12},{4,10},{6,8},{8,6},{10,4},{12,2},{14,0},{1,15},{3,13... | collective-permute-start | bytes 589832 | tf_op jit(solution)/shard_map/ppermute | solution.py:52
  49.6 4.2 %collective-permute-start.16 = (bf16[512,768]{1,0:T(8,128)(2,1)S(1)}, bf16[512,768]{1,0:T(8,128)(2,1)S(1)}, u32[]{:S(2)}, u32[]{:S(2)}) collective-permute-start(bf16[512,768]{1,0:T(8,128)(2,1)S(1)} %get-tuple-element.25), channel_id=1, source_target_pairs={{0,1},{1,0},{2,3},{3,2},{4,5},{5,4},{6,7},{7,6},{8,9},{9,8},{10,11... | collective-permute-start | bytes 2359304 | tf_op jit(solution)/shard_map/ppermute | solution.py:70
  51.4 5.8 %collective-permute-start.11 = (bf16[512,768]{1,0:T(8,128)(2,1)S(1)}, bf16[512,768]{1,0:T(8,128)(2,1)S(1)}, u32[]{:S(2)}, u32[]{:S(2)}) collective-permute-start(bf16[512,768]{1,0:T(8,128)(2,1)S(1)} %get-tuple-element.26), channel_id=1, source_target_pairs={{0,1},{1,0},{2,3},{3,2},{4,5},{5,4},{6,7},{7,6},{8,9},{9,8},{10,11... | collective-permute-start | bytes 2359304 | tf_op jit(solution)/shard_map/ppermute | solution.py:70
  56.4 3.6 %collective-permute-start.17 = (bf16[512,768]{1,0:T(8,128)(2,1)S(1)}, bf16[512,768]{1,0:T(8,128)(2,1)S(1)}, u32[]{:S(2)}, u32[]{:S(2)}) collective-permute-start(bf16[512,768]{1,0:T(8,128)(2,1)S(1)} %convolution_convert_fusion.1), channel_id=1, source_target_pairs={{0,1},{1,0},{2,3},{3,2},{4,5},{5,4},{6,7},{7,6},{8,9},{9,8},{10,11... | collective-permute-start | bytes 2359304 | tf_op jit(solution)/shard_map/ppermute | solution.py:86
  58.9 3.1 %collective-permute-start.12 = (bf16[512,768]{1,0:T(8,128)(2,1)S(1)}, bf16[512,768]{1,0:T(8,128)(2,1)S(1)}, u32[]{:S(2)}, u32[]{:S(2)}) collective-permute-start(bf16[512,768]{1,0:T(8,128)(2,1)S(1)} %convolution_convert_fusion.3), channel_id=1, source_target_pairs={{0,1},{1,0},{2,3},{3,2},{4,5},{5,4},{6,7},{7,6},{8,9},{9,8},{10,11... | collective-permute-start | bytes 2359304 | tf_op jit(solution)/shard_map/ppermute | solution.py:86
  60.3 19.1 %collective-permute-start.18 = (bf16[128,768]{1,0:T(8,128)(2,1)S(1)}, bf16[128,768]{1,0:T(8,128)(2,1)S(1)}, u32[]{:S(2)}, u32[]{:S(2)}) collective-permute-start(bf16[128,768]{1,0:T(8,128)(2,1)S(1)} %get-tuple-element.49), channel_id=1, source_target_pairs={{0,8},{2,10},{4,12},{6,14},{8,0},{10,2},{12,4},{14,6},{1,9},{3,11}... | collective-permute-start | bytes 589832 | tf_op jit(solution)/shard_map/ppermute | solution.py:52
  62.2 12.1 %collective-permute-start.13 = (bf16[128,768]{1,0:T(8,128)(2,1)S(1)}, bf16[128,768]{1,0:T(8,128)(2,1)S(1)}, u32[]{:S(2)}, u32[]{:S(2)}) collective-permute-start(bf16[128,768]{1,0:T(8,128)(2,1)S(1)} %get-tuple-element.52), channel_id=1, source_target_pairs={{0,2},{2,0},{4,6},{6,4},{8,10},{10,8},{12,14},{14,12},{1,3},{3,1},... | collective-permute-start | bytes 589832 | tf_op jit(solution)/shard_map/ppermute | solution.py:52
  62.8 12.3 %collective-permute-start.14 = (bf16[128,768]{1,0:T(8,128)(2,1)S(1)}, bf16[128,768]{1,0:T(8,128)(2,1)S(1)}, u32[]{:S(2)}, u32[]{:S(2)}) collective-permute-start(bf16[128,768]{1,0:T(8,128)(2,1)S(1)} %get-tuple-element.51), channel_id=1, source_target_pairs={{0,4},{2,6},{4,0},{6,2},{8,12},{10,14},{12,8},{14,10},{1,5},{3,7},... | collective-permute-start | bytes 589832 | tf_op jit(solution)/shard_map/ppermute | solution.py:52
  63.3 16.0 %collective-permute-start.15 = (bf16[128,768]{1,0:T(8,128)(2,1)S(1)}, bf16[128,768]{1,0:T(8,128)(2,1)S(1)}, u32[]{:S(2)}, u32[]{:S(2)}) collective-permute-start(bf16[128,768]{1,0:T(8,128)(2,1)S(1)} %get-tuple-element.50), channel_id=1, source_target_pairs={{0,6},{2,4},{4,2},{6,0},{8,14},{10,12},{12,10},{14,8},{1,7},{3,5},... | collective-permute-start | bytes 589832 | tf_op jit(solution)/shard_map/ppermute | solution.py:52
  65.7 13.7 %collective-permute-start.19 = (bf16[128,768]{1,0:T(8,128)(2,1)S(1)}, bf16[128,768]{1,0:T(8,128)(2,1)S(1)}, u32[]{:S(2)}, u32[]{:S(2)}) collective-permute-start(bf16[128,768]{1,0:T(8,128)(2,1)S(1)} %get-tuple-element.48), channel_id=1, source_target_pairs={{0,10},{2,8},{4,14},{6,12},{8,2},{10,0},{12,6},{14,4},{1,11},{3,9}... | collective-permute-start | bytes 589832 | tf_op jit(solution)/shard_map/ppermute | solution.py:52
  74.3 9.5 %collective-permute-start.20 = (bf16[128,768]{1,0:T(8,128)(2,1)S(1)}, bf16[128,768]{1,0:T(8,128)(2,1)S(1)}, u32[]{:S(2)}, u32[]{:S(2)}) collective-permute-start(bf16[128,768]{1,0:T(8,128)(2,1)S(1)} %get-tuple-element.47), channel_id=1, source_target_pairs={{0,12},{2,14},{4,8},{6,10},{8,4},{10,6},{12,0},{14,2},{1,13},{3,15... | collective-permute-start | bytes 589832 | tf_op jit(solution)/shard_map/ppermute | solution.py:52
  75.2 10.5 %collective-permute-start.21 = (bf16[128,768]{1,0:T(8,128)(2,1)S(1)}, bf16[128,768]{1,0:T(8,128)(2,1)S(1)}, u32[]{:S(2)}, u32[]{:S(2)}) collective-permute-start(bf16[128,768]{1,0:T(8,128)(2,1)S(1)} %get-tuple-element.46), channel_id=1, source_target_pairs={{0,14},{2,12},{4,10},{6,8},{8,6},{10,4},{12,2},{14,0},{1,15},{3,13... | collective-permute-start | bytes 589832 | tf_op jit(solution)/shard_map/ppermute | solution.py:52
  86.6 1.2 %collective-permute-start.22 = (f32[128]{0:T(128)S(1)}, f32[128]{0:T(128)S(1)}, u32[]{:S(2)}, u32[]{:S(2)}) collective-permute-start(f32[128]{0:T(128)S(1)} %get-tuple-element.63), channel_id=1, source_target_pairs={{0,1},{1,0},{2,3},{3,2},{4,5},{5,4},{6,7},{7,6},{8,9},{9,8},{10,11... | collective-permute-start | bytes 1544 | tf_op jit(solution)/shard_map/ppermute | solution.py:94
  (8 other events, 18.0 us)

commit v8 on v7

--- a/solution.py
+++ b/solution.py
@@ -155,7 +155,10 @@
     def one_group(local):
         query_count = lax.dynamic_index_in_dim(query_lens, local, 0, keepdims=False)
         past_count = lax.dynamic_index_in_dim(past_lens, local, 0, keepdims=False)
-        row_ends = jnp.cumsum(query_count)
+        req_iota = jnp.arange(req_count, dtype=jnp.int32)
+        row_ends = jnp.sum(
+            jnp.where(req_iota[None, :] <= req_iota[:, None], query_count[None, :], 0), axis=1
+        )
         row_starts = row_ends - query_count
         row_iota = jnp.arange(group_rows, dtype=jnp.int32)
         row_req = jnp.sum((row_iota[:, None] >= row_ends[None, :]).astype(jnp.int32), axis=1)
@@ -253,18 +256,16 @@
     arrived = exchange(outgoing.reshape(experts, capacity, feat_part), half_count)
     flat_rows = lax.optimization_barrier(arrived.reshape(buffer_len, feat_part))
     group_rows = buffer_len // 2
-    summed = jnp.concatenate(
-        [
-            expert_block(
-                flat_rows[start : start + group_rows], gate_w[0], up_w[0], down_w[0]
-            )
-            for start in (0, group_rows)
-        ],
-        axis=0,
-    )
-    returned = exchange(summed.reshape(experts, capacity, feat_part), half_count).reshape(
-        buffer_len, feat_part
-    )
+    first_done = expert_block(flat_rows[:group_rows], gate_w[0], up_w[0], down_w[0])
+    first_done, second_rows = lax.optimization_barrier((first_done, flat_rows[group_rows:]))
+    second_done = expert_block(second_rows, gate_w[0], up_w[0], down_w[0])
+    per_group = group_rows // capacity
+    result_chunks = [
+        done[index * capacity : (index + 1) * capacity]
+        for done in (first_done, second_done)
+        for index in range(per_group)
+    ]
+    returned = exchange(result_chunks, half_count).reshape(buffer_len, feat_part)
     combine = jnp.sum(
         jnp.where(
             target[:, :, None] == slot_iota[None, None, :],

time: 88.9 us -> 105 us (1.18)
  waiting for transfers between devices: 31.2 us -> 38.7 us
  matrix products: 16.5 us -> 22.5 us
  other arithmetic: 7.52 us -> 10.4 us
    ppermute x14, waiting for transfers between devices: 29 us -> 36.1 us  [exchange(): pieces.append(lax.ppermute(chunks[step], 'el', perm=pairs))]
    dot_general x8, matrix products: 4.67 us -> 9.64 us  [half_product(): return jnp.dot(x, weight, preferred_element_type=jnp.float32)]
    dot_general x4, matrix products: 2.51 us -> 4.39 us  [down_product(): jnp.dot(hidden, weight, preferred_element_type=jnp.float32)]
    unnamed x36 -> x52, local copies, waits for them, and re-layouts: 3.93 us -> 2.64 us
    convert_element_type x2, other arithmetic: 0.4 us -> 1.5 us  [expert_block(): (kept.astype(jnp.float32) + sent.astype(jnp.float32)).astype(jnp.bfloat16)]
    slice x1 -> x3, local copies, waits for them, and re-layouts: 0.1 us -> 1.19 us  [the longest x1 1.09 us: shards(): flat_rows[group_rows:]]
  transfers between devices with their start and end apart: 23 -> 23, of which waited for: 13 -> 15; matrix products, arithmetic and copies ran while one was open for 14% -> 14% of each run, Pallas kernels for 0% -> 0%
where the time goes in v8:
time: 105 us
  waiting for transfers between devices  38.7 us (37%)
  starting transfers between devices  23.8 us (23%)
  matrix products  22.5 us (21%)
  other arithmetic  10.4 us (10%)
  local copies, waits for them, and re-layouts  8.77 us (8%)
    ppermute x14, waiting for transfers between devices, exchange(): pieces.append(lax.ppermute(chunks[step], 'el', perm=pairs))  36.1 us
    ppermute x14, starting transfers between devices, exchange(): pieces.append(lax.ppermute(chunks[step], 'el', perm=pairs))  21 us
    dot_general x8, matrix products, half_product(): return jnp.dot(x, weight, preferred_element_type=jnp.float32)  9.64 us
    dot_general x4, matrix products, down_product(): jnp.dot(hidden, weight, preferred_element_type=jnp.float32)  4.39 us
    dot_general x2, matrix products, one_group(): jnp.einsum('rgd,ld->rgl', head_rows, head_keys, preferred_element_type=jn...  3.85 us
    gather x1, local copies, waits for them, and re-layouts, one_group(): page_row_block = group_pages[local_table.reshape(-1)]  3.33 us
    unnamed x52, local copies, waits for them, and re-layouts  2.64 us
    dot_general x2, matrix products, one_group(): jnp.einsum('rgl,ld->rgd', soft.astype(jnp.bfloat16), head_values, preferr...  2.19 us
  transfers between devices with their start and end apart: 23, of which 15 were waited for; matrix products, arithmetic and copies ran while one was open for 14% of the time, Pallas kernels for 0%

profile of v8, /device:TPU:0, one launch (start us, length us, event | category | flops | bytes accessed | tf_op | source)
XLA Modules:
  0.0 104.6 jit_solution(16676217654888985547)
XLA Ops:
  4.2 3.3 %gather_fusion = bf16[96,16,512]{2,1,0:T(8,128)(2,1)} fusion(bf16[96,16,512]{2,1,0:T(8,128)(2,1)} %bitcast.188, s32[1024]{0:T(1024)S(1)} %pad_clamp_fusion), kind=kCustom, calls=%fused_computation | custom fusion | bytes 3146112 | tf_op jit(solution)/shard_map/while/body/eval_jaxpr/gather | solution.py:173
  8.5 1.9 %fusion.3 = (f32[128,6]{0,1:T(8,128)S(1)}, f32[1536,128,6]{1,0,2:T(8,128)S(1)}) fusion(pred[128,1536]{0,1:T(8,128)(4,1)S(1)} %compare_and_fusion, bf16[128,6,128]{0,2,1:T(8,128)(2,1)S(1)} %bitcast.190, bf16[1536,512]{1,0:T(8,128)(2,1)} %bitcast.183), kind=kOutput, calls=%fused_computation.8 | convolution fusion | flops 305528064 | bytes 5508096 | tf_op jit(solution)/shard_map/while/body/eval_jaxpr/rgd,ld->rgl/dot_general | solution.py:198
  10.4 1.9 %fusion.6 = (bf16[128,6]{0,1:T(8,128)(2,1)S(1)}, f32[128,6]{0,1:T(8,128)S(1)}, f32[1536,128,6]{1,0,2:T(8,128)S(1)}) fusion(f32[1536,128,6]{1,0,2:T(8,128)S(1)} %get-tuple-element.63, f32[128,6]{0,1:T(8,128)S(1)} %get-tuple-element.62, pred[128,1536]{0,1:T(8,128)(4,1)S(1)} %compare_and_fusion, bf16[128,6,128]{0,2,1:T(8,128)(2,1)S(1)} %bitcast.191, ...), kind=kOutput, calls=%fused_computation.11 | convolution fusion | flops 310245888 | bytes 10232320 | tf_op jit(solution)/shard_map/while/body/eval_jaxpr/rgd,ld->rgl/dot_general | solution.py:198
  23.7 2.8 %collective-permute-start.4 = (bf16[128,768]{1,0:T(8,128)(2,1)S(1)}, bf16[128,768]{1,0:T(8,128)(2,1)S(1)}, u32[]{:S(2)}, u32[]{:S(2)}) collective-permute-start(bf16[128,768]{1,0:T(8,128)(2,1)S(1)} %get-tuple-element.49), channel_id=1, source_target_pairs={{0,2},{2,0},{4,6},{6,4},{8,10},{10,8},{12,14},{14,12},{1,3},{3,1},... | collective-permute-start | bytes 589832 | tf_op jit(solution)/shard_map/ppermute | solution.py:52
  26.5 1.5 %collective-permute-start.5 = (bf16[128,768]{1,0:T(8,128)(2,1)S(1)}, bf16[128,768]{1,0:T(8,128)(2,1)S(1)}, u32[]{:S(2)}, u32[]{:S(2)}) collective-permute-start(bf16[128,768]{1,0:T(8,128)(2,1)S(1)} %get-tuple-element.48), channel_id=1, source_target_pairs={{0,4},{2,6},{4,0},{6,2},{8,12},{10,14},{12,8},{14,10},{1,5},{3,7},... | collective-permute-start | bytes 589832 | tf_op jit(solution)/shard_map/ppermute | solution.py:52
  28.0 2.0 %collective-permute-start.7 = (bf16[128,768]{1,0:T(8,128)(2,1)S(1)}, bf16[128,768]{1,0:T(8,128)(2,1)S(1)}, u32[]{:S(2)}, u32[]{:S(2)}) collective-permute-start(bf16[128,768]{1,0:T(8,128)(2,1)S(1)} %get-tuple-element.46), channel_id=1, source_target_pairs={{0,8},{2,10},{4,12},{6,14},{8,0},{10,2},{12,4},{14,6},{1,9},{3,11}... | collective-permute-start | bytes 589832 | tf_op jit(solution)/shard_map/ppermute | solution.py:52
  32.1 3.1 %collective-permute-start.9 = (bf16[128,768]{1,0:T(8,128)(2,1)S(1)}, bf16[128,768]{1,0:T(8,128)(2,1)S(1)}, u32[]{:S(2)}, u32[]{:S(2)}) collective-permute-start(bf16[128,768]{1,0:T(8,128)(2,1)S(1)} %get-tuple-element.44), channel_id=1, source_target_pairs={{0,12},{2,14},{4,8},{6,10},{8,4},{10,6},{12,0},{14,2},{1,13},{3,15... | collective-permute-start | bytes 589832 | tf_op jit(solution)/shard_map/ppermute | solution.py:52
  37.1 3.4 %collective-permute-done.6 = bf16[128,768]{1,0:T(8,128)(2,1)S(1)} collective-permute-done((bf16[128,768]{1,0:T(8,128)(2,1)S(1)}, bf16[128,768]{1,0:T(8,128)(2,1)S(1)}, u32[]{:S(2)}, u32[]{:S(2)}) %collective-permute-start.6) | collective-permute-done | bytes 196640 | tf_op jit(solution)/shard_map/ppermute | solution.py:52
  41.5 4.2 %collective-permute-done.9 = bf16[128,768]{1,0:T(8,128)(2,1)S(1)} collective-permute-done((bf16[128,768]{1,0:T(8,128)(2,1)S(1)}, bf16[128,768]{1,0:T(8,128)(2,1)S(1)}, u32[]{:S(2)}, u32[]{:S(2)}) %collective-permute-start.9) | collective-permute-done | bytes 196640 | tf_op jit(solution)/shard_map/ppermute | solution.py:52
  45.7 3.5 %collective-permute-done.10 = bf16[128,768]{1,0:T(8,128)(2,1)S(1)} collective-permute-done((bf16[128,768]{1,0:T(8,128)(2,1)S(1)}, bf16[128,768]{1,0:T(8,128)(2,1)S(1)}, u32[]{:S(2)}, u32[]{:S(2)}) %collective-permute-start.10) | collective-permute-done | bytes 196640 | tf_op jit(solution)/shard_map/ppermute | solution.py:52
  50.7 2.0 %fusion.52 = f32[512,384]{1,0:T(8,128)S(1)} fusion(bf16[2,768,384]{2,1,0:T(8,128)(2,1)} %bitcast.179, s32[]{:T(128)S(6)} %select_n.115, bf16[1024,768]{1,0:T(8,128)(2,1)} %bitcast.173), kind=kOutput, calls=%fused_computation.64 | convolution fusion | flops 301989888 | bytes 2162692 | tf_op jit(solution)/shard_map/dot_general | solution.py:76
  52.8 1.7 %fusion.43 = f32[512,384]{1,0:T(8,128)S(1)} fusion(bf16[2,768,384]{2,1,0:T(8,128)(2,1)} %bitcast.175, s32[]{:T(128)S(6)} %select_n.115, bf16[1024,768]{1,0:T(8,128)(2,1)S(1)} %bitcast.174), kind=kOutput, calls=%fused_computation.57 | convolution fusion | flops 301989888 | bytes 2162692 | tf_op jit(solution)/shard_map/dot_general | solution.py:76
  54.5 1.8 %fusion.18 = f32[512,384]{1,0:T(8,128)S(1)} fusion(f32[512,384]{1,0:T(8,128)S(1)} %fusion.52, bf16[512,768]{1,0:T(8,128)(2,1)} %collective-permute-done.11, bf16[2,768,384]{2,1,0:T(8,128)(2,1)S(1)} %bitcast.180, s32[]{:T(128)S(6)} %select_n.122), kind=kOutput, calls=%fused_computation.33 | convolution fusion | flops 302383104 | bytes 2949124 | tf_op jit(solution)/shard_map/dot_general | solution.py:76
  56.4 1.8 %fusion.19 = bf16[512,384]{1,0:T(8,128)(2,1)S(1)} fusion(f32[512,384]{1,0:T(8,128)S(1)} %fusion.18, f32[512,384]{1,0:T(8,128)S(1)} %fusion.43, bf16[512,768]{1,0:T(8,128)(2,1)} %collective-permute-done.11, bf16[2,768,384]{2,1,0:T(8,128)(2,1)S(1)} %bitcast.176, s32[]{:T(128)S(6)} %select_n.122), kind=kOutput, calls=%fused_computation.34 | convolution fusion | flops 302579712 | bytes 3342340 | tf_op jit(solution)/shard_map/dot_general | solution.py:76
  60.2 1.8 %convolution_convert_fusion.4 = bf16[512,768]{1,0:T(8,128)(2,1)S(1)} fusion(bf16[512,384]{1,0:T(8,128)(2,1)} %copy-done.9, bf16[1,384,1536]{2,1,0:T(8,128)(2,1)} %param.26, s32[]{:T(128)S(6)} %select_n.123), kind=kOutput, calls=%fused_computation.29 | convolution fusion | flops 302383104 | bytes 1769476 | tf_op jit(solution)/shard_map/dot_general | solution.py:84
  70.5 1.6 %collective-permute-start.15 = (bf16[128,768]{1,0:T(8,128)(2,1)S(1)}, bf16[128,768]{1,0:T(8,128)(2,1)S(1)}, u32[]{:S(2)}, u32[]{:S(2)}) collective-permute-start(bf16[128,768]{1,0:T(8,128)(2,1)S(1)} %get-tuple-element.54), channel_id=1, source_target_pairs={{0,6},{2,4},{4,2},{6,0},{8,14},{10,12},{12,10},{14,8},{1,7},{3,5},... | collective-permute-start | bytes 589832 | tf_op jit(solution)/shard_map/ppermute | solution.py:52
  72.1 8.9 %collective-permute-done.14 = bf16[128,768]{1,0:T(8,128)(2,1)S(1)} collective-permute-done((bf16[128,768]{1,0:T(8,128)(2,1)S(1)}, bf16[128,768]{1,0:T(8,128)(2,1)S(1)}, u32[]{:S(2)}, u32[]{:S(2)}) %collective-permute-start.14) | collective-permute-done | bytes 196640 | tf_op jit(solution)/shard_map/ppermute | solution.py:52
  81.9 1.6 %collective-permute-start.18 = (bf16[128,768]{1,0:T(8,128)(2,1)S(1)}, bf16[128,768]{1,0:T(8,128)(2,1)S(1)}, u32[]{:S(2)}, u32[]{:S(2)}) collective-permute-start(bf16[128,768]{1,0:T(8,128)(2,1)S(1)} %get-tuple-element.53), channel_id=1, source_target_pairs={{0,8},{2,10},{4,12},{6,14},{8,0},{10,2},{12,4},{14,6},{1,9},{3,11}... | collective-permute-start | bytes 589832 | tf_op jit(solution)/shard_map/ppermute | solution.py:52
  84.6 1.5 %collective-permute-start.20 = (bf16[128,768]{1,0:T(8,128)(2,1)S(1)}, bf16[128,768]{1,0:T(8,128)(2,1)S(1)}, u32[]{:S(2)}, u32[]{:S(2)}) collective-permute-start(bf16[128,768]{1,0:T(8,128)(2,1)S(1)} %get-tuple-element.51), channel_id=1, source_target_pairs={{0,12},{2,14},{4,8},{6,10},{8,4},{10,6},{12,0},{14,2},{1,13},{3,15... | collective-permute-start | bytes 589832 | tf_op jit(solution)/shard_map/ppermute | solution.py:52
  86.1 1.7 %collective-permute-start.21 = (bf16[128,768]{1,0:T(8,128)(2,1)S(1)}, bf16[128,768]{1,0:T(8,128)(2,1)S(1)}, u32[]{:S(2)}, u32[]{:S(2)}) collective-permute-start(bf16[128,768]{1,0:T(8,128)(2,1)S(1)} %get-tuple-element.50), channel_id=1, source_target_pairs={{0,14},{2,12},{4,10},{6,8},{8,6},{10,4},{12,2},{14,0},{1,15},{3,13... | collective-permute-start | bytes 589832 | tf_op jit(solution)/shard_map/ppermute | solution.py:52
  87.9 1.9 %collective-permute-done.18 = bf16[128,768]{1,0:T(8,128)(2,1)S(1)} collective-permute-done((bf16[128,768]{1,0:T(8,128)(2,1)S(1)}, bf16[128,768]{1,0:T(8,128)(2,1)S(1)}, u32[]{:S(2)}, u32[]{:S(2)}) %collective-permute-start.18) | collective-permute-done | bytes 196640 | tf_op jit(solution)/shard_map/ppermute | solution.py:52
  89.8 4.7 %collective-permute-done.19 = bf16[128,768]{1,0:T(8,128)(2,1)S(1)} collective-permute-done((bf16[128,768]{1,0:T(8,128)(2,1)S(1)}, bf16[128,768]{1,0:T(8,128)(2,1)S(1)}, u32[]{:S(2)}, u32[]{:S(2)}) %collective-permute-start.19) | collective-permute-done | bytes 196640 | tf_op jit(solution)/shard_map/ppermute | solution.py:52
  94.5 3.8 %collective-permute-done.20 = bf16[128,768]{1,0:T(8,128)(2,1)S(1)} collective-permute-done((bf16[128,768]{1,0:T(8,128)(2,1)S(1)}, bf16[128,768]{1,0:T(8,128)(2,1)S(1)}, u32[]{:S(2)}, u32[]{:S(2)}) %collective-permute-start.20) | collective-permute-done | bytes 196640 | tf_op jit(solution)/shard_map/ppermute | solution.py:52
  98.3 3.4 %collective-permute-done.21 = bf16[128,768]{1,0:T(8,128)(2,1)S(1)} collective-permute-done((bf16[128,768]{1,0:T(8,128)(2,1)S(1)}, bf16[128,768]{1,0:T(8,128)(2,1)S(1)}, u32[]{:S(2)}, u32[]{:S(2)}) %collective-permute-start.21) | collective-permute-done | bytes 196640 | tf_op jit(solution)/shard_map/ppermute | solution.py:52
  (133 shorter events, 38.1 us)
Async XLA Ops:
  0.0 21.1 %copy-start = (bf16[1536,768]{1,0:T(8,128)(2,1)S(1)}, bf16[1536,768]{1,0:T(8,128)(2,1)}, u32[]{:S(2)}) copy-start(bf16[1536,768]{1,0:T(8,128)(2,1)} %param.20) | copy-start | bytes 7077892
  13.9 5.3 %collective-permute-start.2 = (bf16[128,2,6]{0,2,1:T(8,128)(2,1)}, bf16[128,2,6]{0,2,1:T(8,128)(2,1)}, u32[]{:S(2)}, u32[]{:S(2)}) collective-permute-start(bf16[128,2,6]{0,2,1:T(8,128)(2,1)} %pad_maximum_fusion.2), channel_id=1, source_target_pairs={{0,1},{1,0},{2,3},{3,2},{4,5},{5,4},{6,7},{7,6},{8,9},{9,8},{10,11... | collective-permute-start | bytes 9224 | tf_op jit(solution)/shard_map/ppermute | solution.py:18
  15.0 4.2 %collective-permute-start = (bf16[128,2,6]{0,2,1:T(8,128)(2,1)}, bf16[128,2,6]{0,2,1:T(8,128)(2,1)}, u32[]{:S(2)}, u32[]{:S(2)}) collective-permute-start(bf16[128,2,6]{0,2,1:T(8,128)(2,1)} %pad_maximum_fusion.1), channel_id=1, source_target_pairs={{0,1},{1,0},{2,3},{3,2},{4,5},{5,4},{6,7},{7,6},{8,9},{9,8},{10,11... | collective-permute-start | bytes 9224 | tf_op jit(solution)/shard_map/ppermute | solution.py:18
  17.3 2.6 %collective-permute-start.1 = (bf16[128,2,6,128]{0,3,2,1:T(8,128)(2,1)S(1)}, bf16[128,2,6,128]{0,3,2,1:T(8,128)(2,1)}, u32[]{:S(2)}, u32[]{:S(2)}) collective-permute-start(bf16[128,2,6,128]{0,3,2,1:T(8,128)(2,1)S(1)} %pad_maximum_fusion), channel_id=1, source_target_pairs={{0,1},{1,0},{2,3},{3,2},{4,5},{5,4},{6,7},{7,6},{8,9},{9,8},{10,11... | collective-permute-start | bytes 1179656 | tf_op jit(solution)/shard_map/ppermute | solution.py:18
  21.8 1.2 %collective-permute-start.3 = (f32[128]{0:T(128)S(1)}, f32[128]{0:T(128)S(1)}, u32[]{:S(2)}, u32[]{:S(2)}) collective-permute-start(f32[128]{0:T(128)S(1)} %get-tuple-element.65), channel_id=1, source_target_pairs={{0,1},{1,0},{2,3},{3,2},{4,5},{5,4},{6,7},{7,6},{8,9},{9,8},{10,11... | collective-permute-start | bytes 1544 | tf_op jit(solution)/shard_map/ppermute | solution.py:94
  23.7 8.4 %collective-permute-start.4 = (bf16[128,768]{1,0:T(8,128)(2,1)S(1)}, bf16[128,768]{1,0:T(8,128)(2,1)S(1)}, u32[]{:S(2)}, u32[]{:S(2)}) collective-permute-start(bf16[128,768]{1,0:T(8,128)(2,1)S(1)} %get-tuple-element.49), channel_id=1, source_target_pairs={{0,2},{2,0},{4,6},{6,4},{8,10},{10,8},{12,14},{14,12},{1,3},{3,1},... | collective-permute-start | bytes 589832 | tf_op jit(solution)/shard_map/ppermute | solution.py:52
  26.5 9.4 %collective-permute-start.5 = (bf16[128,768]{1,0:T(8,128)(2,1)S(1)}, bf16[128,768]{1,0:T(8,128)(2,1)S(1)}, u32[]{:S(2)}, u32[]{:S(2)}) collective-permute-start(bf16[128,768]{1,0:T(8,128)(2,1)S(1)} %get-tuple-element.48), channel_id=1, source_target_pairs={{0,4},{2,6},{4,0},{6,2},{8,12},{10,14},{12,8},{14,10},{1,5},{3,7},... | collective-permute-start | bytes 589832 | tf_op jit(solution)/shard_map/ppermute | solution.py:52
  28.0 12.6 %collective-permute-start.6 = (bf16[128,768]{1,0:T(8,128)(2,1)S(1)}, bf16[128,768]{1,0:T(8,128)(2,1)S(1)}, u32[]{:S(2)}, u32[]{:S(2)}) collective-permute-start(bf16[128,768]{1,0:T(8,128)(2,1)S(1)} %get-tuple-element.47), channel_id=1, source_target_pairs={{0,6},{2,4},{4,2},{6,0},{8,14},{10,12},{12,10},{14,8},{1,7},{3,5},... | collective-permute-start | bytes 589832 | tf_op jit(solution)/shard_map/ppermute | solution.py:52
  28.0 12.6 %collective-permute-start.7 = (bf16[128,768]{1,0:T(8,128)(2,1)S(1)}, bf16[128,768]{1,0:T(8,128)(2,1)S(1)}, u32[]{:S(2)}, u32[]{:S(2)}) collective-permute-start(bf16[128,768]{1,0:T(8,128)(2,1)S(1)} %get-tuple-element.46), channel_id=1, source_target_pairs={{0,8},{2,10},{4,12},{6,14},{8,0},{10,2},{12,4},{14,6},{1,9},{3,11}... | collective-permute-start | bytes 589832 | tf_op jit(solution)/shard_map/ppermute | solution.py:52
  30.0 11.5 %collective-permute-start.8 = (bf16[128,768]{1,0:T(8,128)(2,1)S(1)}, bf16[128,768]{1,0:T(8,128)(2,1)S(1)}, u32[]{:S(2)}, u32[]{:S(2)}) collective-permute-start(bf16[128,768]{1,0:T(8,128)(2,1)S(1)} %get-tuple-element.45), channel_id=1, source_target_pairs={{0,10},{2,8},{4,14},{6,12},{8,2},{10,0},{12,6},{14,4},{1,11},{3,9}... | collective-permute-start | bytes 589832 | tf_op jit(solution)/shard_map/ppermute | solution.py:52
  32.1 13.6 %collective-permute-start.9 = (bf16[128,768]{1,0:T(8,128)(2,1)S(1)}, bf16[128,768]{1,0:T(8,128)(2,1)S(1)}, u32[]{:S(2)}, u32[]{:S(2)}) collective-permute-start(bf16[128,768]{1,0:T(8,128)(2,1)S(1)} %get-tuple-element.44), channel_id=1, source_target_pairs={{0,12},{2,14},{4,8},{6,10},{8,4},{10,6},{12,0},{14,2},{1,13},{3,15... | collective-permute-start | bytes 589832 | tf_op jit(solution)/shard_map/ppermute | solution.py:52
  35.9 13.4 %collective-permute-start.10 = (bf16[128,768]{1,0:T(8,128)(2,1)S(1)}, bf16[128,768]{1,0:T(8,128)(2,1)S(1)}, u32[]{:S(2)}, u32[]{:S(2)}) collective-permute-start(bf16[128,768]{1,0:T(8,128)(2,1)S(1)} %get-tuple-element.42), channel_id=1, source_target_pairs={{0,14},{2,12},{4,10},{6,8},{8,6},{10,4},{12,2},{14,0},{1,15},{3,13... | collective-permute-start | bytes 589832 | tf_op jit(solution)/shard_map/ppermute | solution.py:52
  50.7 3.8 %collective-permute-start.11 = (bf16[512,768]{1,0:T(8,128)(2,1)}, bf16[512,768]{1,0:T(8,128)(2,1)}, u32[]{:S(2)}, u32[]{:S(2)}) collective-permute-start(bf16[512,768]{1,0:T(8,128)(2,1)} %get-tuple-element.40), channel_id=1, source_target_pairs={{0,1},{1,0},{2,3},{3,2},{4,5},{5,4},{6,7},{7,6},{8,9},{9,8},{10,11... | collective-permute-start | bytes 2359304 | tf_op jit(solution)/shard_map/ppermute | solution.py:70
  59.7 2.8 %collective-permute-start.12 = (bf16[512,768]{1,0:T(8,128)(2,1)}, bf16[512,768]{1,0:T(8,128)(2,1)}, u32[]{:S(2)}, u32[]{:S(2)}) collective-permute-start(bf16[512,768]{1,0:T(8,128)(2,1)} %convolution_convert_fusion.3), channel_id=1, source_target_pairs={{0,1},{1,0},{2,3},{3,2},{4,5},{5,4},{6,7},{7,6},{8,9},{9,8},{10,11... | collective-permute-start | bytes 2359304 | tf_op jit(solution)/shard_map/ppermute | solution.py:86
  63.8 2.5 %collective-permute-start.16 = (bf16[512,768]{1,0:T(8,128)(2,1)S(1)}, bf16[512,768]{1,0:T(8,128)(2,1)S(1)}, u32[]{:S(2)}, u32[]{:S(2)}) collective-permute-start(bf16[512,768]{1,0:T(8,128)(2,1)S(1)} %get-tuple-element.26), channel_id=1, source_target_pairs={{0,1},{1,0},{2,3},{3,2},{4,5},{5,4},{6,7},{7,6},{8,9},{9,8},{10,11... | collective-permute-start | bytes 2359304 | tf_op jit(solution)/shard_map/ppermute | solution.py:70
  64.7 7.3 %collective-permute-start.13 = (bf16[128,768]{1,0:T(8,128)(2,1)S(1)}, bf16[128,768]{1,0:T(8,128)(2,1)S(1)}, u32[]{:S(2)}, u32[]{:S(2)}) collective-permute-start(bf16[128,768]{1,0:T(8,128)(2,1)S(1)} %get-tuple-element.56), channel_id=1, source_target_pairs={{0,2},{2,0},{4,6},{6,4},{8,10},{10,8},{12,14},{14,12},{1,3},{3,1},... | collective-permute-start | bytes 589832 | tf_op jit(solution)/shard_map/ppermute | solution.py:52
  69.3 12.3 %collective-permute-start.17 = (bf16[512,768]{1,0:T(8,128)(2,1)S(1)}, bf16[512,768]{1,0:T(8,128)(2,1)S(1)}, u32[]{:S(2)}, u32[]{:S(2)}) collective-permute-start(bf16[512,768]{1,0:T(8,128)(2,1)S(1)} %convolution_convert_fusion.1), channel_id=1, source_target_pairs={{0,1},{1,0},{2,3},{3,2},{4,5},{5,4},{6,7},{7,6},{8,9},{9,8},{10,11... | collective-permute-start | bytes 2359304 | tf_op jit(solution)/shard_map/ppermute | solution.py:86
  69.8 11.2 %collective-permute-start.14 = (bf16[128,768]{1,0:T(8,128)(2,1)S(1)}, bf16[128,768]{1,0:T(8,128)(2,1)S(1)}, u32[]{:S(2)}, u32[]{:S(2)}) collective-permute-start(bf16[128,768]{1,0:T(8,128)(2,1)S(1)} %get-tuple-element.55), channel_id=1, source_target_pairs={{0,4},{2,6},{4,0},{6,2},{8,12},{10,14},{12,8},{14,10},{1,5},{3,7},... | collective-permute-start | bytes 589832 | tf_op jit(solution)/shard_map/ppermute | solution.py:52
  70.5 13.0 %collective-permute-start.15 = (bf16[128,768]{1,0:T(8,128)(2,1)S(1)}, bf16[128,768]{1,0:T(8,128)(2,1)S(1)}, u32[]{:S(2)}, u32[]{:S(2)}) collective-permute-start(bf16[128,768]{1,0:T(8,128)(2,1)S(1)} %get-tuple-element.54), channel_id=1, source_target_pairs={{0,6},{2,4},{4,2},{6,0},{8,14},{10,12},{12,10},{14,8},{1,7},{3,5},... | collective-permute-start | bytes 589832 | tf_op jit(solution)/shard_map/ppermute | solution.py:52
  81.9 7.9 %collective-permute-start.18 = (bf16[128,768]{1,0:T(8,128)(2,1)S(1)}, bf16[128,768]{1,0:T(8,128)(2,1)S(1)}, u32[]{:S(2)}, u32[]{:S(2)}) collective-permute-start(bf16[128,768]{1,0:T(8,128)(2,1)S(1)} %get-tuple-element.53), channel_id=1, source_target_pairs={{0,8},{2,10},{4,12},{6,14},{8,0},{10,2},{12,4},{14,6},{1,9},{3,11}... | collective-permute-start | bytes 589832 | tf_op jit(solution)/shard_map/ppermute | solution.py:52
  83.5 11.0 %collective-permute-start.19 = (bf16[128,768]{1,0:T(8,128)(2,1)S(1)}, bf16[128,768]{1,0:T(8,128)(2,1)S(1)}, u32[]{:S(2)}, u32[]{:S(2)}) collective-permute-start(bf16[128,768]{1,0:T(8,128)(2,1)S(1)} %get-tuple-element.52), channel_id=1, source_target_pairs={{0,10},{2,8},{4,14},{6,12},{8,2},{10,0},{12,6},{14,4},{1,11},{3,9}... | collective-permute-start | bytes 589832 | tf_op jit(solution)/shard_map/ppermute | solution.py:52
  84.6 13.7 %collective-permute-start.20 = (bf16[128,768]{1,0:T(8,128)(2,1)S(1)}, bf16[128,768]{1,0:T(8,128)(2,1)S(1)}, u32[]{:S(2)}, u32[]{:S(2)}) collective-permute-start(bf16[128,768]{1,0:T(8,128)(2,1)S(1)} %get-tuple-element.51), channel_id=1, source_target_pairs={{0,12},{2,14},{4,8},{6,10},{8,4},{10,6},{12,0},{14,2},{1,13},{3,15... | collective-permute-start | bytes 589832 | tf_op jit(solution)/shard_map/ppermute | solution.py:52
  86.1 15.6 %collective-permute-start.21 = (bf16[128,768]{1,0:T(8,128)(2,1)S(1)}, bf16[128,768]{1,0:T(8,128)(2,1)S(1)}, u32[]{:S(2)}, u32[]{:S(2)}) collective-permute-start(bf16[128,768]{1,0:T(8,128)(2,1)S(1)} %get-tuple-element.50), channel_id=1, source_target_pairs={{0,14},{2,12},{4,10},{6,8},{8,6},{10,4},{12,2},{14,0},{1,15},{3,13... | collective-permute-start | bytes 589832 | tf_op jit(solution)/shard_map/ppermute | solution.py:52
  102.7 1.2 %collective-permute-start.22 = (f32[128]{0:T(128)S(1)}, f32[128]{0:T(128)S(1)}, u32[]{:S(2)}, u32[]{:S(2)}) collective-permute-start(f32[128]{0:T(128)S(1)} %get-tuple-element.67), channel_id=1, source_target_pairs={{0,1},{1,0},{2,3},{3,2},{4,5},{5,4},{6,7},{7,6},{8,9},{9,8},{10,11... | collective-permute-start | bytes 1544 | tf_op jit(solution)/shard_map/ppermute | solution.py:94
  (16 other events, 35.0 us)

commit v9 on v7

--- a/solution.py
+++ b/solution.py
@@ -155,7 +155,10 @@
     def one_group(local):
         query_count = lax.dynamic_index_in_dim(query_lens, local, 0, keepdims=False)
         past_count = lax.dynamic_index_in_dim(past_lens, local, 0, keepdims=False)
-        row_ends = jnp.cumsum(query_count)
+        req_iota = jnp.arange(req_count, dtype=jnp.int32)
+        row_ends = jnp.sum(
+            jnp.where(req_iota[None, :] <= req_iota[:, None], query_count[None, :], 0), axis=1
+        )
         row_starts = row_ends - query_count
         row_iota = jnp.arange(group_rows, dtype=jnp.int32)
         row_req = jnp.sum((row_iota[:, None] >= row_ends[None, :]).astype(jnp.int32), axis=1)
@@ -163,9 +166,9 @@
             jnp.int32
         )
         row_pos = row_iota + jnp.sum(req_onehot * (past_count - row_starts)[None, :], axis=1)
-        local_table = lax.dynamic_index_in_dim(
-            page_table.reshape(req_count, per_device, tp_count), tp_index, axis=2, keepdims=False
-        )
+        local_table = page_table[:, 0::tp_count]
+        for other in range(1, tp_count):
+            local_table = jnp.where(tp_index == other, page_table[:, other::tp_count], local_table)
         group_pages = lax.dynamic_index_in_dim(kv_cache, local, 0, keepdims=False)[0]
         page_row_block = group_pages[local_table.reshape(-1)]
         key_count_total = page_row_block.shape[0] * PAGE_POSITIONS

time: 88.9 us -> 89.6 us (level)
    slice x0 -> x2, local copies, waits for them, and re-layouts: none -> 1.72 us  [the longest x1 0.93 us: one_group(): page_table[:, other::tp_count]]
    unnamed x36 -> x35, local copies, waits for them, and re-layouts: 3.93 us -> 2.6 us
where the time goes in v9:
time: 89.6 us; the launch traced here: 89.2 us
  waiting for transfers between devices  31.2 us (35%)
  starting transfers between devices  24.2 us (27%)
  matrix products  16.5 us (18%)
  local copies, waits for them, and re-layouts  9.36 us (10%)
  other arithmetic  7.44 us (8%)
    ppermute x14, waiting for transfers between devices, exchange(): pieces.append(lax.ppermute(chunks[step], 'el', perm=pairs))  28.9 us
    ppermute x14, starting transfers between devices, exchange(): pieces.append(lax.ppermute(chunks[step], 'el', perm=pairs))  21.4 us
    dot_general x8, matrix products, half_product(): return jnp.dot(x, weight, preferred_element_type=jnp.float32)  4.65 us
    dot_general x2, matrix products, one_group(): jnp.einsum('rgd,ld->rgl', head_rows, head_keys, preferred_element_type=jn...  3.84 us
    gather x1, local copies, waits for them, and re-layouts, one_group(): page_row_block = group_pages[local_table.reshape(-1)]  3.32 us
    unnamed x35, local copies, waits for them, and re-layouts  2.6 us
    dot_general x4, matrix products, down_product(): jnp.dot(hidden, weight, preferred_element_type=jnp.float32)  2.51 us
    dot_general x2, matrix products, one_group(): jnp.einsum('rgl,ld->rgd', soft.astype(jnp.bfloat16), head_values, preferr...  2.19 us
  transfers between devices with their start and end apart: 23, of which 13 were waited for; matrix products, arithmetic and copies ran while one was open for 14% of the time, Pallas kernels for 0%

profile of v9, /device:TPU:0, one launch (start us, length us, event | category | flops | bytes accessed | tf_op | source)
XLA Modules:
  0.0 89.2 jit_solution(17850957842944134743)
XLA Ops:
  4.9 3.3 %gather_fusion = bf16[96,16,512]{2,1,0:T(8,128)(2,1)} fusion(bf16[96,16,512]{2,1,0:T(8,128)(2,1)} %bitcast.185, s32[1024]{0:T(1024)S(1)} %pad_clamp_fusion), kind=kCustom, calls=%fused_computation | custom fusion | bytes 3146112 | tf_op jit(solution)/shard_map/while/body/eval_jaxpr/gather | solution.py:173
  9.2 1.9 %fusion.3 = (f32[128,6]{0,1:T(8,128)S(1)}, f32[1536,128,6]{1,0,2:T(8,128)S(1)}) fusion(pred[128,1536]{0,1:T(8,128)(4,1)S(1)} %compare_and_fusion, bf16[128,6,128]{0,2,1:T(8,128)(2,1)S(1)} %bitcast.187, bf16[1536,512]{1,0:T(8,128)(2,1)} %bitcast.180), kind=kOutput, calls=%fused_computation.8 | convolution fusion | flops 305528064 | bytes 5508096 | tf_op jit(solution)/shard_map/while/body/eval_jaxpr/rgd,ld->rgl/dot_general | solution.py:198
  11.1 1.9 %fusion.6 = (bf16[128,6]{0,1:T(8,128)(2,1)S(1)}, f32[128,6]{0,1:T(8,128)S(1)}, f32[1536,128,6]{1,0,2:T(8,128)S(1)}) fusion(f32[1536,128,6]{1,0,2:T(8,128)S(1)} %get-tuple-element.59, f32[128,6]{0,1:T(8,128)S(1)} %get-tuple-element.58, pred[128,1536]{0,1:T(8,128)(4,1)S(1)} %compare_and_fusion, bf16[128,6,128]{0,2,1:T(8,128)(2,1)S(1)} %bitcast.188, ...), kind=kOutput, calls=%fused_computation.11 | convolution fusion | flops 310245888 | bytes 10232320 | tf_op jit(solution)/shard_map/while/body/eval_jaxpr/rgd,ld->rgl/dot_general | solution.py:198
  14.7 1.1 %fusion.29 = bf16[128,1,6,128]{0,3,2,1:T(8,128)(2,1)S(1)} fusion(f32[1536,128,6]{1,0,2:T(8,128)S(1)} %get-tuple-element.60, f32[128,6]{0,1:T(8,128)S(1)} %get-tuple-element.24, pred[128,1536]{0,1:T(8,128)(4,1)S(1)} %compare_and_fusion, bf16[1536,512]{1,0:T(8,128)(2,1)S(1)} %bitcast.182), kind=kOutput, calls=%fused_computation.44 | convolution fusion | flops 306806784 | bytes 5509120 | tf_op jit(solution)/shard_map/while/body/eval_jaxpr/rgl,ld->rgd/dot_general | solution.py:204
  15.8 1.1 %fusion.32 = bf16[128,1,6,128]{0,3,2,1:T(8,128)(2,1)S(1)} fusion(f32[1536,128,6]{1,0,2:T(8,128)S(1)} %get-tuple-element.59, f32[128,6]{0,1:T(8,128)S(1)} %get-tuple-element.58, pred[128,1536]{0,1:T(8,128)(4,1)S(1)} %compare_and_fusion, bf16[1536,512]{1,0:T(8,128)(2,1)S(1)} %bitcast.183), kind=kOutput, calls=%fused_computation.45 | convolution fusion | flops 306806784 | bytes 5509120 | tf_op jit(solution)/shard_map/while/body/eval_jaxpr/rgl,ld->rgd/dot_general | solution.py:204
  19.8 1.2 %divide_convert_fusion = bf16[128,2,6,128]{0,3,2,1:T(8,128)(2,1)S(1)} fusion(bf16[128,2,6,128]{0,3,2,1:T(8,128)(2,1)} %collective-permute-done.1, f32[128,2,6]{0,2,1:T(8,128)S(1)} %get-tuple-element.56, f32[128,2,6]{0,2,1:T(8,128)S(1)} %get-tuple-element.57, f32[128,2,6]{0,2,1:T(8,128)S(1)} %get-tuple-element.55, bf16[128,1,6,128]{0,3,2,1:T(8,128)(2,1)S(1)} %fusion.29, ...), kind=kLoop, calls=%fused_computation.50 | loop fusion | flops 1572864 | bytes 1198080 | tf_op jit(solution)/shard_map/convert_element_type | solution.py:224
  21.0 1.5 %multiply_reduce_fusion.1 = (f32[128]{0:T(128)S(1)}, f32[128,768]{1,0:T(8,128)S(1)}) fusion(bf16[128,1536]{0,1:T(8,128)(2,1)S(1)} %bitcast.186, bf16[1536,768]{1,0:T(8,128)(2,1)S(1)} %copy-done, bf16[128,768]{1,0:T(8,128)(2,1)} %param.14), kind=kOutput, calls=%fused_computation.90 | convolution fusion | flops 302382976 | bytes 3342848 | tf_op jit(solution)/shard_map/dot_general | solution.py:226
  24.6 2.9 %collective-permute-start.4 = (bf16[128,768]{1,0:T(8,128)(2,1)S(1)}, bf16[128,768]{1,0:T(8,128)(2,1)S(1)}, u32[]{:S(2)}, u32[]{:S(2)}) collective-permute-start(bf16[128,768]{1,0:T(8,128)(2,1)S(1)} %get-tuple-element.45), channel_id=1, source_target_pairs={{0,2},{2,0},{4,6},{6,4},{8,10},{10,8},{12,14},{14,12},{1,3},{3,1},... | collective-permute-start | bytes 589832 | tf_op jit(solution)/shard_map/ppermute | solution.py:52
  27.4 1.5 %collective-permute-start.5 = (bf16[128,768]{1,0:T(8,128)(2,1)S(1)}, bf16[128,768]{1,0:T(8,128)(2,1)S(1)}, u32[]{:S(2)}, u32[]{:S(2)}) collective-permute-start(bf16[128,768]{1,0:T(8,128)(2,1)S(1)} %get-tuple-element.44), channel_id=1, source_target_pairs={{0,4},{2,6},{4,0},{6,2},{8,12},{10,14},{12,8},{14,10},{1,5},{3,7},... | collective-permute-start | bytes 589832 | tf_op jit(solution)/shard_map/ppermute | solution.py:52
  29.0 2.0 %collective-permute-start.7 = (bf16[128,768]{1,0:T(8,128)(2,1)S(1)}, bf16[128,768]{1,0:T(8,128)(2,1)S(1)}, u32[]{:S(2)}, u32[]{:S(2)}) collective-permute-start(bf16[128,768]{1,0:T(8,128)(2,1)S(1)} %get-tuple-element.40), channel_id=1, source_target_pairs={{0,8},{2,10},{4,12},{6,14},{8,0},{10,2},{12,4},{14,6},{1,9},{3,11}... | collective-permute-start | bytes 589832 | tf_op jit(solution)/shard_map/ppermute | solution.py:52
  31.0 1.4 %collective-permute-start.8 = (bf16[128,768]{1,0:T(8,128)(2,1)S(1)}, bf16[128,768]{1,0:T(8,128)(2,1)S(1)}, u32[]{:S(2)}, u32[]{:S(2)}) collective-permute-start(bf16[128,768]{1,0:T(8,128)(2,1)S(1)} %get-tuple-element.29), channel_id=1, source_target_pairs={{0,10},{2,8},{4,14},{6,12},{8,2},{10,0},{12,6},{14,4},{1,11},{3,9}... | collective-permute-start | bytes 589832 | tf_op jit(solution)/shard_map/ppermute | solution.py:52
  33.1 3.1 %collective-permute-start.9 = (bf16[128,768]{1,0:T(8,128)(2,1)S(1)}, bf16[128,768]{1,0:T(8,128)(2,1)S(1)}, u32[]{:S(2)}, u32[]{:S(2)}) collective-permute-start(bf16[128,768]{1,0:T(8,128)(2,1)S(1)} %get-tuple-element.28), channel_id=1, source_target_pairs={{0,12},{2,14},{4,8},{6,10},{8,4},{10,6},{12,0},{14,2},{1,13},{3,15... | collective-permute-start | bytes 589832 | tf_op jit(solution)/shard_map/ppermute | solution.py:52
  36.7 1.3 %collective-permute-start.10 = (bf16[128,768]{1,0:T(8,128)(2,1)S(1)}, bf16[128,768]{1,0:T(8,128)(2,1)S(1)}, u32[]{:S(2)}, u32[]{:S(2)}) collective-permute-start(bf16[128,768]{1,0:T(8,128)(2,1)S(1)} %get-tuple-element.27), channel_id=1, source_target_pairs={{0,14},{2,12},{4,10},{6,8},{8,6},{10,4},{12,2},{14,0},{1,15},{3,13... | collective-permute-start | bytes 589832 | tf_op jit(solution)/shard_map/ppermute | solution.py:52
  38.0 3.4 %collective-permute-done.6 = bf16[128,768]{1,0:T(8,128)(2,1)S(1)} collective-permute-done((bf16[128,768]{1,0:T(8,128)(2,1)S(1)}, bf16[128,768]{1,0:T(8,128)(2,1)S(1)}, u32[]{:S(2)}, u32[]{:S(2)}) %collective-permute-start.6) | collective-permute-done | bytes 196640 | tf_op jit(solution)/shard_map/ppermute | solution.py:52
  42.4 4.2 %collective-permute-done.9 = bf16[128,768]{1,0:T(8,128)(2,1)S(1)} collective-permute-done((bf16[128,768]{1,0:T(8,128)(2,1)S(1)}, bf16[128,768]{1,0:T(8,128)(2,1)S(1)}, u32[]{:S(2)}, u32[]{:S(2)}) %collective-permute-start.9) | collective-permute-done | bytes 196640 | tf_op jit(solution)/shard_map/ppermute | solution.py:52
  46.7 3.4 %collective-permute-done.10 = bf16[128,768]{1,0:T(8,128)(2,1)S(1)} collective-permute-done((bf16[128,768]{1,0:T(8,128)(2,1)S(1)}, bf16[128,768]{1,0:T(8,128)(2,1)S(1)}, u32[]{:S(2)}, u32[]{:S(2)}) %collective-permute-start.10) | collective-permute-done | bytes 196640 | tf_op jit(solution)/shard_map/ppermute | solution.py:52
  60.9 1.6 %collective-permute-start.18 = (bf16[128,768]{1,0:T(8,128)(2,1)S(1)}, bf16[128,768]{1,0:T(8,128)(2,1)S(1)}, u32[]{:S(2)}, u32[]{:S(2)}) collective-permute-start(bf16[128,768]{1,0:T(8,128)(2,1)S(1)} %get-tuple-element.49), channel_id=1, source_target_pairs={{0,8},{2,10},{4,12},{6,14},{8,0},{10,2},{12,4},{14,6},{1,9},{3,11}... | collective-permute-start | bytes 589832 | tf_op jit(solution)/shard_map/ppermute | solution.py:52
  64.0 2.4 %collective-permute-start.15 = (bf16[128,768]{1,0:T(8,128)(2,1)S(1)}, bf16[128,768]{1,0:T(8,128)(2,1)S(1)}, u32[]{:S(2)}, u32[]{:S(2)}) collective-permute-start(bf16[128,768]{1,0:T(8,128)(2,1)S(1)} %get-tuple-element.50), channel_id=1, source_target_pairs={{0,6},{2,4},{4,2},{6,0},{8,14},{10,12},{12,10},{14,8},{1,7},{3,5},... | collective-permute-start | bytes 589832 | tf_op jit(solution)/shard_map/ppermute | solution.py:52
  67.4 7.5 %collective-permute-done.13 = bf16[128,768]{1,0:T(8,128)(2,1)S(1)} collective-permute-done((bf16[128,768]{1,0:T(8,128)(2,1)S(1)}, bf16[128,768]{1,0:T(8,128)(2,1)S(1)}, u32[]{:S(2)}, u32[]{:S(2)}) %collective-permute-start.13) | collective-permute-done | bytes 196640 | tf_op jit(solution)/shard_map/ppermute | solution.py:52
  75.8 2.1 %collective-permute-start.21 = (bf16[128,768]{1,0:T(8,128)(2,1)S(1)}, bf16[128,768]{1,0:T(8,128)(2,1)S(1)}, u32[]{:S(2)}, u32[]{:S(2)}) collective-permute-start(bf16[128,768]{1,0:T(8,128)(2,1)S(1)} %get-tuple-element.46), channel_id=1, source_target_pairs={{0,14},{2,12},{4,10},{6,8},{8,6},{10,4},{12,2},{14,0},{1,15},{3,13... | collective-permute-start | bytes 589832 | tf_op jit(solution)/shard_map/ppermute | solution.py:52
  77.9 2.1 %collective-permute-done.15 = bf16[128,768]{1,0:T(8,128)(2,1)S(1)} collective-permute-done((bf16[128,768]{1,0:T(8,128)(2,1)S(1)}, bf16[128,768]{1,0:T(8,128)(2,1)S(1)}, u32[]{:S(2)}, u32[]{:S(2)}) %collective-permute-start.15) | collective-permute-done | bytes 196640 | tf_op jit(solution)/shard_map/ppermute | solution.py:52
  80.1 4.3 %collective-permute-done.20 = bf16[128,768]{1,0:T(8,128)(2,1)S(1)} collective-permute-done((bf16[128,768]{1,0:T(8,128)(2,1)S(1)}, bf16[128,768]{1,0:T(8,128)(2,1)S(1)}, u32[]{:S(2)}, u32[]{:S(2)}) %collective-permute-start.20) | collective-permute-done | bytes 196640 | tf_op jit(solution)/shard_map/ppermute | solution.py:52
  84.4 1.9 %collective-permute-done.21 = bf16[128,768]{1,0:T(8,128)(2,1)S(1)} collective-permute-done((bf16[128,768]{1,0:T(8,128)(2,1)S(1)}, bf16[128,768]{1,0:T(8,128)(2,1)S(1)}, u32[]{:S(2)}, u32[]{:S(2)}) %collective-permute-start.21) | collective-permute-done | bytes 196640 | tf_op jit(solution)/shard_map/ppermute | solution.py:52
  87.3 1.1 %collective-permute-done.22 = f32[128]{0:T(128)S(1)} collective-permute-done((f32[128]{0:T(128)S(1)}, f32[128]{0:T(128)S(1)}, u32[]{:S(2)}, u32[]{:S(2)}) %collective-permute-start.22) | collective-permute-done | bytes 544 | tf_op jit(solution)/shard_map/ppermute | solution.py:94
  (117 shorter events, 30.3 us)
Async XLA Ops:
  0.0 21.0 %copy-start = (bf16[1536,768]{1,0:T(8,128)(2,1)S(1)}, bf16[1536,768]{1,0:T(8,128)(2,1)}, u32[]{:S(2)}) copy-start(bf16[1536,768]{1,0:T(8,128)(2,1)} %param.20) | copy-start | bytes 7077892
  14.0 5.5 %collective-permute-start.2 = (bf16[128,2,6]{0,2,1:T(8,128)(2,1)S(1)}, bf16[128,2,6]{0,2,1:T(8,128)(2,1)S(1)}, u32[]{:S(2)}, u32[]{:S(2)}) collective-permute-start(bf16[128,2,6]{0,2,1:T(8,128)(2,1)S(1)} %pad_maximum_fusion.2), channel_id=1, source_target_pairs={{0,1},{1,0},{2,3},{3,2},{4,5},{5,4},{6,7},{7,6},{8,9},{9,8},{10,11... | collective-permute-start | bytes 9224 | tf_op jit(solution)/shard_map/ppermute | solution.py:18
  14.6 5.0 %collective-permute-start = (bf16[128,2,6]{0,2,1:T(8,128)(2,1)S(1)}, bf16[128,2,6]{0,2,1:T(8,128)(2,1)S(1)}, u32[]{:S(2)}, u32[]{:S(2)}) collective-permute-start(bf16[128,2,6]{0,2,1:T(8,128)(2,1)S(1)} %pad_maximum_fusion.1), channel_id=1, source_target_pairs={{0,1},{1,0},{2,3},{3,2},{4,5},{5,4},{6,7},{7,6},{8,9},{9,8},{10,11... | collective-permute-start | bytes 9224 | tf_op jit(solution)/shard_map/ppermute | solution.py:18
  17.7 2.1 %collective-permute-start.1 = (bf16[128,2,6,128]{0,3,2,1:T(8,128)(2,1)}, bf16[128,2,6,128]{0,3,2,1:T(8,128)(2,1)}, u32[]{:S(2)}, u32[]{:S(2)}) collective-permute-start(bf16[128,2,6,128]{0,3,2,1:T(8,128)(2,1)} %pad_maximum_fusion), channel_id=1, source_target_pairs={{0,1},{1,0},{2,3},{3,2},{4,5},{5,4},{6,7},{7,6},{8,9},{9,8},{10,11... | collective-permute-start | bytes 1179656 | tf_op jit(solution)/shard_map/ppermute | solution.py:18
  22.6 1.3 %collective-permute-start.3 = (f32[128]{0:T(128)S(1)}, f32[128]{0:T(128)S(1)}, u32[]{:S(2)}, u32[]{:S(2)}) collective-permute-start(f32[128]{0:T(128)S(1)} %get-tuple-element.61), channel_id=1, source_target_pairs={{0,1},{1,0},{2,3},{3,2},{4,5},{5,4},{6,7},{7,6},{8,9},{9,8},{10,11... | collective-permute-start | bytes 1544 | tf_op jit(solution)/shard_map/ppermute | solution.py:94
  24.6 8.5 %collective-permute-start.4 = (bf16[128,768]{1,0:T(8,128)(2,1)S(1)}, bf16[128,768]{1,0:T(8,128)(2,1)S(1)}, u32[]{:S(2)}, u32[]{:S(2)}) collective-permute-start(bf16[128,768]{1,0:T(8,128)(2,1)S(1)} %get-tuple-element.45), channel_id=1, source_target_pairs={{0,2},{2,0},{4,6},{6,4},{8,10},{10,8},{12,14},{14,12},{1,3},{3,1},... | collective-permute-start | bytes 589832 | tf_op jit(solution)/shard_map/ppermute | solution.py:52
  27.4 9.2 %collective-permute-start.5 = (bf16[128,768]{1,0:T(8,128)(2,1)S(1)}, bf16[128,768]{1,0:T(8,128)(2,1)S(1)}, u32[]{:S(2)}, u32[]{:S(2)}) collective-permute-start(bf16[128,768]{1,0:T(8,128)(2,1)S(1)} %get-tuple-element.44), channel_id=1, source_target_pairs={{0,4},{2,6},{4,0},{6,2},{8,12},{10,14},{12,8},{14,10},{1,5},{3,7},... | collective-permute-start | bytes 589832 | tf_op jit(solution)/shard_map/ppermute | solution.py:52
  29.0 12.4 %collective-permute-start.6 = (bf16[128,768]{1,0:T(8,128)(2,1)S(1)}, bf16[128,768]{1,0:T(8,128)(2,1)S(1)}, u32[]{:S(2)}, u32[]{:S(2)}) collective-permute-start(bf16[128,768]{1,0:T(8,128)(2,1)S(1)} %get-tuple-element.42), channel_id=1, source_target_pairs={{0,6},{2,4},{4,2},{6,0},{8,14},{10,12},{12,10},{14,8},{1,7},{3,5},... | collective-permute-start | bytes 589832 | tf_op jit(solution)/shard_map/ppermute | solution.py:52
  29.0 12.4 %collective-permute-start.7 = (bf16[128,768]{1,0:T(8,128)(2,1)S(1)}, bf16[128,768]{1,0:T(8,128)(2,1)S(1)}, u32[]{:S(2)}, u32[]{:S(2)}) collective-permute-start(bf16[128,768]{1,0:T(8,128)(2,1)S(1)} %get-tuple-element.40), channel_id=1, source_target_pairs={{0,8},{2,10},{4,12},{6,14},{8,0},{10,2},{12,4},{14,6},{1,9},{3,11}... | collective-permute-start | bytes 589832 | tf_op jit(solution)/shard_map/ppermute | solution.py:52
  31.0 11.4 %collective-permute-start.8 = (bf16[128,768]{1,0:T(8,128)(2,1)S(1)}, bf16[128,768]{1,0:T(8,128)(2,1)S(1)}, u32[]{:S(2)}, u32[]{:S(2)}) collective-permute-start(bf16[128,768]{1,0:T(8,128)(2,1)S(1)} %get-tuple-element.29), channel_id=1, source_target_pairs={{0,10},{2,8},{4,14},{6,12},{8,2},{10,0},{12,6},{14,4},{1,11},{3,9}... | collective-permute-start | bytes 589832 | tf_op jit(solution)/shard_map/ppermute | solution.py:52
  33.1 13.6 %collective-permute-start.9 = (bf16[128,768]{1,0:T(8,128)(2,1)S(1)}, bf16[128,768]{1,0:T(8,128)(2,1)S(1)}, u32[]{:S(2)}, u32[]{:S(2)}) collective-permute-start(bf16[128,768]{1,0:T(8,128)(2,1)S(1)} %get-tuple-element.28), channel_id=1, source_target_pairs={{0,12},{2,14},{4,8},{6,10},{8,4},{10,6},{12,0},{14,2},{1,13},{3,15... | collective-permute-start | bytes 589832 | tf_op jit(solution)/shard_map/ppermute | solution.py:52
  36.7 13.5 %collective-permute-start.10 = (bf16[128,768]{1,0:T(8,128)(2,1)S(1)}, bf16[128,768]{1,0:T(8,128)(2,1)S(1)}, u32[]{:S(2)}, u32[]{:S(2)}) collective-permute-start(bf16[128,768]{1,0:T(8,128)(2,1)S(1)} %get-tuple-element.27), channel_id=1, source_target_pairs={{0,14},{2,12},{4,10},{6,8},{8,6},{10,4},{12,2},{14,0},{1,15},{3,13... | collective-permute-start | bytes 589832 | tf_op jit(solution)/shard_map/ppermute | solution.py:52
  50.3 4.2 %collective-permute-start.16 = (bf16[512,768]{1,0:T(8,128)(2,1)S(1)}, bf16[512,768]{1,0:T(8,128)(2,1)S(1)}, u32[]{:S(2)}, u32[]{:S(2)}) collective-permute-start(bf16[512,768]{1,0:T(8,128)(2,1)S(1)} %get-tuple-element.25), channel_id=1, source_target_pairs={{0,1},{1,0},{2,3},{3,2},{4,5},{5,4},{6,7},{7,6},{8,9},{9,8},{10,11... | collective-permute-start | bytes 2359304 | tf_op jit(solution)/shard_map/ppermute | solution.py:70
  50.4 7.4 %collective-permute-start.11 = (bf16[512,768]{1,0:T(8,128)(2,1)S(1)}, bf16[512,768]{1,0:T(8,128)(2,1)S(1)}, u32[]{:S(2)}, u32[]{:S(2)}) collective-permute-start(bf16[512,768]{1,0:T(8,128)(2,1)S(1)} %get-tuple-element.26), channel_id=1, source_target_pairs={{0,1},{1,0},{2,3},{3,2},{4,5},{5,4},{6,7},{7,6},{8,9},{9,8},{10,11... | collective-permute-start | bytes 2359304 | tf_op jit(solution)/shard_map/ppermute | solution.py:70
  57.1 3.6 %collective-permute-start.17 = (bf16[512,768]{1,0:T(8,128)(2,1)S(1)}, bf16[512,768]{1,0:T(8,128)(2,1)S(1)}, u32[]{:S(2)}, u32[]{:S(2)}) collective-permute-start(bf16[512,768]{1,0:T(8,128)(2,1)S(1)} %convolution_convert_fusion.1), channel_id=1, source_target_pairs={{0,1},{1,0},{2,3},{3,2},{4,5},{5,4},{6,7},{7,6},{8,9},{9,8},{10,11... | collective-permute-start | bytes 2359304 | tf_op jit(solution)/shard_map/ppermute | solution.py:86
  59.5 3.0 %collective-permute-start.12 = (bf16[512,768]{1,0:T(8,128)(2,1)S(1)}, bf16[512,768]{1,0:T(8,128)(2,1)S(1)}, u32[]{:S(2)}, u32[]{:S(2)}) collective-permute-start(bf16[512,768]{1,0:T(8,128)(2,1)S(1)} %convolution_convert_fusion.3), channel_id=1, source_target_pairs={{0,1},{1,0},{2,3},{3,2},{4,5},{5,4},{6,7},{7,6},{8,9},{9,8},{10,11... | collective-permute-start | bytes 2359304 | tf_op jit(solution)/shard_map/ppermute | solution.py:86
  60.9 19.1 %collective-permute-start.18 = (bf16[128,768]{1,0:T(8,128)(2,1)S(1)}, bf16[128,768]{1,0:T(8,128)(2,1)S(1)}, u32[]{:S(2)}, u32[]{:S(2)}) collective-permute-start(bf16[128,768]{1,0:T(8,128)(2,1)S(1)} %get-tuple-element.49), channel_id=1, source_target_pairs={{0,8},{2,10},{4,12},{6,14},{8,0},{10,2},{12,4},{14,6},{1,9},{3,11}... | collective-permute-start | bytes 589832 | tf_op jit(solution)/shard_map/ppermute | solution.py:52
  62.8 12.1 %collective-permute-start.13 = (bf16[128,768]{1,0:T(8,128)(2,1)S(1)}, bf16[128,768]{1,0:T(8,128)(2,1)S(1)}, u32[]{:S(2)}, u32[]{:S(2)}) collective-permute-start(bf16[128,768]{1,0:T(8,128)(2,1)S(1)} %get-tuple-element.52), channel_id=1, source_target_pairs={{0,2},{2,0},{4,6},{6,4},{8,10},{10,8},{12,14},{14,12},{1,3},{3,1},... | collective-permute-start | bytes 589832 | tf_op jit(solution)/shard_map/ppermute | solution.py:52
  63.5 12.3 %collective-permute-start.14 = (bf16[128,768]{1,0:T(8,128)(2,1)S(1)}, bf16[128,768]{1,0:T(8,128)(2,1)S(1)}, u32[]{:S(2)}, u32[]{:S(2)}) collective-permute-start(bf16[128,768]{1,0:T(8,128)(2,1)S(1)} %get-tuple-element.51), channel_id=1, source_target_pairs={{0,4},{2,6},{4,0},{6,2},{8,12},{10,14},{12,8},{14,10},{1,5},{3,7},... | collective-permute-start | bytes 589832 | tf_op jit(solution)/shard_map/ppermute | solution.py:52
  64.0 16.0 %collective-permute-start.15 = (bf16[128,768]{1,0:T(8,128)(2,1)S(1)}, bf16[128,768]{1,0:T(8,128)(2,1)S(1)}, u32[]{:S(2)}, u32[]{:S(2)}) collective-permute-start(bf16[128,768]{1,0:T(8,128)(2,1)S(1)} %get-tuple-element.50), channel_id=1, source_target_pairs={{0,6},{2,4},{4,2},{6,0},{8,14},{10,12},{12,10},{14,8},{1,7},{3,5},... | collective-permute-start | bytes 589832 | tf_op jit(solution)/shard_map/ppermute | solution.py:52
  66.4 13.7 %collective-permute-start.19 = (bf16[128,768]{1,0:T(8,128)(2,1)S(1)}, bf16[128,768]{1,0:T(8,128)(2,1)S(1)}, u32[]{:S(2)}, u32[]{:S(2)}) collective-permute-start(bf16[128,768]{1,0:T(8,128)(2,1)S(1)} %get-tuple-element.48), channel_id=1, source_target_pairs={{0,10},{2,8},{4,14},{6,12},{8,2},{10,0},{12,6},{14,4},{1,11},{3,9}... | collective-permute-start | bytes 589832 | tf_op jit(solution)/shard_map/ppermute | solution.py:52
  74.9 9.5 %collective-permute-start.20 = (bf16[128,768]{1,0:T(8,128)(2,1)S(1)}, bf16[128,768]{1,0:T(8,128)(2,1)S(1)}, u32[]{:S(2)}, u32[]{:S(2)}) collective-permute-start(bf16[128,768]{1,0:T(8,128)(2,1)S(1)} %get-tuple-element.47), channel_id=1, source_target_pairs={{0,12},{2,14},{4,8},{6,10},{8,4},{10,6},{12,0},{14,2},{1,13},{3,15... | collective-permute-start | bytes 589832 | tf_op jit(solution)/shard_map/ppermute | solution.py:52
  75.8 10.5 %collective-permute-start.21 = (bf16[128,768]{1,0:T(8,128)(2,1)S(1)}, bf16[128,768]{1,0:T(8,128)(2,1)S(1)}, u32[]{:S(2)}, u32[]{:S(2)}) collective-permute-start(bf16[128,768]{1,0:T(8,128)(2,1)S(1)} %get-tuple-element.46), channel_id=1, source_target_pairs={{0,14},{2,12},{4,10},{6,8},{8,6},{10,4},{12,2},{14,0},{1,15},{3,13... | collective-permute-start | bytes 589832 | tf_op jit(solution)/shard_map/ppermute | solution.py:52
  87.2 1.2 %collective-permute-start.22 = (f32[128]{0:T(128)S(1)}, f32[128]{0:T(128)S(1)}, u32[]{:S(2)}, u32[]{:S(2)}) collective-permute-start(f32[128]{0:T(128)S(1)} %get-tuple-element.63), channel_id=1, source_target_pairs={{0,1},{1,0},{2,3},{3,2},{4,5},{5,4},{6,7},{7,6},{8,9},{9,8},{10,11... | collective-permute-start | bytes 1544 | tf_op jit(solution)/shard_map/ppermute | solution.py:94
  (8 other events, 18.0 us)

commit v10 on v7

--- a/solution.py
+++ b/solution.py
@@ -146,48 +146,53 @@
     tp_count = lax.axis_size("tp")
     count_of_rows, feat_part = tokens.shape
     full_width = feat_part * tp_count
-    local_groups = query_lens.shape[0]
     req_count = query_lens.shape[1]
-    group_rows = count_of_rows // local_groups
     head_groups = QUERY_HEADS // KEY_VALUE_HEADS
     per_device = page_table.shape[1] // tp_count
 
-    def one_group(local):
-        query_count = lax.dynamic_index_in_dim(query_lens, local, 0, keepdims=False)
-        past_count = lax.dynamic_index_in_dim(past_lens, local, 0, keepdims=False)
-        row_ends = jnp.cumsum(query_count)
-        row_starts = row_ends - query_count
-        row_iota = jnp.arange(group_rows, dtype=jnp.int32)
-        row_req = jnp.sum((row_iota[:, None] >= row_ends[None, :]).astype(jnp.int32), axis=1)
-        req_onehot = (row_req[:, None] == jnp.arange(req_count, dtype=jnp.int32)[None, :]).astype(
-            jnp.int32
-        )
-        row_pos = row_iota + jnp.sum(req_onehot * (past_count - row_starts)[None, :], axis=1)
-        local_table = lax.dynamic_index_in_dim(
-            page_table.reshape(req_count, per_device, tp_count), tp_index, axis=2, keepdims=False
-        )
-        group_pages = lax.dynamic_index_in_dim(kv_cache, local, 0, keepdims=False)[0]
-        page_row_block = group_pages[local_table.reshape(-1)]
-        key_count_total = page_row_block.shape[0] * PAGE_POSITIONS
-        flattened_cache = page_row_block.reshape(key_count_total, 2 * KEY_VALUE_HEADS * HEAD_SIZE)
-        gathered_keys = flattened_cache[:, : KEY_VALUE_HEADS * HEAD_SIZE].reshape(
-            key_count_total, KEY_VALUE_HEADS, HEAD_SIZE
-        )
-        gathered_values = flattened_cache[:, KEY_VALUE_HEADS * HEAD_SIZE :].reshape(
-            key_count_total, KEY_VALUE_HEADS, HEAD_SIZE
-        )
-        key_iota = jnp.arange(key_count_total, dtype=jnp.int32)
-        key_req = key_iota // (per_device * PAGE_POSITIONS)
-        within = key_iota % (per_device * PAGE_POSITIONS)
-        key_pos = (
-            within // PAGE_POSITIONS * tp_count + tp_index
-        ) * PAGE_POSITIONS + within % PAGE_POSITIONS
-        allowed = (row_req[:, None] == key_req[None, :]) & (key_pos[None, :] <= row_pos[:, None])
-        score_mask = allowed[:, None, :]
+    query_count = query_lens[0]
+    past_count = past_lens[0]
+    req_iota = jnp.arange(req_count, dtype=jnp.int32)
+    row_ends = jnp.sum(
+        jnp.where(req_iota[None, :] <= req_iota[:, None], query_count[None, :], 0), axis=1
+    )
+    row_starts = row_ends - query_count
+    row_iota = jnp.arange(count_of_rows, dtype=jnp.int32)
+    row_req = jnp.sum((row_iota[:, None] >= row_ends[None, :]).astype(jnp.int32), axis=1)
+    req_onehot = (row_req[:, None] == req_iota[None, :]).astype(jnp.int32)
+    row_pos = row_iota + jnp.sum(req_onehot * (past_count - row_starts)[None, :], axis=1)
+    local_table = page_table[:, 0::tp_count]
+    for other in range(1, tp_count):
+        local_table = jnp.where(tp_index == other, page_table[:, other::tp_count], local_table)
+    page_row_block = kv_cache[0, 0][local_table.reshape(-1)]
+    key_count_total = page_row_block.shape[0] * PAGE_POSITIONS
+    flattened_cache = page_row_block.reshape(key_count_total, 2 * KEY_VALUE_HEADS * HEAD_SIZE)
+    key_iota = jnp.arange(key_count_total, dtype=jnp.int32)
+    key_req = key_iota // (per_device * PAGE_POSITIONS)
+    within = key_iota % (per_device * PAGE_POSITIONS)
+    key_pos = (
+        within // PAGE_POSITIONS * tp_count + tp_index
+    ) * PAGE_POSITIONS + within % PAGE_POSITIONS
+    allowed = (row_req[:, None] == key_req[None, :]) & (key_pos[None, :] <= row_pos[:, None])
+
+    top_count = route_ids.shape[1]
+    half_count = lax.axis_size("el")
+    experts = half_count
+    most = count_of_rows * top_count * 2 // experts
+    chunk_count = 2 if count_of_rows % 16 == 0 else 1
+    chunk_rows = count_of_rows // chunk_count
+    capacity = min(most, chunk_rows)
+    buffer_len = experts * capacity
+    my_half = lax.axis_index("el")
+
+    def attend(rows):
+        score_mask = allowed[rows][:, None, :]
+        chunk_queries = queries[rows]
         outs = []
         for kv_head in range(KEY_VALUE_HEADS):
-            head_rows = queries[:, kv_head * head_groups * HEAD_SIZE : (kv_head + 1) * head_groups * HEAD_SIZE]
-            head_rows = head_rows.reshape(group_rows, head_groups, HEAD_SIZE)
+            head_rows = chunk_queries[
+                :, kv_head * head_groups * HEAD_SIZE : (kv_head + 1) * head_groups * HEAD_SIZE
+            ].reshape(chunk_rows, head_groups, HEAD_SIZE)
             head_keys = flattened_cache[:, kv_head * HEAD_SIZE : (kv_head + 1) * HEAD_SIZE]
             head_values = flattened_cache[
                 :, (KEY_VALUE_HEADS + kv_head) * HEAD_SIZE : (KEY_VALUE_HEADS + kv_head + 1) * HEAD_SIZE
@@ -205,85 +210,97 @@
                 preferred_element_type=jnp.float32,
             )
             outs.append((top, total, weighted_part))
-        part_max = jnp.stack([o[0] for o in outs], axis=1)
-        part_sum = jnp.stack([o[1] for o in outs], axis=1)
-        part_weighted = jnp.stack([o[2] for o in outs], axis=1)
-        return (part_max, part_sum, part_weighted)
-
-    row_max, row_sum, weighted = lax.map(one_group, jnp.arange(local_groups, dtype=jnp.int32))
-    row_max = row_max.reshape(count_of_rows, KEY_VALUE_HEADS, head_groups)
-    row_sum = row_sum.reshape(count_of_rows, KEY_VALUE_HEADS, head_groups)
-    weighted = weighted.reshape(count_of_rows, KEY_VALUE_HEADS, head_groups, HEAD_SIZE)
-    row_max, row_sum, weighted = merged((row_max, row_sum, weighted), "tp", merge_parts)
-    attended = (
-        (weighted / row_sum[..., None])
-        .reshape(count_of_rows, QUERY_HEADS * HEAD_SIZE)
-        .astype(jnp.bfloat16)
-    )
-    resid = tokens.astype(jnp.float32) + jnp.dot(
-        attended, out_weight, preferred_element_type=jnp.float32
-    )
-    mid_squares = tp_sum(jnp.sum(resid * resid, axis=1))
-    normed = (resid * lax.rsqrt(mid_squares / full_width + EPSILON)[:, None] * norm_gain).astype(
-        jnp.bfloat16
-    )
-    top_count = route_ids.shape[1]
-    half_count = lax.axis_size("el")
-    experts = half_count
-    capacity = count_of_rows * top_count * 2 // experts
-    buffer_len = experts * capacity
-    flat_ids = route_ids.reshape(-1)
-    expert_onehot = (flat_ids[:, None] == jnp.arange(experts, dtype=jnp.int32)[None, :]).astype(
-        jnp.int32
-    )
-    assign_iota = jnp.arange(flat_ids.shape[0], dtype=jnp.int32)
-    earlier = (assign_iota[None, :] < assign_iota[:, None]).astype(jnp.bfloat16)
-    before = jnp.dot(
-        earlier, expert_onehot.astype(jnp.bfloat16), preferred_element_type=jnp.float32
-    ).astype(jnp.int32)
-    expert_rank = jnp.sum(before * expert_onehot, axis=1)
-    my_half = lax.axis_index("el")
-    target = (relative(flat_ids, my_half, half_count) * capacity + expert_rank).reshape(
-        count_of_rows, top_count
-    )
-    slot_iota = jnp.arange(buffer_len, dtype=jnp.int32)
-    hits = target[None, :, :] == slot_iota[:, None, None]
-    dispatch = jnp.any(hits, axis=2).astype(jnp.bfloat16)
-    outgoing = jnp.dot(dispatch, normed, preferred_element_type=jnp.float32).astype(jnp.bfloat16)
-    arrived = exchange(outgoing.reshape(experts, capacity, feat_part), half_count)
-    flat_rows = lax.optimization_barrier(arrived.reshape(buffer_len, feat_part))
-    group_rows = buffer_len // 2
-    summed = jnp.concatenate(
-        [
-            expert_block(
-                flat_rows[start : start + group_rows], gate_w[0], up_w[0], down_w[0]
-            )
-            for start in (0, group_rows)
-        ],
+        row_max = jnp.stack([o[0] for o in outs], axis=1)
+        row_sum = jnp.stack([o[1] for o in outs], axis=1)
+        weighted = jnp.stack([o[2] for o in outs], axis=1)
+        row_max, row_sum, weighted = merged((row_max, row_sum, weighted), "tp", merge_parts)
+        attended = (
+            (weighted / row_sum[..., None])
+            .reshape(chunk_rows, QUERY_HEADS * HEAD_SIZE)
+            .astype(jnp.bfloat16)
+        )
+        resid = tokens[rows].astype(jnp.float32) + jnp.dot(
+            attended, out_weight, preferred_element_type=jnp.float32
+        )
+        mid_squares = tp_sum(jnp.sum(resid * resid, axis=1))
+        normed = (
+            resid * lax.rsqrt(mid_squares / full_width + EPSILON)[:, None] * norm_gain
+        ).astype(jnp.bfloat16)
+        return resid, normed
+
+    def send_rows(rows, normed):
+        flat_ids = route_ids[rows].reshape(-1)
+        expert_onehot = (
+            flat_ids[:, None] == jnp.arange(experts, dtype=jnp.int32)[None, :]
+        ).astype(jnp.int32)
+        assign_iota = jnp.arange(flat_ids.shape[0], dtype=jnp.int32)
+        earlier = (assign_iota[None, :] < assign_iota[:, None]).astype(jnp.bfloat16)
+        before = jnp.dot(
+            earlier, expert_onehot.astype(jnp.bfloat16), preferred_element_type=jnp.float32
+        ).astype(jnp.int32)
+        expert_rank = jnp.sum(before * expert_onehot, axis=1)
+        target = (relative(flat_ids, my_half, half_count) * capacity + expert_rank).reshape(
+            chunk_rows, top_count
+        )
+        slot_iota = jnp.arange(buffer_len, dtype=jnp.int32)
+        hits = target[None, :, :] == slot_iota[:, None, None]
+        dispatch = jnp.any(hits, axis=2).astype(jnp.bfloat16)
+        outgoing = jnp.dot(dispatch, normed, preferred_element_type=jnp.float32).astype(
+            jnp.bfloat16
+        )
+        arrived = exchange(outgoing.reshape(experts, capacity, feat_part), half_count)
+        return target, outgoing, arrived
+
+    def expert_rows(arrived):
+        flat_rows = lax.optimization_barrier(arrived.reshape(buffer_len, feat_part))
+        return expert_block(flat_rows, gate_w[0], up_w[0], down_w[0])
+
+    def finish(rows, resid, target, summed):
+        slot_iota = jnp.arange(buffer_len, dtype=jnp.int32)
+        returned = exchange(summed.reshape(experts, capacity, feat_part), half_count).reshape(
+            buffer_len, feat_part
+        )
+        combine = jnp.sum(
+            jnp.where(
+                target[:, :, None] == slot_iota[None, None, :],
+                route_weights[rows][:, :, None],
+                0.0,
+            ),
+            axis=1,
+        )
+        branch = jnp.dot(
+            combine,
+            returned.astype(jnp.float32),
+            precision=lax.Precision.HIGHEST,
+            preferred_element_type=jnp.float32,
+        )
+        mixed_rows = resid + branch
+        out_squares = tp_sum(jnp.sum(mixed_rows * mixed_rows, axis=1))
+        return (
+            mixed_rows * lax.rsqrt(out_squares / full_width + EPSILON)[:, None] * final_gain
+        ).astype(jnp.bfloat16)
+
+    if chunk_count == 1:
+        rows = slice(0, count_of_rows)
+        resid, normed = attend(rows)
+        target, _, arrived = send_rows(rows, normed)
+        return finish(rows, resid, target, expert_rows(arrived))
+    first = slice(0, chunk_rows)
+    second = slice(chunk_rows, count_of_rows)
+    resid_a, normed_a = attend(first)
+    target_a, outgoing_a, arrived_a = send_rows(first, normed_a)
+    outgoing_a, queries = lax.optimization_barrier((outgoing_a, queries))
+    resid_b, normed_b = attend(second)
+    arrived_a, normed_b = lax.optimization_barrier((arrived_a, normed_b))
+    summed_a = expert_rows(arrived_a)
+    summed_a, normed_b = lax.optimization_barrier((summed_a, normed_b))
+    target_b, _, arrived_b = send_rows(second, normed_b)
+    summed_b = expert_rows(arrived_b)
+    summed_a, summed_b = lax.optimization_barrier((summed_a, summed_b))
+    return jnp.concatenate(
+        [finish(first, resid_a, target_a, summed_a), finish(second, resid_b, target_b, summed_b)],
         axis=0,
     )
-    returned = exchange(summed.reshape(experts, capacity, feat_part), half_count).reshape(
-        buffer_len, feat_part
-    )
-    combine = jnp.sum(
-        jnp.where(
-            target[:, :, None] == slot_iota[None, None, :],
-            route_weights[:, :, None],
-            0.0,
-        ),
-        axis=1,
-    )
-    branch = jnp.dot(
-        combine,
-        returned.astype(jnp.float32),
-        precision=lax.Precision.HIGHEST,
-        preferred_element_type=jnp.float32,
-    )
-    mixed_rows = resid + branch
-    out_squares = tp_sum(jnp.sum(mixed_rows * mixed_rows, axis=1))
-    return (
-        mixed_rows * lax.rsqrt(out_squares / full_width + EPSILON)[:, None] * final_gain
-    ).astype(jnp.bfloat16)
 
 
 def solution(mesh):

time: 88.9 us -> 114 us (1.28)
  starting transfers between devices: 23.7 us -> 43 us
  waiting for transfers between devices: 31.2 us -> 19.3 us
  matrix products: 16.5 us -> 25.4 us
  local copies, waits for them, and re-layouts: 9.06 us -> 17.4 us
    ppermute x14 -> x28, starting transfers between devices: 21.4 us -> 39.9 us  [exchange(): pieces.append(lax.ppermute(chunks[step], 'el', perm=pairs))]
    ppermute x14 -> x28, waiting for transfers between devices: 29 us -> 13.1 us  [exchange(): pieces.append(lax.ppermute(chunks[step], 'el', perm=pairs))]
    dot_general x8, matrix products: 4.67 us -> 9.55 us  [half_product(): return jnp.dot(x, weight, preferred_element_type=jnp.float32)]
    convert_element_type x0 -> x4, local copies, waits for them, and re-layouts: none -> 3.09 us  [attend(): attended = (weighted / row_sum[..., None]).reshape(chunk_rows, QUERY_HEAD...]
    ppermute x2, waiting for transfers between devices: 0.01 us -> 2.27 us  [expert_block(): rows_other = lax.ppermute(rows, 'tp', perm=swap)]
    dot_general x8 -> x16, matrix products: 9.36 us -> 11.4 us  [the longest x4 4.52 us: attend(): jnp.einsum('rgd,ld->rgl', head_rows, head_keys, preferred_element_type=jn...]
    ppermute x2, waiting for transfers between devices: 0.01 us -> 1.91 us  [expert_block(): sent = lax.ppermute(down_product(other), 'tp', perm=swap)]
    unnamed x36 -> x70, local copies, waits for them, and re-layouts: 3.93 us -> 5.82 us
  transfers between devices with their start and end apart: 23 -> 42, of which waited for: 13 -> 15; matrix products, arithmetic and copies ran while one was open for 14% -> 18% of each run, Pallas kernels for 0% -> 0%
where the time goes in v10:
time: 114 us; the launch traced here: 113 us
  starting transfers between devices  43 us (38%)
  matrix products  25.4 us (22%)
  waiting for transfers between devices  19.3 us (17%)
  local copies, waits for them, and re-layouts  17.4 us (15%)
  other arithmetic  7.66 us (7%)
    ppermute x28, starting transfers between devices, exchange(): pieces.append(lax.ppermute(chunks[step], 'el', perm=pairs))  39.9 us
    ppermute x28, waiting for transfers between devices, exchange(): pieces.append(lax.ppermute(chunks[step], 'el', perm=pairs))  13.1 us
    dot_general x8, matrix products, half_product(): return jnp.dot(x, weight, preferred_element_type=jnp.float32)  9.55 us
    unnamed x70, local copies, waits for them, and re-layouts  5.82 us
    dot_general x4, matrix products, attend(): jnp.einsum('rgd,ld->rgl', head_rows, head_keys, preferred_element_type=jn...  4.52 us
    dot_general x4, matrix products, down_product(): jnp.dot(hidden, weight, preferred_element_type=jnp.float32)  4.38 us
    gather x1, local copies, waits for them, and re-layouts, shards(): page_row_block = kv_cache[0, 0][local_table.reshape(-1)]  3.34 us
    convert_element_type x4, local copies, waits for them, and re-layouts, attend(): attended = (weighted / row_sum[..., None]).reshape(chunk_rows, QUERY_HEAD...  3.09 us
  transfers between devices with their start and end apart: 42, of which 15 were waited for; matrix products, arithmetic and copies ran while one was open for 18% of the time, Pallas kernels for 0%

profile of v10, /device:TPU:0, one launch (start us, length us, event | category | flops | bytes accessed | tf_op | source)
XLA Modules:
  0.0 113.5 jit_solution(7405110164302424581)
XLA Ops:
  4.7 3.3 %gather_fusion = bf16[96,16,512]{2,1,0:T(8,128)(2,1)} fusion(bf16[96,16,512]{2,1,0:T(8,128)(2,1)} %bitcast.243, s32[1024]{0:T(1024)S(1)} %pad_clamp_fusion), kind=kCustom, calls=%fused_computation | custom fusion | bytes 3146112 | tf_op jit(solution)/shard_map/gather | solution.py:167
  8.1 1.7 %select_reduce_fusion.3 = (f32[64,6]{0,1:T(8,128)S(1)}, f32[64,6,1536]{2,0,1:T(8,128)S(1)}) fusion(pred[64,1536]{1,0:T(8,128)(4,1)S(1)} %get-tuple-element.56, bf16[8,6,8,128]{3,2,1,0:T(8,128)(2,1)S(1)} %get-tuple-element.53, bf16[1536,512]{1,0:T(8,128)(2,1)} %bitcast.235), kind=kOutput, calls=%fused_computation.14 | convolution fusion | flops 152764032 | bytes 2950656 | tf_op jit(solution)/shard_map/rgd,ld->rgl/dot_general | solution.py:200
  24.0 2.8 %collective-permute-start.4 = (bf16[64,768]{1,0:T(8,128)(2,1)S(1)}, bf16[64,768]{1,0:T(8,128)(2,1)S(1)}, u32[]{:S(2)}, u32[]{:S(2)}) collective-permute-start(bf16[64,768]{1,0:T(8,128)(2,1)S(1)} %get-tuple-element.50), channel_id=1, source_target_pairs={{0,2},{2,0},{4,6},{6,4},{8,10},{10,8},{12,14},{14,12},{1,3},{3,1},... | collective-permute-start | bytes 294920 | tf_op jit(solution)/shard_map/ppermute | solution.py:52
  28.3 2.0 %collective-permute-start.7 = (bf16[64,768]{1,0:T(8,128)(2,1)S(1)}, bf16[64,768]{1,0:T(8,128)(2,1)S(1)}, u32[]{:S(2)}, u32[]{:S(2)}) collective-permute-start(bf16[64,768]{1,0:T(8,128)(2,1)S(1)} %get-tuple-element.47), channel_id=1, source_target_pairs={{0,8},{2,10},{4,12},{6,14},{8,0},{10,2},{12,4},{14,6},{1,9},{3,11}... | collective-permute-start | bytes 294920 | tf_op jit(solution)/shard_map/ppermute | solution.py:52
  30.4 3.0 %collective-permute-start.8 = (bf16[64,768]{1,0:T(8,128)(2,1)S(1)}, bf16[64,768]{1,0:T(8,128)(2,1)S(1)}, u32[]{:S(2)}, u32[]{:S(2)}) collective-permute-start(bf16[64,768]{1,0:T(8,128)(2,1)S(1)} %get-tuple-element.46), channel_id=1, source_target_pairs={{0,10},{2,8},{4,14},{6,12},{8,2},{10,0},{12,6},{14,4},{1,11},{3,9}... | collective-permute-start | bytes 294920 | tf_op jit(solution)/shard_map/ppermute | solution.py:52
  34.1 2.0 %collective-permute-start.9 = (bf16[64,768]{1,0:T(8,128)(2,1)S(1)}, bf16[64,768]{1,0:T(8,128)(2,1)S(1)}, u32[]{:S(2)}, u32[]{:S(2)}) collective-permute-start(bf16[64,768]{1,0:T(8,128)(2,1)S(1)} %get-tuple-element.45), channel_id=1, source_target_pairs={{0,12},{2,14},{4,8},{6,10},{8,4},{10,6},{12,0},{14,2},{1,13},{3,15... | collective-permute-start | bytes 294920 | tf_op jit(solution)/shard_map/ppermute | solution.py:52
  38.8 1.8 %collective-permute-done.9 = bf16[64,768]{1,0:T(8,128)(2,1)S(1)} collective-permute-done((bf16[64,768]{1,0:T(8,128)(2,1)S(1)}, bf16[64,768]{1,0:T(8,128)(2,1)S(1)}, u32[]{:S(2)}, u32[]{:S(2)}) %collective-permute-start.9) | collective-permute-done | bytes 98336 | tf_op jit(solution)/shard_map/ppermute | solution.py:52
  42.5 1.9 %convert_element_type.181 = bf16[64,1536]{1,0:T(8,128)(2,1)} reshape(bf16[64,2,6,128]{3,2,1,0:T(8,128)(2,1)} %copy.50) | data formatting | bytes 393216 | tf_op jit(solution)/shard_map/convert_element_type | solution.py:220
  44.3 1.6 %multiply_reduce_fusion.2 = (f32[64]{0:T(128)S(1)}, f32[64,768]{1,0:T(8,128)S(1)}) fusion(bf16[64,1536]{1,0:T(8,128)(2,1)} %convert_element_type.181, bf16[1536,768]{1,0:T(8,128)(2,1)S(1)} %copy-done, bf16[128,768]{1,0:T(8,128)(2,1)} %param.14), kind=kOutput, calls=%fused_computation.127 | convolution fusion | flops 151191488 | bytes 2851072 | tf_op jit(solution)/shard_map/dot_general | solution.py:222
  48.9 1.8 %fusion.78 = f32[512,384]{1,0:T(8,128)S(1)} fusion(bf16[512,768]{1,0:T(8,128)(2,1)} %bitcast.32, bf16[2,768,384]{2,1,0:T(8,128)(2,1)S(1)} %bitcast.224, s32[]{:T(128)S(6)} %select_n.129), kind=kOutput, calls=%fused_computation.90 | convolution fusion | flops 301989888 | bytes 2162692 | tf_op jit(solution)/shard_map/dot_general | solution.py:76
  50.7 1.9 %fusion.72 = f32[512,384]{1,0:T(8,128)S(1)} fusion(bf16[512,768]{1,0:T(8,128)(2,1)} %bitcast.32, bf16[2,768,384]{2,1,0:T(8,128)(2,1)S(1)} %bitcast.228, s32[]{:T(128)S(6)} %select_n.129), kind=kOutput, calls=%fused_computation.84 | convolution fusion | flops 301989888 | bytes 2162692 | tf_op jit(solution)/shard_map/dot_general | solution.py:76
  52.6 1.7 %fusion.13 = f32[512,384]{1,0:T(8,128)S(1)} fusion(f32[512,384]{1,0:T(8,128)S(1)} %fusion.78, bf16[512,768]{1,0:T(8,128)(2,1)} %collective-permute-done.15, bf16[2,768,384]{2,1,0:T(8,128)(2,1)S(1)} %bitcast.225, s32[]{:T(128)S(6)} %select_n.130), kind=kOutput, calls=%fused_computation.38 | convolution fusion | flops 302383104 | bytes 2949124 | tf_op jit(solution)/shard_map/dot_general | solution.py:76
  54.3 1.8 %fusion.14 = bf16[512,384]{1,0:T(8,128)(2,1)S(1)} fusion(f32[512,384]{1,0:T(8,128)S(1)} %fusion.13, f32[512,384]{1,0:T(8,128)S(1)} %fusion.72, bf16[512,768]{1,0:T(8,128)(2,1)} %collective-permute-done.15, bf16[2,768,384]{2,1,0:T(8,128)(2,1)S(1)} %bitcast.229, s32[]{:T(128)S(6)} %select_n.130), kind=kOutput, calls=%fused_computation.39 | convolution fusion | flops 302579712 | bytes 3342340 | tf_op jit(solution)/shard_map/dot_general | solution.py:76
  57.8 1.8 %convolution_convert_fusion.5 = bf16[512,768]{1,0:T(8,128)(2,1)S(1)} fusion(bf16[512,384]{1,0:T(8,128)(2,1)} %copy-done.6, bf16[1,384,1536]{2,1,0:T(8,128)(2,1)} %param.26, s32[]{:T(128)S(6)} %select_n.131), kind=kOutput, calls=%fused_computation.30 | convolution fusion | flops 302383104 | bytes 1769476 | tf_op jit(solution)/shard_map/dot_general | solution.py:84
  65.9 1.7 %collective-permute-start.21 = (bf16[64,768]{1,0:T(8,128)(2,1)S(1)}, bf16[64,768]{1,0:T(8,128)(2,1)S(1)}, u32[]{:S(2)}, u32[]{:S(2)}) collective-permute-start(bf16[64,768]{1,0:T(8,128)(2,1)S(1)} %get-tuple-element.39), channel_id=1, source_target_pairs={{0,10},{2,8},{4,14},{6,12},{8,2},{10,0},{12,6},{14,4},{1,11},{3,9}... | collective-permute-start | bytes 294920 | tf_op jit(solution)/shard_map/ppermute | solution.py:52
  67.7 1.9 %collective-permute-start.22 = (bf16[64,768]{1,0:T(8,128)(2,1)S(1)}, bf16[64,768]{1,0:T(8,128)(2,1)S(1)}, u32[]{:S(2)}, u32[]{:S(2)}) collective-permute-start(bf16[64,768]{1,0:T(8,128)(2,1)S(1)} %get-tuple-element.38), channel_id=1, source_target_pairs={{0,12},{2,14},{4,8},{6,10},{8,4},{10,6},{12,0},{14,2},{1,13},{3,15... | collective-permute-start | bytes 294920 | tf_op jit(solution)/shard_map/ppermute | solution.py:52
  69.6 2.2 %collective-permute-start.23 = (bf16[64,768]{1,0:T(8,128)(2,1)S(1)}, bf16[64,768]{1,0:T(8,128)(2,1)S(1)}, u32[]{:S(2)}, u32[]{:S(2)}) collective-permute-start(bf16[64,768]{1,0:T(8,128)(2,1)S(1)} %get-tuple-element.37), channel_id=1, source_target_pairs={{0,14},{2,12},{4,10},{6,8},{8,6},{10,4},{12,2},{14,0},{1,15},{3,13... | collective-permute-start | bytes 294920 | tf_op jit(solution)/shard_map/ppermute | solution.py:52
  73.1 2.7 %collective-permute-done.22 = bf16[64,768]{1,0:T(8,128)(2,1)S(1)} collective-permute-done((bf16[64,768]{1,0:T(8,128)(2,1)S(1)}, bf16[64,768]{1,0:T(8,128)(2,1)S(1)}, u32[]{:S(2)}, u32[]{:S(2)}) %collective-permute-start.22) | collective-permute-done | bytes 98336 | tf_op jit(solution)/shard_map/ppermute | solution.py:52
  77.2 2.3 %collective-permute-done.24 = bf16[512,768]{1,0:T(8,128)(2,1)S(1)} collective-permute-done((bf16[512,768]{1,0:T(8,128)(2,1)S(1)}, bf16[512,768]{1,0:T(8,128)(2,1)S(1)}, u32[]{:S(2)}, u32[]{:S(2)}) %collective-permute-start.24) | collective-permute-done | bytes 786464 | tf_op jit(solution)/shard_map/ppermute | solution.py:70
  87.2 1.6 %collective-permute-start.36 = (bf16[64,768]{1,0:T(8,128)(2,1)S(1)}, bf16[64,768]{1,0:T(8,128)(2,1)S(1)}, u32[]{:S(2)}, u32[]{:S(2)}) collective-permute-start(bf16[64,768]{1,0:T(8,128)(2,1)S(1)} %get-tuple-element.34), channel_id=1, source_target_pairs={{0,6},{2,4},{4,2},{6,0},{8,14},{10,12},{12,10},{14,8},{1,7},{3,5},... | collective-permute-start | bytes 294920 | tf_op jit(solution)/shard_map/ppermute | solution.py:52
  92.9 1.9 %collective-permute-start.40 = (bf16[64,768]{1,0:T(8,128)(2,1)S(1)}, bf16[64,768]{1,0:T(8,128)(2,1)S(1)}, u32[]{:S(2)}, u32[]{:S(2)}) collective-permute-start(bf16[64,768]{1,0:T(8,128)(2,1)S(1)} %get-tuple-element.30), channel_id=1, source_target_pairs={{0,14},{2,12},{4,10},{6,8},{8,6},{10,4},{12,2},{14,0},{1,15},{3,13... | collective-permute-start | bytes 294920 | tf_op jit(solution)/shard_map/ppermute | solution.py:52
  100.1 1.8 %collective-permute-start.30 = (bf16[64,768]{1,0:T(8,128)(2,1)S(1)}, bf16[64,768]{1,0:T(8,128)(2,1)S(1)}, u32[]{:S(2)}, u32[]{:S(2)}) collective-permute-start(bf16[64,768]{1,0:T(8,128)(2,1)S(1)} %get-tuple-element.25), channel_id=1, source_target_pairs={{0,10},{2,8},{4,14},{6,12},{8,2},{10,0},{12,6},{14,4},{1,11},{3,9}... | collective-permute-start | bytes 294920 | tf_op jit(solution)/shard_map/ppermute | solution.py:52
  102.5 1.9 %collective-permute-start.31 = (bf16[64,768]{1,0:T(8,128)(2,1)S(1)}, bf16[64,768]{1,0:T(8,128)(2,1)S(1)}, u32[]{:S(2)}, u32[]{:S(2)}) collective-permute-start(bf16[64,768]{1,0:T(8,128)(2,1)S(1)} %get-tuple-element.24), channel_id=1, source_target_pairs={{0,12},{2,14},{4,8},{6,10},{8,4},{10,6},{12,0},{14,2},{1,13},{3,15... | collective-permute-start | bytes 294920 | tf_op jit(solution)/shard_map/ppermute | solution.py:52
  106.6 2.7 %collective-permute-done.31 = bf16[64,768]{1,0:T(8,128)(2,1)S(1)} collective-permute-done((bf16[64,768]{1,0:T(8,128)(2,1)S(1)}, bf16[64,768]{1,0:T(8,128)(2,1)S(1)}, u32[]{:S(2)}, u32[]{:S(2)}) %collective-permute-start.31) | collective-permute-done | bytes 98336 | tf_op jit(solution)/shard_map/ppermute | solution.py:52
  (226 shorter events, 62.9 us)
Async XLA Ops:
  23.7 17.5 %collective-permute-start.12 = (bf16[64,2,6,128]{3,0,2,1:T(8,128)(2,1)S(1)}, bf16[64,2,6,128]{3,0,2,1:T(8,128)(2,1)S(1)}, u32[]{:S(2)}, u32[]{:S(2)}) collective-permute-start(bf16[64,2,6,128]{3,0,2,1:T(8,128)(2,1)S(1)} %pad_maximum_fusion.1), channel_id=1, source_target_pairs={{0,1},{1,0},{2,3},{3,2},{4,5},{5,4},{6,7},{7,6},{8,9},{9,8},{10,11... | collective-permute-start | bytes 589832 | tf_op jit(solution)/shard_map/ppermute | solution.py:18
  26.8 7.3 %collective-permute-start.5 = (bf16[64,768]{1,0:T(8,128)(2,1)S(1)}, bf16[64,768]{1,0:T(8,128)(2,1)S(1)}, u32[]{:S(2)}, u32[]{:S(2)}) collective-permute-start(bf16[64,768]{1,0:T(8,128)(2,1)S(1)} %get-tuple-element.49), channel_id=1, source_target_pairs={{0,4},{2,6},{4,0},{6,2},{8,12},{10,14},{12,8},{14,10},{1,5},{3,7},... | collective-permute-start | bytes 294920 | tf_op jit(solution)/shard_map/ppermute | solution.py:52
  28.3 8.4 %collective-permute-start.6 = (bf16[64,768]{1,0:T(8,128)(2,1)S(1)}, bf16[64,768]{1,0:T(8,128)(2,1)S(1)}, u32[]{:S(2)}, u32[]{:S(2)}) collective-permute-start(bf16[64,768]{1,0:T(8,128)(2,1)S(1)} %get-tuple-element.48), channel_id=1, source_target_pairs={{0,6},{2,4},{4,2},{6,0},{8,14},{10,12},{12,10},{14,8},{1,7},{3,5},... | collective-permute-start | bytes 294920 | tf_op jit(solution)/shard_map/ppermute | solution.py:52
  28.3 9.2 %collective-permute-start.7 = (bf16[64,768]{1,0:T(8,128)(2,1)S(1)}, bf16[64,768]{1,0:T(8,128)(2,1)S(1)}, u32[]{:S(2)}, u32[]{:S(2)}) collective-permute-start(bf16[64,768]{1,0:T(8,128)(2,1)S(1)} %get-tuple-element.47), channel_id=1, source_target_pairs={{0,8},{2,10},{4,12},{6,14},{8,0},{10,2},{12,4},{14,6},{1,9},{3,11}... | collective-permute-start | bytes 294920 | tf_op jit(solution)/shard_map/ppermute | solution.py:52
  30.4 7.8 %collective-permute-start.8 = (bf16[64,768]{1,0:T(8,128)(2,1)S(1)}, bf16[64,768]{1,0:T(8,128)(2,1)S(1)}, u32[]{:S(2)}, u32[]{:S(2)}) collective-permute-start(bf16[64,768]{1,0:T(8,128)(2,1)S(1)} %get-tuple-element.46), channel_id=1, source_target_pairs={{0,10},{2,8},{4,14},{6,12},{8,2},{10,0},{12,6},{14,4},{1,11},{3,9}... | collective-permute-start | bytes 294920 | tf_op jit(solution)/shard_map/ppermute | solution.py:52
  34.1 6.5 %collective-permute-start.9 = (bf16[64,768]{1,0:T(8,128)(2,1)S(1)}, bf16[64,768]{1,0:T(8,128)(2,1)S(1)}, u32[]{:S(2)}, u32[]{:S(2)}) collective-permute-start(bf16[64,768]{1,0:T(8,128)(2,1)S(1)} %get-tuple-element.45), channel_id=1, source_target_pairs={{0,12},{2,14},{4,8},{6,10},{8,4},{10,6},{12,0},{14,2},{1,13},{3,15... | collective-permute-start | bytes 294920 | tf_op jit(solution)/shard_map/ppermute | solution.py:52
  36.7 9.4 %collective-permute-start.10 = (bf16[64,768]{1,0:T(8,128)(2,1)}, bf16[64,768]{1,0:T(8,128)(2,1)}, u32[]{:S(2)}, u32[]{:S(2)}) collective-permute-start(bf16[64,768]{1,0:T(8,128)(2,1)} %get-tuple-element.44), channel_id=1, source_target_pairs={{0,14},{2,12},{4,10},{6,8},{8,6},{10,4},{12,2},{14,0},{1,15},{3,13... | collective-permute-start | bytes 294920 | tf_op jit(solution)/shard_map/ppermute | solution.py:52
  62.6 7.0 %collective-permute-start.18 = (bf16[64,768]{1,0:T(8,128)(2,1)S(1)}, bf16[64,768]{1,0:T(8,128)(2,1)S(1)}, u32[]{:S(2)}, u32[]{:S(2)}) collective-permute-start(bf16[64,768]{1,0:T(8,128)(2,1)S(1)} %get-tuple-element.42), channel_id=1, source_target_pairs={{0,4},{2,6},{4,0},{6,2},{8,12},{10,14},{12,8},{14,10},{1,5},{3,7},... | collective-permute-start | bytes 294920 | tf_op jit(solution)/shard_map/ppermute | solution.py:52
  64.2 7.7 %collective-permute-start.19 = (bf16[64,768]{1,0:T(8,128)(2,1)S(1)}, bf16[64,768]{1,0:T(8,128)(2,1)S(1)}, u32[]{:S(2)}, u32[]{:S(2)}) collective-permute-start(bf16[64,768]{1,0:T(8,128)(2,1)S(1)} %get-tuple-element.41), channel_id=1, source_target_pairs={{0,6},{2,4},{4,2},{6,0},{8,14},{10,12},{12,10},{14,8},{1,7},{3,5},... | collective-permute-start | bytes 294920 | tf_op jit(solution)/shard_map/ppermute | solution.py:52
  65.9 7.2 %collective-permute-start.21 = (bf16[64,768]{1,0:T(8,128)(2,1)S(1)}, bf16[64,768]{1,0:T(8,128)(2,1)S(1)}, u32[]{:S(2)}, u32[]{:S(2)}) collective-permute-start(bf16[64,768]{1,0:T(8,128)(2,1)S(1)} %get-tuple-element.39), channel_id=1, source_target_pairs={{0,10},{2,8},{4,14},{6,12},{8,2},{10,0},{12,6},{14,4},{1,11},{3,9}... | collective-permute-start | bytes 294920 | tf_op jit(solution)/shard_map/ppermute | solution.py:52
  67.7 8.0 %collective-permute-start.22 = (bf16[64,768]{1,0:T(8,128)(2,1)S(1)}, bf16[64,768]{1,0:T(8,128)(2,1)S(1)}, u32[]{:S(2)}, u32[]{:S(2)}) collective-permute-start(bf16[64,768]{1,0:T(8,128)(2,1)S(1)} %get-tuple-element.38), channel_id=1, source_target_pairs={{0,12},{2,14},{4,8},{6,10},{8,4},{10,6},{12,0},{14,2},{1,13},{3,15... | collective-permute-start | bytes 294920 | tf_op jit(solution)/shard_map/ppermute | solution.py:52
  69.6 7.5 %collective-permute-start.23 = (bf16[64,768]{1,0:T(8,128)(2,1)S(1)}, bf16[64,768]{1,0:T(8,128)(2,1)S(1)}, u32[]{:S(2)}, u32[]{:S(2)}) collective-permute-start(bf16[64,768]{1,0:T(8,128)(2,1)S(1)} %get-tuple-element.37), channel_id=1, source_target_pairs={{0,14},{2,12},{4,10},{6,8},{8,6},{10,4},{12,2},{14,0},{1,15},{3,13... | collective-permute-start | bytes 294920 | tf_op jit(solution)/shard_map/ppermute | solution.py:52
  86.2 6.7 %collective-permute-start.35 = (bf16[64,768]{1,0:T(8,128)(2,1)S(1)}, bf16[64,768]{1,0:T(8,128)(2,1)S(1)}, u32[]{:S(2)}, u32[]{:S(2)}) collective-permute-start(bf16[64,768]{1,0:T(8,128)(2,1)S(1)} %get-tuple-element.35), channel_id=1, source_target_pairs={{0,4},{2,6},{4,0},{6,2},{8,12},{10,14},{12,8},{14,10},{1,5},{3,7},... | collective-permute-start | bytes 294920 | tf_op jit(solution)/shard_map/ppermute | solution.py:52
  87.2 7.6 %collective-permute-start.36 = (bf16[64,768]{1,0:T(8,128)(2,1)S(1)}, bf16[64,768]{1,0:T(8,128)(2,1)S(1)}, u32[]{:S(2)}, u32[]{:S(2)}) collective-permute-start(bf16[64,768]{1,0:T(8,128)(2,1)S(1)} %get-tuple-element.34), channel_id=1, source_target_pairs={{0,6},{2,4},{4,2},{6,0},{8,14},{10,12},{12,10},{14,8},{1,7},{3,5},... | collective-permute-start | bytes 294920 | tf_op jit(solution)/shard_map/ppermute | solution.py:52
  88.8 7.0 %collective-permute-start.37 = (bf16[64,768]{1,0:T(8,128)(2,1)S(1)}, bf16[64,768]{1,0:T(8,128)(2,1)S(1)}, u32[]{:S(2)}, u32[]{:S(2)}) collective-permute-start(bf16[64,768]{1,0:T(8,128)(2,1)S(1)} %get-tuple-element.33), channel_id=1, source_target_pairs={{0,8},{2,10},{4,12},{6,14},{8,0},{10,2},{12,4},{14,6},{1,9},{3,11}... | collective-permute-start | bytes 294920 | tf_op jit(solution)/shard_map/ppermute | solution.py:52
  89.8 7.3 %collective-permute-start.38 = (bf16[64,768]{1,0:T(8,128)(2,1)S(1)}, bf16[64,768]{1,0:T(8,128)(2,1)S(1)}, u32[]{:S(2)}, u32[]{:S(2)}) collective-permute-start(bf16[64,768]{1,0:T(8,128)(2,1)S(1)} %get-tuple-element.32), channel_id=1, source_target_pairs={{0,10},{2,8},{4,14},{6,12},{8,2},{10,0},{12,6},{14,4},{1,11},{3,9}... | collective-permute-start | bytes 294920 | tf_op jit(solution)/shard_map/ppermute | solution.py:52
  91.2 7.3 %collective-permute-start.39 = (bf16[64,768]{1,0:T(8,128)(2,1)S(1)}, bf16[64,768]{1,0:T(8,128)(2,1)S(1)}, u32[]{:S(2)}, u32[]{:S(2)}) collective-permute-start(bf16[64,768]{1,0:T(8,128)(2,1)S(1)} %get-tuple-element.31), channel_id=1, source_target_pairs={{0,12},{2,14},{4,8},{6,10},{8,4},{10,6},{12,0},{14,2},{1,13},{3,15... | collective-permute-start | bytes 294920 | tf_op jit(solution)/shard_map/ppermute | solution.py:52
  92.9 7.2 %collective-permute-start.40 = (bf16[64,768]{1,0:T(8,128)(2,1)S(1)}, bf16[64,768]{1,0:T(8,128)(2,1)S(1)}, u32[]{:S(2)}, u32[]{:S(2)}) collective-permute-start(bf16[64,768]{1,0:T(8,128)(2,1)S(1)} %get-tuple-element.30), channel_id=1, source_target_pairs={{0,14},{2,12},{4,10},{6,8},{8,6},{10,4},{12,2},{14,0},{1,15},{3,13... | collective-permute-start | bytes 294920 | tf_op jit(solution)/shard_map/ppermute | solution.py:52
  94.8 7.7 %collective-permute-start.26 = (bf16[64,768]{1,0:T(8,128)(2,1)S(1)}, bf16[64,768]{1,0:T(8,128)(2,1)S(1)}, u32[]{:S(2)}, u32[]{:S(2)}) collective-permute-start(bf16[64,768]{1,0:T(8,128)(2,1)S(1)} %get-tuple-element.29), channel_id=1, source_target_pairs={{0,2},{2,0},{4,6},{6,4},{8,10},{10,8},{12,14},{14,12},{1,3},{3,1},... | collective-permute-start | bytes 294920 | tf_op jit(solution)/shard_map/ppermute | solution.py:52
  95.8 8.6 %collective-permute-start.27 = (bf16[64,768]{1,0:T(8,128)(2,1)S(1)}, bf16[64,768]{1,0:T(8,128)(2,1)S(1)}, u32[]{:S(2)}, u32[]{:S(2)}) collective-permute-start(bf16[64,768]{1,0:T(8,128)(2,1)S(1)} %get-tuple-element.28), channel_id=1, source_target_pairs={{0,4},{2,6},{4,0},{6,2},{8,12},{10,14},{12,8},{14,10},{1,5},{3,7},... | collective-permute-start | bytes 294920 | tf_op jit(solution)/shard_map/ppermute | solution.py:52
  97.1 8.6 %collective-permute-start.28 = (bf16[64,768]{1,0:T(8,128)(2,1)S(1)}, bf16[64,768]{1,0:T(8,128)(2,1)S(1)}, u32[]{:S(2)}, u32[]{:S(2)}) collective-permute-start(bf16[64,768]{1,0:T(8,128)(2,1)S(1)} %get-tuple-element.27), channel_id=1, source_target_pairs={{0,6},{2,4},{4,2},{6,0},{8,14},{10,12},{12,10},{14,8},{1,7},{3,5},... | collective-permute-start | bytes 294920 | tf_op jit(solution)/shard_map/ppermute | solution.py:52
  98.5 7.3 %collective-permute-start.29 = (bf16[64,768]{1,0:T(8,128)(2,1)S(1)}, bf16[64,768]{1,0:T(8,128)(2,1)S(1)}, u32[]{:S(2)}, u32[]{:S(2)}) collective-permute-start(bf16[64,768]{1,0:T(8,128)(2,1)S(1)} %get-tuple-element.26), channel_id=1, source_target_pairs={{0,8},{2,10},{4,12},{6,14},{8,0},{10,2},{12,4},{14,6},{1,9},{3,11}... | collective-permute-start | bytes 294920 | tf_op jit(solution)/shard_map/ppermute | solution.py:52
  100.1 6.6 %collective-permute-start.30 = (bf16[64,768]{1,0:T(8,128)(2,1)S(1)}, bf16[64,768]{1,0:T(8,128)(2,1)S(1)}, u32[]{:S(2)}, u32[]{:S(2)}) collective-permute-start(bf16[64,768]{1,0:T(8,128)(2,1)S(1)} %get-tuple-element.25), channel_id=1, source_target_pairs={{0,10},{2,8},{4,14},{6,12},{8,2},{10,0},{12,6},{14,4},{1,11},{3,9}... | collective-permute-start | bytes 294920 | tf_op jit(solution)/shard_map/ppermute | solution.py:52
  102.5 6.8 %collective-permute-start.31 = (bf16[64,768]{1,0:T(8,128)(2,1)S(1)}, bf16[64,768]{1,0:T(8,128)(2,1)S(1)}, u32[]{:S(2)}, u32[]{:S(2)}) collective-permute-start(bf16[64,768]{1,0:T(8,128)(2,1)S(1)} %get-tuple-element.24), channel_id=1, source_target_pairs={{0,12},{2,14},{4,8},{6,10},{8,4},{10,6},{12,0},{14,2},{1,13},{3,15... | collective-permute-start | bytes 294920 | tf_op jit(solution)/shard_map/ppermute | solution.py:52
  (38 other events, 186.5 us)

commit v11 on v7

--- a/solution.py
+++ b/solution.py
@@ -252,13 +252,14 @@
     outgoing = jnp.dot(dispatch, normed, preferred_element_type=jnp.float32).astype(jnp.bfloat16)
     arrived = exchange(outgoing.reshape(experts, capacity, feat_part), half_count)
     flat_rows = lax.optimization_barrier(arrived.reshape(buffer_len, feat_part))
-    group_rows = buffer_len // 2
+    group_count = 4 if buffer_len % 4 == 0 else 1
+    group_rows = buffer_len // group_count
     summed = jnp.concatenate(
         [
             expert_block(
                 flat_rows[start : start + group_rows], gate_w[0], up_w[0], down_w[0]
             )
-            for start in (0, group_rows)
+            for start in range(0, buffer_len, group_rows)
         ],
         axis=0,
     )

time: 88.9 us -> 89 us (level)
  waiting for transfers between devices: 31.2 us -> 28.9 us
  matrix products: 16.5 us -> 18.5 us
  starting transfers between devices: 23.7 us -> 24.9 us
    ppermute x14, waiting for transfers between devices: 29 us -> 26.7 us  [exchange(): pieces.append(lax.ppermute(chunks[step], 'el', perm=pairs))]
    dot_general x8 -> x16, matrix products: 4.67 us -> 6.16 us  [half_product(): return jnp.dot(x, weight, preferred_element_type=jnp.float32)]
    ppermute x2 -> x4, starting transfers between devices: 0.14 us -> 1.08 us  [expert_block(): rows_other = lax.ppermute(rows, 'tp', perm=swap)]
    unnamed x36, local copies, waits for them, and re-layouts: 3.93 us -> 3.04 us
    dot_general x4 -> x8, matrix products: 2.51 us -> 2.95 us  [down_product(): jnp.dot(hidden, weight, preferred_element_type=jnp.float32)]
  transfers between devices with their start and end apart: 23 -> 27, of which waited for: 13 -> 14; matrix products, arithmetic and copies ran while one was open for 14% -> 13% of each run, Pallas kernels for 0% -> 0%
where the time goes in v11:
time: 89 us; the launch traced here: 88.6 us
  waiting for transfers between devices  28.9 us (32%)
  starting transfers between devices  24.9 us (28%)
  matrix products  18.5 us (21%)
  local copies, waits for them, and re-layouts  8.2 us (9%)
  other arithmetic  7.51 us (8%)
    ppermute x14, waiting for transfers between devices, exchange(): pieces.append(lax.ppermute(chunks[step], 'el', perm=pairs))  26.7 us
    ppermute x14, starting transfers between devices, exchange(): pieces.append(lax.ppermute(chunks[step], 'el', perm=pairs))  21 us
    dot_general x16, matrix products, half_product(): return jnp.dot(x, weight, preferred_element_type=jnp.float32)  6.16 us
    dot_general x2, matrix products, one_group(): jnp.einsum('rgd,ld->rgl', head_rows, head_keys, preferred_element_type=jn...  3.84 us
    gather x1, local copies, waits for them, and re-layouts, one_group(): page_row_block = group_pages[local_table.reshape(-1)]  3.34 us
    unnamed x36, local copies, waits for them, and re-layouts  3.04 us
    dot_general x8, matrix products, down_product(): jnp.dot(hidden, weight, preferred_element_type=jnp.float32)  2.95 us
    dot_general x2, matrix products, one_group(): jnp.einsum('rgl,ld->rgd', soft.astype(jnp.bfloat16), head_values, preferr...  2.18 us
  transfers between devices with their start and end apart: 27, of which 14 were waited for; matrix products, arithmetic and copies ran while one was open for 13% of the time, Pallas kernels for 0%

profile of v11, /device:TPU:0, one launch (start us, length us, event | category | flops | bytes accessed | tf_op | source)
XLA Modules:
  0.0 88.6 jit_solution(12963720791794701552)
XLA Ops:
  4.2 3.3 %gather_fusion = bf16[96,16,512]{2,1,0:T(8,128)(2,1)} fusion(bf16[96,16,512]{2,1,0:T(8,128)(2,1)} %bitcast.233, s32[1024]{0:T(1024)S(1)} %pad_clamp_fusion), kind=kCustom, calls=%fused_computation | custom fusion | bytes 3146112 | tf_op jit(solution)/shard_map/while/body/eval_jaxpr/gather | solution.py:170
  8.5 1.9 %fusion.3 = (f32[128,6]{0,1:T(8,128)S(1)}, f32[1536,128,6]{1,0,2:T(8,128)S(1)}) fusion(pred[128,1536]{0,1:T(8,128)(4,1)S(1)} %compare_and_fusion, bf16[128,6,128]{0,2,1:T(8,128)(2,1)S(1)} %bitcast.235, bf16[1536,512]{1,0:T(8,128)(2,1)} %bitcast.228), kind=kOutput, calls=%fused_computation.8 | convolution fusion | flops 305528064 | bytes 5508096 | tf_op jit(solution)/shard_map/while/body/eval_jaxpr/rgd,ld->rgl/dot_general | solution.py:195
  10.5 1.9 %fusion.6 = (bf16[128,6]{0,1:T(8,128)(2,1)S(1)}, f32[128,6]{0,1:T(8,128)S(1)}, f32[1536,128,6]{1,0,2:T(8,128)S(1)}) fusion(f32[1536,128,6]{1,0,2:T(8,128)S(1)} %get-tuple-element.60, f32[128,6]{0,1:T(8,128)S(1)} %get-tuple-element.59, pred[128,1536]{0,1:T(8,128)(4,1)S(1)} %compare_and_fusion, bf16[128,6,128]{0,2,1:T(8,128)(2,1)S(1)} %bitcast.236, ...), kind=kOutput, calls=%fused_computation.11 | convolution fusion | flops 310245888 | bytes 10232320 | tf_op jit(solution)/shard_map/while/body/eval_jaxpr/rgd,ld->rgl/dot_general | solution.py:195
  19.2 1.2 %divide_convert_fusion = bf16[128,2,6,128]{0,3,2,1:T(8,128)(2,1)S(1)} fusion(bf16[128,2,6,128]{0,3,2,1:T(8,128)(2,1)} %collective-permute-done.1, f32[128,2,6]{0,2,1:T(8,128)S(1)} %get-tuple-element.57, f32[128,2,6]{0,2,1:T(8,128)S(1)} %get-tuple-element.58, f32[128,2,6]{0,2,1:T(8,128)S(1)} %get-tuple-element.56, bf16[128,1,6,128]{0,3,2,1:T(8,128)(2,1)S(1)} %fusion.35, ...), kind=kLoop, calls=%fused_computation.66 | loop fusion | flops 1572864 | bytes 1198080 | tf_op jit(solution)/shard_map/convert_element_type | solution.py:221
  20.4 1.5 %multiply_reduce_fusion.1 = (f32[128]{0:T(128)S(1)}, f32[128,768]{1,0:T(8,128)S(1)}) fusion(bf16[128,1536]{0,1:T(8,128)(2,1)S(1)} %bitcast.234, bf16[1536,768]{1,0:T(8,128)(2,1)S(1)} %copy-done, bf16[128,768]{1,0:T(8,128)(2,1)} %param.14), kind=kOutput, calls=%fused_computation.110 | convolution fusion | flops 302382976 | bytes 3342848 | tf_op jit(solution)/shard_map/dot_general | solution.py:223
  23.9 2.9 %collective-permute-start.4 = (bf16[128,768]{1,0:T(8,128)(2,1)S(1)}, bf16[128,768]{1,0:T(8,128)(2,1)S(1)}, u32[]{:S(2)}, u32[]{:S(2)}) collective-permute-start(bf16[128,768]{1,0:T(8,128)(2,1)S(1)} %get-tuple-element.47), channel_id=1, source_target_pairs={{0,2},{2,0},{4,6},{6,4},{8,10},{10,8},{12,14},{14,12},{1,3},{3,1},... | collective-permute-start | bytes 589832 | tf_op jit(solution)/shard_map/ppermute | solution.py:52
  26.8 1.5 %collective-permute-start.5 = (bf16[128,768]{1,0:T(8,128)(2,1)S(1)}, bf16[128,768]{1,0:T(8,128)(2,1)S(1)}, u32[]{:S(2)}, u32[]{:S(2)}) collective-permute-start(bf16[128,768]{1,0:T(8,128)(2,1)S(1)} %get-tuple-element.46), channel_id=1, source_target_pairs={{0,4},{2,6},{4,0},{6,2},{8,12},{10,14},{12,8},{14,10},{1,5},{3,7},... | collective-permute-start | bytes 589832 | tf_op jit(solution)/shard_map/ppermute | solution.py:52
  28.3 2.0 %collective-permute-start.7 = (bf16[128,768]{1,0:T(8,128)(2,1)S(1)}, bf16[128,768]{1,0:T(8,128)(2,1)S(1)}, u32[]{:S(2)}, u32[]{:S(2)}) collective-permute-start(bf16[128,768]{1,0:T(8,128)(2,1)S(1)} %get-tuple-element.44), channel_id=1, source_target_pairs={{0,8},{2,10},{4,12},{6,14},{8,0},{10,2},{12,4},{14,6},{1,9},{3,11}... | collective-permute-start | bytes 589832 | tf_op jit(solution)/shard_map/ppermute | solution.py:52
  30.4 1.4 %collective-permute-start.8 = (bf16[128,768]{1,0:T(8,128)(2,1)S(1)}, bf16[128,768]{1,0:T(8,128)(2,1)S(1)}, u32[]{:S(2)}, u32[]{:S(2)}) collective-permute-start(bf16[128,768]{1,0:T(8,128)(2,1)S(1)} %get-tuple-element.42), channel_id=1, source_target_pairs={{0,10},{2,8},{4,14},{6,12},{8,2},{10,0},{12,6},{14,4},{1,11},{3,9}... | collective-permute-start | bytes 589832 | tf_op jit(solution)/shard_map/ppermute | solution.py:52
  32.5 3.1 %collective-permute-start.9 = (bf16[128,768]{1,0:T(8,128)(2,1)S(1)}, bf16[128,768]{1,0:T(8,128)(2,1)S(1)}, u32[]{:S(2)}, u32[]{:S(2)}) collective-permute-start(bf16[128,768]{1,0:T(8,128)(2,1)S(1)} %get-tuple-element.40), channel_id=1, source_target_pairs={{0,12},{2,14},{4,8},{6,10},{8,4},{10,6},{12,0},{14,2},{1,13},{3,15... | collective-permute-start | bytes 589832 | tf_op jit(solution)/shard_map/ppermute | solution.py:52
  36.0 1.3 %collective-permute-start.10 = (bf16[128,768]{1,0:T(8,128)(2,1)S(1)}, bf16[128,768]{1,0:T(8,128)(2,1)S(1)}, u32[]{:S(2)}, u32[]{:S(2)}) collective-permute-start(bf16[128,768]{1,0:T(8,128)(2,1)S(1)} %get-tuple-element.29), channel_id=1, source_target_pairs={{0,14},{2,12},{4,10},{6,8},{8,6},{10,4},{12,2},{14,0},{1,15},{3,13... | collective-permute-start | bytes 589832 | tf_op jit(solution)/shard_map/ppermute | solution.py:52
  37.3 3.5 %collective-permute-done.6 = bf16[128,768]{1,0:T(8,128)(2,1)S(1)} collective-permute-done((bf16[128,768]{1,0:T(8,128)(2,1)S(1)}, bf16[128,768]{1,0:T(8,128)(2,1)S(1)}, u32[]{:S(2)}, u32[]{:S(2)}) %collective-permute-start.6) | collective-permute-done | bytes 196640 | tf_op jit(solution)/shard_map/ppermute | solution.py:52
  41.8 4.2 %collective-permute-done.9 = bf16[128,768]{1,0:T(8,128)(2,1)S(1)} collective-permute-done((bf16[128,768]{1,0:T(8,128)(2,1)S(1)}, bf16[128,768]{1,0:T(8,128)(2,1)S(1)}, u32[]{:S(2)}, u32[]{:S(2)}) %collective-permute-start.9) | collective-permute-done | bytes 196640 | tf_op jit(solution)/shard_map/ppermute | solution.py:52
  46.0 3.5 %collective-permute-done.10 = bf16[128,768]{1,0:T(8,128)(2,1)S(1)} collective-permute-done((bf16[128,768]{1,0:T(8,128)(2,1)S(1)}, bf16[128,768]{1,0:T(8,128)(2,1)S(1)}, u32[]{:S(2)}, u32[]{:S(2)}) %collective-permute-start.10) | collective-permute-done | bytes 196640 | tf_op jit(solution)/shard_map/ppermute | solution.py:52
  49.6 1.1 %copy-done.1 = bf16[1,1536,384]{2,1,0:T(8,128)(2,1)S(1)} copy-done((bf16[1,1536,384]{2,1,0:T(8,128)(2,1)S(1)}, bf16[1,1536,384]{2,1,0:T(8,128)(2,1)}, u32[]{:S(2)}) %copy-start.1) | copy-done | bytes 1179672
  62.9 1.6 %collective-permute-start.24 = (bf16[128,768]{1,0:T(8,128)(2,1)S(1)}, bf16[128,768]{1,0:T(8,128)(2,1)S(1)}, u32[]{:S(2)}, u32[]{:S(2)}) collective-permute-start(bf16[128,768]{1,0:T(8,128)(2,1)S(1)} %get-tuple-element.49), channel_id=1, source_target_pairs={{0,12},{2,14},{4,8},{6,10},{8,4},{10,6},{12,0},{14,2},{1,13},{3,15... | collective-permute-start | bytes 589832 | tf_op jit(solution)/shard_map/ppermute | solution.py:52
  65.3 1.6 %collective-permute-start.16 = (bf16[128,768]{1,0:T(8,128)(2,1)S(1)}, bf16[128,768]{1,0:T(8,128)(2,1)S(1)}, u32[]{:S(2)}, u32[]{:S(2)}) collective-permute-start(bf16[128,768]{1,0:T(8,128)(2,1)S(1)} %get-tuple-element.53), channel_id=1, source_target_pairs={{0,4},{2,6},{4,0},{6,2},{8,12},{10,14},{12,8},{14,10},{1,5},{3,7},... | collective-permute-start | bytes 589832 | tf_op jit(solution)/shard_map/ppermute | solution.py:52
  67.6 1.4 %collective-permute-start.17 = (bf16[128,768]{1,0:T(8,128)(2,1)S(1)}, bf16[128,768]{1,0:T(8,128)(2,1)S(1)}, u32[]{:S(2)}, u32[]{:S(2)}) collective-permute-start(bf16[128,768]{1,0:T(8,128)(2,1)S(1)} %get-tuple-element.52), channel_id=1, source_target_pairs={{0,6},{2,4},{4,2},{6,0},{8,14},{10,12},{12,10},{14,8},{1,7},{3,5},... | collective-permute-start | bytes 589832 | tf_op jit(solution)/shard_map/ppermute | solution.py:52
  69.1 5.8 %collective-permute-done.13 = bf16[128,768]{1,0:T(8,128)(2,1)S(1)} collective-permute-done((bf16[128,768]{1,0:T(8,128)(2,1)S(1)}, bf16[128,768]{1,0:T(8,128)(2,1)S(1)}, u32[]{:S(2)}, u32[]{:S(2)}) %collective-permute-start.13) | collective-permute-done | bytes 196640 | tf_op jit(solution)/shard_map/ppermute | solution.py:52
  74.9 1.6 %collective-permute-start.21 = (bf16[128,768]{1,0:T(8,128)(2,1)S(1)}, bf16[128,768]{1,0:T(8,128)(2,1)S(1)}, u32[]{:S(2)}, u32[]{:S(2)}) collective-permute-start(bf16[128,768]{1,0:T(8,128)(2,1)S(1)} %get-tuple-element.50), channel_id=1, source_target_pairs={{0,10},{2,8},{4,14},{6,12},{8,2},{10,0},{12,6},{14,4},{1,11},{3,9}... | collective-permute-start | bytes 589832 | tf_op jit(solution)/shard_map/ppermute | solution.py:52
  77.0 1.5 %collective-permute-start.25 = (bf16[128,768]{1,0:T(8,128)(2,1)S(1)}, bf16[128,768]{1,0:T(8,128)(2,1)S(1)}, u32[]{:S(2)}, u32[]{:S(2)}) collective-permute-start(bf16[128,768]{1,0:T(8,128)(2,1)S(1)} %get-tuple-element.48), channel_id=1, source_target_pairs={{0,14},{2,12},{4,10},{6,8},{8,6},{10,4},{12,2},{14,0},{1,15},{3,13... | collective-permute-start | bytes 589832 | tf_op jit(solution)/shard_map/ppermute | solution.py:52
  79.5 3.2 %collective-permute-done.21 = bf16[128,768]{1,0:T(8,128)(2,1)S(1)} collective-permute-done((bf16[128,768]{1,0:T(8,128)(2,1)S(1)}, bf16[128,768]{1,0:T(8,128)(2,1)S(1)}, u32[]{:S(2)}, u32[]{:S(2)}) %collective-permute-start.21) | collective-permute-done | bytes 196640 | tf_op jit(solution)/shard_map/ppermute | solution.py:52
  82.7 3.0 %collective-permute-done.25 = bf16[128,768]{1,0:T(8,128)(2,1)S(1)} collective-permute-done((bf16[128,768]{1,0:T(8,128)(2,1)S(1)}, bf16[128,768]{1,0:T(8,128)(2,1)S(1)}, u32[]{:S(2)}, u32[]{:S(2)}) %collective-permute-start.25) | collective-permute-done | bytes 196640 | tf_op jit(solution)/shard_map/ppermute | solution.py:52
  86.7 1.1 %collective-permute-done.26 = f32[128]{0:T(128)S(1)} collective-permute-done((f32[128]{0:T(128)S(1)}, f32[128]{0:T(128)S(1)}, u32[]{:S(2)}, u32[]{:S(2)}) %collective-permute-start.26) | collective-permute-done | bytes 544 | tf_op jit(solution)/shard_map/ppermute | solution.py:94
  (141 shorter events, 33.0 us)
Async XLA Ops:
  13.4 5.5 %collective-permute-start.2 = (bf16[128,2,6]{0,2,1:T(8,128)(2,1)S(1)}, bf16[128,2,6]{0,2,1:T(8,128)(2,1)S(1)}, u32[]{:S(2)}, u32[]{:S(2)}) collective-permute-start(bf16[128,2,6]{0,2,1:T(8,128)(2,1)S(1)} %pad_maximum_fusion.2), channel_id=1, source_target_pairs={{0,1},{1,0},{2,3},{3,2},{4,5},{5,4},{6,7},{7,6},{8,9},{9,8},{10,11... | collective-permute-start | bytes 9224 | tf_op jit(solution)/shard_map/ppermute | solution.py:18
  13.9 4.9 %collective-permute-start = (bf16[128,2,6]{0,2,1:T(8,128)(2,1)S(1)}, bf16[128,2,6]{0,2,1:T(8,128)(2,1)S(1)}, u32[]{:S(2)}, u32[]{:S(2)}) collective-permute-start(bf16[128,2,6]{0,2,1:T(8,128)(2,1)S(1)} %pad_maximum_fusion.1), channel_id=1, source_target_pairs={{0,1},{1,0},{2,3},{3,2},{4,5},{5,4},{6,7},{7,6},{8,9},{9,8},{10,11... | collective-permute-start | bytes 9224 | tf_op jit(solution)/shard_map/ppermute | solution.py:18
  17.0 2.1 %collective-permute-start.1 = (bf16[128,2,6,128]{0,3,2,1:T(8,128)(2,1)}, bf16[128,2,6,128]{0,3,2,1:T(8,128)(2,1)}, u32[]{:S(2)}, u32[]{:S(2)}) collective-permute-start(bf16[128,2,6,128]{0,3,2,1:T(8,128)(2,1)} %pad_maximum_fusion), channel_id=1, source_target_pairs={{0,1},{1,0},{2,3},{3,2},{4,5},{5,4},{6,7},{7,6},{8,9},{9,8},{10,11... | collective-permute-start | bytes 1179656 | tf_op jit(solution)/shard_map/ppermute | solution.py:18
  23.9 8.5 %collective-permute-start.4 = (bf16[128,768]{1,0:T(8,128)(2,1)S(1)}, bf16[128,768]{1,0:T(8,128)(2,1)S(1)}, u32[]{:S(2)}, u32[]{:S(2)}) collective-permute-start(bf16[128,768]{1,0:T(8,128)(2,1)S(1)} %get-tuple-element.47), channel_id=1, source_target_pairs={{0,2},{2,0},{4,6},{6,4},{8,10},{10,8},{12,14},{14,12},{1,3},{3,1},... | collective-permute-start | bytes 589832 | tf_op jit(solution)/shard_map/ppermute | solution.py:52
  26.8 9.2 %collective-permute-start.5 = (bf16[128,768]{1,0:T(8,128)(2,1)S(1)}, bf16[128,768]{1,0:T(8,128)(2,1)S(1)}, u32[]{:S(2)}, u32[]{:S(2)}) collective-permute-start(bf16[128,768]{1,0:T(8,128)(2,1)S(1)} %get-tuple-element.46), channel_id=1, source_target_pairs={{0,4},{2,6},{4,0},{6,2},{8,12},{10,14},{12,8},{14,10},{1,5},{3,7},... | collective-permute-start | bytes 589832 | tf_op jit(solution)/shard_map/ppermute | solution.py:52
  28.3 12.4 %collective-permute-start.6 = (bf16[128,768]{1,0:T(8,128)(2,1)S(1)}, bf16[128,768]{1,0:T(8,128)(2,1)S(1)}, u32[]{:S(2)}, u32[]{:S(2)}) collective-permute-start(bf16[128,768]{1,0:T(8,128)(2,1)S(1)} %get-tuple-element.45), channel_id=1, source_target_pairs={{0,6},{2,4},{4,2},{6,0},{8,14},{10,12},{12,10},{14,8},{1,7},{3,5},... | collective-permute-start | bytes 589832 | tf_op jit(solution)/shard_map/ppermute | solution.py:52
  28.3 12.4 %collective-permute-start.7 = (bf16[128,768]{1,0:T(8,128)(2,1)S(1)}, bf16[128,768]{1,0:T(8,128)(2,1)S(1)}, u32[]{:S(2)}, u32[]{:S(2)}) collective-permute-start(bf16[128,768]{1,0:T(8,128)(2,1)S(1)} %get-tuple-element.44), channel_id=1, source_target_pairs={{0,8},{2,10},{4,12},{6,14},{8,0},{10,2},{12,4},{14,6},{1,9},{3,11}... | collective-permute-start | bytes 589832 | tf_op jit(solution)/shard_map/ppermute | solution.py:52
  30.4 11.4 %collective-permute-start.8 = (bf16[128,768]{1,0:T(8,128)(2,1)S(1)}, bf16[128,768]{1,0:T(8,128)(2,1)S(1)}, u32[]{:S(2)}, u32[]{:S(2)}) collective-permute-start(bf16[128,768]{1,0:T(8,128)(2,1)S(1)} %get-tuple-element.42), channel_id=1, source_target_pairs={{0,10},{2,8},{4,14},{6,12},{8,2},{10,0},{12,6},{14,4},{1,11},{3,9}... | collective-permute-start | bytes 589832 | tf_op jit(solution)/shard_map/ppermute | solution.py:52
  32.5 13.5 %collective-permute-start.9 = (bf16[128,768]{1,0:T(8,128)(2,1)S(1)}, bf16[128,768]{1,0:T(8,128)(2,1)S(1)}, u32[]{:S(2)}, u32[]{:S(2)}) collective-permute-start(bf16[128,768]{1,0:T(8,128)(2,1)S(1)} %get-tuple-element.40), channel_id=1, source_target_pairs={{0,12},{2,14},{4,8},{6,10},{8,4},{10,6},{12,0},{14,2},{1,13},{3,15... | collective-permute-start | bytes 589832 | tf_op jit(solution)/shard_map/ppermute | solution.py:52
  36.0 13.5 %collective-permute-start.10 = (bf16[128,768]{1,0:T(8,128)(2,1)S(1)}, bf16[128,768]{1,0:T(8,128)(2,1)S(1)}, u32[]{:S(2)}, u32[]{:S(2)}) collective-permute-start(bf16[128,768]{1,0:T(8,128)(2,1)S(1)} %get-tuple-element.29), channel_id=1, source_target_pairs={{0,14},{2,12},{4,10},{6,8},{8,6},{10,4},{12,2},{14,0},{1,15},{3,13... | collective-permute-start | bytes 589832 | tf_op jit(solution)/shard_map/ppermute | solution.py:52
  53.1 3.9 %collective-permute-start.18 = (bf16[256,768]{1,0:T(8,128)(2,1)S(1)}, bf16[256,768]{1,0:T(8,128)(2,1)S(1)}, u32[]{:S(2)}, u32[]{:S(2)}) collective-permute-start(bf16[256,768]{1,0:T(8,128)(2,1)S(1)} %get-tuple-element.26), channel_id=1, source_target_pairs={{0,1},{1,0},{2,3},{3,2},{4,5},{5,4},{6,7},{7,6},{8,9},{9,8},{10,11... | collective-permute-start | bytes 1179656 | tf_op jit(solution)/shard_map/ppermute | solution.py:70
  53.6 5.4 %collective-permute-start.14 = (bf16[256,768]{1,0:T(8,128)(2,1)S(1)}, bf16[256,768]{1,0:T(8,128)(2,1)S(1)}, u32[]{:S(2)}, u32[]{:S(2)}) collective-permute-start(bf16[256,768]{1,0:T(8,128)(2,1)S(1)} %get-tuple-element.27), channel_id=1, source_target_pairs={{0,1},{1,0},{2,3},{3,2},{4,5},{5,4},{6,7},{7,6},{8,9},{9,8},{10,11... | collective-permute-start | bytes 1179656 | tf_op jit(solution)/shard_map/ppermute | solution.py:70
  53.7 7.0 %collective-permute-start.11 = (bf16[256,768]{1,0:T(8,128)(2,1)S(1)}, bf16[256,768]{1,0:T(8,128)(2,1)S(1)}, u32[]{:S(2)}, u32[]{:S(2)}) collective-permute-start(bf16[256,768]{1,0:T(8,128)(2,1)S(1)} %get-tuple-element.28), channel_id=1, source_target_pairs={{0,1},{1,0},{2,3},{3,2},{4,5},{5,4},{6,7},{7,6},{8,9},{9,8},{10,11... | collective-permute-start | bytes 1179656 | tf_op jit(solution)/shard_map/ppermute | solution.py:70
  56.5 6.2 %collective-permute-start.23 = (bf16[256,768]{1,0:T(8,128)(2,1)S(1)}, bf16[256,768]{1,0:T(8,128)(2,1)S(1)}, u32[]{:S(2)}, u32[]{:S(2)}) collective-permute-start(bf16[256,768]{1,0:T(8,128)(2,1)S(1)} %convolution_convert_fusion.1), channel_id=1, source_target_pairs={{0,1},{1,0},{2,3},{3,2},{4,5},{5,4},{6,7},{7,6},{8,9},{9,8},{10,11... | collective-permute-start | bytes 1179656 | tf_op jit(solution)/shard_map/ppermute | solution.py:86
  58.2 6.3 %collective-permute-start.19 = (bf16[256,768]{1,0:T(8,128)(2,1)S(1)}, bf16[256,768]{1,0:T(8,128)(2,1)S(1)}, u32[]{:S(2)}, u32[]{:S(2)}) collective-permute-start(bf16[256,768]{1,0:T(8,128)(2,1)S(1)} %convolution_convert_fusion.3), channel_id=1, source_target_pairs={{0,1},{1,0},{2,3},{3,2},{4,5},{5,4},{6,7},{7,6},{8,9},{9,8},{10,11... | collective-permute-start | bytes 1179656 | tf_op jit(solution)/shard_map/ppermute | solution.py:86
  60.2 5.0 %collective-permute-start.15 = (bf16[256,768]{1,0:T(8,128)(2,1)S(1)}, bf16[256,768]{1,0:T(8,128)(2,1)S(1)}, u32[]{:S(2)}, u32[]{:S(2)}) collective-permute-start(bf16[256,768]{1,0:T(8,128)(2,1)S(1)} %convolution_convert_fusion.5), channel_id=1, source_target_pairs={{0,1},{1,0},{2,3},{3,2},{4,5},{5,4},{6,7},{7,6},{8,9},{9,8},{10,11... | collective-permute-start | bytes 1179656 | tf_op jit(solution)/shard_map/ppermute | solution.py:86
  61.9 5.0 %collective-permute-start.12 = (bf16[256,768]{1,0:T(8,128)(2,1)S(1)}, bf16[256,768]{1,0:T(8,128)(2,1)S(1)}, u32[]{:S(2)}, u32[]{:S(2)}) collective-permute-start(bf16[256,768]{1,0:T(8,128)(2,1)S(1)} %convolution_convert_fusion.7), channel_id=1, source_target_pairs={{0,1},{1,0},{2,3},{3,2},{4,5},{5,4},{6,7},{7,6},{8,9},{9,8},{10,11... | collective-permute-start | bytes 1179656 | tf_op jit(solution)/shard_map/ppermute | solution.py:86
  62.9 19.8 %collective-permute-start.24 = (bf16[128,768]{1,0:T(8,128)(2,1)S(1)}, bf16[128,768]{1,0:T(8,128)(2,1)S(1)}, u32[]{:S(2)}, u32[]{:S(2)}) collective-permute-start(bf16[128,768]{1,0:T(8,128)(2,1)S(1)} %get-tuple-element.49), channel_id=1, source_target_pairs={{0,12},{2,14},{4,8},{6,10},{8,4},{10,6},{12,0},{14,2},{1,13},{3,15... | collective-permute-start | bytes 589832 | tf_op jit(solution)/shard_map/ppermute | solution.py:52
  64.6 14.8 %collective-permute-start.20 = (bf16[128,768]{1,0:T(8,128)(2,1)S(1)}, bf16[128,768]{1,0:T(8,128)(2,1)S(1)}, u32[]{:S(2)}, u32[]{:S(2)}) collective-permute-start(bf16[128,768]{1,0:T(8,128)(2,1)S(1)} %get-tuple-element.51), channel_id=1, source_target_pairs={{0,8},{2,10},{4,12},{6,14},{8,0},{10,2},{12,4},{14,6},{1,9},{3,11}... | collective-permute-start | bytes 589832 | tf_op jit(solution)/shard_map/ppermute | solution.py:52
  65.3 11.7 %collective-permute-start.16 = (bf16[128,768]{1,0:T(8,128)(2,1)S(1)}, bf16[128,768]{1,0:T(8,128)(2,1)S(1)}, u32[]{:S(2)}, u32[]{:S(2)}) collective-permute-start(bf16[128,768]{1,0:T(8,128)(2,1)S(1)} %get-tuple-element.53), channel_id=1, source_target_pairs={{0,4},{2,6},{4,0},{6,2},{8,12},{10,14},{12,8},{14,10},{1,5},{3,7},... | collective-permute-start | bytes 589832 | tf_op jit(solution)/shard_map/ppermute | solution.py:52
  67.0 7.9 %collective-permute-start.13 = (bf16[128,768]{1,0:T(8,128)(2,1)S(1)}, bf16[128,768]{1,0:T(8,128)(2,1)S(1)}, u32[]{:S(2)}, u32[]{:S(2)}) collective-permute-start(bf16[128,768]{1,0:T(8,128)(2,1)S(1)} %slice.156), channel_id=1, source_target_pairs={{0,2},{2,0},{4,6},{6,4},{8,10},{10,8},{12,14},{14,12},{1,3},{3,1},... | collective-permute-start | bytes 589832 | tf_op jit(solution)/shard_map/ppermute | solution.py:52
  67.6 11.8 %collective-permute-start.17 = (bf16[128,768]{1,0:T(8,128)(2,1)S(1)}, bf16[128,768]{1,0:T(8,128)(2,1)S(1)}, u32[]{:S(2)}, u32[]{:S(2)}) collective-permute-start(bf16[128,768]{1,0:T(8,128)(2,1)S(1)} %get-tuple-element.52), channel_id=1, source_target_pairs={{0,6},{2,4},{4,2},{6,0},{8,14},{10,12},{12,10},{14,8},{1,7},{3,5},... | collective-permute-start | bytes 589832 | tf_op jit(solution)/shard_map/ppermute | solution.py:52
  74.9 7.8 %collective-permute-start.21 = (bf16[128,768]{1,0:T(8,128)(2,1)S(1)}, bf16[128,768]{1,0:T(8,128)(2,1)S(1)}, u32[]{:S(2)}, u32[]{:S(2)}) collective-permute-start(bf16[128,768]{1,0:T(8,128)(2,1)S(1)} %get-tuple-element.50), channel_id=1, source_target_pairs={{0,10},{2,8},{4,14},{6,12},{8,2},{10,0},{12,6},{14,4},{1,11},{3,9}... | collective-permute-start | bytes 589832 | tf_op jit(solution)/shard_map/ppermute | solution.py:52
  77.0 8.8 %collective-permute-start.25 = (bf16[128,768]{1,0:T(8,128)(2,1)S(1)}, bf16[128,768]{1,0:T(8,128)(2,1)S(1)}, u32[]{:S(2)}, u32[]{:S(2)}) collective-permute-start(bf16[128,768]{1,0:T(8,128)(2,1)S(1)} %get-tuple-element.48), channel_id=1, source_target_pairs={{0,14},{2,12},{4,10},{6,8},{8,6},{10,4},{12,2},{14,0},{1,15},{3,13... | collective-permute-start | bytes 589832 | tf_op jit(solution)/shard_map/ppermute | solution.py:52
  (12 other events, 44.4 us)

commit v12 on v7

--- a/solution.py
+++ b/solution.py
@@ -43,14 +43,17 @@
 
 
 def exchange(chunks, count):
-    pieces = [chunks[0]]
-    for step in range(1, count):
+    pieces = {0: chunks[0]}
+    steps = list(range(1, count))
+    if count & (count - 1) == 0:
+        steps.sort(key=lambda step: (bin(step).count("1"), step))
+    for step in steps:
         if count & (count - 1) == 0:
             pairs = [(i, i ^ step) for i in range(count)]
         else:
             pairs = [(i, (i + step) % count) for i in range(count)]
-        pieces.append(lax.ppermute(chunks[step], "el", perm=pairs))
-    return jnp.stack(pieces)
+        pieces[step] = lax.ppermute(chunks[step], "el", perm=pairs)
+    return jnp.stack([pieces[step] for step in range(count)])
 
 
 def expert_block(rows, gate_w, up_w, down_w):

time: 88.9 us -> 88.9 us (level)
  no operation moved by 1% of the time
where the time goes in v12:
time: 88.9 us; the launch traced here: 88.5 us
  waiting for transfers between devices  31.2 us (35%)
  starting transfers between devices  23.7 us (27%)
  matrix products  16.5 us (19%)
  local copies, waits for them, and re-layouts  9.06 us (10%)
  other arithmetic  7.52 us (8%)
    ppermute x14, waiting for transfers between devices, exchange(): pieces[step] = lax.ppermute(chunks[step], 'el', perm=pairs)  29 us
    ppermute x14, starting transfers between devices, exchange(): pieces[step] = lax.ppermute(chunks[step], 'el', perm=pairs)  21.4 us
    dot_general x8, matrix products, half_product(): return jnp.dot(x, weight, preferred_element_type=jnp.float32)  4.67 us
    unnamed x36, local copies, waits for them, and re-layouts  3.93 us
    dot_general x2, matrix products, one_group(): jnp.einsum('rgd,ld->rgl', head_rows, head_keys, preferred_element_type=jn...  3.85 us
    gather x1, local copies, waits for them, and re-layouts, one_group(): page_row_block = group_pages[local_table.reshape(-1)]  3.32 us
    dot_general x4, matrix products, down_product(): jnp.dot(hidden, weight, preferred_element_type=jnp.float32)  2.51 us
    dot_general x2, matrix products, one_group(): jnp.einsum('rgl,ld->rgd', soft.astype(jnp.bfloat16), head_values, preferr...  2.19 us
  transfers between devices with their start and end apart: 23, of which 13 were waited for; matrix products, arithmetic and copies ran while one was open for 14% of the time, Pallas kernels for 0%

profile of v12, /device:TPU:0, one launch (start us, length us, event | category | flops | bytes accessed | tf_op | source)
XLA Modules:
  0.0 88.5 jit_solution(5288920605972785651)
XLA Ops:
  4.2 3.3 %gather_fusion = bf16[96,16,512]{2,1,0:T(8,128)(2,1)} fusion(bf16[96,16,512]{2,1,0:T(8,128)(2,1)} %bitcast.189, s32[1024]{0:T(1024)S(1)} %pad_clamp_fusion), kind=kCustom, calls=%fused_computation | custom fusion | bytes 3146112 | tf_op jit(solution)/shard_map/while/body/eval_jaxpr/gather | solution.py:173
  8.5 1.9 %fusion.3 = (f32[128,6]{0,1:T(8,128)S(1)}, f32[1536,128,6]{1,0,2:T(8,128)S(1)}) fusion(pred[128,1536]{0,1:T(8,128)(4,1)S(1)} %compare_and_fusion, bf16[128,6,128]{0,2,1:T(8,128)(2,1)S(1)} %bitcast.191, bf16[1536,512]{1,0:T(8,128)(2,1)} %bitcast.184), kind=kOutput, calls=%fused_computation.8 | convolution fusion | flops 305528064 | bytes 5508096 | tf_op jit(solution)/shard_map/while/body/eval_jaxpr/rgd,ld->rgl/dot_general | solution.py:198
  10.5 1.9 %fusion.6 = (bf16[128,6]{0,1:T(8,128)(2,1)S(1)}, f32[128,6]{0,1:T(8,128)S(1)}, f32[1536,128,6]{1,0,2:T(8,128)S(1)}) fusion(f32[1536,128,6]{1,0,2:T(8,128)S(1)} %get-tuple-element.59, f32[128,6]{0,1:T(8,128)S(1)} %get-tuple-element.58, pred[128,1536]{0,1:T(8,128)(4,1)S(1)} %compare_and_fusion, bf16[128,6,128]{0,2,1:T(8,128)(2,1)S(1)} %bitcast.192, ...), kind=kOutput, calls=%fused_computation.11 | convolution fusion | flops 310245888 | bytes 10232320 | tf_op jit(solution)/shard_map/while/body/eval_jaxpr/rgd,ld->rgl/dot_general | solution.py:198
  14.0 1.1 %fusion.29 = bf16[128,1,6,128]{0,3,2,1:T(8,128)(2,1)S(1)} fusion(f32[1536,128,6]{1,0,2:T(8,128)S(1)} %get-tuple-element.60, f32[128,6]{0,1:T(8,128)S(1)} %get-tuple-element.24, pred[128,1536]{0,1:T(8,128)(4,1)S(1)} %compare_and_fusion, bf16[1536,512]{1,0:T(8,128)(2,1)S(1)} %bitcast.186), kind=kOutput, calls=%fused_computation.44 | convolution fusion | flops 306806784 | bytes 5509120 | tf_op jit(solution)/shard_map/while/body/eval_jaxpr/rgl,ld->rgd/dot_general | solution.py:204
  15.1 1.1 %fusion.32 = bf16[128,1,6,128]{0,3,2,1:T(8,128)(2,1)S(1)} fusion(f32[1536,128,6]{1,0,2:T(8,128)S(1)} %get-tuple-element.59, f32[128,6]{0,1:T(8,128)S(1)} %get-tuple-element.58, pred[128,1536]{0,1:T(8,128)(4,1)S(1)} %compare_and_fusion, bf16[1536,512]{1,0:T(8,128)(2,1)S(1)} %bitcast.187), kind=kOutput, calls=%fused_computation.45 | convolution fusion | flops 306806784 | bytes 5509120 | tf_op jit(solution)/shard_map/while/body/eval_jaxpr/rgl,ld->rgd/dot_general | solution.py:204
  19.2 1.2 %divide_convert_fusion = bf16[128,2,6,128]{0,3,2,1:T(8,128)(2,1)S(1)} fusion(bf16[128,2,6,128]{0,3,2,1:T(8,128)(2,1)} %collective-permute-done.1, f32[128,2,6]{0,2,1:T(8,128)S(1)} %get-tuple-element.56, f32[128,2,6]{0,2,1:T(8,128)S(1)} %get-tuple-element.57, f32[128,2,6]{0,2,1:T(8,128)S(1)} %get-tuple-element.55, bf16[128,1,6,128]{0,3,2,1:T(8,128)(2,1)S(1)} %fusion.29, ...), kind=kLoop, calls=%fused_computation.50 | loop fusion | flops 1572864 | bytes 1198080 | tf_op jit(solution)/shard_map/convert_element_type | solution.py:224
  20.4 1.5 %multiply_reduce_fusion.1 = (f32[128]{0:T(128)S(1)}, f32[128,768]{1,0:T(8,128)S(1)}) fusion(bf16[128,1536]{0,1:T(8,128)(2,1)S(1)} %bitcast.190, bf16[1536,768]{1,0:T(8,128)(2,1)S(1)} %copy-done, bf16[128,768]{1,0:T(8,128)(2,1)} %param.14), kind=kOutput, calls=%fused_computation.90 | convolution fusion | flops 302382976 | bytes 3342848 | tf_op jit(solution)/shard_map/dot_general | solution.py:226
  23.9 2.9 %collective-permute-start.4 = (bf16[128,768]{1,0:T(8,128)(2,1)S(1)}, bf16[128,768]{1,0:T(8,128)(2,1)S(1)}, u32[]{:S(2)}, u32[]{:S(2)}) collective-permute-start(bf16[128,768]{1,0:T(8,128)(2,1)S(1)} %get-tuple-element.45), channel_id=1, source_target_pairs={{0,2},{2,0},{4,6},{6,4},{8,10},{10,8},{12,14},{14,12},{1,3},{3,1},... | collective-permute-start | bytes 589832 | tf_op jit(solution)/shard_map/ppermute | solution.py:55
  26.8 1.5 %collective-permute-start.5 = (bf16[128,768]{1,0:T(8,128)(2,1)S(1)}, bf16[128,768]{1,0:T(8,128)(2,1)S(1)}, u32[]{:S(2)}, u32[]{:S(2)}) collective-permute-start(bf16[128,768]{1,0:T(8,128)(2,1)S(1)} %get-tuple-element.44), channel_id=1, source_target_pairs={{0,4},{2,6},{4,0},{6,2},{8,12},{10,14},{12,8},{14,10},{1,5},{3,7},... | collective-permute-start | bytes 589832 | tf_op jit(solution)/shard_map/ppermute | solution.py:55
  28.3 2.0 %collective-permute-start.7 = (bf16[128,768]{1,0:T(8,128)(2,1)S(1)}, bf16[128,768]{1,0:T(8,128)(2,1)S(1)}, u32[]{:S(2)}, u32[]{:S(2)}) collective-permute-start(bf16[128,768]{1,0:T(8,128)(2,1)S(1)} %get-tuple-element.40), channel_id=1, source_target_pairs={{0,8},{2,10},{4,12},{6,14},{8,0},{10,2},{12,4},{14,6},{1,9},{3,11}... | collective-permute-start | bytes 589832 | tf_op jit(solution)/shard_map/ppermute | solution.py:55
  30.4 1.4 %collective-permute-start.8 = (bf16[128,768]{1,0:T(8,128)(2,1)S(1)}, bf16[128,768]{1,0:T(8,128)(2,1)S(1)}, u32[]{:S(2)}, u32[]{:S(2)}) collective-permute-start(bf16[128,768]{1,0:T(8,128)(2,1)S(1)} %get-tuple-element.29), channel_id=1, source_target_pairs={{0,10},{2,8},{4,14},{6,12},{8,2},{10,0},{12,6},{14,4},{1,11},{3,9}... | collective-permute-start | bytes 589832 | tf_op jit(solution)/shard_map/ppermute | solution.py:55
  32.5 3.1 %collective-permute-start.9 = (bf16[128,768]{1,0:T(8,128)(2,1)S(1)}, bf16[128,768]{1,0:T(8,128)(2,1)S(1)}, u32[]{:S(2)}, u32[]{:S(2)}) collective-permute-start(bf16[128,768]{1,0:T(8,128)(2,1)S(1)} %get-tuple-element.28), channel_id=1, source_target_pairs={{0,12},{2,14},{4,8},{6,10},{8,4},{10,6},{12,0},{14,2},{1,13},{3,15... | collective-permute-start | bytes 589832 | tf_op jit(solution)/shard_map/ppermute | solution.py:55
  36.0 1.3 %collective-permute-start.10 = (bf16[128,768]{1,0:T(8,128)(2,1)S(1)}, bf16[128,768]{1,0:T(8,128)(2,1)S(1)}, u32[]{:S(2)}, u32[]{:S(2)}) collective-permute-start(bf16[128,768]{1,0:T(8,128)(2,1)S(1)} %get-tuple-element.27), channel_id=1, source_target_pairs={{0,14},{2,12},{4,10},{6,8},{8,6},{10,4},{12,2},{14,0},{1,15},{3,13... | collective-permute-start | bytes 589832 | tf_op jit(solution)/shard_map/ppermute | solution.py:55
  37.3 3.5 %collective-permute-done.6 = bf16[128,768]{1,0:T(8,128)(2,1)S(1)} collective-permute-done((bf16[128,768]{1,0:T(8,128)(2,1)S(1)}, bf16[128,768]{1,0:T(8,128)(2,1)S(1)}, u32[]{:S(2)}, u32[]{:S(2)}) %collective-permute-start.6) | collective-permute-done | bytes 196640 | tf_op jit(solution)/shard_map/ppermute | solution.py:55
  41.8 4.2 %collective-permute-done.9 = bf16[128,768]{1,0:T(8,128)(2,1)S(1)} collective-permute-done((bf16[128,768]{1,0:T(8,128)(2,1)S(1)}, bf16[128,768]{1,0:T(8,128)(2,1)S(1)}, u32[]{:S(2)}, u32[]{:S(2)}) %collective-permute-start.9) | collective-permute-done | bytes 196640 | tf_op jit(solution)/shard_map/ppermute | solution.py:55
  46.0 3.4 %collective-permute-done.10 = bf16[128,768]{1,0:T(8,128)(2,1)S(1)} collective-permute-done((bf16[128,768]{1,0:T(8,128)(2,1)S(1)}, bf16[128,768]{1,0:T(8,128)(2,1)S(1)}, u32[]{:S(2)}, u32[]{:S(2)}) %collective-permute-start.10) | collective-permute-done | bytes 196640 | tf_op jit(solution)/shard_map/ppermute | solution.py:55
  60.3 1.6 %collective-permute-start.18 = (bf16[128,768]{1,0:T(8,128)(2,1)S(1)}, bf16[128,768]{1,0:T(8,128)(2,1)S(1)}, u32[]{:S(2)}, u32[]{:S(2)}) collective-permute-start(bf16[128,768]{1,0:T(8,128)(2,1)S(1)} %get-tuple-element.49), channel_id=1, source_target_pairs={{0,8},{2,10},{4,12},{6,14},{8,0},{10,2},{12,4},{14,6},{1,9},{3,11}... | collective-permute-start | bytes 589832 | tf_op jit(solution)/shard_map/ppermute | solution.py:55
  63.3 2.4 %collective-permute-start.15 = (bf16[128,768]{1,0:T(8,128)(2,1)S(1)}, bf16[128,768]{1,0:T(8,128)(2,1)S(1)}, u32[]{:S(2)}, u32[]{:S(2)}) collective-permute-start(bf16[128,768]{1,0:T(8,128)(2,1)S(1)} %get-tuple-element.50), channel_id=1, source_target_pairs={{0,6},{2,4},{4,2},{6,0},{8,14},{10,12},{12,10},{14,8},{1,7},{3,5},... | collective-permute-start | bytes 589832 | tf_op jit(solution)/shard_map/ppermute | solution.py:55
  66.7 7.5 %collective-permute-done.13 = bf16[128,768]{1,0:T(8,128)(2,1)S(1)} collective-permute-done((bf16[128,768]{1,0:T(8,128)(2,1)S(1)}, bf16[128,768]{1,0:T(8,128)(2,1)S(1)}, u32[]{:S(2)}, u32[]{:S(2)}) %collective-permute-start.13) | collective-permute-done | bytes 196640 | tf_op jit(solution)/shard_map/ppermute | solution.py:55
  75.2 2.1 %collective-permute-start.21 = (bf16[128,768]{1,0:T(8,128)(2,1)S(1)}, bf16[128,768]{1,0:T(8,128)(2,1)S(1)}, u32[]{:S(2)}, u32[]{:S(2)}) collective-permute-start(bf16[128,768]{1,0:T(8,128)(2,1)S(1)} %get-tuple-element.46), channel_id=1, source_target_pairs={{0,14},{2,12},{4,10},{6,8},{8,6},{10,4},{12,2},{14,0},{1,15},{3,13... | collective-permute-start | bytes 589832 | tf_op jit(solution)/shard_map/ppermute | solution.py:55
  77.3 2.0 %collective-permute-done.15 = bf16[128,768]{1,0:T(8,128)(2,1)S(1)} collective-permute-done((bf16[128,768]{1,0:T(8,128)(2,1)S(1)}, bf16[128,768]{1,0:T(8,128)(2,1)S(1)}, u32[]{:S(2)}, u32[]{:S(2)}) %collective-permute-start.15) | collective-permute-done | bytes 196640 | tf_op jit(solution)/shard_map/ppermute | solution.py:55
  79.4 4.3 %collective-permute-done.20 = bf16[128,768]{1,0:T(8,128)(2,1)S(1)} collective-permute-done((bf16[128,768]{1,0:T(8,128)(2,1)S(1)}, bf16[128,768]{1,0:T(8,128)(2,1)S(1)}, u32[]{:S(2)}, u32[]{:S(2)}) %collective-permute-start.20) | collective-permute-done | bytes 196640 | tf_op jit(solution)/shard_map/ppermute | solution.py:55
  83.8 1.9 %collective-permute-done.21 = bf16[128,768]{1,0:T(8,128)(2,1)S(1)} collective-permute-done((bf16[128,768]{1,0:T(8,128)(2,1)S(1)}, bf16[128,768]{1,0:T(8,128)(2,1)S(1)}, u32[]{:S(2)}, u32[]{:S(2)}) %collective-permute-start.21) | collective-permute-done | bytes 196640 | tf_op jit(solution)/shard_map/ppermute | solution.py:55
  86.6 1.1 %collective-permute-done.22 = f32[128]{0:T(128)S(1)} collective-permute-done((f32[128]{0:T(128)S(1)}, f32[128]{0:T(128)S(1)}, u32[]{:S(2)}, u32[]{:S(2)}) %collective-permute-start.22) | collective-permute-done | bytes 544 | tf_op jit(solution)/shard_map/ppermute | solution.py:97
  (117 shorter events, 29.6 us)
Async XLA Ops:
  0.0 20.4 %copy-start = (bf16[1536,768]{1,0:T(8,128)(2,1)S(1)}, bf16[1536,768]{1,0:T(8,128)(2,1)}, u32[]{:S(2)}) copy-start(bf16[1536,768]{1,0:T(8,128)(2,1)} %param.20) | copy-start | bytes 7077892
  13.4 5.5 %collective-permute-start.2 = (bf16[128,2,6]{0,2,1:T(8,128)(2,1)S(1)}, bf16[128,2,6]{0,2,1:T(8,128)(2,1)S(1)}, u32[]{:S(2)}, u32[]{:S(2)}) collective-permute-start(bf16[128,2,6]{0,2,1:T(8,128)(2,1)S(1)} %pad_maximum_fusion.2), channel_id=1, source_target_pairs={{0,1},{1,0},{2,3},{3,2},{4,5},{5,4},{6,7},{7,6},{8,9},{9,8},{10,11... | collective-permute-start | bytes 9224 | tf_op jit(solution)/shard_map/ppermute | solution.py:18
  13.9 5.0 %collective-permute-start = (bf16[128,2,6]{0,2,1:T(8,128)(2,1)S(1)}, bf16[128,2,6]{0,2,1:T(8,128)(2,1)S(1)}, u32[]{:S(2)}, u32[]{:S(2)}) collective-permute-start(bf16[128,2,6]{0,2,1:T(8,128)(2,1)S(1)} %pad_maximum_fusion.1), channel_id=1, source_target_pairs={{0,1},{1,0},{2,3},{3,2},{4,5},{5,4},{6,7},{7,6},{8,9},{9,8},{10,11... | collective-permute-start | bytes 9224 | tf_op jit(solution)/shard_map/ppermute | solution.py:18
  17.0 2.1 %collective-permute-start.1 = (bf16[128,2,6,128]{0,3,2,1:T(8,128)(2,1)}, bf16[128,2,6,128]{0,3,2,1:T(8,128)(2,1)}, u32[]{:S(2)}, u32[]{:S(2)}) collective-permute-start(bf16[128,2,6,128]{0,3,2,1:T(8,128)(2,1)} %pad_maximum_fusion), channel_id=1, source_target_pairs={{0,1},{1,0},{2,3},{3,2},{4,5},{5,4},{6,7},{7,6},{8,9},{9,8},{10,11... | collective-permute-start | bytes 1179656 | tf_op jit(solution)/shard_map/ppermute | solution.py:18
  21.9 1.3 %collective-permute-start.3 = (f32[128]{0:T(128)S(1)}, f32[128]{0:T(128)S(1)}, u32[]{:S(2)}, u32[]{:S(2)}) collective-permute-start(f32[128]{0:T(128)S(1)} %get-tuple-element.61), channel_id=1, source_target_pairs={{0,1},{1,0},{2,3},{3,2},{4,5},{5,4},{6,7},{7,6},{8,9},{9,8},{10,11... | collective-permute-start | bytes 1544 | tf_op jit(solution)/shard_map/ppermute | solution.py:97
  23.9 8.5 %collective-permute-start.4 = (bf16[128,768]{1,0:T(8,128)(2,1)S(1)}, bf16[128,768]{1,0:T(8,128)(2,1)S(1)}, u32[]{:S(2)}, u32[]{:S(2)}) collective-permute-start(bf16[128,768]{1,0:T(8,128)(2,1)S(1)} %get-tuple-element.45), channel_id=1, source_target_pairs={{0,2},{2,0},{4,6},{6,4},{8,10},{10,8},{12,14},{14,12},{1,3},{3,1},... | collective-permute-start | bytes 589832 | tf_op jit(solution)/shard_map/ppermute | solution.py:55
  26.8 9.2 %collective-permute-start.5 = (bf16[128,768]{1,0:T(8,128)(2,1)S(1)}, bf16[128,768]{1,0:T(8,128)(2,1)S(1)}, u32[]{:S(2)}, u32[]{:S(2)}) collective-permute-start(bf16[128,768]{1,0:T(8,128)(2,1)S(1)} %get-tuple-element.44), channel_id=1, source_target_pairs={{0,4},{2,6},{4,0},{6,2},{8,12},{10,14},{12,8},{14,10},{1,5},{3,7},... | collective-permute-start | bytes 589832 | tf_op jit(solution)/shard_map/ppermute | solution.py:55
  28.3 12.5 %collective-permute-start.6 = (bf16[128,768]{1,0:T(8,128)(2,1)S(1)}, bf16[128,768]{1,0:T(8,128)(2,1)S(1)}, u32[]{:S(2)}, u32[]{:S(2)}) collective-permute-start(bf16[128,768]{1,0:T(8,128)(2,1)S(1)} %get-tuple-element.42), channel_id=1, source_target_pairs={{0,6},{2,4},{4,2},{6,0},{8,14},{10,12},{12,10},{14,8},{1,7},{3,5},... | collective-permute-start | bytes 589832 | tf_op jit(solution)/shard_map/ppermute | solution.py:55
  28.3 12.5 %collective-permute-start.7 = (bf16[128,768]{1,0:T(8,128)(2,1)S(1)}, bf16[128,768]{1,0:T(8,128)(2,1)S(1)}, u32[]{:S(2)}, u32[]{:S(2)}) collective-permute-start(bf16[128,768]{1,0:T(8,128)(2,1)S(1)} %get-tuple-element.40), channel_id=1, source_target_pairs={{0,8},{2,10},{4,12},{6,14},{8,0},{10,2},{12,4},{14,6},{1,9},{3,11}... | collective-permute-start | bytes 589832 | tf_op jit(solution)/shard_map/ppermute | solution.py:55
  30.4 11.4 %collective-permute-start.8 = (bf16[128,768]{1,0:T(8,128)(2,1)S(1)}, bf16[128,768]{1,0:T(8,128)(2,1)S(1)}, u32[]{:S(2)}, u32[]{:S(2)}) collective-permute-start(bf16[128,768]{1,0:T(8,128)(2,1)S(1)} %get-tuple-element.29), channel_id=1, source_target_pairs={{0,10},{2,8},{4,14},{6,12},{8,2},{10,0},{12,6},{14,4},{1,11},{3,9}... | collective-permute-start | bytes 589832 | tf_op jit(solution)/shard_map/ppermute | solution.py:55
  32.5 13.6 %collective-permute-start.9 = (bf16[128,768]{1,0:T(8,128)(2,1)S(1)}, bf16[128,768]{1,0:T(8,128)(2,1)S(1)}, u32[]{:S(2)}, u32[]{:S(2)}) collective-permute-start(bf16[128,768]{1,0:T(8,128)(2,1)S(1)} %get-tuple-element.28), channel_id=1, source_target_pairs={{0,12},{2,14},{4,8},{6,10},{8,4},{10,6},{12,0},{14,2},{1,13},{3,15... | collective-permute-start | bytes 589832 | tf_op jit(solution)/shard_map/ppermute | solution.py:55
  36.0 13.5 %collective-permute-start.10 = (bf16[128,768]{1,0:T(8,128)(2,1)S(1)}, bf16[128,768]{1,0:T(8,128)(2,1)S(1)}, u32[]{:S(2)}, u32[]{:S(2)}) collective-permute-start(bf16[128,768]{1,0:T(8,128)(2,1)S(1)} %get-tuple-element.27), channel_id=1, source_target_pairs={{0,14},{2,12},{4,10},{6,8},{8,6},{10,4},{12,2},{14,0},{1,15},{3,13... | collective-permute-start | bytes 589832 | tf_op jit(solution)/shard_map/ppermute | solution.py:55
  49.6 4.2 %collective-permute-start.16 = (bf16[512,768]{1,0:T(8,128)(2,1)S(1)}, bf16[512,768]{1,0:T(8,128)(2,1)S(1)}, u32[]{:S(2)}, u32[]{:S(2)}) collective-permute-start(bf16[512,768]{1,0:T(8,128)(2,1)S(1)} %get-tuple-element.25), channel_id=1, source_target_pairs={{0,1},{1,0},{2,3},{3,2},{4,5},{5,4},{6,7},{7,6},{8,9},{9,8},{10,11... | collective-permute-start | bytes 2359304 | tf_op jit(solution)/shard_map/ppermute | solution.py:73
  51.4 5.8 %collective-permute-start.11 = (bf16[512,768]{1,0:T(8,128)(2,1)S(1)}, bf16[512,768]{1,0:T(8,128)(2,1)S(1)}, u32[]{:S(2)}, u32[]{:S(2)}) collective-permute-start(bf16[512,768]{1,0:T(8,128)(2,1)S(1)} %get-tuple-element.26), channel_id=1, source_target_pairs={{0,1},{1,0},{2,3},{3,2},{4,5},{5,4},{6,7},{7,6},{8,9},{9,8},{10,11... | collective-permute-start | bytes 2359304 | tf_op jit(solution)/shard_map/ppermute | solution.py:73
  56.4 3.6 %collective-permute-start.17 = (bf16[512,768]{1,0:T(8,128)(2,1)S(1)}, bf16[512,768]{1,0:T(8,128)(2,1)S(1)}, u32[]{:S(2)}, u32[]{:S(2)}) collective-permute-start(bf16[512,768]{1,0:T(8,128)(2,1)S(1)} %convolution_convert_fusion.1), channel_id=1, source_target_pairs={{0,1},{1,0},{2,3},{3,2},{4,5},{5,4},{6,7},{7,6},{8,9},{9,8},{10,11... | collective-permute-start | bytes 2359304 | tf_op jit(solution)/shard_map/ppermute | solution.py:89
  58.9 3.1 %collective-permute-start.12 = (bf16[512,768]{1,0:T(8,128)(2,1)S(1)}, bf16[512,768]{1,0:T(8,128)(2,1)S(1)}, u32[]{:S(2)}, u32[]{:S(2)}) collective-permute-start(bf16[512,768]{1,0:T(8,128)(2,1)S(1)} %convolution_convert_fusion.3), channel_id=1, source_target_pairs={{0,1},{1,0},{2,3},{3,2},{4,5},{5,4},{6,7},{7,6},{8,9},{9,8},{10,11... | collective-permute-start | bytes 2359304 | tf_op jit(solution)/shard_map/ppermute | solution.py:89
  60.3 19.1 %collective-permute-start.18 = (bf16[128,768]{1,0:T(8,128)(2,1)S(1)}, bf16[128,768]{1,0:T(8,128)(2,1)S(1)}, u32[]{:S(2)}, u32[]{:S(2)}) collective-permute-start(bf16[128,768]{1,0:T(8,128)(2,1)S(1)} %get-tuple-element.49), channel_id=1, source_target_pairs={{0,8},{2,10},{4,12},{6,14},{8,0},{10,2},{12,4},{14,6},{1,9},{3,11}... | collective-permute-start | bytes 589832 | tf_op jit(solution)/shard_map/ppermute | solution.py:55
  62.2 12.1 %collective-permute-start.13 = (bf16[128,768]{1,0:T(8,128)(2,1)S(1)}, bf16[128,768]{1,0:T(8,128)(2,1)S(1)}, u32[]{:S(2)}, u32[]{:S(2)}) collective-permute-start(bf16[128,768]{1,0:T(8,128)(2,1)S(1)} %get-tuple-element.52), channel_id=1, source_target_pairs={{0,2},{2,0},{4,6},{6,4},{8,10},{10,8},{12,14},{14,12},{1,3},{3,1},... | collective-permute-start | bytes 589832 | tf_op jit(solution)/shard_map/ppermute | solution.py:55
  62.8 12.3 %collective-permute-start.14 = (bf16[128,768]{1,0:T(8,128)(2,1)S(1)}, bf16[128,768]{1,0:T(8,128)(2,1)S(1)}, u32[]{:S(2)}, u32[]{:S(2)}) collective-permute-start(bf16[128,768]{1,0:T(8,128)(2,1)S(1)} %get-tuple-element.51), channel_id=1, source_target_pairs={{0,4},{2,6},{4,0},{6,2},{8,12},{10,14},{12,8},{14,10},{1,5},{3,7},... | collective-permute-start | bytes 589832 | tf_op jit(solution)/shard_map/ppermute | solution.py:55
  63.3 16.0 %collective-permute-start.15 = (bf16[128,768]{1,0:T(8,128)(2,1)S(1)}, bf16[128,768]{1,0:T(8,128)(2,1)S(1)}, u32[]{:S(2)}, u32[]{:S(2)}) collective-permute-start(bf16[128,768]{1,0:T(8,128)(2,1)S(1)} %get-tuple-element.50), channel_id=1, source_target_pairs={{0,6},{2,4},{4,2},{6,0},{8,14},{10,12},{12,10},{14,8},{1,7},{3,5},... | collective-permute-start | bytes 589832 | tf_op jit(solution)/shard_map/ppermute | solution.py:55
  65.7 13.7 %collective-permute-start.19 = (bf16[128,768]{1,0:T(8,128)(2,1)S(1)}, bf16[128,768]{1,0:T(8,128)(2,1)S(1)}, u32[]{:S(2)}, u32[]{:S(2)}) collective-permute-start(bf16[128,768]{1,0:T(8,128)(2,1)S(1)} %get-tuple-element.48), channel_id=1, source_target_pairs={{0,10},{2,8},{4,14},{6,12},{8,2},{10,0},{12,6},{14,4},{1,11},{3,9}... | collective-permute-start | bytes 589832 | tf_op jit(solution)/shard_map/ppermute | solution.py:55
  74.3 9.5 %collective-permute-start.20 = (bf16[128,768]{1,0:T(8,128)(2,1)S(1)}, bf16[128,768]{1,0:T(8,128)(2,1)S(1)}, u32[]{:S(2)}, u32[]{:S(2)}) collective-permute-start(bf16[128,768]{1,0:T(8,128)(2,1)S(1)} %get-tuple-element.47), channel_id=1, source_target_pairs={{0,12},{2,14},{4,8},{6,10},{8,4},{10,6},{12,0},{14,2},{1,13},{3,15... | collective-permute-start | bytes 589832 | tf_op jit(solution)/shard_map/ppermute | solution.py:55
  75.2 10.5 %collective-permute-start.21 = (bf16[128,768]{1,0:T(8,128)(2,1)S(1)}, bf16[128,768]{1,0:T(8,128)(2,1)S(1)}, u32[]{:S(2)}, u32[]{:S(2)}) collective-permute-start(bf16[128,768]{1,0:T(8,128)(2,1)S(1)} %get-tuple-element.46), channel_id=1, source_target_pairs={{0,14},{2,12},{4,10},{6,8},{8,6},{10,4},{12,2},{14,0},{1,15},{3,13... | collective-permute-start | bytes 589832 | tf_op jit(solution)/shard_map/ppermute | solution.py:55
  86.6 1.2 %collective-permute-start.22 = (f32[128]{0:T(128)S(1)}, f32[128]{0:T(128)S(1)}, u32[]{:S(2)}, u32[]{:S(2)}) collective-permute-start(f32[128]{0:T(128)S(1)} %get-tuple-element.63), channel_id=1, source_target_pairs={{0,1},{1,0},{2,3},{3,2},{4,5},{5,4},{6,7},{7,6},{8,9},{9,8},{10,11... | collective-permute-start | bytes 1544 | tf_op jit(solution)/shard_map/ppermute | solution.py:97
  (8 other events, 18.0 us)

commit v13 on v7

--- a/solution.py
+++ b/solution.py
@@ -265,20 +265,11 @@
     returned = exchange(summed.reshape(experts, capacity, feat_part), half_count).reshape(
         buffer_len, feat_part
     )
-    combine = jnp.sum(
-        jnp.where(
-            target[:, :, None] == slot_iota[None, None, :],
-            route_weights[:, :, None],
-            0.0,
-        ),
-        axis=1,
-    )
-    branch = jnp.dot(
-        combine,
-        returned.astype(jnp.float32),
-        precision=lax.Precision.HIGHEST,
-        preferred_element_type=jnp.float32,
-    )
+    branch = jnp.zeros(resid.shape, jnp.float32)
+    for pick in range(top_count):
+        choose = (target[:, pick][:, None] == slot_iota[None, :]).astype(jnp.bfloat16)
+        picked = jnp.dot(choose, returned, preferred_element_type=jnp.float32)
+        branch = branch + route_weights[:, pick][:, None] * picked
     mixed_rows = resid + branch
     out_squares = tp_sum(jnp.sum(mixed_rows * mixed_rows, axis=1))
     return (

time: 88.9 us -> 90.4 us (1.017)
  local copies, waits for them, and re-layouts: 9.06 us -> 11.5 us
  waiting for transfers between devices: 31.2 us -> 29.7 us
    mul x0 -> x1, local copies, waits for them, and re-layouts: none -> 1.44 us  [shards(): branch = branch + route_weights[:, pick][:, None] * picked]
    ppermute x14, waiting for transfers between devices: 29 us -> 27.5 us  [exchange(): pieces.append(lax.ppermute(chunks[step], 'el', perm=pairs))]
    dot_general x1, matrix products: 1.54 us -> 0.61 us  [shards(): jnp.dot(attended, out_weight, preferred_element_type=jnp.float32)]
    unnamed x36 -> x52, local copies, waits for them, and re-layouts: 3.93 us -> 4.17 us
  transfers between devices with their start and end apart: 23 -> 23, of which waited for: 13 -> 12; matrix products, arithmetic and copies ran while one was open for 14% -> 16% of each run, Pallas kernels for 0% -> 0%
where the time goes in v13:
time: 90.4 us; the launch traced here: 89.9 us
  waiting for transfers between devices  29.7 us (33%)
  starting transfers between devices  23.3 us (26%)
  matrix products  16.5 us (18%)
  local copies, waits for them, and re-layouts  11.5 us (13%)
  other arithmetic  8.36 us (9%)
    ppermute x14, waiting for transfers between devices, exchange(): pieces.append(lax.ppermute(chunks[step], 'el', perm=pairs))  27.5 us
    ppermute x14, starting transfers between devices, exchange(): pieces.append(lax.ppermute(chunks[step], 'el', perm=pairs))  21.3 us
    dot_general x8, matrix products, half_product(): return jnp.dot(x, weight, preferred_element_type=jnp.float32)  4.67 us
    unnamed x52, local copies, waits for them, and re-layouts  4.17 us
    dot_general x2, matrix products, one_group(): jnp.einsum('rgd,ld->rgl', head_rows, head_keys, preferred_element_type=jn...  3.84 us
    gather x1, local copies, waits for them, and re-layouts, one_group(): page_row_block = group_pages[local_table.reshape(-1)]  3.32 us
    dot_general x4, matrix products, down_product(): jnp.dot(hidden, weight, preferred_element_type=jnp.float32)  2.49 us
    dot_general x2, matrix products, one_group(): jnp.einsum('rgl,ld->rgd', soft.astype(jnp.bfloat16), head_values, preferr...  2.19 us
  transfers between devices with their start and end apart: 23, of which 12 were waited for; matrix products, arithmetic and copies ran while one was open for 16% of the time, Pallas kernels for 0%

profile of v13, /device:TPU:0, one launch (start us, length us, event | category | flops | bytes accessed | tf_op | source)
XLA Modules:
  0.0 89.9 jit_solution(16803519111761138575)
XLA Ops:
  4.2 3.3 %gather_fusion = bf16[96,16,512]{2,1,0:T(8,128)(2,1)} fusion(bf16[96,16,512]{2,1,0:T(8,128)(2,1)} %bitcast.202, s32[1024]{0:T(1024)S(1)} %pad_clamp_fusion), kind=kCustom, calls=%fused_computation | custom fusion | bytes 3146112 | tf_op jit(solution)/shard_map/while/body/eval_jaxpr/gather | solution.py:170
  8.5 1.9 %fusion.3 = (f32[128,6]{0,1:T(8,128)S(1)}, f32[1536,128,6]{1,0,2:T(8,128)S(1)}) fusion(pred[128,1536]{0,1:T(8,128)(4,1)S(1)} %compare_and_fusion, bf16[128,6,128]{0,2,1:T(8,128)(2,1)S(1)} %bitcast.204, bf16[1536,512]{1,0:T(8,128)(2,1)} %bitcast.198), kind=kOutput, calls=%fused_computation.8 | convolution fusion | flops 305528064 | bytes 5508096 | tf_op jit(solution)/shard_map/while/body/eval_jaxpr/rgd,ld->rgl/dot_general | solution.py:195
  10.5 1.9 %fusion.6 = (bf16[128,6]{0,1:T(8,128)(2,1)S(1)}, f32[128,6]{0,1:T(8,128)S(1)}, f32[1536,128,6]{1,0,2:T(8,128)S(1)}) fusion(f32[1536,128,6]{1,0,2:T(8,128)S(1)} %get-tuple-element.67, f32[128,6]{0,1:T(8,128)S(1)} %get-tuple-element.66, pred[128,1536]{0,1:T(8,128)(4,1)S(1)} %compare_and_fusion, bf16[128,6,128]{0,2,1:T(8,128)(2,1)S(1)} %bitcast.205, ...), kind=kOutput, calls=%fused_computation.11 | convolution fusion | flops 310245888 | bytes 10232320 | tf_op jit(solution)/shard_map/while/body/eval_jaxpr/rgd,ld->rgl/dot_general | solution.py:195
  15.1 1.1 %fusion.33 = bf16[128,1,6,128]{0,3,2,1:T(8,128)(2,1)S(1)} fusion(f32[1536,128,6]{1,0,2:T(8,128)S(1)} %get-tuple-element.68, f32[128,6]{0,1:T(8,128)S(1)} %get-tuple-element.24, pred[128,1536]{0,1:T(8,128)(4,1)S(1)} %compare_and_fusion, bf16[1536,512]{1,0:T(8,128)(2,1)S(1)} %bitcast.200), kind=kOutput, calls=%fused_computation.49 | convolution fusion | flops 306806784 | bytes 5509120 | tf_op jit(solution)/shard_map/while/body/eval_jaxpr/rgl,ld->rgd/dot_general | solution.py:201
  16.2 1.1 %fusion.36 = bf16[128,1,6,128]{0,3,2,1:T(8,128)(2,1)S(1)} fusion(f32[1536,128,6]{1,0,2:T(8,128)S(1)} %get-tuple-element.67, f32[128,6]{0,1:T(8,128)S(1)} %get-tuple-element.66, pred[128,1536]{0,1:T(8,128)(4,1)S(1)} %compare_and_fusion, bf16[1536,512]{1,0:T(8,128)(2,1)S(1)} %bitcast.201), kind=kOutput, calls=%fused_computation.50 | convolution fusion | flops 306806784 | bytes 5509120 | tf_op jit(solution)/shard_map/while/body/eval_jaxpr/rgl,ld->rgd/dot_general | solution.py:201
  18.6 1.4 %slice_bitcast_fusion.10 = (f32[128]{0:T(128)}, f32[128]{0:T(128)}, f32[128]{0:T(128)}, f32[128]{0:T(128)}) fusion(f32[128,4]{0,1:T(4,128)} %param.23), kind=kLoop, calls=%fused_computation.194 | loop fusion | bytes 4096 | tf_op jit(solution)/shard_map/mul | solution.py:272
  21.9 1.2 %divide_convert_fusion = bf16[128,2,6,128]{0,3,2,1:T(8,128)(2,1)S(1)} fusion(bf16[128,2,6,128]{0,3,2,1:T(8,128)(2,1)} %collective-permute-done.1, f32[128,2,6]{0,2,1:T(8,128)S(1)} %get-tuple-element.60, f32[128,2,6]{0,2,1:T(8,128)S(1)} %get-tuple-element.61, f32[128,2,6]{0,2,1:T(8,128)S(1)} %get-tuple-element.59, bf16[128,1,6,128]{0,3,2,1:T(8,128)(2,1)S(1)} %fusion.33, ...), kind=kLoop, calls=%fused_computation.55 | loop fusion | flops 1572864 | bytes 1198080 | tf_op jit(solution)/shard_map/convert_element_type | solution.py:221
  25.6 2.8 %collective-permute-start.4 = (bf16[128,768]{1,0:T(8,128)(2,1)S(1)}, bf16[128,768]{1,0:T(8,128)(2,1)S(1)}, u32[]{:S(2)}, u32[]{:S(2)}) collective-permute-start(bf16[128,768]{1,0:T(8,128)(2,1)S(1)} %get-tuple-element.49), channel_id=1, source_target_pairs={{0,2},{2,0},{4,6},{6,4},{8,10},{10,8},{12,14},{14,12},{1,3},{3,1},... | collective-permute-start | bytes 589832 | tf_op jit(solution)/shard_map/ppermute | solution.py:52
  28.4 1.5 %collective-permute-start.5 = (bf16[128,768]{1,0:T(8,128)(2,1)S(1)}, bf16[128,768]{1,0:T(8,128)(2,1)S(1)}, u32[]{:S(2)}, u32[]{:S(2)}) collective-permute-start(bf16[128,768]{1,0:T(8,128)(2,1)S(1)} %get-tuple-element.48), channel_id=1, source_target_pairs={{0,4},{2,6},{4,0},{6,2},{8,12},{10,14},{12,8},{14,10},{1,5},{3,7},... | collective-permute-start | bytes 589832 | tf_op jit(solution)/shard_map/ppermute | solution.py:52
  29.9 2.1 %collective-permute-start.7 = (bf16[128,768]{1,0:T(8,128)(2,1)S(1)}, bf16[128,768]{1,0:T(8,128)(2,1)S(1)}, u32[]{:S(2)}, u32[]{:S(2)}) collective-permute-start(bf16[128,768]{1,0:T(8,128)(2,1)S(1)} %get-tuple-element.46), channel_id=1, source_target_pairs={{0,8},{2,10},{4,12},{6,14},{8,0},{10,2},{12,4},{14,6},{1,9},{3,11}... | collective-permute-start | bytes 589832 | tf_op jit(solution)/shard_map/ppermute | solution.py:52
  32.0 1.4 %collective-permute-start.8 = (bf16[128,768]{1,0:T(8,128)(2,1)S(1)}, bf16[128,768]{1,0:T(8,128)(2,1)S(1)}, u32[]{:S(2)}, u32[]{:S(2)}) collective-permute-start(bf16[128,768]{1,0:T(8,128)(2,1)S(1)} %get-tuple-element.45), channel_id=1, source_target_pairs={{0,10},{2,8},{4,14},{6,12},{8,2},{10,0},{12,6},{14,4},{1,11},{3,9}... | collective-permute-start | bytes 589832 | tf_op jit(solution)/shard_map/ppermute | solution.py:52
  34.0 3.1 %collective-permute-start.9 = (bf16[128,768]{1,0:T(8,128)(2,1)S(1)}, bf16[128,768]{1,0:T(8,128)(2,1)S(1)}, u32[]{:S(2)}, u32[]{:S(2)}) collective-permute-start(bf16[128,768]{1,0:T(8,128)(2,1)S(1)} %get-tuple-element.44), channel_id=1, source_target_pairs={{0,12},{2,14},{4,8},{6,10},{8,4},{10,6},{12,0},{14,2},{1,13},{3,15... | collective-permute-start | bytes 589832 | tf_op jit(solution)/shard_map/ppermute | solution.py:52
  37.8 1.3 %collective-permute-start.10 = (bf16[128,768]{1,0:T(8,128)(2,1)S(1)}, bf16[128,768]{1,0:T(8,128)(2,1)S(1)}, u32[]{:S(2)}, u32[]{:S(2)}) collective-permute-start(bf16[128,768]{1,0:T(8,128)(2,1)S(1)} %get-tuple-element.42), channel_id=1, source_target_pairs={{0,14},{2,12},{4,10},{6,8},{8,6},{10,4},{12,2},{14,0},{1,15},{3,13... | collective-permute-start | bytes 589832 | tf_op jit(solution)/shard_map/ppermute | solution.py:52
  39.1 3.4 %collective-permute-done.6 = bf16[128,768]{1,0:T(8,128)(2,1)S(1)} collective-permute-done((bf16[128,768]{1,0:T(8,128)(2,1)S(1)}, bf16[128,768]{1,0:T(8,128)(2,1)S(1)}, u32[]{:S(2)}, u32[]{:S(2)}) %collective-permute-start.6) | collective-permute-done | bytes 196640 | tf_op jit(solution)/shard_map/ppermute | solution.py:52
  43.4 4.2 %collective-permute-done.9 = bf16[128,768]{1,0:T(8,128)(2,1)S(1)} collective-permute-done((bf16[128,768]{1,0:T(8,128)(2,1)S(1)}, bf16[128,768]{1,0:T(8,128)(2,1)S(1)}, u32[]{:S(2)}, u32[]{:S(2)}) %collective-permute-start.9) | collective-permute-done | bytes 196640 | tf_op jit(solution)/shard_map/ppermute | solution.py:52
  47.7 3.5 %collective-permute-done.10 = bf16[128,768]{1,0:T(8,128)(2,1)S(1)} collective-permute-done((bf16[128,768]{1,0:T(8,128)(2,1)S(1)}, bf16[128,768]{1,0:T(8,128)(2,1)S(1)}, u32[]{:S(2)}, u32[]{:S(2)}) %collective-permute-start.10) | collective-permute-done | bytes 196640 | tf_op jit(solution)/shard_map/ppermute | solution.py:52
  62.0 1.6 %collective-permute-start.18 = (bf16[128,768]{1,0:T(8,128)(2,1)S(1)}, bf16[128,768]{1,0:T(8,128)(2,1)S(1)}, u32[]{:S(2)}, u32[]{:S(2)}) collective-permute-start(bf16[128,768]{1,0:T(8,128)(2,1)S(1)} %get-tuple-element.53), channel_id=1, source_target_pairs={{0,8},{2,10},{4,12},{6,14},{8,0},{10,2},{12,4},{14,6},{1,9},{3,11}... | collective-permute-start | bytes 589832 | tf_op jit(solution)/shard_map/ppermute | solution.py:52
  65.1 2.4 %collective-permute-start.15 = (bf16[128,768]{1,0:T(8,128)(2,1)S(1)}, bf16[128,768]{1,0:T(8,128)(2,1)S(1)}, u32[]{:S(2)}, u32[]{:S(2)}) collective-permute-start(bf16[128,768]{1,0:T(8,128)(2,1)S(1)} %get-tuple-element.54), channel_id=1, source_target_pairs={{0,6},{2,4},{4,2},{6,0},{8,14},{10,12},{12,10},{14,8},{1,7},{3,5},... | collective-permute-start | bytes 589832 | tf_op jit(solution)/shard_map/ppermute | solution.py:52
  68.5 7.5 %collective-permute-done.13 = bf16[128,768]{1,0:T(8,128)(2,1)S(1)} collective-permute-done((bf16[128,768]{1,0:T(8,128)(2,1)S(1)}, bf16[128,768]{1,0:T(8,128)(2,1)S(1)}, u32[]{:S(2)}, u32[]{:S(2)}) %collective-permute-start.13) | collective-permute-done | bytes 196640 | tf_op jit(solution)/shard_map/ppermute | solution.py:52
  76.9 2.1 %collective-permute-start.21 = (bf16[128,768]{1,0:T(8,128)(2,1)S(1)}, bf16[128,768]{1,0:T(8,128)(2,1)S(1)}, u32[]{:S(2)}, u32[]{:S(2)}) collective-permute-start(bf16[128,768]{1,0:T(8,128)(2,1)S(1)} %get-tuple-element.50), channel_id=1, source_target_pairs={{0,14},{2,12},{4,10},{6,8},{8,6},{10,4},{12,2},{14,0},{1,15},{3,13... | collective-permute-start | bytes 589832 | tf_op jit(solution)/shard_map/ppermute | solution.py:52
  79.0 3.2 %collective-permute-done.15 = bf16[128,768]{1,0:T(8,128)(2,1)S(1)} collective-permute-done((bf16[128,768]{1,0:T(8,128)(2,1)S(1)}, bf16[128,768]{1,0:T(8,128)(2,1)S(1)}, u32[]{:S(2)}, u32[]{:S(2)}) %collective-permute-start.15) | collective-permute-done | bytes 196640 | tf_op jit(solution)/shard_map/ppermute | solution.py:52
  82.4 1.1 %collective-permute-done.20 = bf16[128,768]{1,0:T(8,128)(2,1)S(1)} collective-permute-done((bf16[128,768]{1,0:T(8,128)(2,1)S(1)}, bf16[128,768]{1,0:T(8,128)(2,1)S(1)}, u32[]{:S(2)}, u32[]{:S(2)}) %collective-permute-start.20) | collective-permute-done | bytes 196640 | tf_op jit(solution)/shard_map/ppermute | solution.py:52
  83.5 2.3 %collective-permute-done.21 = bf16[128,768]{1,0:T(8,128)(2,1)S(1)} collective-permute-done((bf16[128,768]{1,0:T(8,128)(2,1)S(1)}, bf16[128,768]{1,0:T(8,128)(2,1)S(1)}, u32[]{:S(2)}, u32[]{:S(2)}) %collective-permute-start.21) | collective-permute-done | bytes 196640 | tf_op jit(solution)/shard_map/ppermute | solution.py:52
  88.0 1.1 %collective-permute-done.22 = f32[128]{0:T(128)S(1)} collective-permute-done((f32[128]{0:T(128)S(1)}, f32[128]{0:T(128)S(1)}, u32[]{:S(2)}, u32[]{:S(2)}) %collective-permute-start.22) | collective-permute-done | bytes 544 | tf_op jit(solution)/shard_map/ppermute | solution.py:94
  (137 shorter events, 32.6 us)
Async XLA Ops:
  0.0 23.1 %copy-start = (bf16[1536,768]{1,0:T(8,128)(2,1)S(1)}, bf16[1536,768]{1,0:T(8,128)(2,1)}, u32[]{:S(2)}) copy-start(bf16[1536,768]{1,0:T(8,128)(2,1)} %param.20) | copy-start | bytes 7077892
  14.0 7.2 %collective-permute-start.2 = (bf16[128,2,6]{0,2,1:T(8,128)(2,1)}, bf16[128,2,6]{0,2,1:T(8,128)(2,1)}, u32[]{:S(2)}, u32[]{:S(2)}) collective-permute-start(bf16[128,2,6]{0,2,1:T(8,128)(2,1)} %pad_maximum_fusion.2), channel_id=1, source_target_pairs={{0,1},{1,0},{2,3},{3,2},{4,5},{5,4},{6,7},{7,6},{8,9},{9,8},{10,11... | collective-permute-start | bytes 9224 | tf_op jit(solution)/shard_map/ppermute | solution.py:18
  15.0 6.1 %collective-permute-start = (bf16[128,2,6]{0,2,1:T(8,128)(2,1)}, bf16[128,2,6]{0,2,1:T(8,128)(2,1)}, u32[]{:S(2)}, u32[]{:S(2)}) collective-permute-start(bf16[128,2,6]{0,2,1:T(8,128)(2,1)} %pad_maximum_fusion.1), channel_id=1, source_target_pairs={{0,1},{1,0},{2,3},{3,2},{4,5},{5,4},{6,7},{7,6},{8,9},{9,8},{10,11... | collective-permute-start | bytes 9224 | tf_op jit(solution)/shard_map/ppermute | solution.py:18
  17.4 4.5 %collective-permute-start.1 = (bf16[128,2,6,128]{0,3,2,1:T(8,128)(2,1)S(1)}, bf16[128,2,6,128]{0,3,2,1:T(8,128)(2,1)}, u32[]{:S(2)}, u32[]{:S(2)}) collective-permute-start(bf16[128,2,6,128]{0,3,2,1:T(8,128)(2,1)S(1)} %pad_maximum_fusion), channel_id=1, source_target_pairs={{0,1},{1,0},{2,3},{3,2},{4,5},{5,4},{6,7},{7,6},{8,9},{9,8},{10,11... | collective-permute-start | bytes 1179656 | tf_op jit(solution)/shard_map/ppermute | solution.py:18
  23.7 1.2 %collective-permute-start.3 = (f32[128]{0:T(128)S(1)}, f32[128]{0:T(128)S(1)}, u32[]{:S(2)}, u32[]{:S(2)}) collective-permute-start(f32[128]{0:T(128)S(1)} %get-tuple-element.69), channel_id=1, source_target_pairs={{0,1},{1,0},{2,3},{3,2},{4,5},{5,4},{6,7},{7,6},{8,9},{9,8},{10,11... | collective-permute-start | bytes 1544 | tf_op jit(solution)/shard_map/ppermute | solution.py:94
  25.6 8.4 %collective-permute-start.4 = (bf16[128,768]{1,0:T(8,128)(2,1)S(1)}, bf16[128,768]{1,0:T(8,128)(2,1)S(1)}, u32[]{:S(2)}, u32[]{:S(2)}) collective-permute-start(bf16[128,768]{1,0:T(8,128)(2,1)S(1)} %get-tuple-element.49), channel_id=1, source_target_pairs={{0,2},{2,0},{4,6},{6,4},{8,10},{10,8},{12,14},{14,12},{1,3},{3,1},... | collective-permute-start | bytes 589832 | tf_op jit(solution)/shard_map/ppermute | solution.py:52
  28.4 9.4 %collective-permute-start.5 = (bf16[128,768]{1,0:T(8,128)(2,1)S(1)}, bf16[128,768]{1,0:T(8,128)(2,1)S(1)}, u32[]{:S(2)}, u32[]{:S(2)}) collective-permute-start(bf16[128,768]{1,0:T(8,128)(2,1)S(1)} %get-tuple-element.48), channel_id=1, source_target_pairs={{0,4},{2,6},{4,0},{6,2},{8,12},{10,14},{12,8},{14,10},{1,5},{3,7},... | collective-permute-start | bytes 589832 | tf_op jit(solution)/shard_map/ppermute | solution.py:52
  29.9 12.6 %collective-permute-start.6 = (bf16[128,768]{1,0:T(8,128)(2,1)S(1)}, bf16[128,768]{1,0:T(8,128)(2,1)S(1)}, u32[]{:S(2)}, u32[]{:S(2)}) collective-permute-start(bf16[128,768]{1,0:T(8,128)(2,1)S(1)} %get-tuple-element.47), channel_id=1, source_target_pairs={{0,6},{2,4},{4,2},{6,0},{8,14},{10,12},{12,10},{14,8},{1,7},{3,5},... | collective-permute-start | bytes 589832 | tf_op jit(solution)/shard_map/ppermute | solution.py:52
  29.9 12.6 %collective-permute-start.7 = (bf16[128,768]{1,0:T(8,128)(2,1)S(1)}, bf16[128,768]{1,0:T(8,128)(2,1)S(1)}, u32[]{:S(2)}, u32[]{:S(2)}) collective-permute-start(bf16[128,768]{1,0:T(8,128)(2,1)S(1)} %get-tuple-element.46), channel_id=1, source_target_pairs={{0,8},{2,10},{4,12},{6,14},{8,0},{10,2},{12,4},{14,6},{1,9},{3,11}... | collective-permute-start | bytes 589832 | tf_op jit(solution)/shard_map/ppermute | solution.py:52
  32.0 11.4 %collective-permute-start.8 = (bf16[128,768]{1,0:T(8,128)(2,1)S(1)}, bf16[128,768]{1,0:T(8,128)(2,1)S(1)}, u32[]{:S(2)}, u32[]{:S(2)}) collective-permute-start(bf16[128,768]{1,0:T(8,128)(2,1)S(1)} %get-tuple-element.45), channel_id=1, source_target_pairs={{0,10},{2,8},{4,14},{6,12},{8,2},{10,0},{12,6},{14,4},{1,11},{3,9}... | collective-permute-start | bytes 589832 | tf_op jit(solution)/shard_map/ppermute | solution.py:52
  34.0 13.6 %collective-permute-start.9 = (bf16[128,768]{1,0:T(8,128)(2,1)S(1)}, bf16[128,768]{1,0:T(8,128)(2,1)S(1)}, u32[]{:S(2)}, u32[]{:S(2)}) collective-permute-start(bf16[128,768]{1,0:T(8,128)(2,1)S(1)} %get-tuple-element.44), channel_id=1, source_target_pairs={{0,12},{2,14},{4,8},{6,10},{8,4},{10,6},{12,0},{14,2},{1,13},{3,15... | collective-permute-start | bytes 589832 | tf_op jit(solution)/shard_map/ppermute | solution.py:52
  37.8 13.4 %collective-permute-start.10 = (bf16[128,768]{1,0:T(8,128)(2,1)S(1)}, bf16[128,768]{1,0:T(8,128)(2,1)S(1)}, u32[]{:S(2)}, u32[]{:S(2)}) collective-permute-start(bf16[128,768]{1,0:T(8,128)(2,1)S(1)} %get-tuple-element.42), channel_id=1, source_target_pairs={{0,14},{2,12},{4,10},{6,8},{8,6},{10,4},{12,2},{14,0},{1,15},{3,13... | collective-permute-start | bytes 589832 | tf_op jit(solution)/shard_map/ppermute | solution.py:52
  51.4 4.2 %collective-permute-start.16 = (bf16[512,768]{1,0:T(8,128)(2,1)S(1)}, bf16[512,768]{1,0:T(8,128)(2,1)S(1)}, u32[]{:S(2)}, u32[]{:S(2)}) collective-permute-start(bf16[512,768]{1,0:T(8,128)(2,1)S(1)} %get-tuple-element.29), channel_id=1, source_target_pairs={{0,1},{1,0},{2,3},{3,2},{4,5},{5,4},{6,7},{7,6},{8,9},{9,8},{10,11... | collective-permute-start | bytes 2359304 | tf_op jit(solution)/shard_map/ppermute | solution.py:70
  53.1 5.7 %collective-permute-start.11 = (bf16[512,768]{1,0:T(8,128)(2,1)S(1)}, bf16[512,768]{1,0:T(8,128)(2,1)S(1)}, u32[]{:S(2)}, u32[]{:S(2)}) collective-permute-start(bf16[512,768]{1,0:T(8,128)(2,1)S(1)} %get-tuple-element.40), channel_id=1, source_target_pairs={{0,1},{1,0},{2,3},{3,2},{4,5},{5,4},{6,7},{7,6},{8,9},{9,8},{10,11... | collective-permute-start | bytes 2359304 | tf_op jit(solution)/shard_map/ppermute | solution.py:70
  58.2 3.6 %collective-permute-start.17 = (bf16[512,768]{1,0:T(8,128)(2,1)S(1)}, bf16[512,768]{1,0:T(8,128)(2,1)S(1)}, u32[]{:S(2)}, u32[]{:S(2)}) collective-permute-start(bf16[512,768]{1,0:T(8,128)(2,1)S(1)} %convolution_convert_fusion.1), channel_id=1, source_target_pairs={{0,1},{1,0},{2,3},{3,2},{4,5},{5,4},{6,7},{7,6},{8,9},{9,8},{10,11... | collective-permute-start | bytes 2359304 | tf_op jit(solution)/shard_map/ppermute | solution.py:86
  60.6 3.1 %collective-permute-start.12 = (bf16[512,768]{1,0:T(8,128)(2,1)S(1)}, bf16[512,768]{1,0:T(8,128)(2,1)S(1)}, u32[]{:S(2)}, u32[]{:S(2)}) collective-permute-start(bf16[512,768]{1,0:T(8,128)(2,1)S(1)} %convolution_convert_fusion.3), channel_id=1, source_target_pairs={{0,1},{1,0},{2,3},{3,2},{4,5},{5,4},{6,7},{7,6},{8,9},{9,8},{10,11... | collective-permute-start | bytes 2359304 | tf_op jit(solution)/shard_map/ppermute | solution.py:86
  62.0 20.2 %collective-permute-start.18 = (bf16[128,768]{1,0:T(8,128)(2,1)S(1)}, bf16[128,768]{1,0:T(8,128)(2,1)S(1)}, u32[]{:S(2)}, u32[]{:S(2)}) collective-permute-start(bf16[128,768]{1,0:T(8,128)(2,1)S(1)} %get-tuple-element.53), channel_id=1, source_target_pairs={{0,8},{2,10},{4,12},{6,14},{8,0},{10,2},{12,4},{14,6},{1,9},{3,11}... | collective-permute-start | bytes 589832 | tf_op jit(solution)/shard_map/ppermute | solution.py:52
  63.9 12.1 %collective-permute-start.13 = (bf16[128,768]{1,0:T(8,128)(2,1)S(1)}, bf16[128,768]{1,0:T(8,128)(2,1)S(1)}, u32[]{:S(2)}, u32[]{:S(2)}) collective-permute-start(bf16[128,768]{1,0:T(8,128)(2,1)S(1)} %get-tuple-element.56), channel_id=1, source_target_pairs={{0,2},{2,0},{4,6},{6,4},{8,10},{10,8},{12,14},{14,12},{1,3},{3,1},... | collective-permute-start | bytes 589832 | tf_op jit(solution)/shard_map/ppermute | solution.py:52
  64.5 12.3 %collective-permute-start.14 = (bf16[128,768]{1,0:T(8,128)(2,1)S(1)}, bf16[128,768]{1,0:T(8,128)(2,1)S(1)}, u32[]{:S(2)}, u32[]{:S(2)}) collective-permute-start(bf16[128,768]{1,0:T(8,128)(2,1)S(1)} %get-tuple-element.55), channel_id=1, source_target_pairs={{0,4},{2,6},{4,0},{6,2},{8,12},{10,14},{12,8},{14,10},{1,5},{3,7},... | collective-permute-start | bytes 589832 | tf_op jit(solution)/shard_map/ppermute | solution.py:52
  65.1 17.2 %collective-permute-start.15 = (bf16[128,768]{1,0:T(8,128)(2,1)S(1)}, bf16[128,768]{1,0:T(8,128)(2,1)S(1)}, u32[]{:S(2)}, u32[]{:S(2)}) collective-permute-start(bf16[128,768]{1,0:T(8,128)(2,1)S(1)} %get-tuple-element.54), channel_id=1, source_target_pairs={{0,6},{2,4},{4,2},{6,0},{8,14},{10,12},{12,10},{14,8},{1,7},{3,5},... | collective-permute-start | bytes 589832 | tf_op jit(solution)/shard_map/ppermute | solution.py:52
  67.5 14.9 %collective-permute-start.19 = (bf16[128,768]{1,0:T(8,128)(2,1)S(1)}, bf16[128,768]{1,0:T(8,128)(2,1)S(1)}, u32[]{:S(2)}, u32[]{:S(2)}) collective-permute-start(bf16[128,768]{1,0:T(8,128)(2,1)S(1)} %get-tuple-element.52), channel_id=1, source_target_pairs={{0,10},{2,8},{4,14},{6,12},{8,2},{10,0},{12,6},{14,4},{1,11},{3,9}... | collective-permute-start | bytes 589832 | tf_op jit(solution)/shard_map/ppermute | solution.py:52
  76.0 7.5 %collective-permute-start.20 = (bf16[128,768]{1,0:T(8,128)(2,1)S(1)}, bf16[128,768]{1,0:T(8,128)(2,1)S(1)}, u32[]{:S(2)}, u32[]{:S(2)}) collective-permute-start(bf16[128,768]{1,0:T(8,128)(2,1)S(1)} %get-tuple-element.51), channel_id=1, source_target_pairs={{0,12},{2,14},{4,8},{6,10},{8,4},{10,6},{12,0},{14,2},{1,13},{3,15... | collective-permute-start | bytes 589832 | tf_op jit(solution)/shard_map/ppermute | solution.py:52
  76.9 8.9 %collective-permute-start.21 = (bf16[128,768]{1,0:T(8,128)(2,1)S(1)}, bf16[128,768]{1,0:T(8,128)(2,1)S(1)}, u32[]{:S(2)}, u32[]{:S(2)}) collective-permute-start(bf16[128,768]{1,0:T(8,128)(2,1)S(1)} %get-tuple-element.50), channel_id=1, source_target_pairs={{0,14},{2,12},{4,10},{6,8},{8,6},{10,4},{12,2},{14,0},{1,15},{3,13... | collective-permute-start | bytes 589832 | tf_op jit(solution)/shard_map/ppermute | solution.py:52
  87.9 1.2 %collective-permute-start.22 = (f32[128]{0:T(128)S(1)}, f32[128]{0:T(128)S(1)}, u32[]{:S(2)}, u32[]{:S(2)}) collective-permute-start(f32[128]{0:T(128)S(1)} %get-tuple-element.71), channel_id=1, source_target_pairs={{0,1},{1,0},{2,3},{3,2},{4,5},{5,4},{6,7},{7,6},{8,9},{9,8},{10,11... | collective-permute-start | bytes 1544 | tf_op jit(solution)/shard_map/ppermute | solution.py:94
  (16 other events, 48.5 us)

commit v14 on v7

--- a/solution.py
+++ b/solution.py
@@ -84,7 +84,7 @@
         return jnp.dot(hidden, weight, preferred_element_type=jnp.float32).astype(jnp.bfloat16)
 
     sent = lax.ppermute(down_product(other), "tp", perm=swap)
-    kept = lax.optimization_barrier(down_product(mine))
+    kept = down_product(mine)
     return (kept.astype(jnp.float32) + sent.astype(jnp.float32)).astype(jnp.bfloat16)
 
 

time: 88.9 us -> 90.2 us (1.015)
  matrix products: 16.5 us -> 19.8 us
  waiting for transfers between devices: 31.2 us -> 30 us
  other arithmetic: 7.52 us -> 6.38 us
    dot_general x4, matrix products: 2.51 us -> 6.66 us  [down_product(): jnp.dot(hidden, weight, preferred_element_type=jnp.float32)]
    ppermute x14, waiting for transfers between devices: 29 us -> 27.7 us  [exchange(): pieces.append(lax.ppermute(chunks[step], 'el', perm=pairs))]
    dot_general x1, matrix products: 1.54 us -> 0.6 us  [shards(): jnp.dot(attended, out_weight, preferred_element_type=jnp.float32)]
    unnamed x36 -> x48, local copies, waits for them, and re-layouts: 3.93 us -> 4.7 us
  transfers between devices with their start and end apart: 23 -> 23, of which waited for: 13 -> 13; matrix products, arithmetic and copies ran while one was open for 14% -> 17% of each run, Pallas kernels for 0% -> 0%
where the time goes in v14:
time: 90.2 us; the launch traced here: 89.8 us
  waiting for transfers between devices  30 us (33%)
  starting transfers between devices  23.3 us (26%)
  matrix products  19.8 us (22%)
  local copies, waits for them, and re-layouts  9.84 us (11%)
  other arithmetic  6.38 us (7%)
    ppermute x14, waiting for transfers between devices, exchange(): pieces.append(lax.ppermute(chunks[step], 'el', perm=pairs))  27.7 us
    ppermute x14, starting transfers between devices, exchange(): pieces.append(lax.ppermute(chunks[step], 'el', perm=pairs))  21 us
    dot_general x4, matrix products, down_product(): jnp.dot(hidden, weight, preferred_element_type=jnp.float32)  6.66 us
    unnamed x48, local copies, waits for them, and re-layouts  4.7 us
    dot_general x8, matrix products, half_product(): return jnp.dot(x, weight, preferred_element_type=jnp.float32)  4.68 us
    dot_general x2, matrix products, one_group(): jnp.einsum('rgd,ld->rgl', head_rows, head_keys, preferred_element_type=jn...  3.84 us
    gather x1, local copies, waits for them, and re-layouts, one_group(): page_row_block = group_pages[local_table.reshape(-1)]  3.33 us
    dot_general x2, matrix products, one_group(): jnp.einsum('rgl,ld->rgd', soft.astype(jnp.bfloat16), head_values, preferr...  2.19 us
  transfers between devices with their start and end apart: 23, of which 13 were waited for; matrix products, arithmetic and copies ran while one was open for 17% of the time, Pallas kernels for 0%

profile of v14, /device:TPU:0, one launch (start us, length us, event | category | flops | bytes accessed | tf_op | source)
XLA Modules:
  0.0 89.8 jit_solution(2361449679005944159)
XLA Ops:
  4.2 3.3 %gather_fusion = bf16[96,16,512]{2,1,0:T(8,128)(2,1)} fusion(bf16[96,16,512]{2,1,0:T(8,128)(2,1)} %bitcast.189, s32[1024]{0:T(1024)S(1)} %pad_clamp_fusion), kind=kCustom, calls=%fused_computation | custom fusion | bytes 3146112 | tf_op jit(solution)/shard_map/while/body/eval_jaxpr/gather | solution.py:170
  8.5 1.9 %fusion.3 = (f32[128,6]{0,1:T(8,128)S(1)}, f32[1536,128,6]{1,0,2:T(8,128)S(1)}) fusion(pred[128,1536]{0,1:T(8,128)(4,1)S(1)} %compare_and_fusion, bf16[128,6,128]{0,2,1:T(8,128)(2,1)S(1)} %bitcast.191, bf16[1536,512]{1,0:T(8,128)(2,1)} %bitcast.184), kind=kOutput, calls=%fused_computation.8 | convolution fusion | flops 305528064 | bytes 5508096 | tf_op jit(solution)/shard_map/while/body/eval_jaxpr/rgd,ld->rgl/dot_general | solution.py:195
  10.5 1.9 %fusion.6 = (bf16[128,6]{0,1:T(8,128)(2,1)S(1)}, f32[128,6]{0,1:T(8,128)S(1)}, f32[1536,128,6]{1,0,2:T(8,128)S(1)}) fusion(f32[1536,128,6]{1,0,2:T(8,128)S(1)} %get-tuple-element.59, f32[128,6]{0,1:T(8,128)S(1)} %get-tuple-element.58, pred[128,1536]{0,1:T(8,128)(4,1)S(1)} %compare_and_fusion, bf16[128,6,128]{0,2,1:T(8,128)(2,1)S(1)} %bitcast.192, ...), kind=kOutput, calls=%fused_computation.11 | convolution fusion | flops 310245888 | bytes 10232320 | tf_op jit(solution)/shard_map/while/body/eval_jaxpr/rgd,ld->rgl/dot_general | solution.py:195
  18.3 1.2 %divide_convert_fusion = bf16[128,2,6,128]{0,3,2,1:T(8,128)(2,1)S(1)} fusion(bf16[128,2,6,128]{0,3,2,1:T(8,128)(2,1)} %collective-permute-done.1, f32[128,2,6]{0,2,1:T(8,128)S(1)} %get-tuple-element.56, f32[128,2,6]{0,2,1:T(8,128)S(1)} %get-tuple-element.57, f32[128,2,6]{0,2,1:T(8,128)S(1)} %get-tuple-element.55, bf16[128,1,6,128]{0,3,2,1:T(8,128)(2,1)S(1)} %fusion.29, ...), kind=kLoop, calls=%fused_computation.50 | loop fusion | flops 1572864 | bytes 1198080 | tf_op jit(solution)/shard_map/convert_element_type | solution.py:221
  22.2 2.9 %collective-permute-start.4 = (bf16[128,768]{1,0:T(8,128)(2,1)S(1)}, bf16[128,768]{1,0:T(8,128)(2,1)S(1)}, u32[]{:S(2)}, u32[]{:S(2)}) collective-permute-start(bf16[128,768]{1,0:T(8,128)(2,1)S(1)} %get-tuple-element.45), channel_id=1, source_target_pairs={{0,2},{2,0},{4,6},{6,4},{8,10},{10,8},{12,14},{14,12},{1,3},{3,1},... | collective-permute-start | bytes 589832 | tf_op jit(solution)/shard_map/ppermute | solution.py:52
  25.0 1.5 %collective-permute-start.5 = (bf16[128,768]{1,0:T(8,128)(2,1)S(1)}, bf16[128,768]{1,0:T(8,128)(2,1)S(1)}, u32[]{:S(2)}, u32[]{:S(2)}) collective-permute-start(bf16[128,768]{1,0:T(8,128)(2,1)S(1)} %get-tuple-element.44), channel_id=1, source_target_pairs={{0,4},{2,6},{4,0},{6,2},{8,12},{10,14},{12,8},{14,10},{1,5},{3,7},... | collective-permute-start | bytes 589832 | tf_op jit(solution)/shard_map/ppermute | solution.py:52
  26.6 2.0 %collective-permute-start.7 = (bf16[128,768]{1,0:T(8,128)(2,1)S(1)}, bf16[128,768]{1,0:T(8,128)(2,1)S(1)}, u32[]{:S(2)}, u32[]{:S(2)}) collective-permute-start(bf16[128,768]{1,0:T(8,128)(2,1)S(1)} %get-tuple-element.40), channel_id=1, source_target_pairs={{0,8},{2,10},{4,12},{6,14},{8,0},{10,2},{12,4},{14,6},{1,9},{3,11}... | collective-permute-start | bytes 589832 | tf_op jit(solution)/shard_map/ppermute | solution.py:52
  28.6 1.4 %collective-permute-start.8 = (bf16[128,768]{1,0:T(8,128)(2,1)S(1)}, bf16[128,768]{1,0:T(8,128)(2,1)S(1)}, u32[]{:S(2)}, u32[]{:S(2)}) collective-permute-start(bf16[128,768]{1,0:T(8,128)(2,1)S(1)} %get-tuple-element.29), channel_id=1, source_target_pairs={{0,10},{2,8},{4,14},{6,12},{8,2},{10,0},{12,6},{14,4},{1,11},{3,9}... | collective-permute-start | bytes 589832 | tf_op jit(solution)/shard_map/ppermute | solution.py:52
  30.7 3.1 %collective-permute-start.9 = (bf16[128,768]{1,0:T(8,128)(2,1)S(1)}, bf16[128,768]{1,0:T(8,128)(2,1)S(1)}, u32[]{:S(2)}, u32[]{:S(2)}) collective-permute-start(bf16[128,768]{1,0:T(8,128)(2,1)S(1)} %get-tuple-element.28), channel_id=1, source_target_pairs={{0,12},{2,14},{4,8},{6,10},{8,4},{10,6},{12,0},{14,2},{1,13},{3,15... | collective-permute-start | bytes 589832 | tf_op jit(solution)/shard_map/ppermute | solution.py:52
  34.2 1.3 %collective-permute-start.10 = (bf16[128,768]{1,0:T(8,128)(2,1)S(1)}, bf16[128,768]{1,0:T(8,128)(2,1)S(1)}, u32[]{:S(2)}, u32[]{:S(2)}) collective-permute-start(bf16[128,768]{1,0:T(8,128)(2,1)S(1)} %get-tuple-element.27), channel_id=1, source_target_pairs={{0,14},{2,12},{4,10},{6,8},{8,6},{10,4},{12,2},{14,0},{1,15},{3,13... | collective-permute-start | bytes 589832 | tf_op jit(solution)/shard_map/ppermute | solution.py:52
  35.5 3.5 %collective-permute-done.6 = bf16[128,768]{1,0:T(8,128)(2,1)S(1)} collective-permute-done((bf16[128,768]{1,0:T(8,128)(2,1)S(1)}, bf16[128,768]{1,0:T(8,128)(2,1)S(1)}, u32[]{:S(2)}, u32[]{:S(2)}) %collective-permute-start.6) | collective-permute-done | bytes 196640 | tf_op jit(solution)/shard_map/ppermute | solution.py:52
  40.0 4.2 %collective-permute-done.9 = bf16[128,768]{1,0:T(8,128)(2,1)S(1)} collective-permute-done((bf16[128,768]{1,0:T(8,128)(2,1)S(1)}, bf16[128,768]{1,0:T(8,128)(2,1)S(1)}, u32[]{:S(2)}, u32[]{:S(2)}) %collective-permute-start.9) | collective-permute-done | bytes 196640 | tf_op jit(solution)/shard_map/ppermute | solution.py:52
  44.3 3.5 %collective-permute-done.10 = bf16[128,768]{1,0:T(8,128)(2,1)S(1)} collective-permute-done((bf16[128,768]{1,0:T(8,128)(2,1)S(1)}, bf16[128,768]{1,0:T(8,128)(2,1)S(1)}, u32[]{:S(2)}, u32[]{:S(2)}) %collective-permute-start.10) | collective-permute-done | bytes 196640 | tf_op jit(solution)/shard_map/ppermute | solution.py:52
  53.9 1.6 %convolution_convert_fusion.1 = bf16[512,768]{1,0:T(8,128)(2,1)} fusion(bf16[512,384]{1,0:T(8,128)(2,1)S(1)} %fusion.22, bf16[1,384,1536]{2,1,0:T(8,128)(2,1)S(1)} %copy-done.3, s32[]{:T(128)S(6)} %select_n.118), kind=kOutput, calls=%fused_computation.26 | convolution fusion | flops 302383104 | bytes 1769476 | tf_op jit(solution)/shard_map/dot_general | solution.py:84
  57.5 1.4 %convolution_convert_fusion.3 = bf16[512,768]{1,0:T(8,128)(2,1)} fusion(bf16[512,384]{1,0:T(8,128)(2,1)S(1)} %fusion.21, bf16[1,384,1536]{2,1,0:T(8,128)(2,1)S(1)} %copy-done.3, s32[]{:T(128)S(6)} %select_n.118), kind=kOutput, calls=%fused_computation.28 | convolution fusion | flops 302383104 | bytes 1769476 | tf_op jit(solution)/shard_map/dot_general | solution.py:84
  59.8 1.9 %add_convert_fusion = bf16[512,768]{1,0:T(8,128)(2,1)S(1)} fusion(bf16[512,768]{1,0:T(8,128)(2,1)} %collective-permute-done.17, bf16[512,384]{1,0:T(8,128)(2,1)} %copy-done.8, bf16[1,384,1536]{2,1,0:T(8,128)(2,1)S(1)} %copy-done.3, s32[]{:T(128)S(6)} %select_n.117), kind=kOutput, calls=%fused_computation.24 | convolution fusion | flops 303955968 | bytes 2555908 | tf_op jit(solution)/shard_map/dot_general | solution.py:84
  61.7 1.6 %collective-permute-start.18 = (bf16[128,768]{1,0:T(8,128)(2,1)S(1)}, bf16[128,768]{1,0:T(8,128)(2,1)S(1)}, u32[]{:S(2)}, u32[]{:S(2)}) collective-permute-start(bf16[128,768]{1,0:T(8,128)(2,1)S(1)} %get-tuple-element.49), channel_id=1, source_target_pairs={{0,8},{2,10},{4,12},{6,14},{8,0},{10,2},{12,4},{14,6},{1,9},{3,11}... | collective-permute-start | bytes 589832 | tf_op jit(solution)/shard_map/ppermute | solution.py:52
  63.4 1.7 %add_convert_fusion.1 = bf16[512,768]{1,0:T(8,128)(2,1)S(1)} fusion(bf16[512,768]{1,0:T(8,128)(2,1)} %collective-permute-done.12, bf16[512,384]{1,0:T(8,128)(2,1)S(1)} %copy-done.7, bf16[1,384,1536]{2,1,0:T(8,128)(2,1)S(1)} %copy-done.3, s32[]{:T(128)S(6)} %select_n.117), kind=kOutput, calls=%fused_computation.25 | convolution fusion | flops 303955968 | bytes 2555908 | tf_op jit(solution)/shard_map/dot_general | solution.py:84
  66.3 2.4 %collective-permute-start.15 = (bf16[128,768]{1,0:T(8,128)(2,1)S(1)}, bf16[128,768]{1,0:T(8,128)(2,1)S(1)}, u32[]{:S(2)}, u32[]{:S(2)}) collective-permute-start(bf16[128,768]{1,0:T(8,128)(2,1)S(1)} %get-tuple-element.50), channel_id=1, source_target_pairs={{0,6},{2,4},{4,2},{6,0},{8,14},{10,12},{12,10},{14,8},{1,7},{3,5},... | collective-permute-start | bytes 589832 | tf_op jit(solution)/shard_map/ppermute | solution.py:52
  69.1 7.8 %collective-permute-done.13 = bf16[128,768]{1,0:T(8,128)(2,1)S(1)} collective-permute-done((bf16[128,768]{1,0:T(8,128)(2,1)S(1)}, bf16[128,768]{1,0:T(8,128)(2,1)S(1)}, u32[]{:S(2)}, u32[]{:S(2)}) %collective-permute-start.13) | collective-permute-done | bytes 196640 | tf_op jit(solution)/shard_map/ppermute | solution.py:52
  77.7 2.6 %collective-permute-start.21 = (bf16[128,768]{1,0:T(8,128)(2,1)S(1)}, bf16[128,768]{1,0:T(8,128)(2,1)S(1)}, u32[]{:S(2)}, u32[]{:S(2)}) collective-permute-start(bf16[128,768]{1,0:T(8,128)(2,1)S(1)} %get-tuple-element.46), channel_id=1, source_target_pairs={{0,14},{2,12},{4,10},{6,8},{8,6},{10,4},{12,2},{14,0},{1,15},{3,13... | collective-permute-start | bytes 589832 | tf_op jit(solution)/shard_map/ppermute | solution.py:52
  80.2 2.9 %collective-permute-done.15 = bf16[128,768]{1,0:T(8,128)(2,1)S(1)} collective-permute-done((bf16[128,768]{1,0:T(8,128)(2,1)S(1)}, bf16[128,768]{1,0:T(8,128)(2,1)S(1)}, u32[]{:S(2)}, u32[]{:S(2)}) %collective-permute-start.15) | collective-permute-done | bytes 196640 | tf_op jit(solution)/shard_map/ppermute | solution.py:52
  83.2 1.2 %collective-permute-done.20 = bf16[128,768]{1,0:T(8,128)(2,1)S(1)} collective-permute-done((bf16[128,768]{1,0:T(8,128)(2,1)S(1)}, bf16[128,768]{1,0:T(8,128)(2,1)S(1)}, u32[]{:S(2)}, u32[]{:S(2)}) %collective-permute-start.20) | collective-permute-done | bytes 196640 | tf_op jit(solution)/shard_map/ppermute | solution.py:52
  84.4 2.5 %collective-permute-done.21 = bf16[128,768]{1,0:T(8,128)(2,1)S(1)} collective-permute-done((bf16[128,768]{1,0:T(8,128)(2,1)S(1)}, bf16[128,768]{1,0:T(8,128)(2,1)S(1)}, u32[]{:S(2)}, u32[]{:S(2)}) %collective-permute-start.21) | collective-permute-done | bytes 196640 | tf_op jit(solution)/shard_map/ppermute | solution.py:52
  (127 shorter events, 29.9 us)
Async XLA Ops:
  0.0 19.5 %copy-start = (bf16[1536,768]{1,0:T(8,128)(2,1)S(1)}, bf16[1536,768]{1,0:T(8,128)(2,1)}, u32[]{:S(2)}) copy-start(bf16[1536,768]{1,0:T(8,128)(2,1)} %param.20) | copy-start | bytes 7077892
  13.4 4.5 %collective-permute-start.2 = (bf16[128,2,6]{0,2,1:T(8,128)(2,1)S(1)}, bf16[128,2,6]{0,2,1:T(8,128)(2,1)S(1)}, u32[]{:S(2)}, u32[]{:S(2)}) collective-permute-start(bf16[128,2,6]{0,2,1:T(8,128)(2,1)S(1)} %pad_maximum_fusion.2), channel_id=1, source_target_pairs={{0,1},{1,0},{2,3},{3,2},{4,5},{5,4},{6,7},{7,6},{8,9},{9,8},{10,11... | collective-permute-start | bytes 9224 | tf_op jit(solution)/shard_map/ppermute | solution.py:18
  13.9 4.0 %collective-permute-start = (bf16[128,2,6]{0,2,1:T(8,128)(2,1)S(1)}, bf16[128,2,6]{0,2,1:T(8,128)(2,1)S(1)}, u32[]{:S(2)}, u32[]{:S(2)}) collective-permute-start(bf16[128,2,6]{0,2,1:T(8,128)(2,1)S(1)} %pad_maximum_fusion.1), channel_id=1, source_target_pairs={{0,1},{1,0},{2,3},{3,2},{4,5},{5,4},{6,7},{7,6},{8,9},{9,8},{10,11... | collective-permute-start | bytes 9224 | tf_op jit(solution)/shard_map/ppermute | solution.py:18
  16.3 2.0 %collective-permute-start.1 = (bf16[128,2,6,128]{0,3,2,1:T(8,128)(2,1)S(1)}, bf16[128,2,6,128]{0,3,2,1:T(8,128)(2,1)}, u32[]{:S(2)}, u32[]{:S(2)}) collective-permute-start(bf16[128,2,6,128]{0,3,2,1:T(8,128)(2,1)S(1)} %pad_maximum_fusion), channel_id=1, source_target_pairs={{0,1},{1,0},{2,3},{3,2},{4,5},{5,4},{6,7},{7,6},{8,9},{9,8},{10,11... | collective-permute-start | bytes 1179656 | tf_op jit(solution)/shard_map/ppermute | solution.py:18
  20.1 1.3 %collective-permute-start.3 = (f32[128]{0:T(128)S(1)}, f32[128]{0:T(128)S(1)}, u32[]{:S(2)}, u32[]{:S(2)}) collective-permute-start(f32[128]{0:T(128)S(1)} %get-tuple-element.61), channel_id=1, source_target_pairs={{0,1},{1,0},{2,3},{3,2},{4,5},{5,4},{6,7},{7,6},{8,9},{9,8},{10,11... | collective-permute-start | bytes 1544 | tf_op jit(solution)/shard_map/ppermute | solution.py:94
  22.2 8.5 %collective-permute-start.4 = (bf16[128,768]{1,0:T(8,128)(2,1)S(1)}, bf16[128,768]{1,0:T(8,128)(2,1)S(1)}, u32[]{:S(2)}, u32[]{:S(2)}) collective-permute-start(bf16[128,768]{1,0:T(8,128)(2,1)S(1)} %get-tuple-element.45), channel_id=1, source_target_pairs={{0,2},{2,0},{4,6},{6,4},{8,10},{10,8},{12,14},{14,12},{1,3},{3,1},... | collective-permute-start | bytes 589832 | tf_op jit(solution)/shard_map/ppermute | solution.py:52
  25.0 9.2 %collective-permute-start.5 = (bf16[128,768]{1,0:T(8,128)(2,1)S(1)}, bf16[128,768]{1,0:T(8,128)(2,1)S(1)}, u32[]{:S(2)}, u32[]{:S(2)}) collective-permute-start(bf16[128,768]{1,0:T(8,128)(2,1)S(1)} %get-tuple-element.44), channel_id=1, source_target_pairs={{0,4},{2,6},{4,0},{6,2},{8,12},{10,14},{12,8},{14,10},{1,5},{3,7},... | collective-permute-start | bytes 589832 | tf_op jit(solution)/shard_map/ppermute | solution.py:52
  26.5 12.4 %collective-permute-start.6 = (bf16[128,768]{1,0:T(8,128)(2,1)S(1)}, bf16[128,768]{1,0:T(8,128)(2,1)S(1)}, u32[]{:S(2)}, u32[]{:S(2)}) collective-permute-start(bf16[128,768]{1,0:T(8,128)(2,1)S(1)} %get-tuple-element.42), channel_id=1, source_target_pairs={{0,6},{2,4},{4,2},{6,0},{8,14},{10,12},{12,10},{14,8},{1,7},{3,5},... | collective-permute-start | bytes 589832 | tf_op jit(solution)/shard_map/ppermute | solution.py:52
  26.6 12.4 %collective-permute-start.7 = (bf16[128,768]{1,0:T(8,128)(2,1)S(1)}, bf16[128,768]{1,0:T(8,128)(2,1)S(1)}, u32[]{:S(2)}, u32[]{:S(2)}) collective-permute-start(bf16[128,768]{1,0:T(8,128)(2,1)S(1)} %get-tuple-element.40), channel_id=1, source_target_pairs={{0,8},{2,10},{4,12},{6,14},{8,0},{10,2},{12,4},{14,6},{1,9},{3,11}... | collective-permute-start | bytes 589832 | tf_op jit(solution)/shard_map/ppermute | solution.py:52
  28.6 11.4 %collective-permute-start.8 = (bf16[128,768]{1,0:T(8,128)(2,1)S(1)}, bf16[128,768]{1,0:T(8,128)(2,1)S(1)}, u32[]{:S(2)}, u32[]{:S(2)}) collective-permute-start(bf16[128,768]{1,0:T(8,128)(2,1)S(1)} %get-tuple-element.29), channel_id=1, source_target_pairs={{0,10},{2,8},{4,14},{6,12},{8,2},{10,0},{12,6},{14,4},{1,11},{3,9}... | collective-permute-start | bytes 589832 | tf_op jit(solution)/shard_map/ppermute | solution.py:52
  30.7 13.5 %collective-permute-start.9 = (bf16[128,768]{1,0:T(8,128)(2,1)S(1)}, bf16[128,768]{1,0:T(8,128)(2,1)S(1)}, u32[]{:S(2)}, u32[]{:S(2)}) collective-permute-start(bf16[128,768]{1,0:T(8,128)(2,1)S(1)} %get-tuple-element.28), channel_id=1, source_target_pairs={{0,12},{2,14},{4,8},{6,10},{8,4},{10,6},{12,0},{14,2},{1,13},{3,15... | collective-permute-start | bytes 589832 | tf_op jit(solution)/shard_map/ppermute | solution.py:52
  34.2 13.5 %collective-permute-start.10 = (bf16[128,768]{1,0:T(8,128)(2,1)S(1)}, bf16[128,768]{1,0:T(8,128)(2,1)S(1)}, u32[]{:S(2)}, u32[]{:S(2)}) collective-permute-start(bf16[128,768]{1,0:T(8,128)(2,1)S(1)} %get-tuple-element.27), channel_id=1, source_target_pairs={{0,14},{2,12},{4,10},{6,8},{8,6},{10,4},{12,2},{14,0},{1,15},{3,13... | collective-permute-start | bytes 589832 | tf_op jit(solution)/shard_map/ppermute | solution.py:52
  47.9 4.2 %collective-permute-start.16 = (bf16[512,768]{1,0:T(8,128)(2,1)S(1)}, bf16[512,768]{1,0:T(8,128)(2,1)S(1)}, u32[]{:S(2)}, u32[]{:S(2)}) collective-permute-start(bf16[512,768]{1,0:T(8,128)(2,1)S(1)} %get-tuple-element.25), channel_id=1, source_target_pairs={{0,1},{1,0},{2,3},{3,2},{4,5},{5,4},{6,7},{7,6},{8,9},{9,8},{10,11... | collective-permute-start | bytes 2359304 | tf_op jit(solution)/shard_map/ppermute | solution.py:70
  49.6 6.0 %collective-permute-start.11 = (bf16[512,768]{1,0:T(8,128)(2,1)S(1)}, bf16[512,768]{1,0:T(8,128)(2,1)S(1)}, u32[]{:S(2)}, u32[]{:S(2)}) collective-permute-start(bf16[512,768]{1,0:T(8,128)(2,1)S(1)} %get-tuple-element.26), channel_id=1, source_target_pairs={{0,1},{1,0},{2,3},{3,2},{4,5},{5,4},{6,7},{7,6},{8,9},{9,8},{10,11... | collective-permute-start | bytes 2359304 | tf_op jit(solution)/shard_map/ppermute | solution.py:70
  55.5 4.2 %collective-permute-start.17 = (bf16[512,768]{1,0:T(8,128)(2,1)}, bf16[512,768]{1,0:T(8,128)(2,1)}, u32[]{:S(2)}, u32[]{:S(2)}) collective-permute-start(bf16[512,768]{1,0:T(8,128)(2,1)} %convolution_convert_fusion.1), channel_id=1, source_target_pairs={{0,1},{1,0},{2,3},{3,2},{4,5},{5,4},{6,7},{7,6},{8,9},{9,8},{10,11... | collective-permute-start | bytes 2359304 | tf_op jit(solution)/shard_map/ppermute | solution.py:86
  59.0 4.4 %collective-permute-start.12 = (bf16[512,768]{1,0:T(8,128)(2,1)}, bf16[512,768]{1,0:T(8,128)(2,1)}, u32[]{:S(2)}, u32[]{:S(2)}) collective-permute-start(bf16[512,768]{1,0:T(8,128)(2,1)} %convolution_convert_fusion.3), channel_id=1, source_target_pairs={{0,1},{1,0},{2,3},{3,2},{4,5},{5,4},{6,7},{7,6},{8,9},{9,8},{10,11... | collective-permute-start | bytes 2359304 | tf_op jit(solution)/shard_map/ppermute | solution.py:86
  61.7 21.4 %collective-permute-start.18 = (bf16[128,768]{1,0:T(8,128)(2,1)S(1)}, bf16[128,768]{1,0:T(8,128)(2,1)S(1)}, u32[]{:S(2)}, u32[]{:S(2)}) collective-permute-start(bf16[128,768]{1,0:T(8,128)(2,1)S(1)} %get-tuple-element.49), channel_id=1, source_target_pairs={{0,8},{2,10},{4,12},{6,14},{8,0},{10,2},{12,4},{14,6},{1,9},{3,11}... | collective-permute-start | bytes 589832 | tf_op jit(solution)/shard_map/ppermute | solution.py:52
  65.1 11.9 %collective-permute-start.13 = (bf16[128,768]{1,0:T(8,128)(2,1)S(1)}, bf16[128,768]{1,0:T(8,128)(2,1)S(1)}, u32[]{:S(2)}, u32[]{:S(2)}) collective-permute-start(bf16[128,768]{1,0:T(8,128)(2,1)S(1)} %get-tuple-element.52), channel_id=1, source_target_pairs={{0,2},{2,0},{4,6},{6,4},{8,10},{10,8},{12,14},{14,12},{1,3},{3,1},... | collective-permute-start | bytes 589832 | tf_op jit(solution)/shard_map/ppermute | solution.py:52
  65.8 11.9 %collective-permute-start.14 = (bf16[128,768]{1,0:T(8,128)(2,1)S(1)}, bf16[128,768]{1,0:T(8,128)(2,1)S(1)}, u32[]{:S(2)}, u32[]{:S(2)}) collective-permute-start(bf16[128,768]{1,0:T(8,128)(2,1)S(1)} %get-tuple-element.51), channel_id=1, source_target_pairs={{0,4},{2,6},{4,0},{6,2},{8,12},{10,14},{12,8},{14,10},{1,5},{3,7},... | collective-permute-start | bytes 589832 | tf_op jit(solution)/shard_map/ppermute | solution.py:52
  66.3 16.8 %collective-permute-start.15 = (bf16[128,768]{1,0:T(8,128)(2,1)S(1)}, bf16[128,768]{1,0:T(8,128)(2,1)S(1)}, u32[]{:S(2)}, u32[]{:S(2)}) collective-permute-start(bf16[128,768]{1,0:T(8,128)(2,1)S(1)} %get-tuple-element.50), channel_id=1, source_target_pairs={{0,6},{2,4},{4,2},{6,0},{8,14},{10,12},{12,10},{14,8},{1,7},{3,5},... | collective-permute-start | bytes 589832 | tf_op jit(solution)/shard_map/ppermute | solution.py:52
  68.7 14.5 %collective-permute-start.19 = (bf16[128,768]{1,0:T(8,128)(2,1)S(1)}, bf16[128,768]{1,0:T(8,128)(2,1)S(1)}, u32[]{:S(2)}, u32[]{:S(2)}) collective-permute-start(bf16[128,768]{1,0:T(8,128)(2,1)S(1)} %get-tuple-element.48), channel_id=1, source_target_pairs={{0,10},{2,8},{4,14},{6,12},{8,2},{10,0},{12,6},{14,4},{1,11},{3,9}... | collective-permute-start | bytes 589832 | tf_op jit(solution)/shard_map/ppermute | solution.py:52
  77.0 7.4 %collective-permute-start.20 = (bf16[128,768]{1,0:T(8,128)(2,1)S(1)}, bf16[128,768]{1,0:T(8,128)(2,1)S(1)}, u32[]{:S(2)}, u32[]{:S(2)}) collective-permute-start(bf16[128,768]{1,0:T(8,128)(2,1)S(1)} %get-tuple-element.47), channel_id=1, source_target_pairs={{0,12},{2,14},{4,8},{6,10},{8,4},{10,6},{12,0},{14,2},{1,13},{3,15... | collective-permute-start | bytes 589832 | tf_op jit(solution)/shard_map/ppermute | solution.py:52
  77.7 9.2 %collective-permute-start.21 = (bf16[128,768]{1,0:T(8,128)(2,1)S(1)}, bf16[128,768]{1,0:T(8,128)(2,1)S(1)}, u32[]{:S(2)}, u32[]{:S(2)}) collective-permute-start(bf16[128,768]{1,0:T(8,128)(2,1)S(1)} %get-tuple-element.46), channel_id=1, source_target_pairs={{0,14},{2,12},{4,10},{6,8},{8,6},{10,4},{12,2},{14,0},{1,15},{3,13... | collective-permute-start | bytes 589832 | tf_op jit(solution)/shard_map/ppermute | solution.py:52
  87.8 1.2 %collective-permute-start.22 = (f32[128]{0:T(128)S(1)}, f32[128]{0:T(128)S(1)}, u32[]{:S(2)}, u32[]{:S(2)}) collective-permute-start(f32[128]{0:T(128)S(1)} %get-tuple-element.63), channel_id=1, source_target_pairs={{0,1},{1,0},{2,3},{3,2},{4,5},{5,4},{6,7},{7,6},{8,9},{9,8},{10,11... | collective-permute-start | bytes 1544 | tf_op jit(solution)/shard_map/ppermute | solution.py:94
  (14 other events, 45.4 us)

commit v15 on v7

--- a/solution.py
+++ b/solution.py
@@ -195,8 +195,10 @@
             scores = jnp.einsum(
                 "rgd,ld->rgl", head_rows, head_keys, preferred_element_type=jnp.float32
             ) * HEAD_SIZE ** (-0.5)
-            top = jnp.max(jnp.where(score_mask, scores, -1e30), axis=-1)
-            soft = jnp.where(score_mask, jnp.exp(scores - top[..., None]), 0.0)
+            masked = jnp.where(score_mask, scores, -1e30)
+            top = jnp.max(masked, axis=-1)
+            shift = jnp.where(top > -1e29, top, 0.0)
+            soft = jnp.exp(masked - shift[..., None])
             total = jnp.sum(soft, axis=-1)
             weighted_part = jnp.einsum(
                 "rgl,ld->rgd",

time: 88.9 us -> 98.9 us (1.11)
  starting transfers between devices: 23.7 us -> 33.7 us
  matrix products: 16.5 us -> 15 us
  waiting for transfers between devices: 31.2 us -> 32.3 us
    ppermute x14, starting transfers between devices: 21.4 us -> 30.9 us  [exchange(): pieces.append(lax.ppermute(chunks[step], 'el', perm=pairs))]
    dot_general x2, matrix products: 3.85 us -> 2.77 us  [one_group(): jnp.einsum('rgd,ld->rgl', head_rows, head_keys, preferred_element_type=jn...]
    ppermute x14, waiting for transfers between devices: 29 us -> 30 us  [exchange(): pieces.append(lax.ppermute(chunks[step], 'el', perm=pairs))]
  transfers between devices with their start and end apart: 23 -> 23, of which waited for: 13 -> 9; matrix products, arithmetic and copies ran while one was open for 14% -> 13% of each run, Pallas kernels for 0% -> 0%
where the time goes in v15:
time: 98.9 us; the launch traced here: 98 us
  starting transfers between devices  33.7 us (34%)
  waiting for transfers between devices  32.3 us (33%)
  matrix products  15 us (15%)
  local copies, waits for them, and re-layouts  8.5 us (9%)
  other arithmetic  7.95 us (8%)
    ppermute x14, starting transfers between devices, exchange(): pieces.append(lax.ppermute(chunks[step], 'el', perm=pairs))  30.9 us
    ppermute x14, waiting for transfers between devices, exchange(): pieces.append(lax.ppermute(chunks[step], 'el', perm=pairs))  30 us
    dot_general x8, matrix products, half_product(): return jnp.dot(x, weight, preferred_element_type=jnp.float32)  4.82 us
    unnamed x36, local copies, waits for them, and re-layouts  3.36 us
    gather x1, local copies, waits for them, and re-layouts, one_group(): page_row_block = group_pages[local_table.reshape(-1)]  3.32 us
    dot_general x2, matrix products, one_group(): jnp.einsum('rgd,ld->rgl', head_rows, head_keys, preferred_element_type=jn...  2.77 us
    dot_general x4, matrix products, down_product(): jnp.dot(hidden, weight, preferred_element_type=jnp.float32)  2.3 us
  transfers between devices with their start and end apart: 23, of which 9 were waited for; matrix products, arithmetic and copies ran while one was open for 13% of the time, Pallas kernels for 0%

profile of v15, /device:TPU:0, one launch (start us, length us, event | category | flops | bytes accessed | tf_op | source)
XLA Modules:
  0.0 98.0 jit_solution(11463026614429950264)
XLA Ops:
  0.0 1.0 reduce-window.4
  2.8 1.1 %fusion.107 = (bf16[128,768]{1,0:T(8,128)(2,1)S(1)}, bf16[128,768]{1,0:T(8,128)(2,1)S(1)}) fusion(bf16[128,1536]{1,0:T(8,128)(2,1)} %param.15), kind=kLoop, calls=%fused_computation.181 | loop fusion | bytes 786432 | tf_op jit(solution)/shard_map/while/body/eval_jaxpr/slice | solution.py:189
  4.2 3.3 %gather_fusion = bf16[96,16,512]{2,1,0:T(8,128)(2,1)} fusion(bf16[96,16,512]{2,1,0:T(8,128)(2,1)} %bitcast.157, s32[1024]{0:T(1024)S(1)} %pad_clamp_fusion), kind=kCustom, calls=%fused_computation | custom fusion | bytes 3146112 | tf_op jit(solution)/shard_map/while/body/eval_jaxpr/gather | solution.py:170
  7.5 0.9 compare_and_fusion
  8.5 1.9 %fusion.108 = (f32[128,6]{0,1:T(8,128)S(1)}, f32[128,6,1536]{0,2,1:T(8,128)S(1)}) fusion(bf16[128,6,128]{0,2,1:T(8,128)(2,1)S(1)} %bitcast.160, bf16[1536,512]{1,0:T(8,128)(2,1)} %bitcast.144, pred[128,1536]{0,1:T(8,128)(4,1)S(1)} %compare_and_fusion), kind=kOutput, calls=%fused_computation.182 | convolution fusion | flops 305528064 | bytes 5508096 | tf_op jit(solution)/shard_map/while/body/eval_jaxpr/rgd,ld->rgl/dot_general | solution.py:195
  18.0 1.2 %divide_convert_fusion = bf16[128,2,6,128]{0,3,2,1:T(8,128)(2,1)S(1)} fusion(bf16[128,2,6,128]{0,3,2,1:T(8,128)(2,1)} %collective-permute-done.1, f32[128,2,6]{0,2,1:T(8,128)S(1)} %get-tuple-element.54, f32[128,2,6]{0,2,1:T(8,128)S(1)} %get-tuple-element.55, f32[128,2,6]{0,2,1:T(8,128)S(1)} %get-tuple-element.53, bf16[128,1,6,128]{0,3,2,1:T(8,128)(2,1)S(1)} %fusion.23, ...), kind=kLoop, calls=%fused_computation.44 | loop fusion | flops 1572864 | bytes 1198080 | tf_op jit(solution)/shard_map/convert_element_type | solution.py:223
  19.2 1.5 %multiply_reduce_fusion.1 = (f32[128]{0:T(128)S(1)}, f32[128,768]{1,0:T(8,128)S(1)}) fusion(bf16[128,1536]{0,1:T(8,128)(2,1)S(1)} %bitcast.158, bf16[1536,768]{1,0:T(8,128)(2,1)S(1)} %copy-done, bf16[128,768]{1,0:T(8,128)(2,1)} %param.14), kind=kOutput, calls=%fused_computation.82 | convolution fusion | flops 302382976 | bytes 3342848 | tf_op jit(solution)/shard_map/dot_general | solution.py:225
  22.8 4.8 %collective-permute-start.10 = (bf16[128,768]{1,0:T(8,128)(2,1)S(1)}, bf16[128,768]{1,0:T(8,128)(2,1)S(1)}, u32[]{:S(2)}, u32[]{:S(2)}) collective-permute-start(bf16[128,768]{1,0:T(8,128)(2,1)S(1)} %get-tuple-element.25), channel_id=1, source_target_pairs={{0,14},{2,12},{4,10},{6,8},{8,6},{10,4},{12,2},{14,0},{1,15},{3,13... | collective-permute-start | bytes 589832 | tf_op jit(solution)/shard_map/ppermute | solution.py:52
  28.0 1.5 %collective-permute-start.8 = (bf16[128,768]{1,0:T(8,128)(2,1)S(1)}, bf16[128,768]{1,0:T(8,128)(2,1)S(1)}, u32[]{:S(2)}, u32[]{:S(2)}) collective-permute-start(bf16[128,768]{1,0:T(8,128)(2,1)S(1)} %get-tuple-element.27), channel_id=1, source_target_pairs={{0,10},{2,8},{4,14},{6,12},{8,2},{10,0},{12,6},{14,4},{1,11},{3,9}... | collective-permute-start | bytes 589832 | tf_op jit(solution)/shard_map/ppermute | solution.py:52
  29.7 1.8 %collective-permute-start.4 = (bf16[128,768]{1,0:T(8,128)(2,1)S(1)}, bf16[128,768]{1,0:T(8,128)(2,1)S(1)}, u32[]{:S(2)}, u32[]{:S(2)}) collective-permute-start(bf16[128,768]{1,0:T(8,128)(2,1)S(1)} %get-tuple-element.42), channel_id=1, source_target_pairs={{0,2},{2,0},{4,6},{6,4},{8,10},{10,8},{12,14},{14,12},{1,3},{3,1},... | collective-permute-start | bytes 589832 | tf_op jit(solution)/shard_map/ppermute | solution.py:52
  31.5 5.7 %collective-permute-done.4 = bf16[128,768]{1,0:T(8,128)(2,1)S(1)} collective-permute-done((bf16[128,768]{1,0:T(8,128)(2,1)S(1)}, bf16[128,768]{1,0:T(8,128)(2,1)S(1)}, u32[]{:S(2)}, u32[]{:S(2)}) %collective-permute-start.4) | collective-permute-done | bytes 196640 | tf_op jit(solution)/shard_map/ppermute | solution.py:52
  37.8 5.8 %collective-permute-done.5 = bf16[128,768]{1,0:T(8,128)(2,1)S(1)} collective-permute-done((bf16[128,768]{1,0:T(8,128)(2,1)S(1)}, bf16[128,768]{1,0:T(8,128)(2,1)S(1)}, u32[]{:S(2)}, u32[]{:S(2)}) %collective-permute-start.5) | collective-permute-done | bytes 196640 | tf_op jit(solution)/shard_map/ppermute | solution.py:52
  43.6 6.7 %collective-permute-start.6 = (bf16[128,768]{1,0:T(8,128)(2,1)S(1)}, bf16[128,768]{1,0:T(8,128)(2,1)S(1)}, u32[]{:S(2)}, u32[]{:S(2)}) collective-permute-start(bf16[128,768]{1,0:T(8,128)(2,1)S(1)} %get-tuple-element.29), channel_id=1, source_target_pairs={{0,6},{2,4},{4,2},{6,0},{8,14},{10,12},{12,10},{14,8},{1,7},{3,5},... | collective-permute-start | bytes 589832 | tf_op jit(solution)/shard_map/ppermute | solution.py:52
  50.3 3.6 %collective-permute-done.6 = bf16[128,768]{1,0:T(8,128)(2,1)S(1)} collective-permute-done((bf16[128,768]{1,0:T(8,128)(2,1)S(1)}, bf16[128,768]{1,0:T(8,128)(2,1)S(1)}, u32[]{:S(2)}, u32[]{:S(2)}) %collective-permute-start.6) | collective-permute-done | bytes 196640 | tf_op jit(solution)/shard_map/ppermute | solution.py:52
  54.2 1.1 %copy-done.3 = bf16[1,1536,384]{2,1,0:T(8,128)(2,1)S(1)} copy-done((bf16[1,1536,384]{2,1,0:T(8,128)(2,1)S(1)}, bf16[1,1536,384]{2,1,0:T(8,128)(2,1)}, u32[]{:S(2)}) %copy-start.3) | copy-done | bytes 1179672
  64.8 4.0 %collective-permute-start.21 = (bf16[128,768]{1,0:T(8,128)(2,1)S(1)}, bf16[128,768]{1,0:T(8,128)(2,1)S(1)}, u32[]{:S(2)}, u32[]{:S(2)}) collective-permute-start(bf16[128,768]{1,0:T(8,128)(2,1)S(1)} %get-tuple-element.44), channel_id=1, source_target_pairs={{0,14},{2,12},{4,10},{6,8},{8,6},{10,4},{12,2},{14,0},{1,15},{3,13... | collective-permute-start | bytes 589832 | tf_op jit(solution)/shard_map/ppermute | solution.py:52
  68.9 1.5 %collective-permute-start.19 = (bf16[128,768]{1,0:T(8,128)(2,1)S(1)}, bf16[128,768]{1,0:T(8,128)(2,1)S(1)}, u32[]{:S(2)}, u32[]{:S(2)}) collective-permute-start(bf16[128,768]{1,0:T(8,128)(2,1)S(1)} %get-tuple-element.46), channel_id=1, source_target_pairs={{0,10},{2,8},{4,14},{6,12},{8,2},{10,0},{12,6},{14,4},{1,11},{3,9}... | collective-permute-start | bytes 589832 | tf_op jit(solution)/shard_map/ppermute | solution.py:52
  71.2 1.5 %collective-permute-start.13 = (bf16[128,768]{1,0:T(8,128)(2,1)S(1)}, bf16[128,768]{1,0:T(8,128)(2,1)S(1)}, u32[]{:S(2)}, u32[]{:S(2)}) collective-permute-start(bf16[128,768]{1,0:T(8,128)(2,1)S(1)} %get-tuple-element.50), channel_id=1, source_target_pairs={{0,2},{2,0},{4,6},{6,4},{8,10},{10,8},{12,14},{14,12},{1,3},{3,1},... | collective-permute-start | bytes 589832 | tf_op jit(solution)/shard_map/ppermute | solution.py:52
  72.7 5.9 %collective-permute-done.13 = bf16[128,768]{1,0:T(8,128)(2,1)S(1)} collective-permute-done((bf16[128,768]{1,0:T(8,128)(2,1)S(1)}, bf16[128,768]{1,0:T(8,128)(2,1)S(1)}, u32[]{:S(2)}, u32[]{:S(2)}) %collective-permute-start.13) | collective-permute-done | bytes 196640 | tf_op jit(solution)/shard_map/ppermute | solution.py:52
  78.6 2.9 %collective-permute-start.14 = (bf16[128,768]{1,0:T(8,128)(2,1)S(1)}, bf16[128,768]{1,0:T(8,128)(2,1)S(1)}, u32[]{:S(2)}, u32[]{:S(2)}) collective-permute-start(bf16[128,768]{1,0:T(8,128)(2,1)S(1)} %get-tuple-element.49), channel_id=1, source_target_pairs={{0,4},{2,6},{4,0},{6,2},{8,12},{10,14},{12,8},{14,10},{1,5},{3,7},... | collective-permute-start | bytes 589832 | tf_op jit(solution)/shard_map/ppermute | solution.py:52
  81.5 5.3 %collective-permute-done.14 = bf16[128,768]{1,0:T(8,128)(2,1)S(1)} collective-permute-done((bf16[128,768]{1,0:T(8,128)(2,1)S(1)}, bf16[128,768]{1,0:T(8,128)(2,1)S(1)}, u32[]{:S(2)}, u32[]{:S(2)}) %collective-permute-start.14) | collective-permute-done | bytes 196640 | tf_op jit(solution)/shard_map/ppermute | solution.py:52
  86.8 4.5 %collective-permute-start.15 = (bf16[128,768]{1,0:T(8,128)(2,1)S(1)}, bf16[128,768]{1,0:T(8,128)(2,1)S(1)}, u32[]{:S(2)}, u32[]{:S(2)}) collective-permute-start(bf16[128,768]{1,0:T(8,128)(2,1)S(1)} %get-tuple-element.48), channel_id=1, source_target_pairs={{0,6},{2,4},{4,2},{6,0},{8,14},{10,12},{12,10},{14,8},{1,7},{3,5},... | collective-permute-start | bytes 589832 | tf_op jit(solution)/shard_map/ppermute | solution.py:52
  91.3 3.6 %collective-permute-done.15 = bf16[128,768]{1,0:T(8,128)(2,1)S(1)} collective-permute-done((bf16[128,768]{1,0:T(8,128)(2,1)S(1)}, bf16[128,768]{1,0:T(8,128)(2,1)S(1)}, u32[]{:S(2)}, u32[]{:S(2)}) %collective-permute-start.15) | collective-permute-done | bytes 196640 | tf_op jit(solution)/shard_map/ppermute | solution.py:52
  96.1 1.1 %collective-permute-done.22 = f32[128]{0:T(128)S(1)} collective-permute-done((f32[128]{0:T(128)S(1)}, f32[128]{0:T(128)S(1)}, u32[]{:S(2)}, u32[]{:S(2)}) %collective-permute-start.22) | collective-permute-done | bytes 544 | tf_op jit(solution)/shard_map/ppermute | solution.py:94
  (118 shorter events, 25.0 us)
Async XLA Ops:
  0.0 19.2 %copy-start = (bf16[1536,768]{1,0:T(8,128)(2,1)S(1)}, bf16[1536,768]{1,0:T(8,128)(2,1)}, u32[]{:S(2)}) copy-start(bf16[1536,768]{1,0:T(8,128)(2,1)} %param.20) | copy-start | bytes 7077892
  11.3 6.4 %collective-permute-start = (bf16[128,2,6]{0,2,1:T(8,128)(2,1)S(1)}, bf16[128,2,6]{0,2,1:T(8,128)(2,1)S(1)}, u32[]{:S(2)}, u32[]{:S(2)}) collective-permute-start(bf16[128,2,6]{0,2,1:T(8,128)(2,1)S(1)} %pad_maximum_fusion.1), channel_id=1, source_target_pairs={{0,1},{1,0},{2,3},{3,2},{4,5},{5,4},{6,7},{7,6},{8,9},{9,8},{10,11... | collective-permute-start | bytes 9224 | tf_op jit(solution)/shard_map/ppermute | solution.py:18
  13.1 4.6 %collective-permute-start.2 = (bf16[128,2,6]{0,2,1:T(8,128)(2,1)S(1)}, bf16[128,2,6]{0,2,1:T(8,128)(2,1)S(1)}, u32[]{:S(2)}, u32[]{:S(2)}) collective-permute-start(bf16[128,2,6]{0,2,1:T(8,128)(2,1)S(1)} %pad_maximum_fusion.2), channel_id=1, source_target_pairs={{0,1},{1,0},{2,3},{3,2},{4,5},{5,4},{6,7},{7,6},{8,9},{9,8},{10,11... | collective-permute-start | bytes 9224 | tf_op jit(solution)/shard_map/ppermute | solution.py:18
  15.9 2.1 %collective-permute-start.1 = (bf16[128,2,6,128]{0,3,2,1:T(8,128)(2,1)}, bf16[128,2,6,128]{0,3,2,1:T(8,128)(2,1)}, u32[]{:S(2)}, u32[]{:S(2)}) collective-permute-start(bf16[128,2,6,128]{0,3,2,1:T(8,128)(2,1)} %pad_maximum_fusion), channel_id=1, source_target_pairs={{0,1},{1,0},{2,3},{3,2},{4,5},{5,4},{6,7},{7,6},{8,9},{9,8},{10,11... | collective-permute-start | bytes 1179656 | tf_op jit(solution)/shard_map/ppermute | solution.py:18
  20.8 1.3 %collective-permute-start.3 = (f32[128]{0:T(128)S(1)}, f32[128]{0:T(128)S(1)}, u32[]{:S(2)}, u32[]{:S(2)}) collective-permute-start(f32[128]{0:T(128)S(1)} %get-tuple-element.64), channel_id=1, source_target_pairs={{0,1},{1,0},{2,3},{3,2},{4,5},{5,4},{6,7},{7,6},{8,9},{9,8},{10,11... | collective-permute-start | bytes 1544 | tf_op jit(solution)/shard_map/ppermute | solution.py:94
  22.8 31.3 %collective-permute-start.10 = (bf16[128,768]{1,0:T(8,128)(2,1)S(1)}, bf16[128,768]{1,0:T(8,128)(2,1)S(1)}, u32[]{:S(2)}, u32[]{:S(2)}) collective-permute-start(bf16[128,768]{1,0:T(8,128)(2,1)S(1)} %get-tuple-element.25), channel_id=1, source_target_pairs={{0,14},{2,12},{4,10},{6,8},{8,6},{10,4},{12,2},{14,0},{1,15},{3,13... | collective-permute-start | bytes 589832 | tf_op jit(solution)/shard_map/ppermute | solution.py:52
  27.6 26.4 %collective-permute-start.9 = (bf16[128,768]{1,0:T(8,128)(2,1)S(1)}, bf16[128,768]{1,0:T(8,128)(2,1)S(1)}, u32[]{:S(2)}, u32[]{:S(2)}) collective-permute-start(bf16[128,768]{1,0:T(8,128)(2,1)S(1)} %get-tuple-element.26), channel_id=1, source_target_pairs={{0,12},{2,14},{4,8},{6,10},{8,4},{10,6},{12,0},{14,2},{1,13},{3,15... | collective-permute-start | bytes 589832 | tf_op jit(solution)/shard_map/ppermute | solution.py:52
  28.0 26.0 %collective-permute-start.8 = (bf16[128,768]{1,0:T(8,128)(2,1)S(1)}, bf16[128,768]{1,0:T(8,128)(2,1)S(1)}, u32[]{:S(2)}, u32[]{:S(2)}) collective-permute-start(bf16[128,768]{1,0:T(8,128)(2,1)S(1)} %get-tuple-element.27), channel_id=1, source_target_pairs={{0,10},{2,8},{4,14},{6,12},{8,2},{10,0},{12,6},{14,4},{1,11},{3,9}... | collective-permute-start | bytes 589832 | tf_op jit(solution)/shard_map/ppermute | solution.py:52
  29.5 24.4 %collective-permute-start.7 = (bf16[128,768]{1,0:T(8,128)(2,1)S(1)}, bf16[128,768]{1,0:T(8,128)(2,1)S(1)}, u32[]{:S(2)}, u32[]{:S(2)}) collective-permute-start(bf16[128,768]{1,0:T(8,128)(2,1)S(1)} %get-tuple-element.28), channel_id=1, source_target_pairs={{0,8},{2,10},{4,12},{6,14},{8,0},{10,2},{12,4},{14,6},{1,9},{3,11}... | collective-permute-start | bytes 589832 | tf_op jit(solution)/shard_map/ppermute | solution.py:52
  29.7 7.5 %collective-permute-start.4 = (bf16[128,768]{1,0:T(8,128)(2,1)S(1)}, bf16[128,768]{1,0:T(8,128)(2,1)S(1)}, u32[]{:S(2)}, u32[]{:S(2)}) collective-permute-start(bf16[128,768]{1,0:T(8,128)(2,1)S(1)} %get-tuple-element.42), channel_id=1, source_target_pairs={{0,2},{2,0},{4,6},{6,4},{8,10},{10,8},{12,14},{14,12},{1,3},{3,1},... | collective-permute-start | bytes 589832 | tf_op jit(solution)/shard_map/ppermute | solution.py:52
  37.2 6.4 %collective-permute-start.5 = (bf16[128,768]{1,0:T(8,128)(2,1)S(1)}, bf16[128,768]{1,0:T(8,128)(2,1)S(1)}, u32[]{:S(2)}, u32[]{:S(2)}) collective-permute-start(bf16[128,768]{1,0:T(8,128)(2,1)S(1)} %get-tuple-element.40), channel_id=1, source_target_pairs={{0,4},{2,6},{4,0},{6,2},{8,12},{10,14},{12,8},{14,10},{1,5},{3,7},... | collective-permute-start | bytes 589832 | tf_op jit(solution)/shard_map/ppermute | solution.py:52
  43.6 10.3 %collective-permute-start.6 = (bf16[128,768]{1,0:T(8,128)(2,1)S(1)}, bf16[128,768]{1,0:T(8,128)(2,1)S(1)}, u32[]{:S(2)}, u32[]{:S(2)}) collective-permute-start(bf16[128,768]{1,0:T(8,128)(2,1)S(1)} %get-tuple-element.29), channel_id=1, source_target_pairs={{0,6},{2,4},{4,2},{6,0},{8,14},{10,12},{12,10},{14,8},{1,7},{3,5},... | collective-permute-start | bytes 589832 | tf_op jit(solution)/shard_map/ppermute | solution.py:52
  55.9 2.4 %collective-permute-start.16 = (bf16[512,768]{1,0:T(8,128)(2,1)S(1)}, bf16[512,768]{1,0:T(8,128)(2,1)S(1)}, u32[]{:S(2)}, u32[]{:S(2)}) collective-permute-start(bf16[512,768]{1,0:T(8,128)(2,1)S(1)} %get-tuple-element.23), channel_id=1, source_target_pairs={{0,1},{1,0},{2,3},{3,2},{4,5},{5,4},{6,7},{7,6},{8,9},{9,8},{10,11... | collective-permute-start | bytes 2359304 | tf_op jit(solution)/shard_map/ppermute | solution.py:70
  56.0 5.5 %collective-permute-start.11 = (bf16[512,768]{1,0:T(8,128)(2,1)S(1)}, bf16[512,768]{1,0:T(8,128)(2,1)S(1)}, u32[]{:S(2)}, u32[]{:S(2)}) collective-permute-start(bf16[512,768]{1,0:T(8,128)(2,1)S(1)} %get-tuple-element.24), channel_id=1, source_target_pairs={{0,1},{1,0},{2,3},{3,2},{4,5},{5,4},{6,7},{7,6},{8,9},{9,8},{10,11... | collective-permute-start | bytes 2359304 | tf_op jit(solution)/shard_map/ppermute | solution.py:70
  61.4 3.2 %collective-permute-start.17 = (bf16[512,768]{1,0:T(8,128)(2,1)S(1)}, bf16[512,768]{1,0:T(8,128)(2,1)S(1)}, u32[]{:S(2)}, u32[]{:S(2)}) collective-permute-start(bf16[512,768]{1,0:T(8,128)(2,1)S(1)} %convolution_convert_fusion.1), channel_id=1, source_target_pairs={{0,1},{1,0},{2,3},{3,2},{4,5},{5,4},{6,7},{7,6},{8,9},{9,8},{10,11... | collective-permute-start | bytes 2359304 | tf_op jit(solution)/shard_map/ppermute | solution.py:86
  63.5 7.5 %collective-permute-start.12 = (bf16[512,768]{1,0:T(8,128)(2,1)S(1)}, bf16[512,768]{1,0:T(8,128)(2,1)S(1)}, u32[]{:S(2)}, u32[]{:S(2)}) collective-permute-start(bf16[512,768]{1,0:T(8,128)(2,1)S(1)} %convolution_convert_fusion.3), channel_id=1, source_target_pairs={{0,1},{1,0},{2,3},{3,2},{4,5},{5,4},{6,7},{7,6},{8,9},{9,8},{10,11... | collective-permute-start | bytes 2359304 | tf_op jit(solution)/shard_map/ppermute | solution.py:86
  64.8 30.3 %collective-permute-start.21 = (bf16[128,768]{1,0:T(8,128)(2,1)S(1)}, bf16[128,768]{1,0:T(8,128)(2,1)S(1)}, u32[]{:S(2)}, u32[]{:S(2)}) collective-permute-start(bf16[128,768]{1,0:T(8,128)(2,1)S(1)} %get-tuple-element.44), channel_id=1, source_target_pairs={{0,14},{2,12},{4,10},{6,8},{8,6},{10,4},{12,2},{14,0},{1,15},{3,13... | collective-permute-start | bytes 589832 | tf_op jit(solution)/shard_map/ppermute | solution.py:52
  68.9 26.2 %collective-permute-start.20 = (bf16[128,768]{1,0:T(8,128)(2,1)S(1)}, bf16[128,768]{1,0:T(8,128)(2,1)S(1)}, u32[]{:S(2)}, u32[]{:S(2)}) collective-permute-start(bf16[128,768]{1,0:T(8,128)(2,1)S(1)} %get-tuple-element.45), channel_id=1, source_target_pairs={{0,12},{2,14},{4,8},{6,10},{8,4},{10,6},{12,0},{14,2},{1,13},{3,15... | collective-permute-start | bytes 589832 | tf_op jit(solution)/shard_map/ppermute | solution.py:52
  68.9 26.2 %collective-permute-start.19 = (bf16[128,768]{1,0:T(8,128)(2,1)S(1)}, bf16[128,768]{1,0:T(8,128)(2,1)S(1)}, u32[]{:S(2)}, u32[]{:S(2)}) collective-permute-start(bf16[128,768]{1,0:T(8,128)(2,1)S(1)} %get-tuple-element.46), channel_id=1, source_target_pairs={{0,10},{2,8},{4,14},{6,12},{8,2},{10,0},{12,6},{14,4},{1,11},{3,9}... | collective-permute-start | bytes 589832 | tf_op jit(solution)/shard_map/ppermute | solution.py:52
  70.3 24.7 %collective-permute-start.18 = (bf16[128,768]{1,0:T(8,128)(2,1)S(1)}, bf16[128,768]{1,0:T(8,128)(2,1)S(1)}, u32[]{:S(2)}, u32[]{:S(2)}) collective-permute-start(bf16[128,768]{1,0:T(8,128)(2,1)S(1)} %get-tuple-element.47), channel_id=1, source_target_pairs={{0,8},{2,10},{4,12},{6,14},{8,0},{10,2},{12,4},{14,6},{1,9},{3,11}... | collective-permute-start | bytes 589832 | tf_op jit(solution)/shard_map/ppermute | solution.py:52
  71.2 7.4 %collective-permute-start.13 = (bf16[128,768]{1,0:T(8,128)(2,1)S(1)}, bf16[128,768]{1,0:T(8,128)(2,1)S(1)}, u32[]{:S(2)}, u32[]{:S(2)}) collective-permute-start(bf16[128,768]{1,0:T(8,128)(2,1)S(1)} %get-tuple-element.50), channel_id=1, source_target_pairs={{0,2},{2,0},{4,6},{6,4},{8,10},{10,8},{12,14},{14,12},{1,3},{3,1},... | collective-permute-start | bytes 589832 | tf_op jit(solution)/shard_map/ppermute | solution.py:52
  78.6 8.3 %collective-permute-start.14 = (bf16[128,768]{1,0:T(8,128)(2,1)S(1)}, bf16[128,768]{1,0:T(8,128)(2,1)S(1)}, u32[]{:S(2)}, u32[]{:S(2)}) collective-permute-start(bf16[128,768]{1,0:T(8,128)(2,1)S(1)} %get-tuple-element.49), channel_id=1, source_target_pairs={{0,4},{2,6},{4,0},{6,2},{8,12},{10,14},{12,8},{14,10},{1,5},{3,7},... | collective-permute-start | bytes 589832 | tf_op jit(solution)/shard_map/ppermute | solution.py:52
  86.8 8.2 %collective-permute-start.15 = (bf16[128,768]{1,0:T(8,128)(2,1)S(1)}, bf16[128,768]{1,0:T(8,128)(2,1)S(1)}, u32[]{:S(2)}, u32[]{:S(2)}) collective-permute-start(bf16[128,768]{1,0:T(8,128)(2,1)S(1)} %get-tuple-element.48), channel_id=1, source_target_pairs={{0,6},{2,4},{4,2},{6,0},{8,14},{10,12},{12,10},{14,8},{1,7},{3,5},... | collective-permute-start | bytes 589832 | tf_op jit(solution)/shard_map/ppermute | solution.py:52
  96.0 1.2 %collective-permute-start.22 = (f32[128]{0:T(128)S(1)}, f32[128]{0:T(128)S(1)}, u32[]{:S(2)}, u32[]{:S(2)}) collective-permute-start(f32[128]{0:T(128)S(1)} %get-tuple-element.66), channel_id=1, source_target_pairs={{0,1},{1,0},{2,3},{3,2},{4,5},{5,4},{6,7},{7,6},{8,9},{9,8},{10,11... | collective-permute-start | bytes 1544 | tf_op jit(solution)/shard_map/ppermute | solution.py:94
  (8 other events, 15.7 us)

commit v16 on v7

--- a/solution.py
+++ b/solution.py
@@ -15,7 +15,9 @@
 def merged(shard, axis, join):
     if lax.axis_size(axis) == 2:
         rounded = jax.tree.map(lambda a: a.astype(jnp.bfloat16), shard)
-        other = jax.tree.map(lambda a: lax.ppermute(a, axis, perm=[(0, 1), (1, 0)]), rounded)
+        swap = [(0, 1), (1, 0)]
+        stats = lax.ppermute(jnp.stack(rounded[:2]), axis, perm=swap)
+        other = (stats[0], stats[1], lax.ppermute(rounded[2], axis, perm=swap))
         widen = lambda tree: jax.tree.map(lambda a, own: a.astype(own.dtype), tree, shard)
         return join(widen(rounded), widen(other))
     gathered = jax.tree.map(

time: 88.9 us -> 88.8 us (level)
  starting transfers between devices: 23.7 us -> 22.8 us
  transfers between devices with their start and end apart: 23 -> 22, of which waited for: 13 -> 13; matrix products, arithmetic and copies ran while one was open for 14% -> 14% of each run, Pallas kernels for 0% -> 0%
where the time goes in v16:
time: 88.8 us; the launch traced here: 88.4 us
  waiting for transfers between devices  32 us (36%)
  starting transfers between devices  22.8 us (26%)
  matrix products  16.5 us (19%)
  local copies, waits for them, and re-layouts  9.07 us (10%)
  other arithmetic  7.51 us (8%)
    ppermute x14, waiting for transfers between devices, exchange(): pieces.append(lax.ppermute(chunks[step], 'el', perm=pairs))  29.3 us
    ppermute x14, starting transfers between devices, exchange(): pieces.append(lax.ppermute(chunks[step], 'el', perm=pairs))  21.2 us
    dot_general x8, matrix products, half_product(): return jnp.dot(x, weight, preferred_element_type=jnp.float32)  4.67 us
    unnamed x36, local copies, waits for them, and re-layouts  3.93 us
    dot_general x2, matrix products, one_group(): jnp.einsum('rgd,ld->rgl', head_rows, head_keys, preferred_element_type=jn...  3.85 us
    gather x1, local copies, waits for them, and re-layouts, one_group(): page_row_block = group_pages[local_table.reshape(-1)]  3.32 us
    dot_general x4, matrix products, down_product(): jnp.dot(hidden, weight, preferred_element_type=jnp.float32)  2.48 us
    dot_general x2, matrix products, one_group(): jnp.einsum('rgl,ld->rgd', soft.astype(jnp.bfloat16), head_values, preferr...  2.19 us
  transfers between devices with their start and end apart: 22, of which 13 were waited for; matrix products, arithmetic and copies ran while one was open for 14% of the time, Pallas kernels for 0%

profile of v16, /device:TPU:0, one launch (start us, length us, event | category | flops | bytes accessed | tf_op | source)
XLA Modules:
  0.0 88.4 jit_solution(4256327843759856111)
XLA Ops:
  4.2 3.3 %gather_fusion = bf16[96,16,512]{2,1,0:T(8,128)(2,1)} fusion(bf16[96,16,512]{2,1,0:T(8,128)(2,1)} %bitcast.215, s32[1024]{0:T(1024)S(1)} %pad_clamp_fusion), kind=kCustom, calls=%fused_computation | custom fusion | bytes 3146112 | tf_op jit(solution)/shard_map/while/body/eval_jaxpr/gather | solution.py:172
  8.5 1.9 %fusion.3 = (f32[128,6]{0,1:T(8,128)S(1)}, f32[1536,128,6]{1,0,2:T(8,128)S(1)}) fusion(pred[128,1536]{0,1:T(8,128)(4,1)S(1)} %compare_and_fusion, bf16[128,6,128]{0,2,1:T(8,128)(2,1)S(1)} %bitcast.217, bf16[1536,512]{1,0:T(8,128)(2,1)} %bitcast.210), kind=kOutput, calls=%fused_computation.8 | convolution fusion | flops 305528064 | bytes 5508096 | tf_op jit(solution)/shard_map/while/body/eval_jaxpr/rgd,ld->rgl/dot_general | solution.py:197
  10.5 1.9 %fusion.6 = (bf16[128,6]{0,1:T(8,128)(2,1)S(1)}, f32[128,6]{0,1:T(8,128)S(1)}, f32[1536,128,6]{1,0,2:T(8,128)S(1)}) fusion(f32[1536,128,6]{1,0,2:T(8,128)S(1)} %get-tuple-element.63, f32[128,6]{0,1:T(8,128)S(1)} %get-tuple-element.62, pred[128,1536]{0,1:T(8,128)(4,1)S(1)} %compare_and_fusion, bf16[128,6,128]{0,2,1:T(8,128)(2,1)S(1)} %bitcast.218, ...), kind=kOutput, calls=%fused_computation.11 | convolution fusion | flops 310245888 | bytes 10232320 | tf_op jit(solution)/shard_map/while/body/eval_jaxpr/rgd,ld->rgl/dot_general | solution.py:197
  13.9 1.1 %fusion.29 = bf16[128,1,6,128]{0,3,2,1:T(8,128)(2,1)S(1)} fusion(f32[1536,128,6]{1,0,2:T(8,128)S(1)} %get-tuple-element.64, f32[128,6]{0,1:T(8,128)S(1)} %get-tuple-element.24, pred[128,1536]{0,1:T(8,128)(4,1)S(1)} %compare_and_fusion, bf16[1536,512]{1,0:T(8,128)(2,1)S(1)} %bitcast.212), kind=kOutput, calls=%fused_computation.44 | convolution fusion | flops 306806784 | bytes 5509120 | tf_op jit(solution)/shard_map/while/body/eval_jaxpr/rgl,ld->rgd/dot_general | solution.py:203
  15.0 1.1 %fusion.32 = bf16[128,1,6,128]{0,3,2,1:T(8,128)(2,1)S(1)} fusion(f32[1536,128,6]{1,0,2:T(8,128)S(1)} %get-tuple-element.63, f32[128,6]{0,1:T(8,128)S(1)} %get-tuple-element.62, pred[128,1536]{0,1:T(8,128)(4,1)S(1)} %compare_and_fusion, bf16[1536,512]{1,0:T(8,128)(2,1)S(1)} %bitcast.213), kind=kOutput, calls=%fused_computation.45 | convolution fusion | flops 306806784 | bytes 5509120 | tf_op jit(solution)/shard_map/while/body/eval_jaxpr/rgl,ld->rgd/dot_general | solution.py:203
  19.0 1.2 %divide_convert_fusion = bf16[128,2,6,128]{0,3,2,1:T(8,128)(2,1)S(1)} fusion(bf16[128,2,6,128]{0,3,2,1:T(8,128)(2,1)} %collective-permute-done.1, f32[128,2,6]{0,2,1:T(8,128)S(1)} %get-tuple-element.57, f32[128,2,6]{0,2,1:T(8,128)S(1)} %get-tuple-element.56, f32[128,2,6]{0,2,1:T(8,128)S(1)} %get-tuple-element.55, bf16[128,1,6,128]{0,3,2,1:T(8,128)(2,1)S(1)} %fusion.29, ...), kind=kLoop, calls=%fused_computation.50 | loop fusion | flops 1572864 | bytes 1198080 | tf_op jit(solution)/shard_map/convert_element_type | solution.py:223
  20.2 1.5 %multiply_reduce_fusion.1 = (f32[128]{0:T(128)S(1)}, f32[128,768]{1,0:T(8,128)S(1)}) fusion(bf16[128,1536]{0,1:T(8,128)(2,1)S(1)} %bitcast.216, bf16[1536,768]{1,0:T(8,128)(2,1)S(1)} %copy-done, bf16[128,768]{1,0:T(8,128)(2,1)} %param.14), kind=kOutput, calls=%fused_computation.90 | convolution fusion | flops 302382976 | bytes 3342848 | tf_op jit(solution)/shard_map/dot_general | solution.py:225
  23.7 2.8 %collective-permute-start.3 = (bf16[128,768]{1,0:T(8,128)(2,1)S(1)}, bf16[128,768]{1,0:T(8,128)(2,1)S(1)}, u32[]{:S(2)}, u32[]{:S(2)}) collective-permute-start(bf16[128,768]{1,0:T(8,128)(2,1)S(1)} %get-tuple-element.45), channel_id=1, source_target_pairs={{0,2},{2,0},{4,6},{6,4},{8,10},{10,8},{12,14},{14,12},{1,3},{3,1},... | collective-permute-start | bytes 589832 | tf_op jit(solution)/shard_map/ppermute | solution.py:54
  26.4 1.5 %collective-permute-start.4 = (bf16[128,768]{1,0:T(8,128)(2,1)S(1)}, bf16[128,768]{1,0:T(8,128)(2,1)S(1)}, u32[]{:S(2)}, u32[]{:S(2)}) collective-permute-start(bf16[128,768]{1,0:T(8,128)(2,1)S(1)} %get-tuple-element.44), channel_id=1, source_target_pairs={{0,4},{2,6},{4,0},{6,2},{8,12},{10,14},{12,8},{14,10},{1,5},{3,7},... | collective-permute-start | bytes 589832 | tf_op jit(solution)/shard_map/ppermute | solution.py:54
  28.0 2.0 %collective-permute-start.6 = (bf16[128,768]{1,0:T(8,128)(2,1)S(1)}, bf16[128,768]{1,0:T(8,128)(2,1)S(1)}, u32[]{:S(2)}, u32[]{:S(2)}) collective-permute-start(bf16[128,768]{1,0:T(8,128)(2,1)S(1)} %get-tuple-element.40), channel_id=1, source_target_pairs={{0,8},{2,10},{4,12},{6,14},{8,0},{10,2},{12,4},{14,6},{1,9},{3,11}... | collective-permute-start | bytes 589832 | tf_op jit(solution)/shard_map/ppermute | solution.py:54
  30.0 1.4 %collective-permute-start.7 = (bf16[128,768]{1,0:T(8,128)(2,1)S(1)}, bf16[128,768]{1,0:T(8,128)(2,1)S(1)}, u32[]{:S(2)}, u32[]{:S(2)}) collective-permute-start(bf16[128,768]{1,0:T(8,128)(2,1)S(1)} %get-tuple-element.29), channel_id=1, source_target_pairs={{0,10},{2,8},{4,14},{6,12},{8,2},{10,0},{12,6},{14,4},{1,11},{3,9}... | collective-permute-start | bytes 589832 | tf_op jit(solution)/shard_map/ppermute | solution.py:54
  32.1 3.1 %collective-permute-start.8 = (bf16[128,768]{1,0:T(8,128)(2,1)S(1)}, bf16[128,768]{1,0:T(8,128)(2,1)S(1)}, u32[]{:S(2)}, u32[]{:S(2)}) collective-permute-start(bf16[128,768]{1,0:T(8,128)(2,1)S(1)} %get-tuple-element.28), channel_id=1, source_target_pairs={{0,12},{2,14},{4,8},{6,10},{8,4},{10,6},{12,0},{14,2},{1,13},{3,15... | collective-permute-start | bytes 589832 | tf_op jit(solution)/shard_map/ppermute | solution.py:54
  35.8 1.3 %collective-permute-start.9 = (bf16[128,768]{1,0:T(8,128)(2,1)S(1)}, bf16[128,768]{1,0:T(8,128)(2,1)S(1)}, u32[]{:S(2)}, u32[]{:S(2)}) collective-permute-start(bf16[128,768]{1,0:T(8,128)(2,1)S(1)} %get-tuple-element.27), channel_id=1, source_target_pairs={{0,14},{2,12},{4,10},{6,8},{8,6},{10,4},{12,2},{14,0},{1,15},{3,13... | collective-permute-start | bytes 589832 | tf_op jit(solution)/shard_map/ppermute | solution.py:54
  37.1 3.4 %collective-permute-done.5 = bf16[128,768]{1,0:T(8,128)(2,1)S(1)} collective-permute-done((bf16[128,768]{1,0:T(8,128)(2,1)S(1)}, bf16[128,768]{1,0:T(8,128)(2,1)S(1)}, u32[]{:S(2)}, u32[]{:S(2)}) %collective-permute-start.5) | collective-permute-done | bytes 196640 | tf_op jit(solution)/shard_map/ppermute | solution.py:54
  41.5 4.2 %collective-permute-done.8 = bf16[128,768]{1,0:T(8,128)(2,1)S(1)} collective-permute-done((bf16[128,768]{1,0:T(8,128)(2,1)S(1)}, bf16[128,768]{1,0:T(8,128)(2,1)S(1)}, u32[]{:S(2)}, u32[]{:S(2)}) %collective-permute-start.8) | collective-permute-done | bytes 196640 | tf_op jit(solution)/shard_map/ppermute | solution.py:54
  45.7 3.6 %collective-permute-done.9 = bf16[128,768]{1,0:T(8,128)(2,1)S(1)} collective-permute-done((bf16[128,768]{1,0:T(8,128)(2,1)S(1)}, bf16[128,768]{1,0:T(8,128)(2,1)S(1)}, u32[]{:S(2)}, u32[]{:S(2)}) %collective-permute-start.9) | collective-permute-done | bytes 196640 | tf_op jit(solution)/shard_map/ppermute | solution.py:54
  49.5 1.1 %copy-done.1 = bf16[1,1536,384]{2,1,0:T(8,128)(2,1)S(1)} copy-done((bf16[1,1536,384]{2,1,0:T(8,128)(2,1)S(1)}, bf16[1,1536,384]{2,1,0:T(8,128)(2,1)}, u32[]{:S(2)}) %copy-start.1) | copy-done | bytes 1179672
  60.1 1.6 %collective-permute-start.17 = (bf16[128,768]{1,0:T(8,128)(2,1)S(1)}, bf16[128,768]{1,0:T(8,128)(2,1)S(1)}, u32[]{:S(2)}, u32[]{:S(2)}) collective-permute-start(bf16[128,768]{1,0:T(8,128)(2,1)S(1)} %get-tuple-element.49), channel_id=1, source_target_pairs={{0,8},{2,10},{4,12},{6,14},{8,0},{10,2},{12,4},{14,6},{1,9},{3,11}... | collective-permute-start | bytes 589832 | tf_op jit(solution)/shard_map/ppermute | solution.py:54
  63.1 2.4 %collective-permute-start.14 = (bf16[128,768]{1,0:T(8,128)(2,1)S(1)}, bf16[128,768]{1,0:T(8,128)(2,1)S(1)}, u32[]{:S(2)}, u32[]{:S(2)}) collective-permute-start(bf16[128,768]{1,0:T(8,128)(2,1)S(1)} %get-tuple-element.50), channel_id=1, source_target_pairs={{0,6},{2,4},{4,2},{6,0},{8,14},{10,12},{12,10},{14,8},{1,7},{3,5},... | collective-permute-start | bytes 589832 | tf_op jit(solution)/shard_map/ppermute | solution.py:54
  66.5 7.5 %collective-permute-done.12 = bf16[128,768]{1,0:T(8,128)(2,1)S(1)} collective-permute-done((bf16[128,768]{1,0:T(8,128)(2,1)S(1)}, bf16[128,768]{1,0:T(8,128)(2,1)S(1)}, u32[]{:S(2)}, u32[]{:S(2)}) %collective-permute-start.12) | collective-permute-done | bytes 196640 | tf_op jit(solution)/shard_map/ppermute | solution.py:54
  74.9 2.1 %collective-permute-start.20 = (bf16[128,768]{1,0:T(8,128)(2,1)S(1)}, bf16[128,768]{1,0:T(8,128)(2,1)S(1)}, u32[]{:S(2)}, u32[]{:S(2)}) collective-permute-start(bf16[128,768]{1,0:T(8,128)(2,1)S(1)} %get-tuple-element.46), channel_id=1, source_target_pairs={{0,14},{2,12},{4,10},{6,8},{8,6},{10,4},{12,2},{14,0},{1,15},{3,13... | collective-permute-start | bytes 589832 | tf_op jit(solution)/shard_map/ppermute | solution.py:54
  77.1 6.1 %collective-permute-done.14 = bf16[128,768]{1,0:T(8,128)(2,1)S(1)} collective-permute-done((bf16[128,768]{1,0:T(8,128)(2,1)S(1)}, bf16[128,768]{1,0:T(8,128)(2,1)S(1)}, u32[]{:S(2)}, u32[]{:S(2)}) %collective-permute-start.14) | collective-permute-done | bytes 196640 | tf_op jit(solution)/shard_map/ppermute | solution.py:54
  83.6 1.9 %collective-permute-done.20 = bf16[128,768]{1,0:T(8,128)(2,1)S(1)} collective-permute-done((bf16[128,768]{1,0:T(8,128)(2,1)S(1)}, bf16[128,768]{1,0:T(8,128)(2,1)S(1)}, u32[]{:S(2)}, u32[]{:S(2)}) %collective-permute-start.20) | collective-permute-done | bytes 196640 | tf_op jit(solution)/shard_map/ppermute | solution.py:54
  86.5 1.1 %collective-permute-done.21 = f32[128]{0:T(128)S(1)} collective-permute-done((f32[128]{0:T(128)S(1)}, f32[128]{0:T(128)S(1)}, u32[]{:S(2)}, u32[]{:S(2)}) %collective-permute-start.21) | collective-permute-done | bytes 544 | tf_op jit(solution)/shard_map/ppermute | solution.py:96
  (114 shorter events, 28.7 us)
Async XLA Ops:
  0.0 20.2 %copy-start = (bf16[1536,768]{1,0:T(8,128)(2,1)S(1)}, bf16[1536,768]{1,0:T(8,128)(2,1)}, u32[]{:S(2)}) copy-start(bf16[1536,768]{1,0:T(8,128)(2,1)} %param.20) | copy-start | bytes 7077892
  13.4 4.9 %collective-permute-start = (bf16[2,128,2,6]{1,3,2,0:T(8,128)(2,1)S(1)}, bf16[2,128,2,6]{1,3,2,0:T(8,128)(2,1)S(1)}, u32[]{:S(2)}, u32[]{:S(2)}) collective-permute-start(bf16[2,128,2,6]{1,3,2,0:T(8,128)(2,1)S(1)} %maximum_maximum_fusion), channel_id=1, source_target_pairs={{0,1},{1,0},{2,3},{3,2},{4,5},{5,4},{6,7},{7,6},{8,9},{9,8},{10,11... | collective-permute-start | bytes 18440 | tf_op jit(solution)/shard_map/ppermute | solution.py:19
  16.9 2.1 %collective-permute-start.1 = (bf16[128,2,6,128]{0,3,2,1:T(8,128)(2,1)}, bf16[128,2,6,128]{0,3,2,1:T(8,128)(2,1)}, u32[]{:S(2)}, u32[]{:S(2)}) collective-permute-start(bf16[128,2,6,128]{0,3,2,1:T(8,128)(2,1)} %pad_maximum_fusion), channel_id=1, source_target_pairs={{0,1},{1,0},{2,3},{3,2},{4,5},{5,4},{6,7},{7,6},{8,9},{9,8},{10,11... | collective-permute-start | bytes 1179656 | tf_op jit(solution)/shard_map/ppermute | solution.py:20
  21.7 1.2 %collective-permute-start.2 = (f32[128]{0:T(128)S(1)}, f32[128]{0:T(128)S(1)}, u32[]{:S(2)}, u32[]{:S(2)}) collective-permute-start(f32[128]{0:T(128)S(1)} %get-tuple-element.65), channel_id=1, source_target_pairs={{0,1},{1,0},{2,3},{3,2},{4,5},{5,4},{6,7},{7,6},{8,9},{9,8},{10,11... | collective-permute-start | bytes 1544 | tf_op jit(solution)/shard_map/ppermute | solution.py:96
  23.7 8.4 %collective-permute-start.3 = (bf16[128,768]{1,0:T(8,128)(2,1)S(1)}, bf16[128,768]{1,0:T(8,128)(2,1)S(1)}, u32[]{:S(2)}, u32[]{:S(2)}) collective-permute-start(bf16[128,768]{1,0:T(8,128)(2,1)S(1)} %get-tuple-element.45), channel_id=1, source_target_pairs={{0,2},{2,0},{4,6},{6,4},{8,10},{10,8},{12,14},{14,12},{1,3},{3,1},... | collective-permute-start | bytes 589832 | tf_op jit(solution)/shard_map/ppermute | solution.py:54
  26.4 9.4 %collective-permute-start.4 = (bf16[128,768]{1,0:T(8,128)(2,1)S(1)}, bf16[128,768]{1,0:T(8,128)(2,1)S(1)}, u32[]{:S(2)}, u32[]{:S(2)}) collective-permute-start(bf16[128,768]{1,0:T(8,128)(2,1)S(1)} %get-tuple-element.44), channel_id=1, source_target_pairs={{0,4},{2,6},{4,0},{6,2},{8,12},{10,14},{12,8},{14,10},{1,5},{3,7},... | collective-permute-start | bytes 589832 | tf_op jit(solution)/shard_map/ppermute | solution.py:54
  27.9 12.6 %collective-permute-start.5 = (bf16[128,768]{1,0:T(8,128)(2,1)S(1)}, bf16[128,768]{1,0:T(8,128)(2,1)S(1)}, u32[]{:S(2)}, u32[]{:S(2)}) collective-permute-start(bf16[128,768]{1,0:T(8,128)(2,1)S(1)} %get-tuple-element.42), channel_id=1, source_target_pairs={{0,6},{2,4},{4,2},{6,0},{8,14},{10,12},{12,10},{14,8},{1,7},{3,5},... | collective-permute-start | bytes 589832 | tf_op jit(solution)/shard_map/ppermute | solution.py:54
  28.0 12.6 %collective-permute-start.6 = (bf16[128,768]{1,0:T(8,128)(2,1)S(1)}, bf16[128,768]{1,0:T(8,128)(2,1)S(1)}, u32[]{:S(2)}, u32[]{:S(2)}) collective-permute-start(bf16[128,768]{1,0:T(8,128)(2,1)S(1)} %get-tuple-element.40), channel_id=1, source_target_pairs={{0,8},{2,10},{4,12},{6,14},{8,0},{10,2},{12,4},{14,6},{1,9},{3,11}... | collective-permute-start | bytes 589832 | tf_op jit(solution)/shard_map/ppermute | solution.py:54
  30.0 11.4 %collective-permute-start.7 = (bf16[128,768]{1,0:T(8,128)(2,1)S(1)}, bf16[128,768]{1,0:T(8,128)(2,1)S(1)}, u32[]{:S(2)}, u32[]{:S(2)}) collective-permute-start(bf16[128,768]{1,0:T(8,128)(2,1)S(1)} %get-tuple-element.29), channel_id=1, source_target_pairs={{0,10},{2,8},{4,14},{6,12},{8,2},{10,0},{12,6},{14,4},{1,11},{3,9}... | collective-permute-start | bytes 589832 | tf_op jit(solution)/shard_map/ppermute | solution.py:54
  32.1 13.6 %collective-permute-start.8 = (bf16[128,768]{1,0:T(8,128)(2,1)S(1)}, bf16[128,768]{1,0:T(8,128)(2,1)S(1)}, u32[]{:S(2)}, u32[]{:S(2)}) collective-permute-start(bf16[128,768]{1,0:T(8,128)(2,1)S(1)} %get-tuple-element.28), channel_id=1, source_target_pairs={{0,12},{2,14},{4,8},{6,10},{8,4},{10,6},{12,0},{14,2},{1,13},{3,15... | collective-permute-start | bytes 589832 | tf_op jit(solution)/shard_map/ppermute | solution.py:54
  35.8 13.4 %collective-permute-start.9 = (bf16[128,768]{1,0:T(8,128)(2,1)S(1)}, bf16[128,768]{1,0:T(8,128)(2,1)S(1)}, u32[]{:S(2)}, u32[]{:S(2)}) collective-permute-start(bf16[128,768]{1,0:T(8,128)(2,1)S(1)} %get-tuple-element.27), channel_id=1, source_target_pairs={{0,14},{2,12},{4,10},{6,8},{8,6},{10,4},{12,2},{14,0},{1,15},{3,13... | collective-permute-start | bytes 589832 | tf_op jit(solution)/shard_map/ppermute | solution.py:54
  49.4 4.2 %collective-permute-start.15 = (bf16[512,768]{1,0:T(8,128)(2,1)S(1)}, bf16[512,768]{1,0:T(8,128)(2,1)S(1)}, u32[]{:S(2)}, u32[]{:S(2)}) collective-permute-start(bf16[512,768]{1,0:T(8,128)(2,1)S(1)} %get-tuple-element.25), channel_id=1, source_target_pairs={{0,1},{1,0},{2,3},{3,2},{4,5},{5,4},{6,7},{7,6},{8,9},{9,8},{10,11... | collective-permute-start | bytes 2359304 | tf_op jit(solution)/shard_map/ppermute | solution.py:72
  51.1 5.7 %collective-permute-start.10 = (bf16[512,768]{1,0:T(8,128)(2,1)S(1)}, bf16[512,768]{1,0:T(8,128)(2,1)S(1)}, u32[]{:S(2)}, u32[]{:S(2)}) collective-permute-start(bf16[512,768]{1,0:T(8,128)(2,1)S(1)} %get-tuple-element.26), channel_id=1, source_target_pairs={{0,1},{1,0},{2,3},{3,2},{4,5},{5,4},{6,7},{7,6},{8,9},{9,8},{10,11... | collective-permute-start | bytes 2359304 | tf_op jit(solution)/shard_map/ppermute | solution.py:72
  56.2 3.6 %collective-permute-start.16 = (bf16[512,768]{1,0:T(8,128)(2,1)S(1)}, bf16[512,768]{1,0:T(8,128)(2,1)S(1)}, u32[]{:S(2)}, u32[]{:S(2)}) collective-permute-start(bf16[512,768]{1,0:T(8,128)(2,1)S(1)} %convolution_convert_fusion.1), channel_id=1, source_target_pairs={{0,1},{1,0},{2,3},{3,2},{4,5},{5,4},{6,7},{7,6},{8,9},{9,8},{10,11... | collective-permute-start | bytes 2359304 | tf_op jit(solution)/shard_map/ppermute | solution.py:88
  58.7 3.1 %collective-permute-start.11 = (bf16[512,768]{1,0:T(8,128)(2,1)S(1)}, bf16[512,768]{1,0:T(8,128)(2,1)S(1)}, u32[]{:S(2)}, u32[]{:S(2)}) collective-permute-start(bf16[512,768]{1,0:T(8,128)(2,1)S(1)} %convolution_convert_fusion.3), channel_id=1, source_target_pairs={{0,1},{1,0},{2,3},{3,2},{4,5},{5,4},{6,7},{7,6},{8,9},{9,8},{10,11... | collective-permute-start | bytes 2359304 | tf_op jit(solution)/shard_map/ppermute | solution.py:88
  60.1 23.1 %collective-permute-start.17 = (bf16[128,768]{1,0:T(8,128)(2,1)S(1)}, bf16[128,768]{1,0:T(8,128)(2,1)S(1)}, u32[]{:S(2)}, u32[]{:S(2)}) collective-permute-start(bf16[128,768]{1,0:T(8,128)(2,1)S(1)} %get-tuple-element.49), channel_id=1, source_target_pairs={{0,8},{2,10},{4,12},{6,14},{8,0},{10,2},{12,4},{14,6},{1,9},{3,11}... | collective-permute-start | bytes 589832 | tf_op jit(solution)/shard_map/ppermute | solution.py:54
  62.0 12.1 %collective-permute-start.12 = (bf16[128,768]{1,0:T(8,128)(2,1)S(1)}, bf16[128,768]{1,0:T(8,128)(2,1)S(1)}, u32[]{:S(2)}, u32[]{:S(2)}) collective-permute-start(bf16[128,768]{1,0:T(8,128)(2,1)S(1)} %get-tuple-element.52), channel_id=1, source_target_pairs={{0,2},{2,0},{4,6},{6,4},{8,10},{10,8},{12,14},{14,12},{1,3},{3,1},... | collective-permute-start | bytes 589832 | tf_op jit(solution)/shard_map/ppermute | solution.py:54
  62.6 12.3 %collective-permute-start.13 = (bf16[128,768]{1,0:T(8,128)(2,1)S(1)}, bf16[128,768]{1,0:T(8,128)(2,1)S(1)}, u32[]{:S(2)}, u32[]{:S(2)}) collective-permute-start(bf16[128,768]{1,0:T(8,128)(2,1)S(1)} %get-tuple-element.51), channel_id=1, source_target_pairs={{0,4},{2,6},{4,0},{6,2},{8,12},{10,14},{12,8},{14,10},{1,5},{3,7},... | collective-permute-start | bytes 589832 | tf_op jit(solution)/shard_map/ppermute | solution.py:54
  63.1 20.1 %collective-permute-start.14 = (bf16[128,768]{1,0:T(8,128)(2,1)S(1)}, bf16[128,768]{1,0:T(8,128)(2,1)S(1)}, u32[]{:S(2)}, u32[]{:S(2)}) collective-permute-start(bf16[128,768]{1,0:T(8,128)(2,1)S(1)} %get-tuple-element.50), channel_id=1, source_target_pairs={{0,6},{2,4},{4,2},{6,0},{8,14},{10,12},{12,10},{14,8},{1,7},{3,5},... | collective-permute-start | bytes 589832 | tf_op jit(solution)/shard_map/ppermute | solution.py:54
  65.5 17.7 %collective-permute-start.18 = (bf16[128,768]{1,0:T(8,128)(2,1)S(1)}, bf16[128,768]{1,0:T(8,128)(2,1)S(1)}, u32[]{:S(2)}, u32[]{:S(2)}) collective-permute-start(bf16[128,768]{1,0:T(8,128)(2,1)S(1)} %get-tuple-element.48), channel_id=1, source_target_pairs={{0,10},{2,8},{4,14},{6,12},{8,2},{10,0},{12,6},{14,4},{1,11},{3,9}... | collective-permute-start | bytes 589832 | tf_op jit(solution)/shard_map/ppermute | solution.py:54
  74.0 9.6 %collective-permute-start.19 = (bf16[128,768]{1,0:T(8,128)(2,1)S(1)}, bf16[128,768]{1,0:T(8,128)(2,1)S(1)}, u32[]{:S(2)}, u32[]{:S(2)}) collective-permute-start(bf16[128,768]{1,0:T(8,128)(2,1)S(1)} %get-tuple-element.47), channel_id=1, source_target_pairs={{0,12},{2,14},{4,8},{6,10},{8,4},{10,6},{12,0},{14,2},{1,13},{3,15... | collective-permute-start | bytes 589832 | tf_op jit(solution)/shard_map/ppermute | solution.py:54
  74.9 10.6 %collective-permute-start.20 = (bf16[128,768]{1,0:T(8,128)(2,1)S(1)}, bf16[128,768]{1,0:T(8,128)(2,1)S(1)}, u32[]{:S(2)}, u32[]{:S(2)}) collective-permute-start(bf16[128,768]{1,0:T(8,128)(2,1)S(1)} %get-tuple-element.46), channel_id=1, source_target_pairs={{0,14},{2,12},{4,10},{6,8},{8,6},{10,4},{12,2},{14,0},{1,15},{3,13... | collective-permute-start | bytes 589832 | tf_op jit(solution)/shard_map/ppermute | solution.py:54
  83.6 4.0 %copy-start.7 = (f32[768]{0:T(1024)S(1)}, f32[768]{0:T(1024)}, u32[]{:S(2)}) copy-start(f32[768]{0:T(1024)} %param.27) | copy-start | bytes 9220
  86.4 1.2 %collective-permute-start.21 = (f32[128]{0:T(128)S(1)}, f32[128]{0:T(128)S(1)}, u32[]{:S(2)}, u32[]{:S(2)}) collective-permute-start(f32[128]{0:T(128)S(1)} %get-tuple-element.67), channel_id=1, source_target_pairs={{0,1},{1,0},{2,3},{3,2},{4,5},{5,4},{6,7},{7,6},{8,9},{9,8},{10,11... | collective-permute-start | bytes 1544 | tf_op jit(solution)/shard_map/ppermute | solution.py:96
  (7 other events, 13.1 us)

commit v17 on v7

--- a/solution.py
+++ b/solution.py
@@ -186,8 +186,9 @@
         score_mask = allowed[:, None, :]
         outs = []
         for kv_head in range(KEY_VALUE_HEADS):
-            head_rows = queries[:, kv_head * head_groups * HEAD_SIZE : (kv_head + 1) * head_groups * HEAD_SIZE]
-            head_rows = head_rows.reshape(group_rows, head_groups, HEAD_SIZE)
+            head_rows = queries.reshape(group_rows, QUERY_HEADS, HEAD_SIZE)[
+                :, kv_head * head_groups : (kv_head + 1) * head_groups, :
+            ]
             head_keys = flattened_cache[:, kv_head * HEAD_SIZE : (kv_head + 1) * HEAD_SIZE]
             head_values = flattened_cache[
                 :, (KEY_VALUE_HEADS + kv_head) * HEAD_SIZE : (KEY_VALUE_HEADS + kv_head + 1) * HEAD_SIZE

time: 88.9 us -> 88.8 us (level)
    slice x1 -> x0, local copies, waits for them, and re-layouts: 1.05 us -> none  [one_group(): queries[:, kv_head * head_groups * HEAD_SIZE:(kv_head + 1) * head_groups...]
    unnamed x36 -> x35, local copies, waits for them, and re-layouts: 3.93 us -> 4.82 us
where the time goes in v17:
time: 88.8 us; the launch traced here: 88.4 us
  waiting for transfers between devices  31.2 us (35%)
  starting transfers between devices  23.7 us (27%)
  matrix products  16.5 us (19%)
  local copies, waits for them, and re-layouts  8.91 us (10%)
  other arithmetic  7.54 us (8%)
    ppermute x14, waiting for transfers between devices, exchange(): pieces.append(lax.ppermute(chunks[step], 'el', perm=pairs))  29 us
    ppermute x14, starting transfers between devices, exchange(): pieces.append(lax.ppermute(chunks[step], 'el', perm=pairs))  21.4 us
    unnamed x35, local copies, waits for them, and re-layouts  4.82 us
    dot_general x8, matrix products, half_product(): return jnp.dot(x, weight, preferred_element_type=jnp.float32)  4.67 us
    dot_general x2, matrix products, one_group(): jnp.einsum('rgd,ld->rgl', head_rows, head_keys, preferred_element_type=jn...  3.84 us
    gather x1, local copies, waits for them, and re-layouts, one_group(): page_row_block = group_pages[local_table.reshape(-1)]  3.32 us
    dot_general x4, matrix products, down_product(): jnp.dot(hidden, weight, preferred_element_type=jnp.float32)  2.51 us
    dot_general x2, matrix products, one_group(): jnp.einsum('rgl,ld->rgd', soft.astype(jnp.bfloat16), head_values, preferr...  2.19 us
  transfers between devices with their start and end apart: 23, of which 13 were waited for; matrix products, arithmetic and copies ran while one was open for 14% of the time, Pallas kernels for 0%

profile of v17, /device:TPU:0, one launch (start us, length us, event | category | flops | bytes accessed | tf_op | source)
XLA Modules:
  0.0 88.4 jit_solution(12828346134549209395)
XLA Ops:
  2.8 1.2 %copy.50 = bf16[128,1536]{0,1:T(8,128)(2,1)S(1)} copy(bf16[128,1536]{1,0:T(8,128)(2,1)} %param.15) | data formatting | bytes 786432 | tf_op args[1]
  4.1 3.3 %gather_fusion = bf16[96,16,512]{2,1,0:T(8,128)(2,1)} fusion(bf16[96,16,512]{2,1,0:T(8,128)(2,1)} %bitcast.186, s32[1024]{0:T(1024)S(1)} %pad_clamp_fusion), kind=kCustom, calls=%fused_computation | custom fusion | bytes 3146112 | tf_op jit(solution)/shard_map/while/body/eval_jaxpr/gather | solution.py:170
  8.3 1.9 %fusion.3 = (f32[128,6]{0,1:T(8,128)S(1)}, f32[1536,128,6]{1,0,2:T(8,128)S(1)}) fusion(pred[128,1536]{0,1:T(8,128)(4,1)S(1)} %compare_and_fusion, bf16[128,12,128]{0,2,1:T(8,128)(2,1)S(1)} %bitcast.188, bf16[1536,512]{1,0:T(8,128)(2,1)} %bitcast.181), kind=kOutput, calls=%fused_computation.8 | convolution fusion | flops 305528064 | bytes 5508096 | tf_op jit(solution)/shard_map/while/body/eval_jaxpr/rgd,ld->rgl/dot_general | solution.py:196
  10.3 1.9 %fusion.6 = (bf16[128,6]{0,1:T(8,128)(2,1)S(1)}, f32[128,6]{0,1:T(8,128)S(1)}, f32[1536,128,6]{1,0,2:T(8,128)S(1)}) fusion(f32[1536,128,6]{1,0,2:T(8,128)S(1)} %get-tuple-element.57, f32[128,6]{0,1:T(8,128)S(1)} %get-tuple-element.56, pred[128,1536]{0,1:T(8,128)(4,1)S(1)} %compare_and_fusion, bf16[128,12,128]{0,2,1:T(8,128)(2,1)S(1)} %bitcast.189, ...), kind=kOutput, calls=%fused_computation.11 | convolution fusion | flops 310245888 | bytes 10232320 | tf_op jit(solution)/shard_map/while/body/eval_jaxpr/rgd,ld->rgl/dot_general | solution.py:196
  13.9 1.1 %fusion.29 = bf16[128,1,6,128]{0,3,2,1:T(8,128)(2,1)S(1)} fusion(f32[1536,128,6]{1,0,2:T(8,128)S(1)} %get-tuple-element.58, f32[128,6]{0,1:T(8,128)S(1)} %get-tuple-element.24, pred[128,1536]{0,1:T(8,128)(4,1)S(1)} %compare_and_fusion, bf16[1536,512]{1,0:T(8,128)(2,1)S(1)} %bitcast.183), kind=kOutput, calls=%fused_computation.44 | convolution fusion | flops 306806784 | bytes 5509120 | tf_op jit(solution)/shard_map/while/body/eval_jaxpr/rgl,ld->rgd/dot_general | solution.py:202
  19.0 1.2 %divide_convert_fusion = bf16[128,2,6,128]{0,3,2,1:T(8,128)(2,1)S(1)} fusion(bf16[128,2,6,128]{0,3,2,1:T(8,128)(2,1)} %collective-permute-done.1, f32[128,2,6]{0,2,1:T(8,128)S(1)} %get-tuple-element.54, f32[128,2,6]{0,2,1:T(8,128)S(1)} %get-tuple-element.55, f32[128,2,6]{0,2,1:T(8,128)S(1)} %get-tuple-element.53, bf16[128,1,6,128]{0,3,2,1:T(8,128)(2,1)S(1)} %fusion.29, ...), kind=kLoop, calls=%fused_computation.50 | loop fusion | flops 1572864 | bytes 1198080 | tf_op jit(solution)/shard_map/convert_element_type | solution.py:222
  20.2 1.5 %multiply_reduce_fusion.1 = (f32[128]{0:T(128)S(1)}, f32[128,768]{1,0:T(8,128)S(1)}) fusion(bf16[128,1536]{0,1:T(8,128)(2,1)S(1)} %bitcast.187, bf16[1536,768]{1,0:T(8,128)(2,1)S(1)} %copy-done, bf16[128,768]{1,0:T(8,128)(2,1)} %param.14), kind=kOutput, calls=%fused_computation.90 | convolution fusion | flops 302382976 | bytes 3342848 | tf_op jit(solution)/shard_map/dot_general | solution.py:224
  23.8 2.9 %collective-permute-start.4 = (bf16[128,768]{1,0:T(8,128)(2,1)S(1)}, bf16[128,768]{1,0:T(8,128)(2,1)S(1)}, u32[]{:S(2)}, u32[]{:S(2)}) collective-permute-start(bf16[128,768]{1,0:T(8,128)(2,1)S(1)} %get-tuple-element.45), channel_id=1, source_target_pairs={{0,2},{2,0},{4,6},{6,4},{8,10},{10,8},{12,14},{14,12},{1,3},{3,1},... | collective-permute-start | bytes 589832 | tf_op jit(solution)/shard_map/ppermute | solution.py:52
  26.6 1.5 %collective-permute-start.5 = (bf16[128,768]{1,0:T(8,128)(2,1)S(1)}, bf16[128,768]{1,0:T(8,128)(2,1)S(1)}, u32[]{:S(2)}, u32[]{:S(2)}) collective-permute-start(bf16[128,768]{1,0:T(8,128)(2,1)S(1)} %get-tuple-element.44), channel_id=1, source_target_pairs={{0,4},{2,6},{4,0},{6,2},{8,12},{10,14},{12,8},{14,10},{1,5},{3,7},... | collective-permute-start | bytes 589832 | tf_op jit(solution)/shard_map/ppermute | solution.py:52
  28.2 2.0 %collective-permute-start.7 = (bf16[128,768]{1,0:T(8,128)(2,1)S(1)}, bf16[128,768]{1,0:T(8,128)(2,1)S(1)}, u32[]{:S(2)}, u32[]{:S(2)}) collective-permute-start(bf16[128,768]{1,0:T(8,128)(2,1)S(1)} %get-tuple-element.40), channel_id=1, source_target_pairs={{0,8},{2,10},{4,12},{6,14},{8,0},{10,2},{12,4},{14,6},{1,9},{3,11}... | collective-permute-start | bytes 589832 | tf_op jit(solution)/shard_map/ppermute | solution.py:52
  30.2 1.4 %collective-permute-start.8 = (bf16[128,768]{1,0:T(8,128)(2,1)S(1)}, bf16[128,768]{1,0:T(8,128)(2,1)S(1)}, u32[]{:S(2)}, u32[]{:S(2)}) collective-permute-start(bf16[128,768]{1,0:T(8,128)(2,1)S(1)} %get-tuple-element.29), channel_id=1, source_target_pairs={{0,10},{2,8},{4,14},{6,12},{8,2},{10,0},{12,6},{14,4},{1,11},{3,9}... | collective-permute-start | bytes 589832 | tf_op jit(solution)/shard_map/ppermute | solution.py:52
  32.3 3.1 %collective-permute-start.9 = (bf16[128,768]{1,0:T(8,128)(2,1)S(1)}, bf16[128,768]{1,0:T(8,128)(2,1)S(1)}, u32[]{:S(2)}, u32[]{:S(2)}) collective-permute-start(bf16[128,768]{1,0:T(8,128)(2,1)S(1)} %get-tuple-element.28), channel_id=1, source_target_pairs={{0,12},{2,14},{4,8},{6,10},{8,4},{10,6},{12,0},{14,2},{1,13},{3,15... | collective-permute-start | bytes 589832 | tf_op jit(solution)/shard_map/ppermute | solution.py:52
  35.8 1.3 %collective-permute-start.10 = (bf16[128,768]{1,0:T(8,128)(2,1)S(1)}, bf16[128,768]{1,0:T(8,128)(2,1)S(1)}, u32[]{:S(2)}, u32[]{:S(2)}) collective-permute-start(bf16[128,768]{1,0:T(8,128)(2,1)S(1)} %get-tuple-element.27), channel_id=1, source_target_pairs={{0,14},{2,12},{4,10},{6,8},{8,6},{10,4},{12,2},{14,0},{1,15},{3,13... | collective-permute-start | bytes 589832 | tf_op jit(solution)/shard_map/ppermute | solution.py:52
  37.2 3.4 %collective-permute-done.6 = bf16[128,768]{1,0:T(8,128)(2,1)S(1)} collective-permute-done((bf16[128,768]{1,0:T(8,128)(2,1)S(1)}, bf16[128,768]{1,0:T(8,128)(2,1)S(1)}, u32[]{:S(2)}, u32[]{:S(2)}) %collective-permute-start.6) | collective-permute-done | bytes 196640 | tf_op jit(solution)/shard_map/ppermute | solution.py:52
  41.6 4.2 %collective-permute-done.9 = bf16[128,768]{1,0:T(8,128)(2,1)S(1)} collective-permute-done((bf16[128,768]{1,0:T(8,128)(2,1)S(1)}, bf16[128,768]{1,0:T(8,128)(2,1)S(1)}, u32[]{:S(2)}, u32[]{:S(2)}) %collective-permute-start.9) | collective-permute-done | bytes 196640 | tf_op jit(solution)/shard_map/ppermute | solution.py:52
  45.9 3.4 %collective-permute-done.10 = bf16[128,768]{1,0:T(8,128)(2,1)S(1)} collective-permute-done((bf16[128,768]{1,0:T(8,128)(2,1)S(1)}, bf16[128,768]{1,0:T(8,128)(2,1)S(1)}, u32[]{:S(2)}, u32[]{:S(2)}) %collective-permute-start.10) | collective-permute-done | bytes 196640 | tf_op jit(solution)/shard_map/ppermute | solution.py:52
  60.2 1.6 %collective-permute-start.18 = (bf16[128,768]{1,0:T(8,128)(2,1)S(1)}, bf16[128,768]{1,0:T(8,128)(2,1)S(1)}, u32[]{:S(2)}, u32[]{:S(2)}) collective-permute-start(bf16[128,768]{1,0:T(8,128)(2,1)S(1)} %get-tuple-element.49), channel_id=1, source_target_pairs={{0,8},{2,10},{4,12},{6,14},{8,0},{10,2},{12,4},{14,6},{1,9},{3,11}... | collective-permute-start | bytes 589832 | tf_op jit(solution)/shard_map/ppermute | solution.py:52
  63.2 2.4 %collective-permute-start.15 = (bf16[128,768]{1,0:T(8,128)(2,1)S(1)}, bf16[128,768]{1,0:T(8,128)(2,1)S(1)}, u32[]{:S(2)}, u32[]{:S(2)}) collective-permute-start(bf16[128,768]{1,0:T(8,128)(2,1)S(1)} %get-tuple-element.50), channel_id=1, source_target_pairs={{0,6},{2,4},{4,2},{6,0},{8,14},{10,12},{12,10},{14,8},{1,7},{3,5},... | collective-permute-start | bytes 589832 | tf_op jit(solution)/shard_map/ppermute | solution.py:52
  66.6 7.5 %collective-permute-done.13 = bf16[128,768]{1,0:T(8,128)(2,1)S(1)} collective-permute-done((bf16[128,768]{1,0:T(8,128)(2,1)S(1)}, bf16[128,768]{1,0:T(8,128)(2,1)S(1)}, u32[]{:S(2)}, u32[]{:S(2)}) %collective-permute-start.13) | collective-permute-done | bytes 196640 | tf_op jit(solution)/shard_map/ppermute | solution.py:52
  75.0 2.1 %collective-permute-start.21 = (bf16[128,768]{1,0:T(8,128)(2,1)S(1)}, bf16[128,768]{1,0:T(8,128)(2,1)S(1)}, u32[]{:S(2)}, u32[]{:S(2)}) collective-permute-start(bf16[128,768]{1,0:T(8,128)(2,1)S(1)} %get-tuple-element.46), channel_id=1, source_target_pairs={{0,14},{2,12},{4,10},{6,8},{8,6},{10,4},{12,2},{14,0},{1,15},{3,13... | collective-permute-start | bytes 589832 | tf_op jit(solution)/shard_map/ppermute | solution.py:52
  77.2 2.0 %collective-permute-done.15 = bf16[128,768]{1,0:T(8,128)(2,1)S(1)} collective-permute-done((bf16[128,768]{1,0:T(8,128)(2,1)S(1)}, bf16[128,768]{1,0:T(8,128)(2,1)S(1)}, u32[]{:S(2)}, u32[]{:S(2)}) %collective-permute-start.15) | collective-permute-done | bytes 196640 | tf_op jit(solution)/shard_map/ppermute | solution.py:52
  79.3 4.3 %collective-permute-done.20 = bf16[128,768]{1,0:T(8,128)(2,1)S(1)} collective-permute-done((bf16[128,768]{1,0:T(8,128)(2,1)S(1)}, bf16[128,768]{1,0:T(8,128)(2,1)S(1)}, u32[]{:S(2)}, u32[]{:S(2)}) %collective-permute-start.20) | collective-permute-done | bytes 196640 | tf_op jit(solution)/shard_map/ppermute | solution.py:52
  83.6 1.9 %collective-permute-done.21 = bf16[128,768]{1,0:T(8,128)(2,1)S(1)} collective-permute-done((bf16[128,768]{1,0:T(8,128)(2,1)S(1)}, bf16[128,768]{1,0:T(8,128)(2,1)S(1)}, u32[]{:S(2)}, u32[]{:S(2)}) %collective-permute-start.21) | collective-permute-done | bytes 196640 | tf_op jit(solution)/shard_map/ppermute | solution.py:52
  86.5 1.1 %collective-permute-done.22 = f32[128]{0:T(128)S(1)} collective-permute-done((f32[128]{0:T(128)S(1)}, f32[128]{0:T(128)S(1)}, u32[]{:S(2)}, u32[]{:S(2)}) %collective-permute-start.22) | collective-permute-done | bytes 544 | tf_op jit(solution)/shard_map/ppermute | solution.py:94
  (115 shorter events, 29.4 us)
Async XLA Ops:
  0.0 20.2 %copy-start = (bf16[1536,768]{1,0:T(8,128)(2,1)S(1)}, bf16[1536,768]{1,0:T(8,128)(2,1)}, u32[]{:S(2)}) copy-start(bf16[1536,768]{1,0:T(8,128)(2,1)} %param.20) | copy-start | bytes 7077892
  13.2 5.5 %collective-permute-start.2 = (bf16[128,2,6]{0,2,1:T(8,128)(2,1)S(1)}, bf16[128,2,6]{0,2,1:T(8,128)(2,1)S(1)}, u32[]{:S(2)}, u32[]{:S(2)}) collective-permute-start(bf16[128,2,6]{0,2,1:T(8,128)(2,1)S(1)} %pad_maximum_fusion.2), channel_id=1, source_target_pairs={{0,1},{1,0},{2,3},{3,2},{4,5},{5,4},{6,7},{7,6},{8,9},{9,8},{10,11... | collective-permute-start | bytes 9224 | tf_op jit(solution)/shard_map/ppermute | solution.py:18
  13.7 5.0 %collective-permute-start = (bf16[128,2,6]{0,2,1:T(8,128)(2,1)S(1)}, bf16[128,2,6]{0,2,1:T(8,128)(2,1)S(1)}, u32[]{:S(2)}, u32[]{:S(2)}) collective-permute-start(bf16[128,2,6]{0,2,1:T(8,128)(2,1)S(1)} %pad_maximum_fusion.1), channel_id=1, source_target_pairs={{0,1},{1,0},{2,3},{3,2},{4,5},{5,4},{6,7},{7,6},{8,9},{9,8},{10,11... | collective-permute-start | bytes 9224 | tf_op jit(solution)/shard_map/ppermute | solution.py:18
  16.9 2.1 %collective-permute-start.1 = (bf16[128,2,6,128]{0,3,2,1:T(8,128)(2,1)}, bf16[128,2,6,128]{0,3,2,1:T(8,128)(2,1)}, u32[]{:S(2)}, u32[]{:S(2)}) collective-permute-start(bf16[128,2,6,128]{0,3,2,1:T(8,128)(2,1)} %pad_maximum_fusion), channel_id=1, source_target_pairs={{0,1},{1,0},{2,3},{3,2},{4,5},{5,4},{6,7},{7,6},{8,9},{9,8},{10,11... | collective-permute-start | bytes 1179656 | tf_op jit(solution)/shard_map/ppermute | solution.py:18
  21.8 1.3 %collective-permute-start.3 = (f32[128]{0:T(128)S(1)}, f32[128]{0:T(128)S(1)}, u32[]{:S(2)}, u32[]{:S(2)}) collective-permute-start(f32[128]{0:T(128)S(1)} %get-tuple-element.59), channel_id=1, source_target_pairs={{0,1},{1,0},{2,3},{3,2},{4,5},{5,4},{6,7},{7,6},{8,9},{9,8},{10,11... | collective-permute-start | bytes 1544 | tf_op jit(solution)/shard_map/ppermute | solution.py:94
  23.8 8.5 %collective-permute-start.4 = (bf16[128,768]{1,0:T(8,128)(2,1)S(1)}, bf16[128,768]{1,0:T(8,128)(2,1)S(1)}, u32[]{:S(2)}, u32[]{:S(2)}) collective-permute-start(bf16[128,768]{1,0:T(8,128)(2,1)S(1)} %get-tuple-element.45), channel_id=1, source_target_pairs={{0,2},{2,0},{4,6},{6,4},{8,10},{10,8},{12,14},{14,12},{1,3},{3,1},... | collective-permute-start | bytes 589832 | tf_op jit(solution)/shard_map/ppermute | solution.py:52
  26.6 9.2 %collective-permute-start.5 = (bf16[128,768]{1,0:T(8,128)(2,1)S(1)}, bf16[128,768]{1,0:T(8,128)(2,1)S(1)}, u32[]{:S(2)}, u32[]{:S(2)}) collective-permute-start(bf16[128,768]{1,0:T(8,128)(2,1)S(1)} %get-tuple-element.44), channel_id=1, source_target_pairs={{0,4},{2,6},{4,0},{6,2},{8,12},{10,14},{12,8},{14,10},{1,5},{3,7},... | collective-permute-start | bytes 589832 | tf_op jit(solution)/shard_map/ppermute | solution.py:52
  28.2 12.4 %collective-permute-start.6 = (bf16[128,768]{1,0:T(8,128)(2,1)S(1)}, bf16[128,768]{1,0:T(8,128)(2,1)S(1)}, u32[]{:S(2)}, u32[]{:S(2)}) collective-permute-start(bf16[128,768]{1,0:T(8,128)(2,1)S(1)} %get-tuple-element.42), channel_id=1, source_target_pairs={{0,6},{2,4},{4,2},{6,0},{8,14},{10,12},{12,10},{14,8},{1,7},{3,5},... | collective-permute-start | bytes 589832 | tf_op jit(solution)/shard_map/ppermute | solution.py:52
  28.2 12.4 %collective-permute-start.7 = (bf16[128,768]{1,0:T(8,128)(2,1)S(1)}, bf16[128,768]{1,0:T(8,128)(2,1)S(1)}, u32[]{:S(2)}, u32[]{:S(2)}) collective-permute-start(bf16[128,768]{1,0:T(8,128)(2,1)S(1)} %get-tuple-element.40), channel_id=1, source_target_pairs={{0,8},{2,10},{4,12},{6,14},{8,0},{10,2},{12,4},{14,6},{1,9},{3,11}... | collective-permute-start | bytes 589832 | tf_op jit(solution)/shard_map/ppermute | solution.py:52
  30.2 11.4 %collective-permute-start.8 = (bf16[128,768]{1,0:T(8,128)(2,1)S(1)}, bf16[128,768]{1,0:T(8,128)(2,1)S(1)}, u32[]{:S(2)}, u32[]{:S(2)}) collective-permute-start(bf16[128,768]{1,0:T(8,128)(2,1)S(1)} %get-tuple-element.29), channel_id=1, source_target_pairs={{0,10},{2,8},{4,14},{6,12},{8,2},{10,0},{12,6},{14,4},{1,11},{3,9}... | collective-permute-start | bytes 589832 | tf_op jit(solution)/shard_map/ppermute | solution.py:52
  32.3 13.6 %collective-permute-start.9 = (bf16[128,768]{1,0:T(8,128)(2,1)S(1)}, bf16[128,768]{1,0:T(8,128)(2,1)S(1)}, u32[]{:S(2)}, u32[]{:S(2)}) collective-permute-start(bf16[128,768]{1,0:T(8,128)(2,1)S(1)} %get-tuple-element.28), channel_id=1, source_target_pairs={{0,12},{2,14},{4,8},{6,10},{8,4},{10,6},{12,0},{14,2},{1,13},{3,15... | collective-permute-start | bytes 589832 | tf_op jit(solution)/shard_map/ppermute | solution.py:52
  35.8 13.5 %collective-permute-start.10 = (bf16[128,768]{1,0:T(8,128)(2,1)S(1)}, bf16[128,768]{1,0:T(8,128)(2,1)S(1)}, u32[]{:S(2)}, u32[]{:S(2)}) collective-permute-start(bf16[128,768]{1,0:T(8,128)(2,1)S(1)} %get-tuple-element.27), channel_id=1, source_target_pairs={{0,14},{2,12},{4,10},{6,8},{8,6},{10,4},{12,2},{14,0},{1,15},{3,13... | collective-permute-start | bytes 589832 | tf_op jit(solution)/shard_map/ppermute | solution.py:52
  49.5 4.2 %collective-permute-start.16 = (bf16[512,768]{1,0:T(8,128)(2,1)S(1)}, bf16[512,768]{1,0:T(8,128)(2,1)S(1)}, u32[]{:S(2)}, u32[]{:S(2)}) collective-permute-start(bf16[512,768]{1,0:T(8,128)(2,1)S(1)} %get-tuple-element.25), channel_id=1, source_target_pairs={{0,1},{1,0},{2,3},{3,2},{4,5},{5,4},{6,7},{7,6},{8,9},{9,8},{10,11... | collective-permute-start | bytes 2359304 | tf_op jit(solution)/shard_map/ppermute | solution.py:70
  51.2 5.8 %collective-permute-start.11 = (bf16[512,768]{1,0:T(8,128)(2,1)S(1)}, bf16[512,768]{1,0:T(8,128)(2,1)S(1)}, u32[]{:S(2)}, u32[]{:S(2)}) collective-permute-start(bf16[512,768]{1,0:T(8,128)(2,1)S(1)} %get-tuple-element.26), channel_id=1, source_target_pairs={{0,1},{1,0},{2,3},{3,2},{4,5},{5,4},{6,7},{7,6},{8,9},{9,8},{10,11... | collective-permute-start | bytes 2359304 | tf_op jit(solution)/shard_map/ppermute | solution.py:70
  56.3 3.6 %collective-permute-start.17 = (bf16[512,768]{1,0:T(8,128)(2,1)S(1)}, bf16[512,768]{1,0:T(8,128)(2,1)S(1)}, u32[]{:S(2)}, u32[]{:S(2)}) collective-permute-start(bf16[512,768]{1,0:T(8,128)(2,1)S(1)} %convolution_convert_fusion.1), channel_id=1, source_target_pairs={{0,1},{1,0},{2,3},{3,2},{4,5},{5,4},{6,7},{7,6},{8,9},{9,8},{10,11... | collective-permute-start | bytes 2359304 | tf_op jit(solution)/shard_map/ppermute | solution.py:86
  58.7 3.1 %collective-permute-start.12 = (bf16[512,768]{1,0:T(8,128)(2,1)S(1)}, bf16[512,768]{1,0:T(8,128)(2,1)S(1)}, u32[]{:S(2)}, u32[]{:S(2)}) collective-permute-start(bf16[512,768]{1,0:T(8,128)(2,1)S(1)} %convolution_convert_fusion.3), channel_id=1, source_target_pairs={{0,1},{1,0},{2,3},{3,2},{4,5},{5,4},{6,7},{7,6},{8,9},{9,8},{10,11... | collective-permute-start | bytes 2359304 | tf_op jit(solution)/shard_map/ppermute | solution.py:86
  60.2 19.1 %collective-permute-start.18 = (bf16[128,768]{1,0:T(8,128)(2,1)S(1)}, bf16[128,768]{1,0:T(8,128)(2,1)S(1)}, u32[]{:S(2)}, u32[]{:S(2)}) collective-permute-start(bf16[128,768]{1,0:T(8,128)(2,1)S(1)} %get-tuple-element.49), channel_id=1, source_target_pairs={{0,8},{2,10},{4,12},{6,14},{8,0},{10,2},{12,4},{14,6},{1,9},{3,11}... | collective-permute-start | bytes 589832 | tf_op jit(solution)/shard_map/ppermute | solution.py:52
  62.0 12.1 %collective-permute-start.13 = (bf16[128,768]{1,0:T(8,128)(2,1)S(1)}, bf16[128,768]{1,0:T(8,128)(2,1)S(1)}, u32[]{:S(2)}, u32[]{:S(2)}) collective-permute-start(bf16[128,768]{1,0:T(8,128)(2,1)S(1)} %get-tuple-element.52), channel_id=1, source_target_pairs={{0,2},{2,0},{4,6},{6,4},{8,10},{10,8},{12,14},{14,12},{1,3},{3,1},... | collective-permute-start | bytes 589832 | tf_op jit(solution)/shard_map/ppermute | solution.py:52
  62.7 12.3 %collective-permute-start.14 = (bf16[128,768]{1,0:T(8,128)(2,1)S(1)}, bf16[128,768]{1,0:T(8,128)(2,1)S(1)}, u32[]{:S(2)}, u32[]{:S(2)}) collective-permute-start(bf16[128,768]{1,0:T(8,128)(2,1)S(1)} %get-tuple-element.51), channel_id=1, source_target_pairs={{0,4},{2,6},{4,0},{6,2},{8,12},{10,14},{12,8},{14,10},{1,5},{3,7},... | collective-permute-start | bytes 589832 | tf_op jit(solution)/shard_map/ppermute | solution.py:52
  63.2 16.0 %collective-permute-start.15 = (bf16[128,768]{1,0:T(8,128)(2,1)S(1)}, bf16[128,768]{1,0:T(8,128)(2,1)S(1)}, u32[]{:S(2)}, u32[]{:S(2)}) collective-permute-start(bf16[128,768]{1,0:T(8,128)(2,1)S(1)} %get-tuple-element.50), channel_id=1, source_target_pairs={{0,6},{2,4},{4,2},{6,0},{8,14},{10,12},{12,10},{14,8},{1,7},{3,5},... | collective-permute-start | bytes 589832 | tf_op jit(solution)/shard_map/ppermute | solution.py:52
  65.6 13.7 %collective-permute-start.19 = (bf16[128,768]{1,0:T(8,128)(2,1)S(1)}, bf16[128,768]{1,0:T(8,128)(2,1)S(1)}, u32[]{:S(2)}, u32[]{:S(2)}) collective-permute-start(bf16[128,768]{1,0:T(8,128)(2,1)S(1)} %get-tuple-element.48), channel_id=1, source_target_pairs={{0,10},{2,8},{4,14},{6,12},{8,2},{10,0},{12,6},{14,4},{1,11},{3,9}... | collective-permute-start | bytes 589832 | tf_op jit(solution)/shard_map/ppermute | solution.py:52
  74.1 9.5 %collective-permute-start.20 = (bf16[128,768]{1,0:T(8,128)(2,1)S(1)}, bf16[128,768]{1,0:T(8,128)(2,1)S(1)}, u32[]{:S(2)}, u32[]{:S(2)}) collective-permute-start(bf16[128,768]{1,0:T(8,128)(2,1)S(1)} %get-tuple-element.47), channel_id=1, source_target_pairs={{0,12},{2,14},{4,8},{6,10},{8,4},{10,6},{12,0},{14,2},{1,13},{3,15... | collective-permute-start | bytes 589832 | tf_op jit(solution)/shard_map/ppermute | solution.py:52
  75.0 10.5 %collective-permute-start.21 = (bf16[128,768]{1,0:T(8,128)(2,1)S(1)}, bf16[128,768]{1,0:T(8,128)(2,1)S(1)}, u32[]{:S(2)}, u32[]{:S(2)}) collective-permute-start(bf16[128,768]{1,0:T(8,128)(2,1)S(1)} %get-tuple-element.46), channel_id=1, source_target_pairs={{0,14},{2,12},{4,10},{6,8},{8,6},{10,4},{12,2},{14,0},{1,15},{3,13... | collective-permute-start | bytes 589832 | tf_op jit(solution)/shard_map/ppermute | solution.py:52
  86.4 1.2 %collective-permute-start.22 = (f32[128]{0:T(128)S(1)}, f32[128]{0:T(128)S(1)}, u32[]{:S(2)}, u32[]{:S(2)}) collective-permute-start(f32[128]{0:T(128)S(1)} %get-tuple-element.61), channel_id=1, source_target_pairs={{0,1},{1,0},{2,3},{3,2},{4,5},{5,4},{6,7},{7,6},{8,9},{9,8},{10,11... | collective-permute-start | bytes 1544 | tf_op jit(solution)/shard_map/ppermute | solution.py:94
  (8 other events, 18.0 us)

commit v18 on v9

--- a/solution.py
+++ b/solution.py
@@ -15,7 +15,9 @@
 def merged(shard, axis, join):
     if lax.axis_size(axis) == 2:
         rounded = jax.tree.map(lambda a: a.astype(jnp.bfloat16), shard)
-        other = jax.tree.map(lambda a: lax.ppermute(a, axis, perm=[(0, 1), (1, 0)]), rounded)
+        swap = [(0, 1), (1, 0)]
+        stats = lax.ppermute(jnp.stack(rounded[:2]), axis, perm=swap)
+        other = (stats[0], stats[1], lax.ppermute(rounded[2], axis, perm=swap))
         widen = lambda tree: jax.tree.map(lambda a, own: a.astype(own.dtype), tree, shard)
         return join(widen(rounded), widen(other))
     gathered = jax.tree.map(

time: 89.6 us -> 89.5 us (level)
  starting transfers between devices: 24.2 us -> 23.3 us
  transfers between devices with their start and end apart: 23 -> 22, of which waited for: 13 -> 13; matrix products, arithmetic and copies ran while one was open for 14% -> 14% of each run, Pallas kernels for 0% -> 0%
where the time goes in v18:
time: 89.5 us; the launch traced here: 89.1 us
  waiting for transfers between devices  32 us (36%)
  starting transfers between devices  23.3 us (26%)
  matrix products  16.5 us (18%)
  local copies, waits for them, and re-layouts  9.36 us (10%)
  other arithmetic  7.43 us (8%)
    ppermute x14, waiting for transfers between devices, exchange(): pieces.append(lax.ppermute(chunks[step], 'el', perm=pairs))  29.2 us
    ppermute x14, starting transfers between devices, exchange(): pieces.append(lax.ppermute(chunks[step], 'el', perm=pairs))  21.3 us
    dot_general x8, matrix products, half_product(): return jnp.dot(x, weight, preferred_element_type=jnp.float32)  4.65 us
    dot_general x2, matrix products, one_group(): jnp.einsum('rgd,ld->rgl', head_rows, head_keys, preferred_element_type=jn...  3.85 us
    gather x1, local copies, waits for them, and re-layouts, one_group(): page_row_block = group_pages[local_table.reshape(-1)]  3.32 us
    unnamed x35, local copies, waits for them, and re-layouts  2.6 us
    dot_general x4, matrix products, down_product(): jnp.dot(hidden, weight, preferred_element_type=jnp.float32)  2.48 us
    dot_general x2, matrix products, one_group(): jnp.einsum('rgl,ld->rgd', soft.astype(jnp.bfloat16), head_values, preferr...  2.19 us
  transfers between devices with their start and end apart: 22, of which 13 were waited for; matrix products, arithmetic and copies ran while one was open for 14% of the time, Pallas kernels for 0%

profile of v18, /device:TPU:0, one launch (start us, length us, event | category | flops | bytes accessed | tf_op | source)
XLA Modules:
  0.0 89.1 jit_solution(3728936998322518498)
XLA Ops:
  3.5 1.0 %fusion.120 = (bf16[128,768]{1,0:T(8,128)(2,1)S(1)}, bf16[128,768]{1,0:T(8,128)(2,1)S(1)}) fusion(bf16[128,1536]{1,0:T(8,128)(2,1)} %param.15), kind=kLoop, calls=%fused_computation.200 | loop fusion | bytes 786432 | tf_op jit(solution)/shard_map/while/body/eval_jaxpr/slice | solution.py:194
  4.9 3.3 %gather_fusion = bf16[96,16,512]{2,1,0:T(8,128)(2,1)} fusion(bf16[96,16,512]{2,1,0:T(8,128)(2,1)} %bitcast.211, s32[1024]{0:T(1024)S(1)} %pad_clamp_fusion), kind=kCustom, calls=%fused_computation | custom fusion | bytes 3146112 | tf_op jit(solution)/shard_map/while/body/eval_jaxpr/gather | solution.py:175
  9.2 1.9 %fusion.3 = (f32[128,6]{0,1:T(8,128)S(1)}, f32[1536,128,6]{1,0,2:T(8,128)S(1)}) fusion(pred[128,1536]{0,1:T(8,128)(4,1)S(1)} %compare_and_fusion, bf16[128,6,128]{0,2,1:T(8,128)(2,1)S(1)} %bitcast.213, bf16[1536,512]{1,0:T(8,128)(2,1)} %bitcast.206), kind=kOutput, calls=%fused_computation.8 | convolution fusion | flops 305528064 | bytes 5508096 | tf_op jit(solution)/shard_map/while/body/eval_jaxpr/rgd,ld->rgl/dot_general | solution.py:200
  11.1 1.9 %fusion.6 = (bf16[128,6]{0,1:T(8,128)(2,1)S(1)}, f32[128,6]{0,1:T(8,128)S(1)}, f32[1536,128,6]{1,0,2:T(8,128)S(1)}) fusion(f32[1536,128,6]{1,0,2:T(8,128)S(1)} %get-tuple-element.63, f32[128,6]{0,1:T(8,128)S(1)} %get-tuple-element.62, pred[128,1536]{0,1:T(8,128)(4,1)S(1)} %compare_and_fusion, bf16[128,6,128]{0,2,1:T(8,128)(2,1)S(1)} %bitcast.214, ...), kind=kOutput, calls=%fused_computation.11 | convolution fusion | flops 310245888 | bytes 10232320 | tf_op jit(solution)/shard_map/while/body/eval_jaxpr/rgd,ld->rgl/dot_general | solution.py:200
  14.6 1.1 %fusion.29 = bf16[128,1,6,128]{0,3,2,1:T(8,128)(2,1)S(1)} fusion(f32[1536,128,6]{1,0,2:T(8,128)S(1)} %get-tuple-element.64, f32[128,6]{0,1:T(8,128)S(1)} %get-tuple-element.24, pred[128,1536]{0,1:T(8,128)(4,1)S(1)} %compare_and_fusion, bf16[1536,512]{1,0:T(8,128)(2,1)S(1)} %bitcast.208), kind=kOutput, calls=%fused_computation.44 | convolution fusion | flops 306806784 | bytes 5509120 | tf_op jit(solution)/shard_map/while/body/eval_jaxpr/rgl,ld->rgd/dot_general | solution.py:206
  15.7 1.1 %fusion.32 = bf16[128,1,6,128]{0,3,2,1:T(8,128)(2,1)S(1)} fusion(f32[1536,128,6]{1,0,2:T(8,128)S(1)} %get-tuple-element.63, f32[128,6]{0,1:T(8,128)S(1)} %get-tuple-element.62, pred[128,1536]{0,1:T(8,128)(4,1)S(1)} %compare_and_fusion, bf16[1536,512]{1,0:T(8,128)(2,1)S(1)} %bitcast.209), kind=kOutput, calls=%fused_computation.45 | convolution fusion | flops 306806784 | bytes 5509120 | tf_op jit(solution)/shard_map/while/body/eval_jaxpr/rgl,ld->rgd/dot_general | solution.py:206
  19.7 1.2 %divide_convert_fusion = bf16[128,2,6,128]{0,3,2,1:T(8,128)(2,1)S(1)} fusion(bf16[128,2,6,128]{0,3,2,1:T(8,128)(2,1)} %collective-permute-done.1, f32[128,2,6]{0,2,1:T(8,128)S(1)} %get-tuple-element.57, f32[128,2,6]{0,2,1:T(8,128)S(1)} %get-tuple-element.56, f32[128,2,6]{0,2,1:T(8,128)S(1)} %get-tuple-element.55, bf16[128,1,6,128]{0,3,2,1:T(8,128)(2,1)S(1)} %fusion.29, ...), kind=kLoop, calls=%fused_computation.50 | loop fusion | flops 1572864 | bytes 1198080 | tf_op jit(solution)/shard_map/convert_element_type | solution.py:226
  20.9 1.5 %multiply_reduce_fusion.1 = (f32[128]{0:T(128)S(1)}, f32[128,768]{1,0:T(8,128)S(1)}) fusion(bf16[128,1536]{0,1:T(8,128)(2,1)S(1)} %bitcast.212, bf16[1536,768]{1,0:T(8,128)(2,1)S(1)} %copy-done, bf16[128,768]{1,0:T(8,128)(2,1)} %param.14), kind=kOutput, calls=%fused_computation.90 | convolution fusion | flops 302382976 | bytes 3342848 | tf_op jit(solution)/shard_map/dot_general | solution.py:228
  24.4 2.7 %collective-permute-start.3 = (bf16[128,768]{1,0:T(8,128)(2,1)S(1)}, bf16[128,768]{1,0:T(8,128)(2,1)S(1)}, u32[]{:S(2)}, u32[]{:S(2)}) collective-permute-start(bf16[128,768]{1,0:T(8,128)(2,1)S(1)} %get-tuple-element.45), channel_id=1, source_target_pairs={{0,2},{2,0},{4,6},{6,4},{8,10},{10,8},{12,14},{14,12},{1,3},{3,1},... | collective-permute-start | bytes 589832 | tf_op jit(solution)/shard_map/ppermute | solution.py:54
  27.1 1.5 %collective-permute-start.4 = (bf16[128,768]{1,0:T(8,128)(2,1)S(1)}, bf16[128,768]{1,0:T(8,128)(2,1)S(1)}, u32[]{:S(2)}, u32[]{:S(2)}) collective-permute-start(bf16[128,768]{1,0:T(8,128)(2,1)S(1)} %get-tuple-element.44), channel_id=1, source_target_pairs={{0,4},{2,6},{4,0},{6,2},{8,12},{10,14},{12,8},{14,10},{1,5},{3,7},... | collective-permute-start | bytes 589832 | tf_op jit(solution)/shard_map/ppermute | solution.py:54
  28.6 2.0 %collective-permute-start.6 = (bf16[128,768]{1,0:T(8,128)(2,1)S(1)}, bf16[128,768]{1,0:T(8,128)(2,1)S(1)}, u32[]{:S(2)}, u32[]{:S(2)}) collective-permute-start(bf16[128,768]{1,0:T(8,128)(2,1)S(1)} %get-tuple-element.40), channel_id=1, source_target_pairs={{0,8},{2,10},{4,12},{6,14},{8,0},{10,2},{12,4},{14,6},{1,9},{3,11}... | collective-permute-start | bytes 589832 | tf_op jit(solution)/shard_map/ppermute | solution.py:54
  30.7 1.4 %collective-permute-start.7 = (bf16[128,768]{1,0:T(8,128)(2,1)S(1)}, bf16[128,768]{1,0:T(8,128)(2,1)S(1)}, u32[]{:S(2)}, u32[]{:S(2)}) collective-permute-start(bf16[128,768]{1,0:T(8,128)(2,1)S(1)} %get-tuple-element.29), channel_id=1, source_target_pairs={{0,10},{2,8},{4,14},{6,12},{8,2},{10,0},{12,6},{14,4},{1,11},{3,9}... | collective-permute-start | bytes 589832 | tf_op jit(solution)/shard_map/ppermute | solution.py:54
  32.8 3.1 %collective-permute-start.8 = (bf16[128,768]{1,0:T(8,128)(2,1)S(1)}, bf16[128,768]{1,0:T(8,128)(2,1)S(1)}, u32[]{:S(2)}, u32[]{:S(2)}) collective-permute-start(bf16[128,768]{1,0:T(8,128)(2,1)S(1)} %get-tuple-element.28), channel_id=1, source_target_pairs={{0,12},{2,14},{4,8},{6,10},{8,4},{10,6},{12,0},{14,2},{1,13},{3,15... | collective-permute-start | bytes 589832 | tf_op jit(solution)/shard_map/ppermute | solution.py:54
  36.5 1.3 %collective-permute-start.9 = (bf16[128,768]{1,0:T(8,128)(2,1)S(1)}, bf16[128,768]{1,0:T(8,128)(2,1)S(1)}, u32[]{:S(2)}, u32[]{:S(2)}) collective-permute-start(bf16[128,768]{1,0:T(8,128)(2,1)S(1)} %get-tuple-element.27), channel_id=1, source_target_pairs={{0,14},{2,12},{4,10},{6,8},{8,6},{10,4},{12,2},{14,0},{1,15},{3,13... | collective-permute-start | bytes 589832 | tf_op jit(solution)/shard_map/ppermute | solution.py:54
  37.8 3.4 %collective-permute-done.5 = bf16[128,768]{1,0:T(8,128)(2,1)S(1)} collective-permute-done((bf16[128,768]{1,0:T(8,128)(2,1)S(1)}, bf16[128,768]{1,0:T(8,128)(2,1)S(1)}, u32[]{:S(2)}, u32[]{:S(2)}) %collective-permute-start.5) | collective-permute-done | bytes 196640 | tf_op jit(solution)/shard_map/ppermute | solution.py:54
  42.1 4.2 %collective-permute-done.8 = bf16[128,768]{1,0:T(8,128)(2,1)S(1)} collective-permute-done((bf16[128,768]{1,0:T(8,128)(2,1)S(1)}, bf16[128,768]{1,0:T(8,128)(2,1)S(1)}, u32[]{:S(2)}, u32[]{:S(2)}) %collective-permute-start.8) | collective-permute-done | bytes 196640 | tf_op jit(solution)/shard_map/ppermute | solution.py:54
  46.4 3.5 %collective-permute-done.9 = bf16[128,768]{1,0:T(8,128)(2,1)S(1)} collective-permute-done((bf16[128,768]{1,0:T(8,128)(2,1)S(1)}, bf16[128,768]{1,0:T(8,128)(2,1)S(1)}, u32[]{:S(2)}, u32[]{:S(2)}) %collective-permute-start.9) | collective-permute-done | bytes 196640 | tf_op jit(solution)/shard_map/ppermute | solution.py:54
  60.7 1.7 %collective-permute-start.17 = (bf16[128,768]{1,0:T(8,128)(2,1)S(1)}, bf16[128,768]{1,0:T(8,128)(2,1)S(1)}, u32[]{:S(2)}, u32[]{:S(2)}) collective-permute-start(bf16[128,768]{1,0:T(8,128)(2,1)S(1)} %get-tuple-element.49), channel_id=1, source_target_pairs={{0,8},{2,10},{4,12},{6,14},{8,0},{10,2},{12,4},{14,6},{1,9},{3,11}... | collective-permute-start | bytes 589832 | tf_op jit(solution)/shard_map/ppermute | solution.py:54
  63.7 2.4 %collective-permute-start.14 = (bf16[128,768]{1,0:T(8,128)(2,1)S(1)}, bf16[128,768]{1,0:T(8,128)(2,1)S(1)}, u32[]{:S(2)}, u32[]{:S(2)}) collective-permute-start(bf16[128,768]{1,0:T(8,128)(2,1)S(1)} %get-tuple-element.50), channel_id=1, source_target_pairs={{0,6},{2,4},{4,2},{6,0},{8,14},{10,12},{12,10},{14,8},{1,7},{3,5},... | collective-permute-start | bytes 589832 | tf_op jit(solution)/shard_map/ppermute | solution.py:54
  67.2 7.5 %collective-permute-done.12 = bf16[128,768]{1,0:T(8,128)(2,1)S(1)} collective-permute-done((bf16[128,768]{1,0:T(8,128)(2,1)S(1)}, bf16[128,768]{1,0:T(8,128)(2,1)S(1)}, u32[]{:S(2)}, u32[]{:S(2)}) %collective-permute-start.12) | collective-permute-done | bytes 196640 | tf_op jit(solution)/shard_map/ppermute | solution.py:54
  75.6 2.1 %collective-permute-start.20 = (bf16[128,768]{1,0:T(8,128)(2,1)S(1)}, bf16[128,768]{1,0:T(8,128)(2,1)S(1)}, u32[]{:S(2)}, u32[]{:S(2)}) collective-permute-start(bf16[128,768]{1,0:T(8,128)(2,1)S(1)} %get-tuple-element.46), channel_id=1, source_target_pairs={{0,14},{2,12},{4,10},{6,8},{8,6},{10,4},{12,2},{14,0},{1,15},{3,13... | collective-permute-start | bytes 589832 | tf_op jit(solution)/shard_map/ppermute | solution.py:54
  77.7 6.2 %collective-permute-done.14 = bf16[128,768]{1,0:T(8,128)(2,1)S(1)} collective-permute-done((bf16[128,768]{1,0:T(8,128)(2,1)S(1)}, bf16[128,768]{1,0:T(8,128)(2,1)S(1)}, u32[]{:S(2)}, u32[]{:S(2)}) %collective-permute-start.14) | collective-permute-done | bytes 196640 | tf_op jit(solution)/shard_map/ppermute | solution.py:54
  84.3 1.9 %collective-permute-done.20 = bf16[128,768]{1,0:T(8,128)(2,1)S(1)} collective-permute-done((bf16[128,768]{1,0:T(8,128)(2,1)S(1)}, bf16[128,768]{1,0:T(8,128)(2,1)S(1)}, u32[]{:S(2)}, u32[]{:S(2)}) %collective-permute-start.20) | collective-permute-done | bytes 196640 | tf_op jit(solution)/shard_map/ppermute | solution.py:54
  87.2 1.1 %collective-permute-done.21 = f32[128]{0:T(128)S(1)} collective-permute-done((f32[128]{0:T(128)S(1)}, f32[128]{0:T(128)S(1)}, u32[]{:S(2)}, u32[]{:S(2)}) %collective-permute-start.21) | collective-permute-done | bytes 544 | tf_op jit(solution)/shard_map/ppermute | solution.py:96
  (114 shorter events, 29.4 us)
Async XLA Ops:
  0.0 20.9 %copy-start = (bf16[1536,768]{1,0:T(8,128)(2,1)S(1)}, bf16[1536,768]{1,0:T(8,128)(2,1)}, u32[]{:S(2)}) copy-start(bf16[1536,768]{1,0:T(8,128)(2,1)} %param.20) | copy-start | bytes 7077892
  14.1 4.9 %collective-permute-start = (bf16[2,128,2,6]{1,3,2,0:T(8,128)(2,1)S(1)}, bf16[2,128,2,6]{1,3,2,0:T(8,128)(2,1)S(1)}, u32[]{:S(2)}, u32[]{:S(2)}) collective-permute-start(bf16[2,128,2,6]{1,3,2,0:T(8,128)(2,1)S(1)} %maximum_maximum_fusion), channel_id=1, source_target_pairs={{0,1},{1,0},{2,3},{3,2},{4,5},{5,4},{6,7},{7,6},{8,9},{9,8},{10,11... | collective-permute-start | bytes 18440 | tf_op jit(solution)/shard_map/ppermute | solution.py:19
  17.6 2.1 %collective-permute-start.1 = (bf16[128,2,6,128]{0,3,2,1:T(8,128)(2,1)}, bf16[128,2,6,128]{0,3,2,1:T(8,128)(2,1)}, u32[]{:S(2)}, u32[]{:S(2)}) collective-permute-start(bf16[128,2,6,128]{0,3,2,1:T(8,128)(2,1)} %pad_maximum_fusion), channel_id=1, source_target_pairs={{0,1},{1,0},{2,3},{3,2},{4,5},{5,4},{6,7},{7,6},{8,9},{9,8},{10,11... | collective-permute-start | bytes 1179656 | tf_op jit(solution)/shard_map/ppermute | solution.py:20
  22.4 1.2 %collective-permute-start.2 = (f32[128]{0:T(128)S(1)}, f32[128]{0:T(128)S(1)}, u32[]{:S(2)}, u32[]{:S(2)}) collective-permute-start(f32[128]{0:T(128)S(1)} %get-tuple-element.65), channel_id=1, source_target_pairs={{0,1},{1,0},{2,3},{3,2},{4,5},{5,4},{6,7},{7,6},{8,9},{9,8},{10,11... | collective-permute-start | bytes 1544 | tf_op jit(solution)/shard_map/ppermute | solution.py:96
  24.4 8.4 %collective-permute-start.3 = (bf16[128,768]{1,0:T(8,128)(2,1)S(1)}, bf16[128,768]{1,0:T(8,128)(2,1)S(1)}, u32[]{:S(2)}, u32[]{:S(2)}) collective-permute-start(bf16[128,768]{1,0:T(8,128)(2,1)S(1)} %get-tuple-element.45), channel_id=1, source_target_pairs={{0,2},{2,0},{4,6},{6,4},{8,10},{10,8},{12,14},{14,12},{1,3},{3,1},... | collective-permute-start | bytes 589832 | tf_op jit(solution)/shard_map/ppermute | solution.py:54
  27.1 9.4 %collective-permute-start.4 = (bf16[128,768]{1,0:T(8,128)(2,1)S(1)}, bf16[128,768]{1,0:T(8,128)(2,1)S(1)}, u32[]{:S(2)}, u32[]{:S(2)}) collective-permute-start(bf16[128,768]{1,0:T(8,128)(2,1)S(1)} %get-tuple-element.44), channel_id=1, source_target_pairs={{0,4},{2,6},{4,0},{6,2},{8,12},{10,14},{12,8},{14,10},{1,5},{3,7},... | collective-permute-start | bytes 589832 | tf_op jit(solution)/shard_map/ppermute | solution.py:54
  28.6 12.6 %collective-permute-start.5 = (bf16[128,768]{1,0:T(8,128)(2,1)S(1)}, bf16[128,768]{1,0:T(8,128)(2,1)S(1)}, u32[]{:S(2)}, u32[]{:S(2)}) collective-permute-start(bf16[128,768]{1,0:T(8,128)(2,1)S(1)} %get-tuple-element.42), channel_id=1, source_target_pairs={{0,6},{2,4},{4,2},{6,0},{8,14},{10,12},{12,10},{14,8},{1,7},{3,5},... | collective-permute-start | bytes 589832 | tf_op jit(solution)/shard_map/ppermute | solution.py:54
  28.6 12.6 %collective-permute-start.6 = (bf16[128,768]{1,0:T(8,128)(2,1)S(1)}, bf16[128,768]{1,0:T(8,128)(2,1)S(1)}, u32[]{:S(2)}, u32[]{:S(2)}) collective-permute-start(bf16[128,768]{1,0:T(8,128)(2,1)S(1)} %get-tuple-element.40), channel_id=1, source_target_pairs={{0,8},{2,10},{4,12},{6,14},{8,0},{10,2},{12,4},{14,6},{1,9},{3,11}... | collective-permute-start | bytes 589832 | tf_op jit(solution)/shard_map/ppermute | solution.py:54
  30.7 11.5 %collective-permute-start.7 = (bf16[128,768]{1,0:T(8,128)(2,1)S(1)}, bf16[128,768]{1,0:T(8,128)(2,1)S(1)}, u32[]{:S(2)}, u32[]{:S(2)}) collective-permute-start(bf16[128,768]{1,0:T(8,128)(2,1)S(1)} %get-tuple-element.29), channel_id=1, source_target_pairs={{0,10},{2,8},{4,14},{6,12},{8,2},{10,0},{12,6},{14,4},{1,11},{3,9}... | collective-permute-start | bytes 589832 | tf_op jit(solution)/shard_map/ppermute | solution.py:54
  32.8 13.6 %collective-permute-start.8 = (bf16[128,768]{1,0:T(8,128)(2,1)S(1)}, bf16[128,768]{1,0:T(8,128)(2,1)S(1)}, u32[]{:S(2)}, u32[]{:S(2)}) collective-permute-start(bf16[128,768]{1,0:T(8,128)(2,1)S(1)} %get-tuple-element.28), channel_id=1, source_target_pairs={{0,12},{2,14},{4,8},{6,10},{8,4},{10,6},{12,0},{14,2},{1,13},{3,15... | collective-permute-start | bytes 589832 | tf_op jit(solution)/shard_map/ppermute | solution.py:54
  36.5 13.4 %collective-permute-start.9 = (bf16[128,768]{1,0:T(8,128)(2,1)S(1)}, bf16[128,768]{1,0:T(8,128)(2,1)S(1)}, u32[]{:S(2)}, u32[]{:S(2)}) collective-permute-start(bf16[128,768]{1,0:T(8,128)(2,1)S(1)} %get-tuple-element.27), channel_id=1, source_target_pairs={{0,14},{2,12},{4,10},{6,8},{8,6},{10,4},{12,2},{14,0},{1,15},{3,13... | collective-permute-start | bytes 589832 | tf_op jit(solution)/shard_map/ppermute | solution.py:54
  50.1 4.2 %collective-permute-start.15 = (bf16[512,768]{1,0:T(8,128)(2,1)S(1)}, bf16[512,768]{1,0:T(8,128)(2,1)S(1)}, u32[]{:S(2)}, u32[]{:S(2)}) collective-permute-start(bf16[512,768]{1,0:T(8,128)(2,1)S(1)} %get-tuple-element.25), channel_id=1, source_target_pairs={{0,1},{1,0},{2,3},{3,2},{4,5},{5,4},{6,7},{7,6},{8,9},{9,8},{10,11... | collective-permute-start | bytes 2359304 | tf_op jit(solution)/shard_map/ppermute | solution.py:72
  50.1 7.4 %collective-permute-start.10 = (bf16[512,768]{1,0:T(8,128)(2,1)S(1)}, bf16[512,768]{1,0:T(8,128)(2,1)S(1)}, u32[]{:S(2)}, u32[]{:S(2)}) collective-permute-start(bf16[512,768]{1,0:T(8,128)(2,1)S(1)} %get-tuple-element.26), channel_id=1, source_target_pairs={{0,1},{1,0},{2,3},{3,2},{4,5},{5,4},{6,7},{7,6},{8,9},{9,8},{10,11... | collective-permute-start | bytes 2359304 | tf_op jit(solution)/shard_map/ppermute | solution.py:72
  56.9 3.6 %collective-permute-start.16 = (bf16[512,768]{1,0:T(8,128)(2,1)S(1)}, bf16[512,768]{1,0:T(8,128)(2,1)S(1)}, u32[]{:S(2)}, u32[]{:S(2)}) collective-permute-start(bf16[512,768]{1,0:T(8,128)(2,1)S(1)} %convolution_convert_fusion.1), channel_id=1, source_target_pairs={{0,1},{1,0},{2,3},{3,2},{4,5},{5,4},{6,7},{7,6},{8,9},{9,8},{10,11... | collective-permute-start | bytes 2359304 | tf_op jit(solution)/shard_map/ppermute | solution.py:88
  59.3 3.0 %collective-permute-start.11 = (bf16[512,768]{1,0:T(8,128)(2,1)S(1)}, bf16[512,768]{1,0:T(8,128)(2,1)S(1)}, u32[]{:S(2)}, u32[]{:S(2)}) collective-permute-start(bf16[512,768]{1,0:T(8,128)(2,1)S(1)} %convolution_convert_fusion.3), channel_id=1, source_target_pairs={{0,1},{1,0},{2,3},{3,2},{4,5},{5,4},{6,7},{7,6},{8,9},{9,8},{10,11... | collective-permute-start | bytes 2359304 | tf_op jit(solution)/shard_map/ppermute | solution.py:88
  60.7 23.2 %collective-permute-start.17 = (bf16[128,768]{1,0:T(8,128)(2,1)S(1)}, bf16[128,768]{1,0:T(8,128)(2,1)S(1)}, u32[]{:S(2)}, u32[]{:S(2)}) collective-permute-start(bf16[128,768]{1,0:T(8,128)(2,1)S(1)} %get-tuple-element.49), channel_id=1, source_target_pairs={{0,8},{2,10},{4,12},{6,14},{8,0},{10,2},{12,4},{14,6},{1,9},{3,11}... | collective-permute-start | bytes 589832 | tf_op jit(solution)/shard_map/ppermute | solution.py:54
  62.6 12.1 %collective-permute-start.12 = (bf16[128,768]{1,0:T(8,128)(2,1)S(1)}, bf16[128,768]{1,0:T(8,128)(2,1)S(1)}, u32[]{:S(2)}, u32[]{:S(2)}) collective-permute-start(bf16[128,768]{1,0:T(8,128)(2,1)S(1)} %get-tuple-element.52), channel_id=1, source_target_pairs={{0,2},{2,0},{4,6},{6,4},{8,10},{10,8},{12,14},{14,12},{1,3},{3,1},... | collective-permute-start | bytes 589832 | tf_op jit(solution)/shard_map/ppermute | solution.py:54
  63.2 12.3 %collective-permute-start.13 = (bf16[128,768]{1,0:T(8,128)(2,1)S(1)}, bf16[128,768]{1,0:T(8,128)(2,1)S(1)}, u32[]{:S(2)}, u32[]{:S(2)}) collective-permute-start(bf16[128,768]{1,0:T(8,128)(2,1)S(1)} %get-tuple-element.51), channel_id=1, source_target_pairs={{0,4},{2,6},{4,0},{6,2},{8,12},{10,14},{12,8},{14,10},{1,5},{3,7},... | collective-permute-start | bytes 589832 | tf_op jit(solution)/shard_map/ppermute | solution.py:54
  63.7 20.1 %collective-permute-start.14 = (bf16[128,768]{1,0:T(8,128)(2,1)S(1)}, bf16[128,768]{1,0:T(8,128)(2,1)S(1)}, u32[]{:S(2)}, u32[]{:S(2)}) collective-permute-start(bf16[128,768]{1,0:T(8,128)(2,1)S(1)} %get-tuple-element.50), channel_id=1, source_target_pairs={{0,6},{2,4},{4,2},{6,0},{8,14},{10,12},{12,10},{14,8},{1,7},{3,5},... | collective-permute-start | bytes 589832 | tf_op jit(solution)/shard_map/ppermute | solution.py:54
  66.1 17.8 %collective-permute-start.18 = (bf16[128,768]{1,0:T(8,128)(2,1)S(1)}, bf16[128,768]{1,0:T(8,128)(2,1)S(1)}, u32[]{:S(2)}, u32[]{:S(2)}) collective-permute-start(bf16[128,768]{1,0:T(8,128)(2,1)S(1)} %get-tuple-element.48), channel_id=1, source_target_pairs={{0,10},{2,8},{4,14},{6,12},{8,2},{10,0},{12,6},{14,4},{1,11},{3,9}... | collective-permute-start | bytes 589832 | tf_op jit(solution)/shard_map/ppermute | solution.py:54
  74.7 9.6 %collective-permute-start.19 = (bf16[128,768]{1,0:T(8,128)(2,1)S(1)}, bf16[128,768]{1,0:T(8,128)(2,1)S(1)}, u32[]{:S(2)}, u32[]{:S(2)}) collective-permute-start(bf16[128,768]{1,0:T(8,128)(2,1)S(1)} %get-tuple-element.47), channel_id=1, source_target_pairs={{0,12},{2,14},{4,8},{6,10},{8,4},{10,6},{12,0},{14,2},{1,13},{3,15... | collective-permute-start | bytes 589832 | tf_op jit(solution)/shard_map/ppermute | solution.py:54
  75.6 10.6 %collective-permute-start.20 = (bf16[128,768]{1,0:T(8,128)(2,1)S(1)}, bf16[128,768]{1,0:T(8,128)(2,1)S(1)}, u32[]{:S(2)}, u32[]{:S(2)}) collective-permute-start(bf16[128,768]{1,0:T(8,128)(2,1)S(1)} %get-tuple-element.46), channel_id=1, source_target_pairs={{0,14},{2,12},{4,10},{6,8},{8,6},{10,4},{12,2},{14,0},{1,15},{3,13... | collective-permute-start | bytes 589832 | tf_op jit(solution)/shard_map/ppermute | solution.py:54
  84.3 4.0 %copy-start.7 = (f32[768]{0:T(1024)S(1)}, f32[768]{0:T(1024)}, u32[]{:S(2)}) copy-start(f32[768]{0:T(1024)} %param.27) | copy-start | bytes 9220
  87.1 1.2 %collective-permute-start.21 = (f32[128]{0:T(128)S(1)}, f32[128]{0:T(128)S(1)}, u32[]{:S(2)}, u32[]{:S(2)}) collective-permute-start(f32[128]{0:T(128)S(1)} %get-tuple-element.67), channel_id=1, source_target_pairs={{0,1},{1,0},{2,3},{3,2},{4,5},{5,4},{6,7},{7,6},{8,9},{9,8},{10,11... | collective-permute-start | bytes 1544 | tf_op jit(solution)/shard_map/ppermute | solution.py:96
  (7 other events, 13.1 us)

commit v19 on v17

--- a/solution.py
+++ b/solution.py
@@ -15,7 +15,9 @@
 def merged(shard, axis, join):
     if lax.axis_size(axis) == 2:
         rounded = jax.tree.map(lambda a: a.astype(jnp.bfloat16), shard)
-        other = jax.tree.map(lambda a: lax.ppermute(a, axis, perm=[(0, 1), (1, 0)]), rounded)
+        swap = [(0, 1), (1, 0)]
+        stats = lax.ppermute(jnp.stack(rounded[:2]), axis, perm=swap)
+        other = (stats[0], stats[1], lax.ppermute(rounded[2], axis, perm=swap))
         widen = lambda tree: jax.tree.map(lambda a, own: a.astype(own.dtype), tree, shard)
         return join(widen(rounded), widen(other))
     gathered = jax.tree.map(

time: 88.8 us -> 88.7 us (level)
  transfers between devices with their start and end apart: 23 -> 22, of which waited for: 13 -> 13; matrix products, arithmetic and copies ran while one was open for 14% -> 14% of each run, Pallas kernels for 0% -> 0%
where the time goes in v19:
time: 88.7 us; the launch traced here: 88.3 us
  waiting for transfers between devices  32 us (36%)
  starting transfers between devices  22.9 us (26%)
  matrix products  16.5 us (19%)
  local copies, waits for them, and re-layouts  8.9 us (10%)
  other arithmetic  7.52 us (8%)
    ppermute x14, waiting for transfers between devices, exchange(): pieces.append(lax.ppermute(chunks[step], 'el', perm=pairs))  29.3 us
    ppermute x14, starting transfers between devices, exchange(): pieces.append(lax.ppermute(chunks[step], 'el', perm=pairs))  21.3 us
    unnamed x35, local copies, waits for them, and re-layouts  4.82 us
    dot_general x8, matrix products, half_product(): return jnp.dot(x, weight, preferred_element_type=jnp.float32)  4.67 us
    dot_general x2, matrix products, one_group(): jnp.einsum('rgd,ld->rgl', head_rows, head_keys, preferred_element_type=jn...  3.85 us
    gather x1, local copies, waits for them, and re-layouts, one_group(): page_row_block = group_pages[local_table.reshape(-1)]  3.31 us
    dot_general x4, matrix products, down_product(): jnp.dot(hidden, weight, preferred_element_type=jnp.float32)  2.48 us
    dot_general x2, matrix products, one_group(): jnp.einsum('rgl,ld->rgd', soft.astype(jnp.bfloat16), head_values, preferr...  2.19 us
  transfers between devices with their start and end apart: 22, of which 13 were waited for; matrix products, arithmetic and copies ran while one was open for 14% of the time, Pallas kernels for 0%

profile of v19, /device:TPU:0, one launch (start us, length us, event | category | flops | bytes accessed | tf_op | source)
XLA Modules:
  0.0 88.3 jit_solution(1695481698340499515)
XLA Ops:
  2.8 1.2 %copy.50 = bf16[128,1536]{0,1:T(8,128)(2,1)S(1)} copy(bf16[128,1536]{1,0:T(8,128)(2,1)} %param.15) | data formatting | bytes 786432 | tf_op args[1]
  4.1 3.3 %gather_fusion = bf16[96,16,512]{2,1,0:T(8,128)(2,1)} fusion(bf16[96,16,512]{2,1,0:T(8,128)(2,1)} %bitcast.212, s32[1024]{0:T(1024)S(1)} %pad_clamp_fusion), kind=kCustom, calls=%fused_computation | custom fusion | bytes 3146112 | tf_op jit(solution)/shard_map/while/body/eval_jaxpr/gather | solution.py:172
  8.3 1.9 %fusion.3 = (f32[128,6]{0,1:T(8,128)S(1)}, f32[1536,128,6]{1,0,2:T(8,128)S(1)}) fusion(pred[128,1536]{0,1:T(8,128)(4,1)S(1)} %compare_and_fusion, bf16[128,12,128]{0,2,1:T(8,128)(2,1)S(1)} %bitcast.214, bf16[1536,512]{1,0:T(8,128)(2,1)} %bitcast.207), kind=kOutput, calls=%fused_computation.8 | convolution fusion | flops 305528064 | bytes 5508096 | tf_op jit(solution)/shard_map/while/body/eval_jaxpr/rgd,ld->rgl/dot_general | solution.py:198
  10.3 1.9 %fusion.6 = (bf16[128,6]{0,1:T(8,128)(2,1)S(1)}, f32[128,6]{0,1:T(8,128)S(1)}, f32[1536,128,6]{1,0,2:T(8,128)S(1)}) fusion(f32[1536,128,6]{1,0,2:T(8,128)S(1)} %get-tuple-element.61, f32[128,6]{0,1:T(8,128)S(1)} %get-tuple-element.60, pred[128,1536]{0,1:T(8,128)(4,1)S(1)} %compare_and_fusion, bf16[128,12,128]{0,2,1:T(8,128)(2,1)S(1)} %bitcast.215, ...), kind=kOutput, calls=%fused_computation.11 | convolution fusion | flops 310245888 | bytes 10232320 | tf_op jit(solution)/shard_map/while/body/eval_jaxpr/rgd,ld->rgl/dot_general | solution.py:198
  13.8 1.1 %fusion.29 = bf16[128,1,6,128]{0,3,2,1:T(8,128)(2,1)S(1)} fusion(f32[1536,128,6]{1,0,2:T(8,128)S(1)} %get-tuple-element.62, f32[128,6]{0,1:T(8,128)S(1)} %get-tuple-element.24, pred[128,1536]{0,1:T(8,128)(4,1)S(1)} %compare_and_fusion, bf16[1536,512]{1,0:T(8,128)(2,1)S(1)} %bitcast.209), kind=kOutput, calls=%fused_computation.44 | convolution fusion | flops 306806784 | bytes 5509120 | tf_op jit(solution)/shard_map/while/body/eval_jaxpr/rgl,ld->rgd/dot_general | solution.py:204
  14.9 1.1 %fusion.32 = bf16[128,1,6,128]{0,3,2,1:T(8,128)(2,1)S(1)} fusion(f32[1536,128,6]{1,0,2:T(8,128)S(1)} %get-tuple-element.61, f32[128,6]{0,1:T(8,128)S(1)} %get-tuple-element.60, pred[128,1536]{0,1:T(8,128)(4,1)S(1)} %compare_and_fusion, bf16[1536,512]{1,0:T(8,128)(2,1)S(1)} %bitcast.210), kind=kOutput, calls=%fused_computation.45 | convolution fusion | flops 306806784 | bytes 5509120 | tf_op jit(solution)/shard_map/while/body/eval_jaxpr/rgl,ld->rgd/dot_general | solution.py:204
  18.8 1.2 %divide_convert_fusion = bf16[128,2,6,128]{0,3,2,1:T(8,128)(2,1)S(1)} fusion(bf16[128,2,6,128]{0,3,2,1:T(8,128)(2,1)} %collective-permute-done.1, f32[128,2,6]{0,2,1:T(8,128)S(1)} %get-tuple-element.55, f32[128,2,6]{0,2,1:T(8,128)S(1)} %get-tuple-element.54, f32[128,2,6]{0,2,1:T(8,128)S(1)} %get-tuple-element.53, bf16[128,1,6,128]{0,3,2,1:T(8,128)(2,1)S(1)} %fusion.29, ...), kind=kLoop, calls=%fused_computation.50 | loop fusion | flops 1572864 | bytes 1198080 | tf_op jit(solution)/shard_map/convert_element_type | solution.py:224
  20.0 1.5 %multiply_reduce_fusion.1 = (f32[128]{0:T(128)S(1)}, f32[128,768]{1,0:T(8,128)S(1)}) fusion(bf16[128,1536]{0,1:T(8,128)(2,1)S(1)} %bitcast.213, bf16[1536,768]{1,0:T(8,128)(2,1)S(1)} %copy-done, bf16[128,768]{1,0:T(8,128)(2,1)} %param.14), kind=kOutput, calls=%fused_computation.90 | convolution fusion | flops 302382976 | bytes 3342848 | tf_op jit(solution)/shard_map/dot_general | solution.py:226
  23.5 2.8 %collective-permute-start.3 = (bf16[128,768]{1,0:T(8,128)(2,1)S(1)}, bf16[128,768]{1,0:T(8,128)(2,1)S(1)}, u32[]{:S(2)}, u32[]{:S(2)}) collective-permute-start(bf16[128,768]{1,0:T(8,128)(2,1)S(1)} %get-tuple-element.45), channel_id=1, source_target_pairs={{0,2},{2,0},{4,6},{6,4},{8,10},{10,8},{12,14},{14,12},{1,3},{3,1},... | collective-permute-start | bytes 589832 | tf_op jit(solution)/shard_map/ppermute | solution.py:54
  26.3 1.5 %collective-permute-start.4 = (bf16[128,768]{1,0:T(8,128)(2,1)S(1)}, bf16[128,768]{1,0:T(8,128)(2,1)S(1)}, u32[]{:S(2)}, u32[]{:S(2)}) collective-permute-start(bf16[128,768]{1,0:T(8,128)(2,1)S(1)} %get-tuple-element.44), channel_id=1, source_target_pairs={{0,4},{2,6},{4,0},{6,2},{8,12},{10,14},{12,8},{14,10},{1,5},{3,7},... | collective-permute-start | bytes 589832 | tf_op jit(solution)/shard_map/ppermute | solution.py:54
  27.8 2.0 %collective-permute-start.6 = (bf16[128,768]{1,0:T(8,128)(2,1)S(1)}, bf16[128,768]{1,0:T(8,128)(2,1)S(1)}, u32[]{:S(2)}, u32[]{:S(2)}) collective-permute-start(bf16[128,768]{1,0:T(8,128)(2,1)S(1)} %get-tuple-element.40), channel_id=1, source_target_pairs={{0,8},{2,10},{4,12},{6,14},{8,0},{10,2},{12,4},{14,6},{1,9},{3,11}... | collective-permute-start | bytes 589832 | tf_op jit(solution)/shard_map/ppermute | solution.py:54
  29.8 1.4 %collective-permute-start.7 = (bf16[128,768]{1,0:T(8,128)(2,1)S(1)}, bf16[128,768]{1,0:T(8,128)(2,1)S(1)}, u32[]{:S(2)}, u32[]{:S(2)}) collective-permute-start(bf16[128,768]{1,0:T(8,128)(2,1)S(1)} %get-tuple-element.29), channel_id=1, source_target_pairs={{0,10},{2,8},{4,14},{6,12},{8,2},{10,0},{12,6},{14,4},{1,11},{3,9}... | collective-permute-start | bytes 589832 | tf_op jit(solution)/shard_map/ppermute | solution.py:54
  31.9 3.1 %collective-permute-start.8 = (bf16[128,768]{1,0:T(8,128)(2,1)S(1)}, bf16[128,768]{1,0:T(8,128)(2,1)S(1)}, u32[]{:S(2)}, u32[]{:S(2)}) collective-permute-start(bf16[128,768]{1,0:T(8,128)(2,1)S(1)} %get-tuple-element.28), channel_id=1, source_target_pairs={{0,12},{2,14},{4,8},{6,10},{8,4},{10,6},{12,0},{14,2},{1,13},{3,15... | collective-permute-start | bytes 589832 | tf_op jit(solution)/shard_map/ppermute | solution.py:54
  35.7 1.3 %collective-permute-start.9 = (bf16[128,768]{1,0:T(8,128)(2,1)S(1)}, bf16[128,768]{1,0:T(8,128)(2,1)S(1)}, u32[]{:S(2)}, u32[]{:S(2)}) collective-permute-start(bf16[128,768]{1,0:T(8,128)(2,1)S(1)} %get-tuple-element.27), channel_id=1, source_target_pairs={{0,14},{2,12},{4,10},{6,8},{8,6},{10,4},{12,2},{14,0},{1,15},{3,13... | collective-permute-start | bytes 589832 | tf_op jit(solution)/shard_map/ppermute | solution.py:54
  37.0 3.4 %collective-permute-done.5 = bf16[128,768]{1,0:T(8,128)(2,1)S(1)} collective-permute-done((bf16[128,768]{1,0:T(8,128)(2,1)S(1)}, bf16[128,768]{1,0:T(8,128)(2,1)S(1)}, u32[]{:S(2)}, u32[]{:S(2)}) %collective-permute-start.5) | collective-permute-done | bytes 196640 | tf_op jit(solution)/shard_map/ppermute | solution.py:54
  41.3 4.2 %collective-permute-done.8 = bf16[128,768]{1,0:T(8,128)(2,1)S(1)} collective-permute-done((bf16[128,768]{1,0:T(8,128)(2,1)S(1)}, bf16[128,768]{1,0:T(8,128)(2,1)S(1)}, u32[]{:S(2)}, u32[]{:S(2)}) %collective-permute-start.8) | collective-permute-done | bytes 196640 | tf_op jit(solution)/shard_map/ppermute | solution.py:54
  45.5 3.6 %collective-permute-done.9 = bf16[128,768]{1,0:T(8,128)(2,1)S(1)} collective-permute-done((bf16[128,768]{1,0:T(8,128)(2,1)S(1)}, bf16[128,768]{1,0:T(8,128)(2,1)S(1)}, u32[]{:S(2)}, u32[]{:S(2)}) %collective-permute-start.9) | collective-permute-done | bytes 196640 | tf_op jit(solution)/shard_map/ppermute | solution.py:54
  59.9 1.6 %collective-permute-start.17 = (bf16[128,768]{1,0:T(8,128)(2,1)S(1)}, bf16[128,768]{1,0:T(8,128)(2,1)S(1)}, u32[]{:S(2)}, u32[]{:S(2)}) collective-permute-start(bf16[128,768]{1,0:T(8,128)(2,1)S(1)} %get-tuple-element.49), channel_id=1, source_target_pairs={{0,8},{2,10},{4,12},{6,14},{8,0},{10,2},{12,4},{14,6},{1,9},{3,11}... | collective-permute-start | bytes 589832 | tf_op jit(solution)/shard_map/ppermute | solution.py:54
  62.9 2.4 %collective-permute-start.14 = (bf16[128,768]{1,0:T(8,128)(2,1)S(1)}, bf16[128,768]{1,0:T(8,128)(2,1)S(1)}, u32[]{:S(2)}, u32[]{:S(2)}) collective-permute-start(bf16[128,768]{1,0:T(8,128)(2,1)S(1)} %get-tuple-element.50), channel_id=1, source_target_pairs={{0,6},{2,4},{4,2},{6,0},{8,14},{10,12},{12,10},{14,8},{1,7},{3,5},... | collective-permute-start | bytes 589832 | tf_op jit(solution)/shard_map/ppermute | solution.py:54
  66.4 7.5 %collective-permute-done.12 = bf16[128,768]{1,0:T(8,128)(2,1)S(1)} collective-permute-done((bf16[128,768]{1,0:T(8,128)(2,1)S(1)}, bf16[128,768]{1,0:T(8,128)(2,1)S(1)}, u32[]{:S(2)}, u32[]{:S(2)}) %collective-permute-start.12) | collective-permute-done | bytes 196640 | tf_op jit(solution)/shard_map/ppermute | solution.py:54
  74.8 2.1 %collective-permute-start.20 = (bf16[128,768]{1,0:T(8,128)(2,1)S(1)}, bf16[128,768]{1,0:T(8,128)(2,1)S(1)}, u32[]{:S(2)}, u32[]{:S(2)}) collective-permute-start(bf16[128,768]{1,0:T(8,128)(2,1)S(1)} %get-tuple-element.46), channel_id=1, source_target_pairs={{0,14},{2,12},{4,10},{6,8},{8,6},{10,4},{12,2},{14,0},{1,15},{3,13... | collective-permute-start | bytes 589832 | tf_op jit(solution)/shard_map/ppermute | solution.py:54
  76.9 6.1 %collective-permute-done.14 = bf16[128,768]{1,0:T(8,128)(2,1)S(1)} collective-permute-done((bf16[128,768]{1,0:T(8,128)(2,1)S(1)}, bf16[128,768]{1,0:T(8,128)(2,1)S(1)}, u32[]{:S(2)}, u32[]{:S(2)}) %collective-permute-start.14) | collective-permute-done | bytes 196640 | tf_op jit(solution)/shard_map/ppermute | solution.py:54
  83.5 1.9 %collective-permute-done.20 = bf16[128,768]{1,0:T(8,128)(2,1)S(1)} collective-permute-done((bf16[128,768]{1,0:T(8,128)(2,1)S(1)}, bf16[128,768]{1,0:T(8,128)(2,1)S(1)}, u32[]{:S(2)}, u32[]{:S(2)}) %collective-permute-start.20) | collective-permute-done | bytes 196640 | tf_op jit(solution)/shard_map/ppermute | solution.py:54
  86.4 1.1 %collective-permute-done.21 = f32[128]{0:T(128)S(1)} collective-permute-done((f32[128]{0:T(128)S(1)}, f32[128]{0:T(128)S(1)}, u32[]{:S(2)}, u32[]{:S(2)}) %collective-permute-start.21) | collective-permute-done | bytes 544 | tf_op jit(solution)/shard_map/ppermute | solution.py:96
  (112 shorter events, 28.4 us)
Async XLA Ops:
  0.0 20.0 %copy-start = (bf16[1536,768]{1,0:T(8,128)(2,1)S(1)}, bf16[1536,768]{1,0:T(8,128)(2,1)}, u32[]{:S(2)}) copy-start(bf16[1536,768]{1,0:T(8,128)(2,1)} %param.20) | copy-start | bytes 7077892
  13.2 4.9 %collective-permute-start = (bf16[2,128,2,6]{1,3,2,0:T(8,128)(2,1)S(1)}, bf16[2,128,2,6]{1,3,2,0:T(8,128)(2,1)S(1)}, u32[]{:S(2)}, u32[]{:S(2)}) collective-permute-start(bf16[2,128,2,6]{1,3,2,0:T(8,128)(2,1)S(1)} %maximum_maximum_fusion), channel_id=1, source_target_pairs={{0,1},{1,0},{2,3},{3,2},{4,5},{5,4},{6,7},{7,6},{8,9},{9,8},{10,11... | collective-permute-start | bytes 18440 | tf_op jit(solution)/shard_map/ppermute | solution.py:19
  16.8 2.1 %collective-permute-start.1 = (bf16[128,2,6,128]{0,3,2,1:T(8,128)(2,1)}, bf16[128,2,6,128]{0,3,2,1:T(8,128)(2,1)}, u32[]{:S(2)}, u32[]{:S(2)}) collective-permute-start(bf16[128,2,6,128]{0,3,2,1:T(8,128)(2,1)} %pad_maximum_fusion), channel_id=1, source_target_pairs={{0,1},{1,0},{2,3},{3,2},{4,5},{5,4},{6,7},{7,6},{8,9},{9,8},{10,11... | collective-permute-start | bytes 1179656 | tf_op jit(solution)/shard_map/ppermute | solution.py:20
  21.6 1.2 %collective-permute-start.2 = (f32[128]{0:T(128)S(1)}, f32[128]{0:T(128)S(1)}, u32[]{:S(2)}, u32[]{:S(2)}) collective-permute-start(f32[128]{0:T(128)S(1)} %get-tuple-element.63), channel_id=1, source_target_pairs={{0,1},{1,0},{2,3},{3,2},{4,5},{5,4},{6,7},{7,6},{8,9},{9,8},{10,11... | collective-permute-start | bytes 1544 | tf_op jit(solution)/shard_map/ppermute | solution.py:96
  23.5 8.4 %collective-permute-start.3 = (bf16[128,768]{1,0:T(8,128)(2,1)S(1)}, bf16[128,768]{1,0:T(8,128)(2,1)S(1)}, u32[]{:S(2)}, u32[]{:S(2)}) collective-permute-start(bf16[128,768]{1,0:T(8,128)(2,1)S(1)} %get-tuple-element.45), channel_id=1, source_target_pairs={{0,2},{2,0},{4,6},{6,4},{8,10},{10,8},{12,14},{14,12},{1,3},{3,1},... | collective-permute-start | bytes 589832 | tf_op jit(solution)/shard_map/ppermute | solution.py:54
  26.3 9.4 %collective-permute-start.4 = (bf16[128,768]{1,0:T(8,128)(2,1)S(1)}, bf16[128,768]{1,0:T(8,128)(2,1)S(1)}, u32[]{:S(2)}, u32[]{:S(2)}) collective-permute-start(bf16[128,768]{1,0:T(8,128)(2,1)S(1)} %get-tuple-element.44), channel_id=1, source_target_pairs={{0,4},{2,6},{4,0},{6,2},{8,12},{10,14},{12,8},{14,10},{1,5},{3,7},... | collective-permute-start | bytes 589832 | tf_op jit(solution)/shard_map/ppermute | solution.py:54
  27.8 12.6 %collective-permute-start.5 = (bf16[128,768]{1,0:T(8,128)(2,1)S(1)}, bf16[128,768]{1,0:T(8,128)(2,1)S(1)}, u32[]{:S(2)}, u32[]{:S(2)}) collective-permute-start(bf16[128,768]{1,0:T(8,128)(2,1)S(1)} %get-tuple-element.42), channel_id=1, source_target_pairs={{0,6},{2,4},{4,2},{6,0},{8,14},{10,12},{12,10},{14,8},{1,7},{3,5},... | collective-permute-start | bytes 589832 | tf_op jit(solution)/shard_map/ppermute | solution.py:54
  27.8 12.6 %collective-permute-start.6 = (bf16[128,768]{1,0:T(8,128)(2,1)S(1)}, bf16[128,768]{1,0:T(8,128)(2,1)S(1)}, u32[]{:S(2)}, u32[]{:S(2)}) collective-permute-start(bf16[128,768]{1,0:T(8,128)(2,1)S(1)} %get-tuple-element.40), channel_id=1, source_target_pairs={{0,8},{2,10},{4,12},{6,14},{8,0},{10,2},{12,4},{14,6},{1,9},{3,11}... | collective-permute-start | bytes 589832 | tf_op jit(solution)/shard_map/ppermute | solution.py:54
  29.8 11.4 %collective-permute-start.7 = (bf16[128,768]{1,0:T(8,128)(2,1)S(1)}, bf16[128,768]{1,0:T(8,128)(2,1)S(1)}, u32[]{:S(2)}, u32[]{:S(2)}) collective-permute-start(bf16[128,768]{1,0:T(8,128)(2,1)S(1)} %get-tuple-element.29), channel_id=1, source_target_pairs={{0,10},{2,8},{4,14},{6,12},{8,2},{10,0},{12,6},{14,4},{1,11},{3,9}... | collective-permute-start | bytes 589832 | tf_op jit(solution)/shard_map/ppermute | solution.py:54
  31.9 13.6 %collective-permute-start.8 = (bf16[128,768]{1,0:T(8,128)(2,1)S(1)}, bf16[128,768]{1,0:T(8,128)(2,1)S(1)}, u32[]{:S(2)}, u32[]{:S(2)}) collective-permute-start(bf16[128,768]{1,0:T(8,128)(2,1)S(1)} %get-tuple-element.28), channel_id=1, source_target_pairs={{0,12},{2,14},{4,8},{6,10},{8,4},{10,6},{12,0},{14,2},{1,13},{3,15... | collective-permute-start | bytes 589832 | tf_op jit(solution)/shard_map/ppermute | solution.py:54
  35.7 13.4 %collective-permute-start.9 = (bf16[128,768]{1,0:T(8,128)(2,1)S(1)}, bf16[128,768]{1,0:T(8,128)(2,1)S(1)}, u32[]{:S(2)}, u32[]{:S(2)}) collective-permute-start(bf16[128,768]{1,0:T(8,128)(2,1)S(1)} %get-tuple-element.27), channel_id=1, source_target_pairs={{0,14},{2,12},{4,10},{6,8},{8,6},{10,4},{12,2},{14,0},{1,15},{3,13... | collective-permute-start | bytes 589832 | tf_op jit(solution)/shard_map/ppermute | solution.py:54
  49.3 4.2 %collective-permute-start.15 = (bf16[512,768]{1,0:T(8,128)(2,1)S(1)}, bf16[512,768]{1,0:T(8,128)(2,1)S(1)}, u32[]{:S(2)}, u32[]{:S(2)}) collective-permute-start(bf16[512,768]{1,0:T(8,128)(2,1)S(1)} %get-tuple-element.25), channel_id=1, source_target_pairs={{0,1},{1,0},{2,3},{3,2},{4,5},{5,4},{6,7},{7,6},{8,9},{9,8},{10,11... | collective-permute-start | bytes 2359304 | tf_op jit(solution)/shard_map/ppermute | solution.py:72
  51.0 5.7 %collective-permute-start.10 = (bf16[512,768]{1,0:T(8,128)(2,1)S(1)}, bf16[512,768]{1,0:T(8,128)(2,1)S(1)}, u32[]{:S(2)}, u32[]{:S(2)}) collective-permute-start(bf16[512,768]{1,0:T(8,128)(2,1)S(1)} %get-tuple-element.26), channel_id=1, source_target_pairs={{0,1},{1,0},{2,3},{3,2},{4,5},{5,4},{6,7},{7,6},{8,9},{9,8},{10,11... | collective-permute-start | bytes 2359304 | tf_op jit(solution)/shard_map/ppermute | solution.py:72
  56.1 3.6 %collective-permute-start.16 = (bf16[512,768]{1,0:T(8,128)(2,1)S(1)}, bf16[512,768]{1,0:T(8,128)(2,1)S(1)}, u32[]{:S(2)}, u32[]{:S(2)}) collective-permute-start(bf16[512,768]{1,0:T(8,128)(2,1)S(1)} %convolution_convert_fusion.1), channel_id=1, source_target_pairs={{0,1},{1,0},{2,3},{3,2},{4,5},{5,4},{6,7},{7,6},{8,9},{9,8},{10,11... | collective-permute-start | bytes 2359304 | tf_op jit(solution)/shard_map/ppermute | solution.py:88
  58.5 3.1 %collective-permute-start.11 = (bf16[512,768]{1,0:T(8,128)(2,1)S(1)}, bf16[512,768]{1,0:T(8,128)(2,1)S(1)}, u32[]{:S(2)}, u32[]{:S(2)}) collective-permute-start(bf16[512,768]{1,0:T(8,128)(2,1)S(1)} %convolution_convert_fusion.3), channel_id=1, source_target_pairs={{0,1},{1,0},{2,3},{3,2},{4,5},{5,4},{6,7},{7,6},{8,9},{9,8},{10,11... | collective-permute-start | bytes 2359304 | tf_op jit(solution)/shard_map/ppermute | solution.py:88
  59.9 23.1 %collective-permute-start.17 = (bf16[128,768]{1,0:T(8,128)(2,1)S(1)}, bf16[128,768]{1,0:T(8,128)(2,1)S(1)}, u32[]{:S(2)}, u32[]{:S(2)}) collective-permute-start(bf16[128,768]{1,0:T(8,128)(2,1)S(1)} %get-tuple-element.49), channel_id=1, source_target_pairs={{0,8},{2,10},{4,12},{6,14},{8,0},{10,2},{12,4},{14,6},{1,9},{3,11}... | collective-permute-start | bytes 589832 | tf_op jit(solution)/shard_map/ppermute | solution.py:54
  61.8 12.1 %collective-permute-start.12 = (bf16[128,768]{1,0:T(8,128)(2,1)S(1)}, bf16[128,768]{1,0:T(8,128)(2,1)S(1)}, u32[]{:S(2)}, u32[]{:S(2)}) collective-permute-start(bf16[128,768]{1,0:T(8,128)(2,1)S(1)} %get-tuple-element.52), channel_id=1, source_target_pairs={{0,2},{2,0},{4,6},{6,4},{8,10},{10,8},{12,14},{14,12},{1,3},{3,1},... | collective-permute-start | bytes 589832 | tf_op jit(solution)/shard_map/ppermute | solution.py:54
  62.4 12.3 %collective-permute-start.13 = (bf16[128,768]{1,0:T(8,128)(2,1)S(1)}, bf16[128,768]{1,0:T(8,128)(2,1)S(1)}, u32[]{:S(2)}, u32[]{:S(2)}) collective-permute-start(bf16[128,768]{1,0:T(8,128)(2,1)S(1)} %get-tuple-element.51), channel_id=1, source_target_pairs={{0,4},{2,6},{4,0},{6,2},{8,12},{10,14},{12,8},{14,10},{1,5},{3,7},... | collective-permute-start | bytes 589832 | tf_op jit(solution)/shard_map/ppermute | solution.py:54
  62.9 20.1 %collective-permute-start.14 = (bf16[128,768]{1,0:T(8,128)(2,1)S(1)}, bf16[128,768]{1,0:T(8,128)(2,1)S(1)}, u32[]{:S(2)}, u32[]{:S(2)}) collective-permute-start(bf16[128,768]{1,0:T(8,128)(2,1)S(1)} %get-tuple-element.50), channel_id=1, source_target_pairs={{0,6},{2,4},{4,2},{6,0},{8,14},{10,12},{12,10},{14,8},{1,7},{3,5},... | collective-permute-start | bytes 589832 | tf_op jit(solution)/shard_map/ppermute | solution.py:54
  65.3 17.7 %collective-permute-start.18 = (bf16[128,768]{1,0:T(8,128)(2,1)S(1)}, bf16[128,768]{1,0:T(8,128)(2,1)S(1)}, u32[]{:S(2)}, u32[]{:S(2)}) collective-permute-start(bf16[128,768]{1,0:T(8,128)(2,1)S(1)} %get-tuple-element.48), channel_id=1, source_target_pairs={{0,10},{2,8},{4,14},{6,12},{8,2},{10,0},{12,6},{14,4},{1,11},{3,9}... | collective-permute-start | bytes 589832 | tf_op jit(solution)/shard_map/ppermute | solution.py:54
  73.9 9.6 %collective-permute-start.19 = (bf16[128,768]{1,0:T(8,128)(2,1)S(1)}, bf16[128,768]{1,0:T(8,128)(2,1)S(1)}, u32[]{:S(2)}, u32[]{:S(2)}) collective-permute-start(bf16[128,768]{1,0:T(8,128)(2,1)S(1)} %get-tuple-element.47), channel_id=1, source_target_pairs={{0,12},{2,14},{4,8},{6,10},{8,4},{10,6},{12,0},{14,2},{1,13},{3,15... | collective-permute-start | bytes 589832 | tf_op jit(solution)/shard_map/ppermute | solution.py:54
  74.8 10.6 %collective-permute-start.20 = (bf16[128,768]{1,0:T(8,128)(2,1)S(1)}, bf16[128,768]{1,0:T(8,128)(2,1)S(1)}, u32[]{:S(2)}, u32[]{:S(2)}) collective-permute-start(bf16[128,768]{1,0:T(8,128)(2,1)S(1)} %get-tuple-element.46), channel_id=1, source_target_pairs={{0,14},{2,12},{4,10},{6,8},{8,6},{10,4},{12,2},{14,0},{1,15},{3,13... | collective-permute-start | bytes 589832 | tf_op jit(solution)/shard_map/ppermute | solution.py:54
  83.5 4.0 %copy-start.7 = (f32[768]{0:T(1024)S(1)}, f32[768]{0:T(1024)}, u32[]{:S(2)}) copy-start(f32[768]{0:T(1024)} %param.27) | copy-start | bytes 9220
  86.3 1.2 %collective-permute-start.21 = (f32[128]{0:T(128)S(1)}, f32[128]{0:T(128)S(1)}, u32[]{:S(2)}, u32[]{:S(2)}) collective-permute-start(f32[128]{0:T(128)S(1)} %get-tuple-element.65), channel_id=1, source_target_pairs={{0,1},{1,0},{2,3},{3,2},{4,5},{5,4},{6,7},{7,6},{8,9},{9,8},{10,11... | collective-permute-start | bytes 1544 | tf_op jit(solution)/shard_map/ppermute | solution.py:96
  (7 other events, 13.1 us)
